TPU v7x, 256 devices: a whole 4x4x8 slice. The times are simulated.
256 devices in a mesh: tm: 4 (over y), space: 64 (over z, x, core).
Axes of the slice: x: 4, y: 4, z: 8, core: 2. Of those that a mesh axis runs over, the one named last changes fastest.
Arguments:
- fine_nodes: float32 [4, 3, 128, 128, 256], P('tm', None, 'space'), may hold values from -1.25 to 1.25
- fine_implicit: float32 [4, 3, 128, 128, 256], P('tm', None, 'space'), may hold values from -18 to 18
Outputs:
- new_nodes: float32 [4, 3, 128, 128, 256], P('tm', None, 'space')
- new_implicit: float32 [4, 2, 128, 128, 256], P('tm', None, 'space')
All inputs are finite; a program needn't handle non-finite values.
Results may differ from a plain program's by a relative error of at most 0.00014.
Values sent between devices are 32-bit elements; how exact they have to be, the bound alone decides.
No kernel may reach another device: no remote copies, remote signals or barrier semaphores. Data moves between devices by JAX's collectives and lax.ppermute only.
A program may use at most 128 MiB of HBM per device.

v0:
```python
import math

import jax
import jax.numpy as jnp
from jax import lax
from jax.sharding import PartitionSpec as P

WEIGHTS = ((5.0 / 24.0, 1.0 / 3.0, -1.0 / 24.0), (-1.0 / 24.0, 1.0 / 3.0, 5.0 / 24.0))
EPS2 = 2.0
HIGHEST = lax.Precision.HIGHEST


def react(u):
    return u - u * u * u


def real_basis(size):
    rows = lax.broadcasted_iota(jnp.int32, (size, size), 0)
    cells = lax.broadcasted_iota(jnp.int32, (size, size), 1)
    half = size // 2
    freq = jnp.where(rows <= half, rows, rows - half)
    phase = (freq * cells % size).astype(jnp.float32) * (2.0 * math.pi / size)
    scale = jnp.where((rows == 0) | (rows == half), 1.0 / math.sqrt(size), math.sqrt(2.0 / size))
    return jnp.where(rows <= half, jnp.cos(phase), jnp.sin(phase)) * scale


def wave_square(index, size):
    half = size // 2
    freq = jnp.where(index <= half, index, index - half).astype(jnp.float32)
    kappa = freq * (2.0 * math.pi / size)
    return kappa * kappa


def interp_matrix(size):
    fine_rows = lax.broadcasted_iota(jnp.int32, (2 * size, size), 0)
    coarse_cols = lax.broadcasted_iota(jnp.int32, (2 * size, size), 1)
    base = fine_rows // 2
    odd = fine_rows % 2
    take_base = jnp.where(coarse_cols == base, jnp.where(odd == 0, 1.0, 0.5), 0.0)
    take_next = jnp.where((odd == 1) & (coarse_cols == (base + 1) % size), 0.5, 0.0)
    return (take_base + take_next).astype(jnp.float32)


def spectral_solve(rhs, basis_x, basis_y, basis_z, factor):
    planes, size_y, size_z = rhs.shape
    flat = jnp.dot(rhs.reshape(planes * size_y, size_z), basis_z.T, precision=HIGHEST)
    field = flat.reshape(planes, size_y, size_z)
    field = jnp.einsum("ky,xyz->kxz", basis_y, field, precision=HIGHEST)
    field = lax.all_to_all(field, "space", split_axis=0, concat_axis=1, tiled=True)
    field = jnp.einsum("kx,yxz->kyz", basis_x, field, precision=HIGHEST) * factor
    field = jnp.einsum("kx,kyz->xyz", basis_x, field, precision=HIGHEST)
    field = lax.all_to_all(field, "space", split_axis=0, concat_axis=1, tiled=True)
    field = jnp.matmul(basis_y.T, field, precision=HIGHEST)
    flat = jnp.dot(field.reshape(planes * size_y, size_z), basis_z, precision=HIGHEST)
    return flat.reshape(planes, size_y, size_z)


def pair_average(size):
    rows = lax.broadcasted_iota(jnp.int32, (size, size // 2), 0)
    cols = lax.broadcasted_iota(jnp.int32, (size, size // 2), 1)
    return jnp.where(rows // 2 == cols, 0.5, 0.0).astype(jnp.float32)


def restrict(fields):
    count, planes, size_y, size_z = fields.shape
    pairs = fields.reshape(count, planes // 2, 2, size_y, size_z)
    summed = (pairs[:, :, 0] + pairs[:, :, 1]) * 0.5
    flat = jnp.dot(summed.reshape(-1, size_z), pair_average(size_z), precision=HIGHEST)
    field = flat.reshape(count, planes // 2, size_y, size_z // 2)
    return jnp.einsum("ya,kpyz->kpaz", pair_average(size_y), field, precision=HIGHEST)


def fetch(value, offset, back):
    count = lax.axis_size("space")
    if back == 0:
        pairs = [((target + offset) % count, target) for target in range(count)]
        return lax.ppermute(value, "space", pairs)
    slices = lax.axis_size("tm")
    pairs = [
        ((slot - back) * count + (target + offset) % count, slot * count + target)
        for slot in range(back, slices)
        for target in range(count)
    ]
    return lax.ppermute(value, ("tm", "space"), pairs)


def halo(groups, back=0):
    local = groups[0][0].shape[0]
    reach = []
    for block, low, high in groups:
        reach.append((-(-low // local), -(-high // local)))
    lowest = max(r[0] for r in reach)
    highest = max(r[1] for r in reach)
    pieces = [[] for _ in groups]
    for offset in range(-lowest, highest + 1):
        wanted = [i for i, r in enumerate(reach) if -r[0] <= offset <= r[1]]
        if offset == 0 and back == 0:
            for i in wanted:
                pieces[i].append(groups[i][0])
            continue
        sizes = [groups[i][0].shape[1] for i in wanted]
        joined = jnp.concatenate([groups[i][0] for i in wanted], axis=1)
        got = fetch(joined, offset, back)
        at = 0
        for i, size in zip(wanted, sizes):
            pieces[i].append(got[:, at:at + size])
            at += size
    result = []
    for i, (block, low, high) in enumerate(groups):
        full = jnp.concatenate(pieces[i], axis=0)
        begin = reach[i][0] * local - low
        result.append(full[begin:begin + local + low + high])
    return result


def coarse_rate(ext):
    mid = ext[1:-1]
    lap = ext[2:] + ext[:-2]
    lap = lap + jnp.roll(mid, -1, 1) + jnp.roll(mid, 1, 1)
    lap = lap + jnp.roll(mid, -1, 2) + jnp.roll(mid, 1, 2)
    return EPS2 * ((lap - 6.0 * mid) * 0.25) + react(mid)


def spread(values, following, axis):
    middle = 0.5 * (values + following)
    both = jnp.stack([values, middle], axis=axis + 1)
    shape = list(values.shape)
    shape[axis] = shape[axis] * 2
    return both.reshape(shape)


def refine(stacked):
    matrix_y = interp_matrix(stacked.shape[2])
    matrix_z = interp_matrix(stacked.shape[3])
    both = jnp.einsum("kayc,zc->kayz", stacked, matrix_z, precision=HIGHEST)
    both = jnp.einsum("Yy,kayz->kaYz", matrix_y, both, precision=HIGHEST)
    planes = stacked.shape[1] - 1
    return spread(both[:, :planes], both[:, 1:], 1)


def coarse_sweep(start, rates, sums):
    first = start[1:-1] + 0.25 * (coarse_rate(start) - rates[0]) + sums[0]
    second = first[1:-1] + 0.25 * (coarse_rate(first) - rates[1]) + sums[1]
    return (first[1:-1], second)


def on_device(fine_nodes, fine_implicit):
    nodes = fine_nodes[0]
    implicit = fine_implicit[0]
    planes, size_y, size_z = (nodes.shape[1], nodes.shape[2], nodes.shape[3])
    devices = lax.axis_size("space")
    size_x = planes * devices
    local_y = size_y // devices
    basis_x = real_basis(size_x)
    basis_y = real_basis(size_y)
    basis_z = real_basis(size_z)
    columns = lax.axis_index("space") * local_y + lax.iota(jnp.int32, local_y)
    lam = wave_square(lax.iota(jnp.int32, size_x), size_x)[:, None, None]
    lam = lam + wave_square(columns, size_y)[None, :, None]
    lam = lam + wave_square(lax.iota(jnp.int32, size_z), size_z)[None, None, :]
    factor = 1.0 / (1.0 + 0.5 * lam)
    explicit_old = react(nodes)
    rates_old = explicit_old + implicit
    values = [nodes[0]]
    terms = [implicit[0]]
    for m in range(2):
        w = WEIGHTS[m]
        quad = 0.5 * (w[0] * rates_old[0] + w[1] * rates_old[1] + w[2] * rates_old[2])
        rhs = (
            values[m] + 0.25 * (react(values[m]) - explicit_old[m]) - 0.25 * implicit[m + 1] + quad
        )
        solved = spectral_solve(rhs, basis_x, basis_y, basis_z, factor)
        values.append(solved)
        terms.append((solved - rhs) * 4.0)
    fresh = jnp.stack(values)
    rates_new = react(fresh) + jnp.stack(terms)
    sums = [0.5 * (w[0] * rates_new[0] + w[1] * rates_new[1] + w[2] * rates_new[2]) for w in WEIGHTS]
    coarse = restrict(jnp.stack([values[0], values[1], values[2], sums[0], sums[1]]))
    by_plane = jnp.moveaxis(coarse, 1, 0)
    slot = lax.axis_index("tm")
    slices = lax.axis_size("tm")
    start_c, rest = halo([(by_plane[:, 0:1], 2, 3), (by_plane[:, 1:5], 1, 2)])
    start_c = start_c[:, 0]
    rates_c = (coarse_rate(start_c), coarse_rate(rest[:, 0]))
    sums_c = (rest[:, 2], rest[1:-1, 3])
    coarse_one = rest[1:-1, 0]
    coarse_two = rest[1:-1, 1]
    local = planes // 2
    previous_two = fetch(values[2], 0, 1)
    previous_coarse_two = fetch(coarse_two, 0, 1)
    start = start_c
    for section in range(slices - 1):
        first, second = coarse_sweep(start, rates_c, sums_c)
        received = halo([(second[:local][:, None], 2, 3)], back=1)[0][:, 0]
        start = jnp.where(slot == 0, start_c, received)
    first, second = coarse_sweep(start, rates_c, sums_c)
    delta = jnp.stack([first - coarse_one, second - coarse_two, start[2:3 + local] - previous_coarse_two])
    corr = refine(delta)
    fixed_one = values[1] + corr[0]
    fixed_two = values[2] + corr[1]
    head = jnp.where(slot == 0, nodes[0], previous_two + corr[2])
    return (jnp.stack([head, fixed_one, fixed_two])[None], jnp.stack([terms[1], terms[2]])[None])


def solution(mesh):
    return jax.shard_map(
        on_device,
        mesh=mesh,
        in_specs=(P("tm", None, "space", None, None), P("tm", None, "space", None, None)),
        out_specs=(P("tm", None, "space", None, None), P("tm", None, "space", None, None)),
        check_vma=False,
    )
```

profile of v0, /device:TPU:8, one launch (start us, length us, event | category | flops | bytes accessed | tf_op | source)
XLA Modules:
  0.0 195.1 jit_solution(16026097733492692300)
XLA Ops:
  0.7 1.4 copy.110
  2.6 1.8 fusion.14
  4.4 0.7 fusion.175
  5.1 0.9 copy.116
  6.0 11.9 %all-to-all-start = ((f32[128,2,256]{2,1,0:T(2,128)}), f32[128,2,256]{2,1,0:T(2,128)S(1)}, u32[]{:S(2)}, u32[]{:S(2)}) async-start(f32[128,2,256]{2,1,0:T(2,128)} %copy.116), calls=%async_computation | async-start | bytes 524288 | tf_op jit(solution)/shard_map/all_to_all | solution.py:49
  18.1 12.8 %all-to-all-done = f32[128,2,256]{2,1,0:T(2,128)S(1)} async-done(((f32[128,2,256]{2,1,0:T(2,128)}), f32[128,2,256]{2,1,0:T(2,128)S(1)}, u32[]{:S(2)}, u32[]{:S(2)}) %all-to-all-start) | async-done | bytes 262176 | tf_op jit(solution)/shard_map/all_to_all | solution.py:49
  31.1 0.7 convolution_multiply_fusion.1
  31.8 0.7 fusion.187
  32.4 0.9 copy.120
  33.4 5.1 %all-to-all-start.1 = ((f32[128,2,256]{2,1,0:T(2,128)}), f32[128,2,256]{2,1,0:T(2,128)S(1)}, u32[]{:S(2)}, u32[]{:S(2)}) async-start(f32[128,2,256]{2,1,0:T(2,128)} %copy.120), calls=%async_computation.1 | async-start | bytes 524288 | tf_op jit(solution)/shard_map/all_to_all | solution.py:52
  38.5 1.0 slice.690
  39.8 0.7 slice_bitcast_fusion.1
  40.5 0.8 copy.124
  41.4 9.9 %all-to-all-done.1 = f32[128,2,256]{2,1,0:T(2,128)S(1)} async-done(((f32[128,2,256]{2,1,0:T(2,128)}), f32[128,2,256]{2,1,0:T(2,128)S(1)}, u32[]{:S(2)}, u32[]{:S(2)}) %all-to-all-start.1) | async-done | bytes 262176 | tf_op jit(solution)/shard_map/all_to_all | solution.py:52
  51.5 0.7 fusion.185
  52.2 2.5 %fusion.23 = (f32[256,256]{1,0:T(8,128)S(1)}, f32[256,256]{1,0:T(8,128)S(1)}) fusion(f32[1,2,128,256]{3,2,1,0:T(8,128)S(1)} %copy.125, f32[1,1,2,128,256]{4,3,2,1,0:T(8,128)} %copy.124, f32[1,2,128,256]{3,2,1,0:T(8,128)S(1)} %copy.122, f32[256,256]{1,0:T(8,128)S(1)} %bitcast.361, f32[256]{0:T(256)S(1)} %fusion.261, s32[256]{0:T(256)S(1)} %iota_add_fusion, ...), kind=kOutput, calls=%fused_computation.45 | convolution fusion | flops 202964992 | bytes 1575168 | tf_op jit(solution)/shard_map/dot_general | solution.py:54
  54.7 1.5 fusion.48
  56.3 0.7 fusion.178
  56.9 0.9 copy.127
  57.8 4.9 %all-to-all-start.2 = ((f32[128,2,256]{2,1,0:T(2,128)}), f32[128,2,256]{2,1,0:T(2,128)S(1)}, u32[]{:S(2)}, u32[]{:S(2)}) async-start(f32[128,2,256]{2,1,0:T(2,128)} %copy.127), calls=%async_computation.2 | async-start | bytes 524288 | tf_op jit(solution)/shard_map/all_to_all | solution.py:49
  63.4 12.4 %all-to-all-done.2 = f32[128,2,256]{2,1,0:T(2,128)S(1)} async-done(((f32[128,2,256]{2,1,0:T(2,128)}), f32[128,2,256]{2,1,0:T(2,128)S(1)}, u32[]{:S(2)}, u32[]{:S(2)}) %all-to-all-start.2) | async-done | bytes 262176 | tf_op jit(solution)/shard_map/all_to_all | solution.py:49
  75.9 0.7 convolution_multiply_fusion
  77.2 0.9 copy.131
  78.1 5.1 %all-to-all-start.3 = ((f32[128,2,256]{2,1,0:T(2,128)}), f32[128,2,256]{2,1,0:T(2,128)S(1)}, u32[]{:S(2)}, u32[]{:S(2)}) async-start(f32[128,2,256]{2,1,0:T(2,128)} %copy.131), calls=%async_computation.3 | async-start | bytes 524288 | tf_op jit(solution)/shard_map/all_to_all | solution.py:52
  83.9 0.7 slice_bitcast_fusion.2
  84.8 11.2 %all-to-all-done.3 = f32[128,2,256]{2,1,0:T(2,128)S(1)} async-done(((f32[128,2,256]{2,1,0:T(2,128)}), f32[128,2,256]{2,1,0:T(2,128)S(1)}, u32[]{:S(2)}, u32[]{:S(2)}) %all-to-all-start.3) | async-done | bytes 262176 | tf_op jit(solution)/shard_map/all_to_all | solution.py:52
  96.9 1.5 fusion.123
  98.5 0.7 copy-done.2
  99.3 1.4 fusion.30
  101.1 1.3 fusion.3
  103.1 4.8 %collective-permute-start.3 = (f32[1,5,64,128]{3,2,0,1:T(8,128)S(1)}, f32[1,5,64,128]{3,2,0,1:T(8,128)S(1)}, u32[]{:S(2)}, u32[]{:S(2)}) collective-permute-start(f32[1,5,64,128]{3,2,0,1:T(8,128)S(1)} %bitcast.355), channel_id=1, source_target_pairs={{1,0},{2,1},{3,2},{4,3},{5,4},{6,5},{7,6},{8,7},{9,8},{10,9},{11,1... | collective-permute-start | bytes 491528 | tf_op jit(solution)/shard_map/ppermute | solution.py:77
  107.9 2.0 %collective-permute-start.1 = (f32[1,1,64,128]{3,2,0,1:T(8,128)S(1)}, f32[1,1,64,128]{3,2,0,1:T(8,128)S(1)}, u32[]{:S(2)}, u32[]{:S(2)}) collective-permute-start(f32[1,1,64,128]{3,2,0,1:T(8,128)S(1)} %slice.698), channel_id=1, source_target_pairs={{62,0},{63,1},{0,2},{1,3},{2,4},{3,5},{4,6},{5,7},{6,8},{7,9},{8,1... | collective-permute-start | bytes 98312 | tf_op jit(solution)/shard_map/ppermute | solution.py:77
  110.0 5.2 %collective-permute-done.1 = f32[1,1,64,128]{3,2,0,1:T(8,128)S(1)} collective-permute-done((f32[1,1,64,128]{3,2,0,1:T(8,128)S(1)}, f32[1,1,64,128]{3,2,0,1:T(8,128)S(1)}, u32[]{:S(2)}, u32[]{:S(2)}) %collective-permute-start.1) | collective-permute-done | bytes 32800 | tf_op jit(solution)/shard_map/ppermute | solution.py:77
  116.4 2.5 %collective-permute-start.6 = (f32[1,1,64,128]{3,2,0,1:T(8,128)S(1)}, f32[1,1,64,128]{3,2,0,1:T(8,128)S(1)}, u32[]{:S(2)}, u32[]{:S(2)}) collective-permute-start(f32[1,1,64,128]{3,2,0,1:T(8,128)S(1)} %fusion.228), channel_id=1, source_target_pairs={{62,64},{63,65},{0,66},{1,67},{2,68},{3,69},{4,70},{5,71},{6,72},{... | collective-permute-start | bytes 98312 | tf_op jit(solution)/shard_map/ppermute | solution.py:84
  119.0 1.9 collective-permute-start.7
  120.9 3.2 %collective-permute-start.8 = (f32[1,1,64,128]{3,2,0,1:T(8,128)S(1)}, f32[1,1,64,128]{3,2,0,1:T(8,128)S(1)}, u32[]{:S(2)}, u32[]{:S(2)}) collective-permute-start(f32[1,1,64,128]{3,2,0,1:T(8,128)S(1)} %fusion.228), channel_id=1, source_target_pairs={{0,64},{1,65},{2,66},{3,67},{4,68},{5,69},{6,70},{7,71},{8,72},{9,... | collective-permute-start | bytes 98312 | tf_op jit(solution)/shard_map/ppermute | solution.py:84
  124.1 6.2 %collective-permute-start.9 = (f32[1,1,64,128]{3,2,0,1:T(8,128)S(1)}, f32[1,1,64,128]{3,2,0,1:T(8,128)S(1)}, u32[]{:S(2)}, u32[]{:S(2)}) collective-permute-start(f32[1,1,64,128]{3,2,0,1:T(8,128)S(1)} %fusion.228), channel_id=1, source_target_pairs={{1,64},{2,65},{3,66},{4,67},{5,68},{6,69},{7,70},{8,71},{9,72},{10... | collective-permute-start | bytes 98312 | tf_op jit(solution)/shard_map/ppermute | solution.py:84
  130.3 2.8 %collective-permute-start.10 = (f32[1,1,64,128]{3,2,0,1:T(8,128)S(1)}, f32[1,1,64,128]{3,2,0,1:T(8,128)S(1)}, u32[]{:S(2)}, u32[]{:S(2)}) collective-permute-start(f32[1,1,64,128]{3,2,0,1:T(8,128)S(1)} %fusion.228), channel_id=1, source_target_pairs={{2,64},{3,65},{4,66},{5,67},{6,68},{7,69},{8,70},{9,71},{10,72},{1... | collective-permute-start | bytes 98312 | tf_op jit(solution)/shard_map/ppermute | solution.py:84
  133.1 2.1 %collective-permute-start.11 = (f32[1,1,64,128]{3,2,0,1:T(8,128)S(1)}, f32[1,1,64,128]{3,2,0,1:T(8,128)S(1)}, u32[]{:S(2)}, u32[]{:S(2)}) collective-permute-start(f32[1,1,64,128]{3,2,0,1:T(8,128)S(1)} %fusion.228), channel_id=1, source_target_pairs={{3,64},{4,65},{5,66},{6,67},{7,68},{8,69},{9,70},{10,71},{11,72},{... | collective-permute-start | bytes 98312 | tf_op jit(solution)/shard_map/ppermute | solution.py:84
  135.3 2.0 %collective-permute-done.10 = f32[1,1,64,128]{3,2,0,1:T(8,128)S(1)} collective-permute-done((f32[1,1,64,128]{3,2,0,1:T(8,128)S(1)}, f32[1,1,64,128]{3,2,0,1:T(8,128)S(1)}, u32[]{:S(2)}, u32[]{:S(2)}) %collective-permute-start.10) | collective-permute-done | bytes 32800 | tf_op jit(solution)/shard_map/ppermute | solution.py:84
  137.3 2.0 %collective-permute-done.11 = f32[1,1,64,128]{3,2,0,1:T(8,128)S(1)} collective-permute-done((f32[1,1,64,128]{3,2,0,1:T(8,128)S(1)}, f32[1,1,64,128]{3,2,0,1:T(8,128)S(1)}, u32[]{:S(2)}, u32[]{:S(2)}) %collective-permute-start.11) | collective-permute-done | bytes 32800 | tf_op jit(solution)/shard_map/ppermute | solution.py:84
  140.1 1.9 collective-permute-start.12
  142.5 1.9 collective-permute-start.13
  144.4 1.9 collective-permute-start.14
  146.3 4.9 %collective-permute-start.15 = (f32[1,1,64,128]{3,2,1,0:T(8,128)S(1)}, f32[1,1,64,128]{3,2,1,0:T(8,128)S(1)}, u32[]{:S(2)}, u32[]{:S(2)}) collective-permute-start(f32[1,1,64,128]{3,2,1,0:T(8,128)S(1)} %fusion.222), channel_id=1, source_target_pairs={{1,64},{2,65},{3,66},{4,67},{5,68},{6,69},{7,70},{8,71},{9,72},{10... | collective-permute-start | bytes 98312 | tf_op jit(solution)/shard_map/ppermute | solution.py:84
  151.2 2.5 %collective-permute-start.16 = (f32[1,1,64,128]{3,2,1,0:T(8,128)S(1)}, f32[1,1,64,128]{3,2,1,0:T(8,128)S(1)}, u32[]{:S(2)}, u32[]{:S(2)}) collective-permute-start(f32[1,1,64,128]{3,2,1,0:T(8,128)S(1)} %fusion.222), channel_id=1, source_target_pairs={{2,64},{3,65},{4,66},{5,67},{6,68},{7,69},{8,70},{9,71},{10,72},{1... | collective-permute-start | bytes 98312 | tf_op jit(solution)/shard_map/ppermute | solution.py:84
  153.8 2.1 %collective-permute-start.17 = (f32[1,1,64,128]{3,2,1,0:T(8,128)S(1)}, f32[1,1,64,128]{3,2,1,0:T(8,128)S(1)}, u32[]{:S(2)}, u32[]{:S(2)}) collective-permute-start(f32[1,1,64,128]{3,2,1,0:T(8,128)S(1)} %fusion.222), channel_id=1, source_target_pairs={{3,64},{4,65},{5,66},{6,67},{7,68},{8,69},{9,70},{10,71},{11,72},{... | collective-permute-start | bytes 98312 | tf_op jit(solution)/shard_map/ppermute | solution.py:84
  156.0 2.0 %collective-permute-done.16 = f32[1,1,64,128]{3,2,1,0:T(8,128)S(1)} collective-permute-done((f32[1,1,64,128]{3,2,1,0:T(8,128)S(1)}, f32[1,1,64,128]{3,2,1,0:T(8,128)S(1)}, u32[]{:S(2)}, u32[]{:S(2)}) %collective-permute-start.16) | collective-permute-done | bytes 32800 | tf_op jit(solution)/shard_map/ppermute | solution.py:84
  158.0 2.0 %collective-permute-done.17 = f32[1,1,64,128]{3,2,1,0:T(8,128)S(1)} collective-permute-done((f32[1,1,64,128]{3,2,1,0:T(8,128)S(1)}, f32[1,1,64,128]{3,2,1,0:T(8,128)S(1)}, u32[]{:S(2)}, u32[]{:S(2)}) %collective-permute-start.17) | collective-permute-done | bytes 32800 | tf_op jit(solution)/shard_map/ppermute | solution.py:84
  160.7 1.9 collective-permute-start.18
  163.4 1.9 collective-permute-start
  165.3 1.9 collective-permute-start.19
  167.2 1.9 collective-permute-start.20
  169.2 5.0 %collective-permute-start.21 = (f32[1,1,64,128]{3,2,1,0:T(8,128)S(1)}, f32[1,1,64,128]{3,2,1,0:T(8,128)S(1)}, u32[]{:S(2)}, u32[]{:S(2)}) collective-permute-start(f32[1,1,64,128]{3,2,1,0:T(8,128)S(1)} %fusion.216), channel_id=1, source_target_pairs={{1,64},{2,65},{3,66},{4,67},{5,68},{6,69},{7,70},{8,71},{9,72},{10... | collective-permute-start | bytes 98312 | tf_op jit(solution)/shard_map/ppermute | solution.py:84
  174.2 2.2 %collective-permute-start.22 = (f32[1,1,64,128]{3,2,1,0:T(8,128)S(1)}, f32[1,1,64,128]{3,2,1,0:T(8,128)S(1)}, u32[]{:S(2)}, u32[]{:S(2)}) collective-permute-start(f32[1,1,64,128]{3,2,1,0:T(8,128)S(1)} %fusion.216), channel_id=1, source_target_pairs={{2,64},{3,65},{4,66},{5,67},{6,68},{7,69},{8,70},{9,71},{10,72},{1... | collective-permute-start | bytes 98312 | tf_op jit(solution)/shard_map/ppermute | solution.py:84
  176.5 5.2 %collective-permute-start.23 = (f32[1,1,64,128]{3,2,1,0:T(8,128)S(1)}, f32[1,1,64,128]{3,2,1,0:T(8,128)S(1)}, u32[]{:S(2)}, u32[]{:S(2)}) collective-permute-start(f32[1,1,64,128]{3,2,1,0:T(8,128)S(1)} %fusion.216), channel_id=1, source_target_pairs={{3,64},{4,65},{5,66},{6,67},{7,68},{8,69},{9,70},{10,71},{11,72},{... | collective-permute-start | bytes 98312 | tf_op jit(solution)/shard_map/ppermute | solution.py:84
  181.8 1.2 collective-permute-done.23
  183.7 0.7 fusion.142
  184.4 2.1 %collective-permute-start.24 = (f32[2,64,128]{2,1,0:T(8,128)}, f32[2,64,128]{2,1,0:T(8,128)S(1)}, u32[]{:S(2)}, u32[]{:S(2)}) collective-permute-start(f32[2,64,128]{2,1,0:T(8,128)} %get-tuple-element.9), channel_id=1, source_target_pairs={{0,64},{1,65},{2,66},{3,67},{4,68},{5,69},{6,70},{7,71},{8,72},{9,... | collective-permute-start | bytes 196616 | tf_op jit(solution)/shard_map/ppermute | solution.py:84
  186.5 1.0 copy.173
  187.5 4.0 %collective-permute-done.24 = f32[2,64,128]{2,1,0:T(8,128)S(1)} collective-permute-done((f32[2,64,128]{2,1,0:T(8,128)}, f32[2,64,128]{2,1,0:T(8,128)S(1)}, u32[]{:S(2)}, u32[]{:S(2)}) %collective-permute-start.24) | collective-permute-done | bytes 65568 | tf_op jit(solution)/shard_map/ppermute | solution.py:84
  191.6 0.7 fusion.62
  192.3 1.4 convolution_bitcast_fusion
  194.0 1.1 copy.172
  (181 shorter events, 10.1 us)
Async XLA Ops:
  0.6 1.5 copy-start.5
  2.6 1.8 copy-start
  6.0 24.9 %all-to-all-start = ((f32[128,2,256]{2,1,0:T(2,128)}), f32[128,2,256]{2,1,0:T(2,128)S(1)}, u32[]{:S(2)}, u32[]{:S(2)}) async-start(f32[128,2,256]{2,1,0:T(2,128)} %copy.116), calls=%async_computation | async-start | bytes 524288 | tf_op jit(solution)/shard_map/all_to_all | solution.py:49
  33.4 17.9 %all-to-all-start.1 = ((f32[128,2,256]{2,1,0:T(2,128)}), f32[128,2,256]{2,1,0:T(2,128)S(1)}, u32[]{:S(2)}, u32[]{:S(2)}) async-start(f32[128,2,256]{2,1,0:T(2,128)} %copy.120), calls=%async_computation.1 | async-start | bytes 524288 | tf_op jit(solution)/shard_map/all_to_all | solution.py:52
  57.8 17.9 %all-to-all-start.2 = ((f32[128,2,256]{2,1,0:T(2,128)}), f32[128,2,256]{2,1,0:T(2,128)S(1)}, u32[]{:S(2)}, u32[]{:S(2)}) async-start(f32[128,2,256]{2,1,0:T(2,128)} %copy.127), calls=%async_computation.2 | async-start | bytes 524288 | tf_op jit(solution)/shard_map/all_to_all | solution.py:49
  62.8 38.3 %copy-start.11 = (pred[256]{0:T(512)(128)(4,1)}, pred[256]{0:T(512)(128)(4,1)S(1)}, u32[]{:S(2)}) copy-start(pred[256]{0:T(512)(128)(4,1)S(1)} %compare_and_fusion.3) | copy-start | bytes 772
  78.1 17.9 %all-to-all-start.3 = ((f32[128,2,256]{2,1,0:T(2,128)}), f32[128,2,256]{2,1,0:T(2,128)S(1)}, u32[]{:S(2)}, u32[]{:S(2)}) async-start(f32[128,2,256]{2,1,0:T(2,128)} %copy.131), calls=%async_computation.3 | async-start | bytes 524288 | tf_op jit(solution)/shard_map/all_to_all | solution.py:52
  83.3 19.1 %copy-start.7 = (pred[128]{0:T(512)(128)(4,1)}, pred[128]{0:T(512)(128)(4,1)S(1)}, u32[]{:S(2)}) copy-start(pred[128]{0:T(512)(128)(4,1)S(1)} %compare_and_fusion.2) | copy-start | bytes 388
  98.5 0.7 copy-start.2
  99.3 1.5 copy-start.1
  99.3 1.5 copy-start.4
  102.8 12.4 %collective-permute-start.2 = (f32[1,5,64,128]{3,2,0,1:T(8,128)S(1)}, f32[1,5,64,128]{3,2,0,1:T(8,128)S(1)}, u32[]{:S(2)}, u32[]{:S(2)}) collective-permute-start(f32[1,5,64,128]{3,2,0,1:T(8,128)S(1)} %bitcast.354), channel_id=1, source_target_pairs={{63,0},{0,1},{1,2},{2,3},{3,4},{4,5},{5,6},{6,7},{7,8},{8,9},{9,10... | collective-permute-start | bytes 491528 | tf_op jit(solution)/shard_map/ppermute | solution.py:77
  103.1 12.1 %collective-permute-start.3 = (f32[1,5,64,128]{3,2,0,1:T(8,128)S(1)}, f32[1,5,64,128]{3,2,0,1:T(8,128)S(1)}, u32[]{:S(2)}, u32[]{:S(2)}) collective-permute-start(f32[1,5,64,128]{3,2,0,1:T(8,128)S(1)} %bitcast.355), channel_id=1, source_target_pairs={{1,0},{2,1},{3,2},{4,3},{5,4},{6,5},{7,6},{8,7},{9,8},{10,9},{11,1... | collective-permute-start | bytes 491528 | tf_op jit(solution)/shard_map/ppermute | solution.py:77
  107.9 7.3 %collective-permute-start.4 = (f32[1,5,64,128]{3,2,0,1:T(8,128)S(1)}, f32[1,5,64,128]{3,2,0,1:T(8,128)S(1)}, u32[]{:S(2)}, u32[]{:S(2)}) collective-permute-start(f32[1,5,64,128]{3,2,0,1:T(8,128)S(1)} %bitcast.356), channel_id=1, source_target_pairs={{2,0},{3,1},{4,2},{5,3},{6,4},{7,5},{8,6},{9,7},{10,8},{11,9},{12,... | collective-permute-start | bytes 491528 | tf_op jit(solution)/shard_map/ppermute | solution.py:77
  107.9 7.2 %collective-permute-start.1 = (f32[1,1,64,128]{3,2,0,1:T(8,128)S(1)}, f32[1,1,64,128]{3,2,0,1:T(8,128)S(1)}, u32[]{:S(2)}, u32[]{:S(2)}) collective-permute-start(f32[1,1,64,128]{3,2,0,1:T(8,128)S(1)} %slice.698), channel_id=1, source_target_pairs={{62,0},{63,1},{0,2},{1,3},{2,4},{3,5},{4,6},{5,7},{6,8},{7,9},{8,1... | collective-permute-start | bytes 98312 | tf_op jit(solution)/shard_map/ppermute | solution.py:77
  109.9 5.6 %collective-permute-start.5 = (f32[1,1,64,128]{3,2,0,1:T(8,128)S(1)}, f32[1,1,64,128]{3,2,0,1:T(8,128)S(1)}, u32[]{:S(2)}, u32[]{:S(2)}) collective-permute-start(f32[1,1,64,128]{3,2,0,1:T(8,128)S(1)} %slice.698), channel_id=1, source_target_pairs={{3,0},{4,1},{5,2},{6,3},{7,4},{8,5},{9,6},{10,7},{11,8},{12,9},{13... | collective-permute-start | bytes 98312 | tf_op jit(solution)/shard_map/ppermute | solution.py:77
  116.4 16.7 %collective-permute-start.6 = (f32[1,1,64,128]{3,2,0,1:T(8,128)S(1)}, f32[1,1,64,128]{3,2,0,1:T(8,128)S(1)}, u32[]{:S(2)}, u32[]{:S(2)}) collective-permute-start(f32[1,1,64,128]{3,2,0,1:T(8,128)S(1)} %fusion.228), channel_id=1, source_target_pairs={{62,64},{63,65},{0,66},{1,67},{2,68},{3,69},{4,70},{5,71},{6,72},{... | collective-permute-start | bytes 98312 | tf_op jit(solution)/shard_map/ppermute | solution.py:84
  119.0 16.3 %collective-permute-start.7 = (f32[1,1,64,128]{3,2,0,1:T(8,128)S(1)}, f32[1,1,64,128]{3,2,0,1:T(8,128)S(1)}, u32[]{:S(2)}, u32[]{:S(2)}) collective-permute-start(f32[1,1,64,128]{3,2,0,1:T(8,128)S(1)} %fusion.228), channel_id=1, source_target_pairs={{63,64},{0,65},{1,66},{2,67},{3,68},{4,69},{5,70},{6,71},{7,72},{8... | collective-permute-start | bytes 98312 | tf_op jit(solution)/shard_map/ppermute | solution.py:84
  120.9 14.4 %collective-permute-start.8 = (f32[1,1,64,128]{3,2,0,1:T(8,128)S(1)}, f32[1,1,64,128]{3,2,0,1:T(8,128)S(1)}, u32[]{:S(2)}, u32[]{:S(2)}) collective-permute-start(f32[1,1,64,128]{3,2,0,1:T(8,128)S(1)} %fusion.228), channel_id=1, source_target_pairs={{0,64},{1,65},{2,66},{3,67},{4,68},{5,69},{6,70},{7,71},{8,72},{9,... | collective-permute-start | bytes 98312 | tf_op jit(solution)/shard_map/ppermute | solution.py:84
  124.1 11.2 %collective-permute-start.9 = (f32[1,1,64,128]{3,2,0,1:T(8,128)S(1)}, f32[1,1,64,128]{3,2,0,1:T(8,128)S(1)}, u32[]{:S(2)}, u32[]{:S(2)}) collective-permute-start(f32[1,1,64,128]{3,2,0,1:T(8,128)S(1)} %fusion.228), channel_id=1, source_target_pairs={{1,64},{2,65},{3,66},{4,67},{5,68},{6,69},{7,70},{8,71},{9,72},{10... | collective-permute-start | bytes 98312 | tf_op jit(solution)/shard_map/ppermute | solution.py:84
  130.3 7.0 %collective-permute-start.10 = (f32[1,1,64,128]{3,2,0,1:T(8,128)S(1)}, f32[1,1,64,128]{3,2,0,1:T(8,128)S(1)}, u32[]{:S(2)}, u32[]{:S(2)}) collective-permute-start(f32[1,1,64,128]{3,2,0,1:T(8,128)S(1)} %fusion.228), channel_id=1, source_target_pairs={{2,64},{3,65},{4,66},{5,67},{6,68},{7,69},{8,70},{9,71},{10,72},{1... | collective-permute-start | bytes 98312 | tf_op jit(solution)/shard_map/ppermute | solution.py:84
  133.1 6.1 %collective-permute-start.11 = (f32[1,1,64,128]{3,2,0,1:T(8,128)S(1)}, f32[1,1,64,128]{3,2,0,1:T(8,128)S(1)}, u32[]{:S(2)}, u32[]{:S(2)}) collective-permute-start(f32[1,1,64,128]{3,2,0,1:T(8,128)S(1)} %fusion.228), channel_id=1, source_target_pairs={{3,64},{4,65},{5,66},{6,67},{7,68},{8,69},{9,70},{10,71},{11,72},{... | collective-permute-start | bytes 98312 | tf_op jit(solution)/shard_map/ppermute | solution.py:84
  140.1 13.7 %collective-permute-start.12 = (f32[1,1,64,128]{3,2,1,0:T(8,128)S(1)}, f32[1,1,64,128]{3,2,1,0:T(8,128)S(1)}, u32[]{:S(2)}, u32[]{:S(2)}) collective-permute-start(f32[1,1,64,128]{3,2,1,0:T(8,128)S(1)} %fusion.222), channel_id=1, source_target_pairs={{62,64},{63,65},{0,66},{1,67},{2,68},{3,69},{4,70},{5,71},{6,72},{... | collective-permute-start | bytes 98312 | tf_op jit(solution)/shard_map/ppermute | solution.py:84
  142.5 13.4 %collective-permute-start.13 = (f32[1,1,64,128]{3,2,1,0:T(8,128)S(1)}, f32[1,1,64,128]{3,2,1,0:T(8,128)S(1)}, u32[]{:S(2)}, u32[]{:S(2)}) collective-permute-start(f32[1,1,64,128]{3,2,1,0:T(8,128)S(1)} %fusion.222), channel_id=1, source_target_pairs={{63,64},{0,65},{1,66},{2,67},{3,68},{4,69},{5,70},{6,71},{7,72},{8... | collective-permute-start | bytes 98312 | tf_op jit(solution)/shard_map/ppermute | solution.py:84
  144.4 11.5 %collective-permute-start.14 = (f32[1,1,64,128]{3,2,1,0:T(8,128)S(1)}, f32[1,1,64,128]{3,2,1,0:T(8,128)S(1)}, u32[]{:S(2)}, u32[]{:S(2)}) collective-permute-start(f32[1,1,64,128]{3,2,1,0:T(8,128)S(1)} %fusion.222), channel_id=1, source_target_pairs={{0,64},{1,65},{2,66},{3,67},{4,68},{5,69},{6,70},{7,71},{8,72},{9,... | collective-permute-start | bytes 98312 | tf_op jit(solution)/shard_map/ppermute | solution.py:84
  146.3 9.6 %collective-permute-start.15 = (f32[1,1,64,128]{3,2,1,0:T(8,128)S(1)}, f32[1,1,64,128]{3,2,1,0:T(8,128)S(1)}, u32[]{:S(2)}, u32[]{:S(2)}) collective-permute-start(f32[1,1,64,128]{3,2,1,0:T(8,128)S(1)} %fusion.222), channel_id=1, source_target_pairs={{1,64},{2,65},{3,66},{4,67},{5,68},{6,69},{7,70},{8,71},{9,72},{10... | collective-permute-start | bytes 98312 | tf_op jit(solution)/shard_map/ppermute | solution.py:84
  151.2 6.7 %collective-permute-start.16 = (f32[1,1,64,128]{3,2,1,0:T(8,128)S(1)}, f32[1,1,64,128]{3,2,1,0:T(8,128)S(1)}, u32[]{:S(2)}, u32[]{:S(2)}) collective-permute-start(f32[1,1,64,128]{3,2,1,0:T(8,128)S(1)} %fusion.222), channel_id=1, source_target_pairs={{2,64},{3,65},{4,66},{5,67},{6,68},{7,69},{8,70},{9,71},{10,72},{1... | collective-permute-start | bytes 98312 | tf_op jit(solution)/shard_map/ppermute | solution.py:84
  153.8 6.1 %collective-permute-start.17 = (f32[1,1,64,128]{3,2,1,0:T(8,128)S(1)}, f32[1,1,64,128]{3,2,1,0:T(8,128)S(1)}, u32[]{:S(2)}, u32[]{:S(2)}) collective-permute-start(f32[1,1,64,128]{3,2,1,0:T(8,128)S(1)} %fusion.222), channel_id=1, source_target_pairs={{3,64},{4,65},{5,66},{6,67},{7,68},{8,69},{9,70},{10,71},{11,72},{... | collective-permute-start | bytes 98312 | tf_op jit(solution)/shard_map/ppermute | solution.py:84
  160.2 3.0 %copy-start.3 = (f32[256,256]{1,0:T(8,128)S(1)}, f32[256,256]{1,0:T(8,128)}, u32[]{:S(2)}) copy-start(f32[256,256]{1,0:T(8,128)} %copy-done.2) | copy-start | bytes 786436
  160.7 13.4 %collective-permute-start.18 = (f32[1,1,64,128]{3,2,1,0:T(8,128)S(1)}, f32[1,1,64,128]{3,2,1,0:T(8,128)S(1)}, u32[]{:S(2)}, u32[]{:S(2)}) collective-permute-start(f32[1,1,64,128]{3,2,1,0:T(8,128)S(1)} %fusion.216), channel_id=1, source_target_pairs={{62,64},{63,65},{0,66},{1,67},{2,68},{3,69},{4,70},{5,71},{6,72},{... | collective-permute-start | bytes 98312 | tf_op jit(solution)/shard_map/ppermute | solution.py:84
  163.4 30.5 %collective-permute-start = (f32[2,128,256]{1,2,0:T(8,128)S(1)}, f32[2,128,256]{1,2,0:T(8,128)S(1)}, u32[]{:S(2)}, u32[]{:S(2)}) collective-permute-start(f32[2,128,256]{1,2,0:T(8,128)S(1)} %copy.133), channel_id=1, source_target_pairs={{0,64},{1,65},{2,66},{3,67},{4,68},{5,69},{6,70},{7,71},{8,72},{9,... | collective-permute-start | bytes 786440 | tf_op jit(solution)/shard_map/ppermute | solution.py:84
  165.3 11.2 %collective-permute-start.19 = (f32[1,1,64,128]{3,2,1,0:T(8,128)S(1)}, f32[1,1,64,128]{3,2,1,0:T(8,128)S(1)}, u32[]{:S(2)}, u32[]{:S(2)}) collective-permute-start(f32[1,1,64,128]{3,2,1,0:T(8,128)S(1)} %fusion.216), channel_id=1, source_target_pairs={{63,64},{0,65},{1,66},{2,67},{3,68},{4,69},{5,70},{6,71},{7,72},{8... | collective-permute-start | bytes 98312 | tf_op jit(solution)/shard_map/ppermute | solution.py:84
  167.2 14.5 %collective-permute-start.20 = (f32[1,1,64,128]{3,2,1,0:T(8,128)S(1)}, f32[1,1,64,128]{3,2,1,0:T(8,128)S(1)}, u32[]{:S(2)}, u32[]{:S(2)}) collective-permute-start(f32[1,1,64,128]{3,2,1,0:T(8,128)S(1)} %fusion.216), channel_id=1, source_target_pairs={{0,64},{1,65},{2,66},{3,67},{4,68},{5,69},{6,70},{7,71},{8,72},{9,... | collective-permute-start | bytes 98312 | tf_op jit(solution)/shard_map/ppermute | solution.py:84
  169.2 12.6 %collective-permute-start.21 = (f32[1,1,64,128]{3,2,1,0:T(8,128)S(1)}, f32[1,1,64,128]{3,2,1,0:T(8,128)S(1)}, u32[]{:S(2)}, u32[]{:S(2)}) collective-permute-start(f32[1,1,64,128]{3,2,1,0:T(8,128)S(1)} %fusion.216), channel_id=1, source_target_pairs={{1,64},{2,65},{3,66},{4,67},{5,68},{6,69},{7,70},{8,71},{9,72},{10... | collective-permute-start | bytes 98312 | tf_op jit(solution)/shard_map/ppermute | solution.py:84
  174.2 7.6 %collective-permute-start.22 = (f32[1,1,64,128]{3,2,1,0:T(8,128)S(1)}, f32[1,1,64,128]{3,2,1,0:T(8,128)S(1)}, u32[]{:S(2)}, u32[]{:S(2)}) collective-permute-start(f32[1,1,64,128]{3,2,1,0:T(8,128)S(1)} %fusion.216), channel_id=1, source_target_pairs={{2,64},{3,65},{4,66},{5,67},{6,68},{7,69},{8,70},{9,71},{10,72},{1... | collective-permute-start | bytes 98312 | tf_op jit(solution)/shard_map/ppermute | solution.py:84
  176.5 6.6 %collective-permute-start.23 = (f32[1,1,64,128]{3,2,1,0:T(8,128)S(1)}, f32[1,1,64,128]{3,2,1,0:T(8,128)S(1)}, u32[]{:S(2)}, u32[]{:S(2)}) collective-permute-start(f32[1,1,64,128]{3,2,1,0:T(8,128)S(1)} %fusion.216), channel_id=1, source_target_pairs={{3,64},{4,65},{5,66},{6,67},{7,68},{8,69},{9,70},{10,71},{11,72},{... | collective-permute-start | bytes 98312 | tf_op jit(solution)/shard_map/ppermute | solution.py:84
  184.4 7.1 %copy-start.6 = (f32[1,2,64,128]{3,2,1,0:T(8,128)S(1)}, f32[1,2,64,128]{3,2,1,0:T(8,128)}, u32[]{:S(2)}) copy-start(f32[1,2,64,128]{3,2,1,0:T(8,128)} %get-tuple-element.62) | copy-start | bytes 196612
  184.4 7.1 %copy-start.9 = (s32[256]{0:T(256)S(1)}, s32[256]{0:T(256)}, u32[]{:S(2)}) copy-start(s32[256]{0:T(256)} %get-tuple-element.126) | copy-start | bytes 3076
  184.4 7.2 %copy-start.10 = (s32[256]{0:T(256)S(1)}, s32[256]{0:T(256)}, u32[]{:S(2)}) copy-start(s32[256]{0:T(256)} %get-tuple-element.127) | copy-start | bytes 3076
  184.4 7.2 %copy-start.12 = (pred[256]{0:T(512)(128)(4,1)S(1)}, pred[256]{0:T(512)(128)(4,1)}, u32[]{:S(2)}) copy-start(pred[256]{0:T(512)(128)(4,1)} %copy-done.11) | copy-start | bytes 772
  184.4 7.2 %copy-start.16 = (pred[256]{0:T(512)(128)(4,1)S(1)}, pred[256]{0:T(512)(128)(4,1)}, u32[]{:S(2)}) copy-start(pred[256]{0:T(512)(128)(4,1)} %compare_and_fusion.1) | copy-start | bytes 772
  184.4 7.1 %collective-permute-start.24 = (f32[2,64,128]{2,1,0:T(8,128)}, f32[2,64,128]{2,1,0:T(8,128)S(1)}, u32[]{:S(2)}, u32[]{:S(2)}) collective-permute-start(f32[2,64,128]{2,1,0:T(8,128)} %get-tuple-element.9), channel_id=1, source_target_pairs={{0,64},{1,65},{2,66},{3,67},{4,68},{5,69},{6,70},{7,71},{8,72},{9,... | collective-permute-start | bytes 196616 | tf_op jit(solution)/shard_map/ppermute | solution.py:84
  186.5 5.8 %copy-start.8 = (pred[128]{0:T(512)(128)(4,1)S(1)}, pred[128]{0:T(512)(128)(4,1)}, u32[]{:S(2)}) copy-start(pred[128]{0:T(512)(128)(4,1)} %copy-done.7) | copy-start | bytes 388
  186.5 5.8 %copy-start.13 = (s32[128]{0:T(128)S(1)}, s32[128]{0:T(128)}, u32[]{:S(2)}) copy-start(s32[128]{0:T(128)} %get-tuple-element.128) | copy-start | bytes 1540
  186.5 5.8 %copy-start.14 = (s32[128]{0:T(128)S(1)}, s32[128]{0:T(128)}, u32[]{:S(2)}) copy-start(s32[128]{0:T(128)} %get-tuple-element.129) | copy-start | bytes 1540
  186.5 5.8 %copy-start.15 = (pred[128]{0:T(512)(128)(4,1)S(1)}, pred[128]{0:T(512)(128)(4,1)}, u32[]{:S(2)}) copy-start(pred[128]{0:T(512)(128)(4,1)} %compare_and_fusion) | copy-start | bytes 388
where the time goes:
time: 196 us; the launch traced here: 195 us
  starting transfers between devices  90.5 us (46%)
  waiting for transfers between devices  64.7 us (33%)
  matrix products  16.6 us (8%)
  local copies, waits for them, and re-layouts  14.1 us (7%)
  other arithmetic  7.17 us (4%)
  between operations  2.07 us (1%)
    ppermute x20, starting transfers between devices, fetch(): return lax.ppermute(value, ('tm', 'space'), pairs)  56.3 us
    all_to_all x4, waiting for transfers between devices, spectral_solve(): lax.all_to_all(field, 'space', split_axis=0, concat_axis=1, tiled=True)  46.4 us
    all_to_all x4, starting transfers between devices, spectral_solve(): lax.all_to_all(field, 'space', split_axis=0, concat_axis=1, tiled=True)  27.1 us
    ppermute x20, waiting for transfers between devices, fetch(): return lax.ppermute(value, ('tm', 'space'), pairs)  13.2 us
    ppermute x5, starting transfers between devices, fetch(): return lax.ppermute(value, 'space', pairs)  7.17 us
    ppermute x5, waiting for transfers between devices, fetch(): return lax.ppermute(value, 'space', pairs)  5.2 us
    unnamed x60, local copies, waits for them, and re-layouts  4.76 us
    dot_general x2, matrix products, spectral_solve(): jnp.dot(field.reshape(planes * size_y, size_z), basis_z, precision=HIGHEST)  4.08 us
  transfers between devices with their start and end apart: 29, of which 11 were waited for; matrix products, arithmetic and copies ran while one was open for 6% of the time, Pallas kernels for 0%

commit v1 on v0

--- a/solution.py
+++ b/solution.py
@@ -84,33 +84,55 @@
     return lax.ppermute(value, ("tm", "space"), pairs)
 
 
-def halo(groups, back=0):
-    local = groups[0][0].shape[0]
-    reach = []
-    for block, low, high in groups:
-        reach.append((-(-low // local), -(-high // local)))
-    lowest = max(r[0] for r in reach)
-    highest = max(r[1] for r in reach)
-    pieces = [[] for _ in groups]
-    for offset in range(-lowest, highest + 1):
-        wanted = [i for i, r in enumerate(reach) if -r[0] <= offset <= r[1]]
+def cover(low, high, have, local, allowed):
+    plan = []
+    at = low
+    while at < high:
+        best = None
+        for offset in allowed:
+            first = offset * local - have[0]
+            last = offset * local + local + have[1]
+            if first <= at < last and (best is None or last > best[2]):
+                best = (offset, first, last)
+        if best is None:
+            offset = (at + have[0]) // local
+            best = (offset, offset * local - have[0], offset * local + local + have[1])
+        upto = min(best[2], high)
+        plan.append((best[0], at - best[1], upto - best[1]))
+        at = upto
+    return plan
+
+
+def gather_bands(items, back=0):
+    local = items[0][0].shape[0] - items[0][1][0] - items[0][1][1]
+    allowed = [0] if back == 0 else []
+    plans = []
+    for band, have, want in items:
+        plan = cover(-want[0], local + want[1], have, local, allowed)
+        for offset, _, _ in plan:
+            if offset not in allowed:
+                allowed.append(offset)
+        plans.append(plan)
+    by_offset = {}
+    for i, plan in enumerate(plans):
+        for j, (offset, first, last) in enumerate(plan):
+            by_offset.setdefault(offset, []).append((i, j, first, last))
+    got = {}
+    for offset, entries in by_offset.items():
+        parts = [items[i][0][first:last] for i, j, first, last in entries]
         if offset == 0 and back == 0:
-            for i in wanted:
-                pieces[i].append(groups[i][0])
+            for (i, j, first, last), part in zip(entries, parts):
+                got[(i, j)] = part
             continue
-        sizes = [groups[i][0].shape[1] for i in wanted]
-        joined = jnp.concatenate([groups[i][0] for i in wanted], axis=1)
-        got = fetch(joined, offset, back)
+        moved = fetch(jnp.concatenate(parts, axis=0), offset, back)
         at = 0
-        for i, size in zip(wanted, sizes):
-            pieces[i].append(got[:, at:at + size])
-            at += size
-    result = []
-    for i, (block, low, high) in enumerate(groups):
-        full = jnp.concatenate(pieces[i], axis=0)
-        begin = reach[i][0] * local - low
-        result.append(full[begin:begin + local + low + high])
-    return result
+        for i, j, first, last in entries:
+            got[(i, j)] = moved[at:at + last - first]
+            at += last - first
+    return [
+        jnp.concatenate([got[(i, j)] for j in range(len(plan))], axis=0)
+        for i, plan in enumerate(plans)
+    ]
 
 
 def coarse_rate(ext):
@@ -176,25 +198,36 @@
     rates_new = react(fresh) + jnp.stack(terms)
     sums = [0.5 * (w[0] * rates_new[0] + w[1] * rates_new[1] + w[2] * rates_new[2]) for w in WEIGHTS]
     coarse = restrict(jnp.stack([values[0], values[1], values[2], sums[0], sums[1]]))
-    by_plane = jnp.moveaxis(coarse, 1, 0)
     slot = lax.axis_index("tm")
     slices = lax.axis_size("tm")
-    start_c, rest = halo([(by_plane[:, 0:1], 2, 3), (by_plane[:, 1:5], 1, 2)])
-    start_c = start_c[:, 0]
-    rates_c = (coarse_rate(start_c), coarse_rate(rest[:, 0]))
-    sums_c = (rest[:, 2], rest[1:-1, 3])
-    coarse_one = rest[1:-1, 0]
-    coarse_two = rest[1:-1, 1]
     local = planes // 2
+    near = gather_bands(
+        [(coarse[0], (0, 0), (1, 1)), (coarse[1], (0, 0), (1, 1)), (coarse[3], (0, 0), (1, 1)),
+         (coarse[4], (0, 0), (1, 1)), (coarse[2], (0, 0), (0, 1))]
+    )
     previous_two = fetch(values[2], 0, 1)
+    previous_two, near = lax.optimization_barrier((previous_two, near))
+    coarse_two = near[4]
+    wide = gather_bands(
+        [(near[0], (1, 1), (4, 3)), (near[1], (1, 1), (3, 2)), (near[2], (1, 1), (3, 2)),
+         (near[3], (1, 1), (2, 1))]
+    )
     previous_coarse_two = fetch(coarse_two, 0, 1)
+    previous_coarse_two, wide = lax.optimization_barrier((previous_coarse_two, wide))
+    start_c = wide[0]
+    rates_c = (coarse_rate(start_c), coarse_rate(wide[1]))
+    sums_c = (wide[2], wide[3])
+    coarse_one = wide[1][3:4 + local]
     start = start_c
     for section in range(slices - 1):
         first, second = coarse_sweep(start, rates_c, sums_c)
-        received = halo([(second[:local][:, None], 2, 3)], back=1)[0][:, 0]
+        received = gather_bands([(second, (2, 1), (4, 3))], back=1)[0]
         start = jnp.where(slot == 0, start_c, received)
     first, second = coarse_sweep(start, rates_c, sums_c)
-    delta = jnp.stack([first - coarse_one, second - coarse_two, start[2:3 + local] - previous_coarse_two])
+    delta = jnp.stack(
+        [first[2:3 + local] - coarse_one, second[2:3 + local] - coarse_two,
+         start[4:5 + local] - previous_coarse_two]
+    )
     corr = refine(delta)
     fixed_one = values[1] + corr[0]
     fixed_two = values[2] + corr[1]

time: 196 us -> 180 us (0.918)
  starting transfers between devices: 90.5 us -> 69.2 us
  local copies, waits for them, and re-layouts: 14.1 us -> 16.4 us
    ppermute x20 -> x8, starting transfers between devices: 56.3 us -> 38.7 us  [fetch(): return lax.ppermute(value, ('tm', 'space'), pairs)]
    ppermute x5 -> x4, waiting for transfers between devices: 5.2 us -> 10.8 us  [fetch(): return lax.ppermute(value, 'space', pairs)]
    ppermute x20 -> x8, waiting for transfers between devices: 13.2 us -> 8.2 us  [fetch(): return lax.ppermute(value, ('tm', 'space'), pairs)]
    ppermute x5 -> x4, starting transfers between devices: 7.17 us -> 3.46 us  [fetch(): return lax.ppermute(value, 'space', pairs)]
    unnamed x60 -> x50, local copies, waits for them, and re-layouts: 4.76 us -> 6.67 us
  transfers between devices with their start and end apart: 29 -> 16, of which waited for: 11 -> 12; matrix products, arithmetic and copies ran while one was open for 6% -> 4% of each run, Pallas kernels for 0% -> 0%
where the time goes in v1:
time: 180 us; the launch traced here: 179 us
  starting transfers between devices  69.2 us (38%)
  waiting for transfers between devices  66 us (37%)
  matrix products  16.6 us (9%)
  local copies, waits for them, and re-layouts  16.4 us (9%)
  other arithmetic  8.8 us (5%)
  between operations  1.95 us (1%)
    all_to_all x4, waiting for transfers between devices, spectral_solve(): lax.all_to_all(field, 'space', split_axis=0, concat_axis=1, tiled=True)  47 us
    ppermute x8, starting transfers between devices, fetch(): return lax.ppermute(value, ('tm', 'space'), pairs)  38.7 us
    all_to_all x4, starting transfers between devices, spectral_solve(): lax.all_to_all(field, 'space', split_axis=0, concat_axis=1, tiled=True)  27.1 us
    ppermute x4, waiting for transfers between devices, fetch(): return lax.ppermute(value, 'space', pairs)  10.8 us
    ppermute x8, waiting for transfers between devices, fetch(): return lax.ppermute(value, ('tm', 'space'), pairs)  8.2 us
    unnamed x50, local copies, waits for them, and re-layouts  6.67 us
    dot_general x2, matrix products, spectral_solve(): jnp.dot(field.reshape(planes * size_y, size_z), basis_z, precision=HIGHEST)  4.08 us
  transfers between devices with their start and end apart: 16, of which 12 were waited for; matrix products, arithmetic and copies ran while one was open for 4% of the time, Pallas kernels for 0%

profile of v1, /device:TPU:8, one launch (start us, length us, event | category | flops | bytes accessed | tf_op | source)
XLA Modules:
  0.0 178.9 jit_solution(5298905885838974591)
XLA Ops:
  0.7 1.4 copy.80
  2.6 1.8 %fusion.14 = f32[2,128,256]{2,1,0:T(8,128)S(1)} fusion(f32[3,2,128,256]{2,3,1,0:T(8,128)S(1)} %get-tuple-element.44, f32[1,3,2,128,256]{3,4,2,1,0:T(8,128)S(1)} %copy.82, f32[1,3,2,128,256]{3,4,2,1,0:T(8,128)S(1)} %copy.80, f32[256]{0:T(256)S(1)} %fusion.246, s32[256]{0:T(256)S(1)} %iota_add_fusion, pred[256]{0:T(512)(128)(4,1)S(1)} %iota_compare_fusion.6, ...), kind=kOutput, calls=%fused_computation.39 | convolution fusion | flops 203423744 | bytes 1837568 | tf_op jit(solution)/shard_map/dot_general | solution.py:46
  4.4 0.7 fusion.178
  5.1 0.9 copy.86
  6.0 11.9 %all-to-all-start = ((f32[128,2,256]{2,1,0:T(2,128)}), f32[128,2,256]{2,1,0:T(2,128)S(1)}, u32[]{:S(2)}, u32[]{:S(2)}) async-start(f32[128,2,256]{2,1,0:T(2,128)} %copy.86), calls=%async_computation | async-start | bytes 524288 | tf_op jit(solution)/shard_map/all_to_all | solution.py:49
  18.1 12.8 %all-to-all-done = f32[128,2,256]{2,1,0:T(2,128)S(1)} async-done(((f32[128,2,256]{2,1,0:T(2,128)}), f32[128,2,256]{2,1,0:T(2,128)S(1)}, u32[]{:S(2)}, u32[]{:S(2)}) %all-to-all-start) | async-done | bytes 262176 | tf_op jit(solution)/shard_map/all_to_all | solution.py:49
  31.1 0.7 convolution_multiply_fusion.1
  31.8 0.7 fusion.190
  32.4 0.9 copy.90
  33.4 5.1 %all-to-all-start.1 = ((f32[128,2,256]{2,1,0:T(2,128)}), f32[128,2,256]{2,1,0:T(2,128)S(1)}, u32[]{:S(2)}, u32[]{:S(2)}) async-start(f32[128,2,256]{2,1,0:T(2,128)} %copy.90), calls=%async_computation.1 | async-start | bytes 524288 | tf_op jit(solution)/shard_map/all_to_all | solution.py:52
  38.5 1.0 slice.731
  39.8 0.7 slice_bitcast_fusion.1
  40.5 0.8 copy.94
  41.4 9.9 %all-to-all-done.1 = f32[128,2,256]{2,1,0:T(2,128)S(1)} async-done(((f32[128,2,256]{2,1,0:T(2,128)}), f32[128,2,256]{2,1,0:T(2,128)S(1)}, u32[]{:S(2)}, u32[]{:S(2)}) %all-to-all-start.1) | async-done | bytes 262176 | tf_op jit(solution)/shard_map/all_to_all | solution.py:52
  51.5 0.7 fusion.188
  52.2 2.6 %fusion.23 = (f32[256,256]{1,0:T(8,128)S(1)}, f32[256,256]{1,0:T(8,128)S(1)}) fusion(f32[1,2,128,256]{3,2,1,0:T(8,128)S(1)} %copy.95, f32[1,1,2,128,256]{4,3,2,1,0:T(8,128)} %copy.94, f32[1,2,128,256]{3,2,1,0:T(8,128)S(1)} %copy.92, f32[256,256]{1,0:T(8,128)S(1)} %bitcast.215, f32[256]{0:T(256)S(1)} %fusion.246, s32[256]{0:T(256)S(1)} %iota_add_fusion, ...), kind=kOutput, calls=%fused_computation.47 | convolution fusion | flops 202964992 | bytes 1575168 | tf_op jit(solution)/shard_map/dot_general | solution.py:54
  54.7 1.5 fusion.48
  56.3 0.7 fusion.181
  56.9 0.9 copy.97
  57.9 4.9 %all-to-all-start.2 = ((f32[128,2,256]{2,1,0:T(2,128)}), f32[128,2,256]{2,1,0:T(2,128)S(1)}, u32[]{:S(2)}, u32[]{:S(2)}) async-start(f32[128,2,256]{2,1,0:T(2,128)} %copy.97), calls=%async_computation.2 | async-start | bytes 524288 | tf_op jit(solution)/shard_map/all_to_all | solution.py:49
  62.8 13.0 %all-to-all-done.2 = f32[128,2,256]{2,1,0:T(2,128)S(1)} async-done(((f32[128,2,256]{2,1,0:T(2,128)}), f32[128,2,256]{2,1,0:T(2,128)S(1)}, u32[]{:S(2)}, u32[]{:S(2)}) %all-to-all-start.2) | async-done | bytes 262176 | tf_op jit(solution)/shard_map/all_to_all | solution.py:49
  75.9 0.7 convolution_multiply_fusion
  76.6 0.7 fusion.186
  77.2 0.9 copy.101
  78.2 5.1 %all-to-all-start.3 = ((f32[128,2,256]{2,1,0:T(2,128)}), f32[128,2,256]{2,1,0:T(2,128)S(1)}, u32[]{:S(2)}, u32[]{:S(2)}) async-start(f32[128,2,256]{2,1,0:T(2,128)} %copy.101), calls=%async_computation.3 | async-start | bytes 524288 | tf_op jit(solution)/shard_map/all_to_all | solution.py:52
  83.3 0.5 compare_and_fusion
  83.8 0.7 slice_bitcast_fusion.2
  84.7 11.3 %all-to-all-done.3 = f32[128,2,256]{2,1,0:T(2,128)S(1)} async-done(((f32[128,2,256]{2,1,0:T(2,128)}), f32[128,2,256]{2,1,0:T(2,128)S(1)}, u32[]{:S(2)}, u32[]{:S(2)}) %all-to-all-start.3) | async-done | bytes 262176 | tf_op jit(solution)/shard_map/all_to_all | solution.py:52
  96.3 0.7 fusion.184
  97.0 1.5 fusion.161
  98.5 0.7 copy-done.3
  99.4 1.4 fusion.30
  101.1 1.3 fusion.3
  102.5 0.3 fusion.215
  102.9 1.5 collective-permute-start.2
  104.6 3.5 %collective-permute-start = (f32[2,128,256]{1,2,0:T(8,128)S(1)}, f32[2,128,256]{1,2,0:T(8,128)S(1)}, u32[]{:S(2)}, u32[]{:S(2)}) collective-permute-start(f32[2,128,256]{1,2,0:T(8,128)S(1)} %copy.103), channel_id=1, source_target_pairs={{0,64},{1,65},{2,66},{3,67},{4,68},{5,69},{6,70},{7,71},{8,72},{9,... | collective-permute-start | bytes 786440 | tf_op jit(solution)/shard_map/ppermute | solution.py:84
  108.1 4.1 %collective-permute-done.1 = f32[4,64,128]{2,1,0:T(8,128)S(1)} collective-permute-done((f32[4,64,128]{2,1,0:T(8,128)S(1)}, f32[4,64,128]{2,1,0:T(8,128)S(1)}, u32[]{:S(2)}, u32[]{:S(2)}) %collective-permute-start.1) | collective-permute-done | bytes 131104 | tf_op jit(solution)/shard_map/ppermute | solution.py:77
  112.3 3.0 %collective-permute-done = f32[2,128,256]{1,2,0:T(8,128)S(1)} collective-permute-done((f32[2,128,256]{1,2,0:T(8,128)S(1)}, f32[2,128,256]{1,2,0:T(8,128)S(1)}, u32[]{:S(2)}, u32[]{:S(2)}) %collective-permute-start) | collective-permute-done | bytes 262176 | tf_op jit(solution)/shard_map/ppermute | solution.py:84
  115.3 0.7 copy-done.8
  116.2 1.7 collective-permute-start.4
  117.9 3.5 %collective-permute-start.3 = (f32[2,64,128]{2,1,0:T(8,128)S(1)}, f32[2,64,128]{2,1,0:T(8,128)S(1)}, u32[]{:S(2)}, u32[]{:S(2)}) collective-permute-start(f32[2,64,128]{2,1,0:T(8,128)S(1)} %pad_maximum_fusion.12), channel_id=1, source_target_pairs={{0,64},{1,65},{2,66},{3,67},{4,68},{5,69},{6,70},{7,71},{8,72},{9,... | collective-permute-start | bytes 196616 | tf_op jit(solution)/shard_map/ppermute | solution.py:84
  121.4 0.5 collective-permute-done.5
  121.9 6.2 %collective-permute-done.4 = f32[8,64,128]{2,1,0:T(8,128)S(1)} collective-permute-done((f32[8,64,128]{2,1,0:T(8,128)S(1)}, f32[8,64,128]{2,1,0:T(8,128)S(1)}, u32[]{:S(2)}, u32[]{:S(2)}) %collective-permute-start.4) | collective-permute-done | bytes 262176 | tf_op jit(solution)/shard_map/ppermute | solution.py:77
  129.6 3.8 %collective-permute-start.6 = (f32[4,64,128]{2,1,0:T(8,128)S(1)}, f32[4,64,128]{2,1,0:T(8,128)S(1)}, u32[]{:S(2)}, u32[]{:S(2)}) collective-permute-start(f32[4,64,128]{2,1,0:T(8,128)S(1)} %get-tuple-element.30), channel_id=1, source_target_pairs={{62,64},{63,65},{0,66},{1,67},{2,68},{3,69},{4,70},{5,71},{6,72},{... | collective-permute-start | bytes 393224 | tf_op jit(solution)/shard_map/ppermute | solution.py:84
  133.4 7.1 %collective-permute-start.7 = (f32[4,64,128]{2,1,0:T(8,128)S(1)}, f32[4,64,128]{2,1,0:T(8,128)S(1)}, u32[]{:S(2)}, u32[]{:S(2)}) collective-permute-start(f32[4,64,128]{2,1,0:T(8,128)S(1)} %get-tuple-element.30), channel_id=1, source_target_pairs={{2,64},{3,65},{4,66},{5,67},{6,68},{7,69},{8,70},{9,71},{10,72},{1... | collective-permute-start | bytes 393224 | tf_op jit(solution)/shard_map/ppermute | solution.py:84
  140.5 2.2 %collective-permute-done.6 = f32[4,64,128]{2,1,0:T(8,128)S(1)} collective-permute-done((f32[4,64,128]{2,1,0:T(8,128)S(1)}, f32[4,64,128]{2,1,0:T(8,128)S(1)}, u32[]{:S(2)}, u32[]{:S(2)}) %collective-permute-start.6) | collective-permute-done | bytes 131104 | tf_op jit(solution)/shard_map/ppermute | solution.py:84
  142.7 0.7 collective-permute-done.7
  144.3 1.9 %collective-permute-start.8 = (f32[4,64,128]{2,1,0:T(8,128)S(1)}, f32[4,64,128]{2,1,0:T(8,128)S(1)}, u32[]{:S(2)}, u32[]{:S(2)}) collective-permute-start(f32[4,64,128]{2,1,0:T(8,128)S(1)} %fusion.117), channel_id=1, source_target_pairs={{62,64},{63,65},{0,66},{1,67},{2,68},{3,69},{4,70},{5,71},{6,72},{... | collective-permute-start | bytes 393224 | tf_op jit(solution)/shard_map/ppermute | solution.py:84
  146.3 8.2 %collective-permute-start.9 = (f32[4,64,128]{2,1,0:T(8,128)S(1)}, f32[4,64,128]{2,1,0:T(8,128)S(1)}, u32[]{:S(2)}, u32[]{:S(2)}) collective-permute-start(f32[4,64,128]{2,1,0:T(8,128)S(1)} %fusion.117), channel_id=1, source_target_pairs={{2,64},{3,65},{4,66},{5,67},{6,68},{7,69},{8,70},{9,71},{10,72},{1... | collective-permute-start | bytes 393224 | tf_op jit(solution)/shard_map/ppermute | solution.py:84
  154.5 0.6 iota_and_fusion.1
  155.1 0.6 iota_and_fusion
  155.6 1.3 collective-permute-done.9
  157.7 0.8 fusion.122
  158.6 1.9 %collective-permute-start.10 = (f32[4,64,128]{2,1,0:T(8,128)}, f32[4,64,128]{2,1,0:T(8,128)}, u32[]{:S(2)}, u32[]{:S(2)}) collective-permute-start(f32[4,64,128]{2,1,0:T(8,128)} %fusion.122), channel_id=1, source_target_pairs={{62,64},{63,65},{0,66},{1,67},{2,68},{3,69},{4,70},{5,71},{6,72},{... | collective-permute-start | bytes 393224 | tf_op jit(solution)/shard_map/ppermute | solution.py:84
  160.5 8.8 %collective-permute-start.11 = (f32[4,64,128]{2,1,0:T(8,128)}, f32[4,64,128]{2,1,0:T(8,128)}, u32[]{:S(2)}, u32[]{:S(2)}) collective-permute-start(f32[4,64,128]{2,1,0:T(8,128)} %fusion.122), channel_id=1, source_target_pairs={{2,64},{3,65},{4,66},{5,67},{6,68},{7,69},{8,70},{9,71},{10,72},{1... | collective-permute-start | bytes 393224 | tf_op jit(solution)/shard_map/ppermute | solution.py:84
  169.3 0.5 compare_and_fusion.1
  169.9 1.0 copy.128
  170.9 1.0 collective-permute-done.11
  171.9 1.0 maximum_select_fusion.2
  173.9 0.5 copy-done.7
  174.4 0.7 fusion.101
  175.2 1.4 convolution_bitcast_fusion
  176.8 0.9 copy-done.9
  177.8 1.1 copy.127
  (159 shorter events, 6.9 us)
Async XLA Ops:
  0.6 1.5 copy-start.5
  2.6 1.8 %copy-start = (f32[3,2,128,256]{2,3,1,0:T(8,128)}, f32[3,2,128,256]{2,3,1,0:T(8,128)S(1)}, u32[]{:S(2)}) copy-start(f32[3,2,128,256]{2,3,1,0:T(8,128)S(1)} %get-tuple-element.44) | copy-start | bytes 2359300
  6.0 24.9 %all-to-all-start = ((f32[128,2,256]{2,1,0:T(2,128)}), f32[128,2,256]{2,1,0:T(2,128)S(1)}, u32[]{:S(2)}, u32[]{:S(2)}) async-start(f32[128,2,256]{2,1,0:T(2,128)} %copy.86), calls=%async_computation | async-start | bytes 524288 | tf_op jit(solution)/shard_map/all_to_all | solution.py:49
  33.4 17.9 %all-to-all-start.1 = ((f32[128,2,256]{2,1,0:T(2,128)}), f32[128,2,256]{2,1,0:T(2,128)S(1)}, u32[]{:S(2)}, u32[]{:S(2)}) async-start(f32[128,2,256]{2,1,0:T(2,128)} %copy.90), calls=%async_computation.1 | async-start | bytes 524288 | tf_op jit(solution)/shard_map/all_to_all | solution.py:52
  57.9 17.9 %all-to-all-start.2 = ((f32[128,2,256]{2,1,0:T(2,128)}), f32[128,2,256]{2,1,0:T(2,128)S(1)}, u32[]{:S(2)}, u32[]{:S(2)}) async-start(f32[128,2,256]{2,1,0:T(2,128)} %copy.97), calls=%async_computation.2 | async-start | bytes 524288 | tf_op jit(solution)/shard_map/all_to_all | solution.py:49
  78.2 17.9 %all-to-all-start.3 = ((f32[128,2,256]{2,1,0:T(2,128)}), f32[128,2,256]{2,1,0:T(2,128)S(1)}, u32[]{:S(2)}, u32[]{:S(2)}) async-start(f32[128,2,256]{2,1,0:T(2,128)} %copy.101), calls=%async_computation.3 | async-start | bytes 524288 | tf_op jit(solution)/shard_map/all_to_all | solution.py:52
  83.3 17.8 %copy-start.14 = (pred[256]{0:T(512)(128)(4,1)}, pred[256]{0:T(512)(128)(4,1)S(1)}, u32[]{:S(2)}) copy-start(pred[256]{0:T(512)(128)(4,1)S(1)} %compare_and_fusion.3) | copy-start | bytes 772
  83.8 18.6 %copy-start.10 = (pred[128]{0:T(512)(128)(4,1)}, pred[128]{0:T(512)(128)(4,1)S(1)}, u32[]{:S(2)}) copy-start(pred[128]{0:T(512)(128)(4,1)S(1)} %get-tuple-element.146) | copy-start | bytes 388
  98.5 0.7 copy-start.3
  99.3 1.5 copy-start.1
  99.3 1.5 copy-start.2
  101.1 3.4 %copy-start.4 = (f32[256,256]{1,0:T(8,128)S(1)}, f32[256,256]{1,0:T(8,128)}, u32[]{:S(2)}) copy-start(f32[256,256]{1,0:T(8,128)} %copy-done.3) | copy-start | bytes 786436
  102.9 9.3 %collective-permute-start.2 = (f32[5,64,128]{2,1,0:T(8,128)S(1)}, f32[5,64,128]{2,1,0:T(8,128)S(1)}, u32[]{:S(2)}, u32[]{:S(2)}) collective-permute-start(f32[5,64,128]{2,1,0:T(8,128)S(1)} %constant_dynamic-update-slice_fusion.3), channel_id=1, source_target_pairs={{1,0},{2,1},{3,2},{4,3},{5,4},{6,5},{7,6},{8,7},{9,8},{10,9},{11,1... | collective-permute-start | bytes 491528 | tf_op jit(solution)/shard_map/ppermute | solution.py:77
  104.4 7.8 %collective-permute-start.1 = (f32[4,64,128]{2,1,0:T(8,128)S(1)}, f32[4,64,128]{2,1,0:T(8,128)S(1)}, u32[]{:S(2)}, u32[]{:S(2)}) collective-permute-start(f32[4,64,128]{2,1,0:T(8,128)S(1)} %pad_maximum_fusion.5), channel_id=1, source_target_pairs={{63,0},{0,1},{1,2},{2,3},{3,4},{4,5},{5,6},{6,7},{7,8},{8,9},{9,10... | collective-permute-start | bytes 393224 | tf_op jit(solution)/shard_map/ppermute | solution.py:77
  104.6 10.7 %collective-permute-start = (f32[2,128,256]{1,2,0:T(8,128)S(1)}, f32[2,128,256]{1,2,0:T(8,128)S(1)}, u32[]{:S(2)}, u32[]{:S(2)}) collective-permute-start(f32[2,128,256]{1,2,0:T(8,128)S(1)} %copy.103), channel_id=1, source_target_pairs={{0,64},{1,65},{2,66},{3,67},{4,68},{5,69},{6,70},{7,71},{8,72},{9,... | collective-permute-start | bytes 786440 | tf_op jit(solution)/shard_map/ppermute | solution.py:84
  112.2 15.9 %copy-start.6 = (f32[2,64,128]{2,1,0:T(8,128)}, f32[2,64,128]{2,1,0:T(8,128)S(1)}, u32[]{:S(2)}) copy-start(f32[2,64,128]{2,1,0:T(8,128)S(1)} %pad_maximum_fusion.12) | copy-start | bytes 196612
  115.3 0.7 copy-start.8
  116.0 5.9 %collective-permute-start.5 = (f32[4,64,128]{2,1,0:T(8,128)S(1)}, f32[4,64,128]{2,1,0:T(8,128)S(1)}, u32[]{:S(2)}, u32[]{:S(2)}) collective-permute-start(f32[4,64,128]{2,1,0:T(8,128)S(1)} %pad_maximum_fusion.6), channel_id=1, source_target_pairs={{3,0},{4,1},{5,2},{6,3},{7,4},{8,5},{9,6},{10,7},{11,8},{12,9},{13... | collective-permute-start | bytes 393224 | tf_op jit(solution)/shard_map/ppermute | solution.py:77
  116.2 11.9 %collective-permute-start.4 = (f32[8,64,128]{2,1,0:T(8,128)S(1)}, f32[8,64,128]{2,1,0:T(8,128)S(1)}, u32[]{:S(2)}, u32[]{:S(2)}) collective-permute-start(f32[8,64,128]{2,1,0:T(8,128)S(1)} %pad_maximum_fusion.1), channel_id=1, source_target_pairs={{61,0},{62,1},{63,2},{0,3},{1,4},{2,5},{3,6},{4,7},{5,8},{6,9},{7,... | collective-permute-start | bytes 786440 | tf_op jit(solution)/shard_map/ppermute | solution.py:77
  117.9 10.3 %collective-permute-start.3 = (f32[2,64,128]{2,1,0:T(8,128)S(1)}, f32[2,64,128]{2,1,0:T(8,128)S(1)}, u32[]{:S(2)}, u32[]{:S(2)}) collective-permute-start(f32[2,64,128]{2,1,0:T(8,128)S(1)} %pad_maximum_fusion.12), channel_id=1, source_target_pairs={{0,64},{1,65},{2,66},{3,67},{4,68},{5,69},{6,70},{7,71},{8,72},{9,... | collective-permute-start | bytes 196616 | tf_op jit(solution)/shard_map/ppermute | solution.py:84
  129.6 13.1 %collective-permute-start.6 = (f32[4,64,128]{2,1,0:T(8,128)S(1)}, f32[4,64,128]{2,1,0:T(8,128)S(1)}, u32[]{:S(2)}, u32[]{:S(2)}) collective-permute-start(f32[4,64,128]{2,1,0:T(8,128)S(1)} %get-tuple-element.30), channel_id=1, source_target_pairs={{62,64},{63,65},{0,66},{1,67},{2,68},{3,69},{4,70},{5,71},{6,72},{... | collective-permute-start | bytes 393224 | tf_op jit(solution)/shard_map/ppermute | solution.py:84
  133.4 10.0 %collective-permute-start.7 = (f32[4,64,128]{2,1,0:T(8,128)S(1)}, f32[4,64,128]{2,1,0:T(8,128)S(1)}, u32[]{:S(2)}, u32[]{:S(2)}) collective-permute-start(f32[4,64,128]{2,1,0:T(8,128)S(1)} %get-tuple-element.30), channel_id=1, source_target_pairs={{2,64},{3,65},{4,66},{5,67},{6,68},{7,69},{8,70},{9,71},{10,72},{1... | collective-permute-start | bytes 393224 | tf_op jit(solution)/shard_map/ppermute | solution.py:84
  144.3 11.3 %collective-permute-start.8 = (f32[4,64,128]{2,1,0:T(8,128)S(1)}, f32[4,64,128]{2,1,0:T(8,128)S(1)}, u32[]{:S(2)}, u32[]{:S(2)}) collective-permute-start(f32[4,64,128]{2,1,0:T(8,128)S(1)} %fusion.117), channel_id=1, source_target_pairs={{62,64},{63,65},{0,66},{1,67},{2,68},{3,69},{4,70},{5,71},{6,72},{... | collective-permute-start | bytes 393224 | tf_op jit(solution)/shard_map/ppermute | solution.py:84
  146.3 10.7 %collective-permute-start.9 = (f32[4,64,128]{2,1,0:T(8,128)S(1)}, f32[4,64,128]{2,1,0:T(8,128)S(1)}, u32[]{:S(2)}, u32[]{:S(2)}) collective-permute-start(f32[4,64,128]{2,1,0:T(8,128)S(1)} %fusion.117), channel_id=1, source_target_pairs={{2,64},{3,65},{4,66},{5,67},{6,68},{7,69},{8,70},{9,71},{10,72},{1... | collective-permute-start | bytes 393224 | tf_op jit(solution)/shard_map/ppermute | solution.py:84
  158.6 12.3 %collective-permute-start.10 = (f32[4,64,128]{2,1,0:T(8,128)}, f32[4,64,128]{2,1,0:T(8,128)}, u32[]{:S(2)}, u32[]{:S(2)}) collective-permute-start(f32[4,64,128]{2,1,0:T(8,128)} %fusion.122), channel_id=1, source_target_pairs={{62,64},{63,65},{0,66},{1,67},{2,68},{3,69},{4,70},{5,71},{6,72},{... | collective-permute-start | bytes 393224 | tf_op jit(solution)/shard_map/ppermute | solution.py:84
  160.5 11.4 %collective-permute-start.11 = (f32[4,64,128]{2,1,0:T(8,128)}, f32[4,64,128]{2,1,0:T(8,128)}, u32[]{:S(2)}, u32[]{:S(2)}) collective-permute-start(f32[4,64,128]{2,1,0:T(8,128)} %fusion.122), channel_id=1, source_target_pairs={{2,64},{3,65},{4,66},{5,67},{6,68},{7,69},{8,70},{9,71},{10,72},{1... | collective-permute-start | bytes 393224 | tf_op jit(solution)/shard_map/ppermute | solution.py:84
  173.5 0.8 copy-start.7
  173.6 0.8 copy-start.12
  173.6 0.8 copy-start.13
  173.6 0.8 copy-start.15
  173.7 0.8 copy-start.19
  173.7 1.4 copy-start.11
  173.7 1.4 copy-start.16
  173.7 1.4 copy-start.17
  173.8 1.4 copy-start.18
  176.7 1.0 copy-start.9

commit v2 on v1

--- a/solution.py
+++ b/solution.py
@@ -8,6 +8,18 @@
 WEIGHTS = ((5.0 / 24.0, 1.0 / 3.0, -1.0 / 24.0), (-1.0 / 24.0, 1.0 / 3.0, 5.0 / 24.0))
 EPS2 = 2.0
 HIGHEST = lax.Precision.HIGHEST
+SPACE = ("outer", "inner")
+
+
+def exchange(field):
+    outer = lax.axis_size("outer")
+    inner = lax.axis_size("inner")
+    size, cols, rest = field.shape
+    chunk = size // (outer * inner)
+    parts = field.reshape(outer, inner, chunk, cols, rest)
+    parts = lax.all_to_all(parts, "inner", 1, 1)
+    parts = lax.all_to_all(parts, "outer", 0, 0)
+    return jnp.transpose(parts, (2, 0, 1, 3, 4)).reshape(chunk, outer * inner * cols, rest)
 
 
 def react(u):
@@ -46,10 +58,10 @@
     flat = jnp.dot(rhs.reshape(planes * size_y, size_z), basis_z.T, precision=HIGHEST)
     field = flat.reshape(planes, size_y, size_z)
     field = jnp.einsum("ky,xyz->kxz", basis_y, field, precision=HIGHEST)
-    field = lax.all_to_all(field, "space", split_axis=0, concat_axis=1, tiled=True)
+    field = exchange(field)
     field = jnp.einsum("kx,yxz->kyz", basis_x, field, precision=HIGHEST) * factor
     field = jnp.einsum("kx,kyz->xyz", basis_x, field, precision=HIGHEST)
-    field = lax.all_to_all(field, "space", split_axis=0, concat_axis=1, tiled=True)
+    field = exchange(field)
     field = jnp.matmul(basis_y.T, field, precision=HIGHEST)
     flat = jnp.dot(field.reshape(planes * size_y, size_z), basis_z, precision=HIGHEST)
     return flat.reshape(planes, size_y, size_z)
@@ -71,17 +83,17 @@
 
 
 def fetch(value, offset, back):
-    count = lax.axis_size("space")
+    count = lax.axis_size(SPACE)
     if back == 0:
         pairs = [((target + offset) % count, target) for target in range(count)]
-        return lax.ppermute(value, "space", pairs)
+        return lax.ppermute(value, SPACE, pairs)
     slices = lax.axis_size("tm")
     pairs = [
         ((slot - back) * count + (target + offset) % count, slot * count + target)
         for slot in range(back, slices)
         for target in range(count)
     ]
-    return lax.ppermute(value, ("tm", "space"), pairs)
+    return lax.ppermute(value, ("tm",) + SPACE, pairs)
 
 
 def cover(low, high, have, local, allowed):
@@ -170,13 +182,13 @@
     nodes = fine_nodes[0]
     implicit = fine_implicit[0]
     planes, size_y, size_z = (nodes.shape[1], nodes.shape[2], nodes.shape[3])
-    devices = lax.axis_size("space")
+    devices = lax.axis_size(SPACE)
     size_x = planes * devices
     local_y = size_y // devices
     basis_x = real_basis(size_x)
     basis_y = real_basis(size_y)
     basis_z = real_basis(size_z)
-    columns = lax.axis_index("space") * local_y + lax.iota(jnp.int32, local_y)
+    columns = lax.axis_index(SPACE) * local_y + lax.iota(jnp.int32, local_y)
     lam = wave_square(lax.iota(jnp.int32, size_x), size_x)[:, None, None]
     lam = lam + wave_square(columns, size_y)[None, :, None]
     lam = lam + wave_square(lax.iota(jnp.int32, size_z), size_z)[None, None, :]
@@ -236,10 +248,10 @@
 
 
 def solution(mesh):
+    slices, devices = mesh.devices.shape
+    inner = math.gcd(devices, 8)
+    fine = jax.sharding.Mesh(mesh.devices.reshape(slices, devices // inner, inner), ("tm",) + SPACE)
+    spec = P("tm", None, SPACE, None, None)
     return jax.shard_map(
-        on_device,
-        mesh=mesh,
-        in_specs=(P("tm", None, "space", None, None), P("tm", None, "space", None, None)),
-        out_specs=(P("tm", None, "space", None, None), P("tm", None, "space", None, None)),
-        check_vma=False,
-    )
+        on_device, mesh=fine, in_specs=(spec, spec), out_specs=(spec, spec), check_vma=False
+    )

time: 180 us -> 208 us (1.16)
  blocking collectives: 0 us -> 35.8 us
  starting transfers between devices: 69.2 us -> 63.7 us
  waiting for transfers between devices: 66 us -> 63.2 us
    all_to_all x0 -> x3, blocking collectives: none -> 35.8 us  [the longest x2 21.6 us: exchange(): parts = lax.all_to_all(parts, 'inner', 1, 1)]
    all_to_all x4 -> x5, starting transfers between devices: 27.1 us -> 22.1 us  [the longest x3 15.3 us: exchange(): parts = lax.all_to_all(parts, 'outer', 0, 0)]
    dot_general x4 -> x0, local copies, waits for them, and re-layouts: 3.66 us -> none  [the longest x2 1.83 us: spectral_solve(): field = jnp.einsum('kx,kyz->xyz', basis_x, field, precision=HIGHEST)]
    reshape x0 -> x10, local copies, waits for them, and re-layouts: none -> 2.6 us  [the longest x8 2.23 us: exchange(): parts = field.reshape(outer, inner, chunk, cols, rest)]
    all_to_all x4 -> x5, waiting for transfers between devices: 47 us -> 45.4 us  [the longest x3 32.1 us: exchange(): parts = lax.all_to_all(parts, 'outer', 0, 0)]
  transfers between devices with their start and end apart: 16 -> 17, of which waited for: 12 -> 13; matrix products, arithmetic and copies ran while one was open for 4% -> 4% of each run, Pallas kernels for 0% -> 0%
where the time goes in v2:
time: 208 us; the launch traced here: 207 us
  starting transfers between devices  63.7 us (31%)
  waiting for transfers between devices  63.2 us (30%)
  blocking collectives  35.8 us (17%)
  local copies, waits for them, and re-layouts  17.3 us (8%)
  matrix products  16.6 us (8%)
  other arithmetic  8.82 us (4%)
    ppermute x8, starting transfers between devices, fetch(): return lax.ppermute(value, ('tm',) + SPACE, pairs)  39 us
    all_to_all x3, waiting for transfers between devices, exchange(): parts = lax.all_to_all(parts, 'outer', 0, 0)  32.1 us
    all_to_all x2, blocking collectives, exchange(): parts = lax.all_to_all(parts, 'inner', 1, 1)  21.6 us
    all_to_all x3, starting transfers between devices, exchange(): parts = lax.all_to_all(parts, 'outer', 0, 0)  15.3 us
    all_to_all x1, blocking collectives, exchange(): parts = lax.all_to_all(parts, 'outer', 0, 0)  14.2 us
    all_to_all x2, waiting for transfers between devices, exchange(): parts = lax.all_to_all(parts, 'inner', 1, 1)  13.2 us
    ppermute x4, waiting for transfers between devices, fetch(): return lax.ppermute(value, SPACE, pairs)  9.81 us
    ppermute x8, waiting for transfers between devices, fetch(): return lax.ppermute(value, ('tm',) + SPACE, pairs)  7.98 us
  transfers between devices with their start and end apart: 17, of which 13 were waited for; matrix products, arithmetic and copies ran while one was open for 4% of the time, Pallas kernels for 0%

profile of v2, /device:TPU:8, one launch (start us, length us, event | category | flops | bytes accessed | tf_op | source)
XLA Modules:
  0.0 207.4 jit_solution(9086649075984430985)
XLA Ops:
  0.7 1.4 copy.131
  2.6 1.8 fusion.14
  4.4 0.7 fusion.178
  5.3 11.6 %all_to_all.40 = f32[8,8,2,2,256]{4,2,3,0,1:T(2,128)S(1)} all-to-all(f32[8,8,2,2,256]{4,2,3,0,1:T(2,128)S(1)} %copy.137), channel_id=1, replica_groups=mesh['tm'=4,'outer'=8,'inner'=8] {'inner'}, dimensions={1} | all-to-all | bytes 524288 | tf_op jit(solution)/shard_map/all_to_all | solution.py:20
  17.0 0.7 copy.138
  17.7 8.5 %all-to-all-start.1 = ((f32[8,8,2,2,256]{4,2,3,1,0:T(2,128)}), f32[8,8,2,2,256]{4,2,3,1,0:T(2,128)S(1)}, u32[]{:S(2)}, u32[]{:S(2)}) async-start(f32[8,8,2,2,256]{4,2,3,1,0:T(2,128)} %copy.138), calls=%async_computation.1 | async-start | bytes 524288 | tf_op jit(solution)/shard_map/all_to_all | solution.py:21
  26.3 11.4 %all-to-all-done.1 = f32[8,8,2,2,256]{4,2,3,1,0:T(2,128)S(1)} async-done(((f32[8,8,2,2,256]{4,2,3,1,0:T(2,128)}), f32[8,8,2,2,256]{4,2,3,1,0:T(2,128)S(1)}, u32[]{:S(2)}, u32[]{:S(2)}) %all-to-all-start.1) | async-done | bytes 262176 | tf_op jit(solution)/shard_map/all_to_all | solution.py:21
  37.7 0.7 convolution_multiply_fusion.1
  38.4 0.7 fusion.190
  39.2 0.8 copy.141
  40.0 3.4 %all-to-all-start.2 = ((f32[8,8,2,2,256]{4,2,0,3,1:T(2,128)}), f32[8,8,2,2,256]{4,2,0,3,1:T(2,128)S(1)}, u32[]{:S(2)}, u32[]{:S(2)}) async-start(f32[8,8,2,2,256]{4,2,0,3,1:T(2,128)} %copy.141), calls=%async_computation.2 | async-start | bytes 524288 | tf_op jit(solution)/shard_map/all_to_all | solution.py:20
  43.4 1.0 slice.731
  44.5 6.3 %all-to-all-done.2 = f32[8,8,2,2,256]{4,2,0,3,1:T(2,128)S(1)} async-done(((f32[8,8,2,2,256]{4,2,0,3,1:T(2,128)}), f32[8,8,2,2,256]{4,2,0,3,1:T(2,128)S(1)}, u32[]{:S(2)}, u32[]{:S(2)}) %all-to-all-start.2) | async-done | bytes 262176 | tf_op jit(solution)/shard_map/all_to_all | solution.py:20
  50.8 0.8 copy.142
  51.6 3.4 %all-to-all-start.3 = ((f32[8,8,2,2,256]{4,2,1,3,0:T(2,128)}), f32[8,8,2,2,256]{4,2,1,3,0:T(2,128)S(1)}, u32[]{:S(2)}, u32[]{:S(2)}) async-start(f32[8,8,2,2,256]{4,2,1,3,0:T(2,128)} %copy.142), calls=%async_computation.3 | async-start | bytes 524288 | tf_op jit(solution)/shard_map/all_to_all | solution.py:21
  55.2 0.7 slice_bitcast_fusion.1
  56.0 0.8 copy.146
  56.8 9.9 %all-to-all-done.3 = f32[8,8,2,2,256]{4,2,1,3,0:T(2,128)S(1)} async-done(((f32[8,8,2,2,256]{4,2,1,3,0:T(2,128)}), f32[8,8,2,2,256]{4,2,1,3,0:T(2,128)S(1)}, u32[]{:S(2)}, u32[]{:S(2)}) %all-to-all-start.3) | async-done | bytes 262176 | tf_op jit(solution)/shard_map/all_to_all | solution.py:21
  67.1 0.7 fusion.188
  67.8 2.5 %fusion.23 = (f32[256,256]{1,0:T(8,128)S(1)}, f32[256,256]{1,0:T(8,128)S(1)}) fusion(f32[1,2,128,256]{3,2,1,0:T(8,128)S(1)} %copy.147, f32[1,1,2,128,256]{4,3,2,1,0:T(8,128)} %copy.146, f32[1,2,128,256]{3,2,1,0:T(8,128)S(1)} %copy.144, f32[256,256]{1,0:T(8,128)S(1)} %bitcast.211, f32[256]{0:T(256)S(1)} %fusion.246, s32[256]{0:T(256)S(1)} %iota_add_fusion, ...), kind=kOutput, calls=%fused_computation.47 | convolution fusion | flops 202964992 | bytes 1575168 | tf_op jit(solution)/shard_map/dot_general | solution.py:66
  70.4 1.5 fusion.48
  71.9 0.7 fusion.181
  72.8 9.9 %all_to_all.41 = f32[8,8,2,2,256]{4,2,3,0,1:T(2,128)S(1)} all-to-all(f32[8,8,2,2,256]{4,2,3,0,1:T(2,128)S(1)} %copy.149), channel_id=1, replica_groups=mesh['tm'=4,'outer'=8,'inner'=8] {'inner'}, dimensions={1} | all-to-all | bytes 524288 | tf_op jit(solution)/shard_map/all_to_all | solution.py:20
  82.8 14.2 %all_to_all.42 = f32[8,8,2,2,256]{4,2,3,1,0:T(2,128)S(1)} all-to-all(f32[8,8,2,2,256]{4,2,3,1,0:T(2,128)S(1)} %copy.150), channel_id=1, replica_groups=mesh['tm'=4,'outer'=8,'inner'=8] {'outer'}, dimensions={0} | all-to-all | bytes 524288 | tf_op jit(solution)/shard_map/all_to_all | solution.py:21
  97.0 0.7 convolution_multiply_fusion
  97.7 0.7 fusion.186
  98.5 0.8 copy.153
  99.3 3.4 %all-to-all-start.6 = ((f32[8,8,2,2,256]{4,2,0,3,1:T(2,128)}), f32[8,8,2,2,256]{4,2,0,3,1:T(2,128)S(1)}, u32[]{:S(2)}, u32[]{:S(2)}) async-start(f32[8,8,2,2,256]{4,2,0,3,1:T(2,128)} %copy.153), calls=%async_computation.6 | async-start | bytes 524288 | tf_op jit(solution)/shard_map/all_to_all | solution.py:20
  103.2 6.9 %all-to-all-done.6 = f32[8,8,2,2,256]{4,2,0,3,1:T(2,128)S(1)} async-done(((f32[8,8,2,2,256]{4,2,0,3,1:T(2,128)}), f32[8,8,2,2,256]{4,2,0,3,1:T(2,128)S(1)}, u32[]{:S(2)}, u32[]{:S(2)}) %all-to-all-start.6) | async-done | bytes 262176 | tf_op jit(solution)/shard_map/all_to_all | solution.py:20
  110.1 0.8 copy.154
  110.9 3.4 %all-to-all-start.7 = ((f32[8,8,2,2,256]{4,2,1,3,0:T(2,128)}), f32[8,8,2,2,256]{4,2,1,3,0:T(2,128)S(1)}, u32[]{:S(2)}, u32[]{:S(2)}) async-start(f32[8,8,2,2,256]{4,2,1,3,0:T(2,128)} %copy.154), calls=%async_computation.7 | async-start | bytes 524288 | tf_op jit(solution)/shard_map/all_to_all | solution.py:21
  114.4 0.7 slice_bitcast_fusion.2
  115.2 10.8 %all-to-all-done.7 = f32[8,8,2,2,256]{4,2,1,3,0:T(2,128)S(1)} async-done(((f32[8,8,2,2,256]{4,2,1,3,0:T(2,128)}), f32[8,8,2,2,256]{4,2,1,3,0:T(2,128)S(1)}, u32[]{:S(2)}, u32[]{:S(2)}) %all-to-all-start.7) | async-done | bytes 262176 | tf_op jit(solution)/shard_map/all_to_all | solution.py:21
  126.4 0.7 fusion.184
  127.1 1.5 fusion.161
  128.6 0.7 copy-done.3
  129.5 1.4 fusion.30
  131.3 1.3 fusion.3
  133.1 0.6 collective-permute-start.1
  133.8 3.5 %collective-permute-start = (f32[2,128,256]{1,2,0:T(8,128)S(1)}, f32[2,128,256]{1,2,0:T(8,128)S(1)}, u32[]{:S(2)}, u32[]{:S(2)}) collective-permute-start(f32[2,128,256]{1,2,0:T(8,128)S(1)} %copy.156), channel_id=1, source_target_pairs={{0,64},{1,65},{2,66},{3,67},{4,68},{5,69},{6,70},{7,71},{8,72},{9,... | collective-permute-start | bytes 786440 | tf_op jit(solution)/shard_map/ppermute | solution.py:96
  137.3 3.6 %collective-permute-done.1 = f32[4,64,128]{2,1,0:T(8,128)S(1)} collective-permute-done((f32[4,64,128]{2,1,0:T(8,128)S(1)}, f32[4,64,128]{2,1,0:T(8,128)S(1)}, u32[]{:S(2)}, u32[]{:S(2)}) %collective-permute-start.1) | collective-permute-done | bytes 131104 | tf_op jit(solution)/shard_map/ppermute | solution.py:89
  141.0 3.1 %collective-permute-done = f32[2,128,256]{1,2,0:T(8,128)S(1)} collective-permute-done((f32[2,128,256]{1,2,0:T(8,128)S(1)}, f32[2,128,256]{1,2,0:T(8,128)S(1)}, u32[]{:S(2)}, u32[]{:S(2)}) %collective-permute-start) | collective-permute-done | bytes 262176 | tf_op jit(solution)/shard_map/ppermute | solution.py:96
  144.2 0.7 copy-done.8
  145.0 1.8 collective-permute-start.4
  146.8 3.5 %collective-permute-start.3 = (f32[2,64,128]{2,1,0:T(8,128)S(1)}, f32[2,64,128]{2,1,0:T(8,128)S(1)}, u32[]{:S(2)}, u32[]{:S(2)}) collective-permute-start(f32[2,64,128]{2,1,0:T(8,128)S(1)} %pad_maximum_fusion.12), channel_id=1, source_target_pairs={{0,64},{1,65},{2,66},{3,67},{4,68},{5,69},{6,70},{7,71},{8,72},{9,... | collective-permute-start | bytes 196616 | tf_op jit(solution)/shard_map/ppermute | solution.py:96
  150.3 6.2 %collective-permute-done.4 = f32[8,64,128]{2,1,0:T(8,128)S(1)} collective-permute-done((f32[8,64,128]{2,1,0:T(8,128)S(1)}, f32[8,64,128]{2,1,0:T(8,128)S(1)}, u32[]{:S(2)}, u32[]{:S(2)}) %collective-permute-start.4) | collective-permute-done | bytes 262176 | tf_op jit(solution)/shard_map/ppermute | solution.py:89
  158.0 3.8 %collective-permute-start.6 = (f32[4,64,128]{2,1,0:T(8,128)S(1)}, f32[4,64,128]{2,1,0:T(8,128)S(1)}, u32[]{:S(2)}, u32[]{:S(2)}) collective-permute-start(f32[4,64,128]{2,1,0:T(8,128)S(1)} %get-tuple-element.32), channel_id=1, source_target_pairs={{62,64},{63,65},{0,66},{1,67},{2,68},{3,69},{4,70},{5,71},{6,72},{... | collective-permute-start | bytes 393224 | tf_op jit(solution)/shard_map/ppermute | solution.py:96
  161.8 7.3 %collective-permute-start.7 = (f32[4,64,128]{2,1,0:T(8,128)S(1)}, f32[4,64,128]{2,1,0:T(8,128)S(1)}, u32[]{:S(2)}, u32[]{:S(2)}) collective-permute-start(f32[4,64,128]{2,1,0:T(8,128)S(1)} %get-tuple-element.32), channel_id=1, source_target_pairs={{2,64},{3,65},{4,66},{5,67},{6,68},{7,69},{8,70},{9,71},{10,72},{1... | collective-permute-start | bytes 393224 | tf_op jit(solution)/shard_map/ppermute | solution.py:96
  169.2 1.3 collective-permute-done.6
  170.5 1.0 collective-permute-done.7
  172.4 2.2 %collective-permute-start.8 = (f32[4,64,128]{2,1,0:T(8,128)S(1)}, f32[4,64,128]{2,1,0:T(8,128)S(1)}, u32[]{:S(2)}, u32[]{:S(2)}) collective-permute-start(f32[4,64,128]{2,1,0:T(8,128)S(1)} %fusion.117), channel_id=1, source_target_pairs={{62,64},{63,65},{0,66},{1,67},{2,68},{3,69},{4,70},{5,71},{6,72},{... | collective-permute-start | bytes 393224 | tf_op jit(solution)/shard_map/ppermute | solution.py:96
  174.6 8.3 %collective-permute-start.9 = (f32[4,64,128]{2,1,0:T(8,128)S(1)}, f32[4,64,128]{2,1,0:T(8,128)S(1)}, u32[]{:S(2)}, u32[]{:S(2)}) collective-permute-start(f32[4,64,128]{2,1,0:T(8,128)S(1)} %fusion.117), channel_id=1, source_target_pairs={{2,64},{3,65},{4,66},{5,67},{6,68},{7,69},{8,70},{9,71},{10,72},{1... | collective-permute-start | bytes 393224 | tf_op jit(solution)/shard_map/ppermute | solution.py:96
  183.4 0.6 iota_and_fusion
  184.0 1.4 collective-permute-done.9
  186.2 0.8 fusion.122
  187.0 3.2 %collective-permute-start.10 = (f32[4,64,128]{2,1,0:T(8,128)}, f32[4,64,128]{2,1,0:T(8,128)}, u32[]{:S(2)}, u32[]{:S(2)}) collective-permute-start(f32[4,64,128]{2,1,0:T(8,128)} %fusion.122), channel_id=1, source_target_pairs={{62,64},{63,65},{0,66},{1,67},{2,68},{3,69},{4,70},{5,71},{6,72},{... | collective-permute-start | bytes 393224 | tf_op jit(solution)/shard_map/ppermute | solution.py:96
  190.2 7.3 %collective-permute-start.11 = (f32[4,64,128]{2,1,0:T(8,128)}, f32[4,64,128]{2,1,0:T(8,128)}, u32[]{:S(2)}, u32[]{:S(2)}) collective-permute-start(f32[4,64,128]{2,1,0:T(8,128)} %fusion.122), channel_id=1, source_target_pairs={{2,64},{3,65},{4,66},{5,67},{6,68},{7,69},{8,70},{9,71},{10,72},{1... | collective-permute-start | bytes 393224 | tf_op jit(solution)/shard_map/ppermute | solution.py:96
  198.1 1.0 copy.181
  199.6 0.7 collective-permute-done.11
  200.3 1.0 maximum_select_fusion.2
  202.9 0.7 fusion.101
  203.6 1.4 convolution_bitcast_fusion
  205.2 0.9 copy-done.9
  206.2 1.1 copy.180
  (170 shorter events, 10.4 us)
Async XLA Ops:
  0.6 1.5 copy-start.5
  2.6 1.8 copy-start
  17.7 20.0 %all-to-all-start.1 = ((f32[8,8,2,2,256]{4,2,3,1,0:T(2,128)}), f32[8,8,2,2,256]{4,2,3,1,0:T(2,128)S(1)}, u32[]{:S(2)}, u32[]{:S(2)}) async-start(f32[8,8,2,2,256]{4,2,3,1,0:T(2,128)} %copy.138), calls=%async_computation.1 | async-start | bytes 524288 | tf_op jit(solution)/shard_map/all_to_all | solution.py:21
  40.0 10.9 %all-to-all-start.2 = ((f32[8,8,2,2,256]{4,2,0,3,1:T(2,128)}), f32[8,8,2,2,256]{4,2,0,3,1:T(2,128)S(1)}, u32[]{:S(2)}, u32[]{:S(2)}) async-start(f32[8,8,2,2,256]{4,2,0,3,1:T(2,128)} %copy.141), calls=%async_computation.2 | async-start | bytes 524288 | tf_op jit(solution)/shard_map/all_to_all | solution.py:20
  51.6 15.1 %all-to-all-start.3 = ((f32[8,8,2,2,256]{4,2,1,3,0:T(2,128)}), f32[8,8,2,2,256]{4,2,1,3,0:T(2,128)S(1)}, u32[]{:S(2)}, u32[]{:S(2)}) async-start(f32[8,8,2,2,256]{4,2,1,3,0:T(2,128)} %copy.142), calls=%async_computation.3 | async-start | bytes 524288 | tf_op jit(solution)/shard_map/all_to_all | solution.py:21
  99.3 10.9 %all-to-all-start.6 = ((f32[8,8,2,2,256]{4,2,0,3,1:T(2,128)}), f32[8,8,2,2,256]{4,2,0,3,1:T(2,128)S(1)}, u32[]{:S(2)}, u32[]{:S(2)}) async-start(f32[8,8,2,2,256]{4,2,0,3,1:T(2,128)} %copy.153), calls=%async_computation.6 | async-start | bytes 524288 | tf_op jit(solution)/shard_map/all_to_all | solution.py:20
  103.2 29.4 %copy-start.10 = (pred[128]{0:T(512)(128)(4,1)}, pred[128]{0:T(512)(128)(4,1)S(1)}, u32[]{:S(2)}) copy-start(pred[128]{0:T(512)(128)(4,1)S(1)} %get-tuple-element.148) | copy-start | bytes 388
  110.9 15.1 %all-to-all-start.7 = ((f32[8,8,2,2,256]{4,2,1,3,0:T(2,128)}), f32[8,8,2,2,256]{4,2,1,3,0:T(2,128)S(1)}, u32[]{:S(2)}, u32[]{:S(2)}) async-start(f32[8,8,2,2,256]{4,2,1,3,0:T(2,128)} %copy.154), calls=%async_computation.7 | async-start | bytes 524288 | tf_op jit(solution)/shard_map/all_to_all | solution.py:21
  114.3 16.9 %copy-start.14 = (pred[256]{0:T(512)(128)(4,1)}, pred[256]{0:T(512)(128)(4,1)S(1)}, u32[]{:S(2)}) copy-start(pred[256]{0:T(512)(128)(4,1)S(1)} %compare_and_fusion.3) | copy-start | bytes 772
  128.6 0.7 copy-start.3
  129.5 1.5 copy-start.1
  129.5 1.5 copy-start.2
  131.2 2.5 %copy-start.4 = (f32[256,256]{1,0:T(8,128)S(1)}, f32[256,256]{1,0:T(8,128)}, u32[]{:S(2)}) copy-start(f32[256,256]{1,0:T(8,128)} %copy-done.3) | copy-start | bytes 786436
  133.0 7.9 %collective-permute-start.2 = (f32[5,64,128]{2,1,0:T(8,128)S(1)}, f32[5,64,128]{2,1,0:T(8,128)S(1)}, u32[]{:S(2)}, u32[]{:S(2)}) collective-permute-start(f32[5,64,128]{2,1,0:T(8,128)S(1)} %constant_dynamic-update-slice_fusion.3), channel_id=1, source_target_pairs={{1,0},{2,1},{3,2},{4,3},{5,4},{6,5},{7,6},{8,7},{9,8},{10,9},{11,1... | collective-permute-start | bytes 491528 | tf_op jit(solution)/shard_map/ppermute | solution.py:89
  133.1 7.8 %collective-permute-start.1 = (f32[4,64,128]{2,1,0:T(8,128)S(1)}, f32[4,64,128]{2,1,0:T(8,128)S(1)}, u32[]{:S(2)}, u32[]{:S(2)}) collective-permute-start(f32[4,64,128]{2,1,0:T(8,128)S(1)} %pad_maximum_fusion.5), channel_id=1, source_target_pairs={{63,0},{0,1},{1,2},{2,3},{3,4},{4,5},{5,6},{6,7},{7,8},{8,9},{9,10... | collective-permute-start | bytes 393224 | tf_op jit(solution)/shard_map/ppermute | solution.py:89
  133.8 10.3 %collective-permute-start = (f32[2,128,256]{1,2,0:T(8,128)S(1)}, f32[2,128,256]{1,2,0:T(8,128)S(1)}, u32[]{:S(2)}, u32[]{:S(2)}) collective-permute-start(f32[2,128,256]{1,2,0:T(8,128)S(1)} %copy.156), channel_id=1, source_target_pairs={{0,64},{1,65},{2,66},{3,67},{4,68},{5,69},{6,70},{7,71},{8,72},{9,... | collective-permute-start | bytes 786440 | tf_op jit(solution)/shard_map/ppermute | solution.py:96
  141.0 15.6 %copy-start.6 = (f32[2,64,128]{2,1,0:T(8,128)}, f32[2,64,128]{2,1,0:T(8,128)S(1)}, u32[]{:S(2)}) copy-start(f32[2,64,128]{2,1,0:T(8,128)S(1)} %pad_maximum_fusion.12) | copy-start | bytes 196612
  144.1 0.7 copy-start.8
  144.9 5.4 %collective-permute-start.5 = (f32[4,64,128]{2,1,0:T(8,128)S(1)}, f32[4,64,128]{2,1,0:T(8,128)S(1)}, u32[]{:S(2)}, u32[]{:S(2)}) collective-permute-start(f32[4,64,128]{2,1,0:T(8,128)S(1)} %pad_maximum_fusion.6), channel_id=1, source_target_pairs={{3,0},{4,1},{5,2},{6,3},{7,4},{8,5},{9,6},{10,7},{11,8},{12,9},{13... | collective-permute-start | bytes 393224 | tf_op jit(solution)/shard_map/ppermute | solution.py:89
  145.0 11.6 %collective-permute-start.4 = (f32[8,64,128]{2,1,0:T(8,128)S(1)}, f32[8,64,128]{2,1,0:T(8,128)S(1)}, u32[]{:S(2)}, u32[]{:S(2)}) collective-permute-start(f32[8,64,128]{2,1,0:T(8,128)S(1)} %pad_maximum_fusion.1), channel_id=1, source_target_pairs={{61,0},{62,1},{63,2},{0,3},{1,4},{2,5},{3,6},{4,7},{5,8},{6,9},{7,... | collective-permute-start | bytes 786440 | tf_op jit(solution)/shard_map/ppermute | solution.py:89
  146.8 9.9 %collective-permute-start.3 = (f32[2,64,128]{2,1,0:T(8,128)S(1)}, f32[2,64,128]{2,1,0:T(8,128)S(1)}, u32[]{:S(2)}, u32[]{:S(2)}) collective-permute-start(f32[2,64,128]{2,1,0:T(8,128)S(1)} %pad_maximum_fusion.12), channel_id=1, source_target_pairs={{0,64},{1,65},{2,66},{3,67},{4,68},{5,69},{6,70},{7,71},{8,72},{9,... | collective-permute-start | bytes 196616 | tf_op jit(solution)/shard_map/ppermute | solution.py:96
  158.0 12.5 %collective-permute-start.6 = (f32[4,64,128]{2,1,0:T(8,128)S(1)}, f32[4,64,128]{2,1,0:T(8,128)S(1)}, u32[]{:S(2)}, u32[]{:S(2)}) collective-permute-start(f32[4,64,128]{2,1,0:T(8,128)S(1)} %get-tuple-element.32), channel_id=1, source_target_pairs={{62,64},{63,65},{0,66},{1,67},{2,68},{3,69},{4,70},{5,71},{6,72},{... | collective-permute-start | bytes 393224 | tf_op jit(solution)/shard_map/ppermute | solution.py:96
  161.8 9.7 %collective-permute-start.7 = (f32[4,64,128]{2,1,0:T(8,128)S(1)}, f32[4,64,128]{2,1,0:T(8,128)S(1)}, u32[]{:S(2)}, u32[]{:S(2)}) collective-permute-start(f32[4,64,128]{2,1,0:T(8,128)S(1)} %get-tuple-element.32), channel_id=1, source_target_pairs={{2,64},{3,65},{4,66},{5,67},{6,68},{7,69},{8,70},{9,71},{10,72},{1... | collective-permute-start | bytes 393224 | tf_op jit(solution)/shard_map/ppermute | solution.py:96
  172.4 11.6 %collective-permute-start.8 = (f32[4,64,128]{2,1,0:T(8,128)S(1)}, f32[4,64,128]{2,1,0:T(8,128)S(1)}, u32[]{:S(2)}, u32[]{:S(2)}) collective-permute-start(f32[4,64,128]{2,1,0:T(8,128)S(1)} %fusion.117), channel_id=1, source_target_pairs={{62,64},{63,65},{0,66},{1,67},{2,68},{3,69},{4,70},{5,71},{6,72},{... | collective-permute-start | bytes 393224 | tf_op jit(solution)/shard_map/ppermute | solution.py:96
  174.6 10.8 %collective-permute-start.9 = (f32[4,64,128]{2,1,0:T(8,128)S(1)}, f32[4,64,128]{2,1,0:T(8,128)S(1)}, u32[]{:S(2)}, u32[]{:S(2)}) collective-permute-start(f32[4,64,128]{2,1,0:T(8,128)S(1)} %fusion.117), channel_id=1, source_target_pairs={{2,64},{3,65},{4,66},{5,67},{6,68},{7,69},{8,70},{9,71},{10,72},{1... | collective-permute-start | bytes 393224 | tf_op jit(solution)/shard_map/ppermute | solution.py:96
  187.0 12.6 %collective-permute-start.10 = (f32[4,64,128]{2,1,0:T(8,128)}, f32[4,64,128]{2,1,0:T(8,128)}, u32[]{:S(2)}, u32[]{:S(2)}) collective-permute-start(f32[4,64,128]{2,1,0:T(8,128)} %fusion.122), channel_id=1, source_target_pairs={{62,64},{63,65},{0,66},{1,67},{2,68},{3,69},{4,70},{5,71},{6,72},{... | collective-permute-start | bytes 393224 | tf_op jit(solution)/shard_map/ppermute | solution.py:96
  190.2 10.1 %collective-permute-start.11 = (f32[4,64,128]{2,1,0:T(8,128)}, f32[4,64,128]{2,1,0:T(8,128)}, u32[]{:S(2)}, u32[]{:S(2)}) collective-permute-start(f32[4,64,128]{2,1,0:T(8,128)} %fusion.122), channel_id=1, source_target_pairs={{2,64},{3,65},{4,66},{5,67},{6,68},{7,69},{8,70},{9,71},{10,72},{1... | collective-permute-start | bytes 393224 | tf_op jit(solution)/shard_map/ppermute | solution.py:96
  201.9 0.8 copy-start.7
  202.1 0.8 copy-start.12
  202.1 0.8 copy-start.13
  202.1 0.8 copy-start.15
  202.1 0.8 copy-start.19
  202.2 1.4 copy-start.11
  202.2 1.4 copy-start.16
  202.2 1.4 copy-start.17
  202.2 1.4 copy-start.18
  205.1 1.0 copy-start.9

commit v3 on v1

--- a/solution.py
+++ b/solution.py
@@ -205,15 +205,18 @@
         [(coarse[0], (0, 0), (1, 1)), (coarse[1], (0, 0), (1, 1)), (coarse[3], (0, 0), (1, 1)),
          (coarse[4], (0, 0), (1, 1)), (coarse[2], (0, 0), (0, 1))]
     )
-    previous_two = fetch(values[2], 0, 1)
-    previous_two, near = lax.optimization_barrier((previous_two, near))
     coarse_two = near[4]
     wide = gather_bands(
         [(near[0], (1, 1), (4, 3)), (near[1], (1, 1), (3, 2)), (near[2], (1, 1), (3, 2)),
          (near[3], (1, 1), (2, 1))]
     )
-    previous_coarse_two = fetch(coarse_two, 0, 1)
-    previous_coarse_two, wide = lax.optimization_barrier((previous_coarse_two, wide))
+    packed = coarse_two.reshape(-1, size_z)
+    packed = jnp.pad(packed, ((0, size_y - packed.shape[0] % size_y), (0, 0)))
+    packed = fetch(jnp.concatenate([values[2], packed.reshape(-1, size_y, size_z)]), 0, 1)
+    packed, wide = lax.optimization_barrier((packed, wide))
+    previous_two = packed[:planes]
+    previous_coarse_two = packed[planes:].reshape(-1, size_z)[: coarse_two.size // size_z]
+    previous_coarse_two = previous_coarse_two.reshape(coarse_two.shape)
     start_c = wide[0]
     rates_c = (coarse_rate(start_c), coarse_rate(wide[1]))
     sums_c = (wide[2], wide[3])

time: 180 us -> 201 us (1.12)
  waiting for transfers between devices: 66 us -> 80.6 us
  local copies, waits for them, and re-layouts: 16.4 us -> 23 us
    ppermute x8 -> x7, waiting for transfers between devices: 8.2 us -> 19.2 us  [fetch(): return lax.ppermute(value, ('tm', 'space'), pairs)]
    ppermute x4, waiting for transfers between devices: 10.8 us -> 15.2 us  [fetch(): return lax.ppermute(value, 'space', pairs)]
    unnamed x50 -> x56, local copies, waits for them, and re-layouts: 6.67 us -> 10.2 us
    ppermute x8 -> x7, starting transfers between devices: 38.7 us -> 35.6 us  [fetch(): return lax.ppermute(value, ('tm', 'space'), pairs)]
    ppermute x4, starting transfers between devices: 3.46 us -> 5.77 us  [fetch(): return lax.ppermute(value, 'space', pairs)]
  transfers between devices with their start and end apart: 16 -> 15, of which waited for: 12 -> 12; matrix products, arithmetic and copies ran while one was open for 4% -> 5% of each run, Pallas kernels for 0% -> 0%
where the time goes in v3:
time: 201 us; the launch traced here: 200 us
  waiting for transfers between devices  80.6 us (40%)
  starting transfers between devices  68.5 us (34%)
  local copies, waits for them, and re-layouts  23 us (11%)
  matrix products  16.6 us (8%)
  other arithmetic  9.47 us (5%)
    all_to_all x4, waiting for transfers between devices, spectral_solve(): lax.all_to_all(field, 'space', split_axis=0, concat_axis=1, tiled=True)  46.2 us
    ppermute x7, starting transfers between devices, fetch(): return lax.ppermute(value, ('tm', 'space'), pairs)  35.6 us
    all_to_all x4, starting transfers between devices, spectral_solve(): lax.all_to_all(field, 'space', split_axis=0, concat_axis=1, tiled=True)  27.1 us
    ppermute x7, waiting for transfers between devices, fetch(): return lax.ppermute(value, ('tm', 'space'), pairs)  19.2 us
    ppermute x4, waiting for transfers between devices, fetch(): return lax.ppermute(value, 'space', pairs)  15.2 us
    unnamed x56, local copies, waits for them, and re-layouts  10.2 us
    ppermute x4, starting transfers between devices, fetch(): return lax.ppermute(value, 'space', pairs)  5.77 us
    dot_general x2, matrix products, spectral_solve(): jnp.dot(field.reshape(planes * size_y, size_z), basis_z, precision=HIGHEST)  4.14 us
  transfers between devices with their start and end apart: 15, of which 12 were waited for; matrix products, arithmetic and copies ran while one was open for 5% of the time, Pallas kernels for 0%

profile of v3, /device:TPU:8, one launch (start us, length us, event | category | flops | bytes accessed | tf_op | source)
XLA Modules:
  0.0 200.1 jit_solution(14501501685688479138)
XLA Ops:
  0.7 1.4 copy.84
  2.6 1.8 fusion.14
  4.4 0.7 fusion.178
  5.1 0.9 copy.90
  6.0 11.9 %all-to-all-start = ((f32[128,2,256]{2,1,0:T(2,128)}), f32[128,2,256]{2,1,0:T(2,128)S(1)}, u32[]{:S(2)}, u32[]{:S(2)}) async-start(f32[128,2,256]{2,1,0:T(2,128)} %copy.90), calls=%async_computation | async-start | bytes 524288 | tf_op jit(solution)/shard_map/all_to_all | solution.py:49
  18.1 12.8 %all-to-all-done = f32[128,2,256]{2,1,0:T(2,128)S(1)} async-done(((f32[128,2,256]{2,1,0:T(2,128)}), f32[128,2,256]{2,1,0:T(2,128)S(1)}, u32[]{:S(2)}, u32[]{:S(2)}) %all-to-all-start) | async-done | bytes 262176 | tf_op jit(solution)/shard_map/all_to_all | solution.py:49
  31.1 0.7 convolution_multiply_fusion.1
  31.8 0.7 fusion.190
  32.4 0.9 copy.94
  33.4 5.1 %all-to-all-start.1 = ((f32[128,2,256]{2,1,0:T(2,128)}), f32[128,2,256]{2,1,0:T(2,128)S(1)}, u32[]{:S(2)}, u32[]{:S(2)}) async-start(f32[128,2,256]{2,1,0:T(2,128)} %copy.94), calls=%async_computation.1 | async-start | bytes 524288 | tf_op jit(solution)/shard_map/all_to_all | solution.py:52
  38.5 1.0 slice.732
  39.6 0.8 copy.99
  40.5 0.7 slice_bitcast_fusion.1
  41.2 0.9 copy.98
  42.1 9.2 %all-to-all-done.1 = f32[128,2,256]{2,1,0:T(2,128)S(1)} async-done(((f32[128,2,256]{2,1,0:T(2,128)}), f32[128,2,256]{2,1,0:T(2,128)S(1)}, u32[]{:S(2)}, u32[]{:S(2)}) %all-to-all-start.1) | async-done | bytes 262176 | tf_op jit(solution)/shard_map/all_to_all | solution.py:52
  51.5 0.7 fusion.188
  52.2 2.6 %fusion.23 = (f32[256,256]{1,0:T(8,128)S(1)}, f32[256,256]{1,0:T(8,128)S(1)}) fusion(f32[1,2,128,256]{3,2,1,0:T(8,128)} %copy.99, f32[1,1,2,128,256]{4,3,2,1,0:T(8,128)} %copy.98, f32[1,2,128,256]{3,2,1,0:T(8,128)S(1)} %copy.96, f32[256,256]{1,0:T(8,128)S(1)} %bitcast.232, f32[256]{0:T(256)S(1)} %fusion.246, s32[256]{0:T(256)S(1)} %iota_add_fusion, ...), kind=kOutput, calls=%fused_computation.48 | convolution fusion | flops 202964992 | bytes 1575168 | tf_op jit(solution)/shard_map/dot_general | solution.py:54
  54.8 1.5 fusion.48
  56.3 0.7 fusion.181
  57.0 0.9 copy.101
  57.9 4.9 %all-to-all-start.2 = ((f32[128,2,256]{2,1,0:T(2,128)}), f32[128,2,256]{2,1,0:T(2,128)S(1)}, u32[]{:S(2)}, u32[]{:S(2)}) async-start(f32[128,2,256]{2,1,0:T(2,128)} %copy.101), calls=%async_computation.2 | async-start | bytes 524288 | tf_op jit(solution)/shard_map/all_to_all | solution.py:49
  62.8 13.0 %all-to-all-done.2 = f32[128,2,256]{2,1,0:T(2,128)S(1)} async-done(((f32[128,2,256]{2,1,0:T(2,128)}), f32[128,2,256]{2,1,0:T(2,128)S(1)}, u32[]{:S(2)}, u32[]{:S(2)}) %all-to-all-start.2) | async-done | bytes 262176 | tf_op jit(solution)/shard_map/all_to_all | solution.py:49
  75.9 0.7 convolution_multiply_fusion
  76.6 0.7 fusion.186
  77.3 0.9 copy.105
  78.2 5.1 %all-to-all-start.3 = ((f32[128,2,256]{2,1,0:T(2,128)}), f32[128,2,256]{2,1,0:T(2,128)S(1)}, u32[]{:S(2)}, u32[]{:S(2)}) async-start(f32[128,2,256]{2,1,0:T(2,128)} %copy.105), calls=%async_computation.3 | async-start | bytes 524288 | tf_op jit(solution)/shard_map/all_to_all | solution.py:52
  84.0 0.8 slice_bitcast_fusion.2
  84.8 11.2 %all-to-all-done.3 = f32[128,2,256]{2,1,0:T(2,128)S(1)} async-done(((f32[128,2,256]{2,1,0:T(2,128)}), f32[128,2,256]{2,1,0:T(2,128)S(1)}, u32[]{:S(2)}, u32[]{:S(2)}) %all-to-all-start.3) | async-done | bytes 262176 | tf_op jit(solution)/shard_map/all_to_all | solution.py:52
  96.3 0.7 fusion.184
  97.0 1.5 fusion.161
  98.5 0.7 copy-done.3
  99.4 1.4 fusion.30
  101.2 1.3 fusion.3
  103.2 7.5 %collective-permute-done.2 = f32[4,64,128]{2,1,0:T(8,128)S(1)} collective-permute-done((f32[4,64,128]{2,1,0:T(8,128)S(1)}, f32[4,64,128]{2,1,0:T(8,128)S(1)}, u32[]{:S(2)}, u32[]{:S(2)}) %collective-permute-start.2) | collective-permute-done | bytes 131104 | tf_op jit(solution)/shard_map/ppermute | solution.py:77
  110.7 0.6 fusion.359
  111.3 0.6 constant_dynamic-update-slice_fusion.13
  112.0 2.8 %collective-permute-done = f32[5,64,128]{2,1,0:T(8,128)S(1)} collective-permute-done((f32[5,64,128]{2,1,0:T(8,128)S(1)}, f32[5,64,128]{2,1,0:T(8,128)S(1)}, u32[]{:S(2)}, u32[]{:S(2)}) %collective-permute-start) | collective-permute-done | bytes 163872 | tf_op jit(solution)/shard_map/ppermute | solution.py:77
  114.8 0.6 constant_dynamic-update-slice_fusion.12
  115.5 0.6 constant_dynamic-update-slice_fusion.11
  116.1 0.6 constant_dynamic-update-slice_fusion.10
  117.3 0.6 constant_dynamic-update-slice_fusion.8
  118.1 0.7 pad_maximum_fusion.3
  118.8 5.4 %collective-permute-start.4 = (f32[4,64,128]{2,1,0:T(8,128)}, f32[4,64,128]{2,1,0:T(8,128)S(1)}, u32[]{:S(2)}, u32[]{:S(2)}) collective-permute-start(f32[4,64,128]{2,1,0:T(8,128)} %pad_maximum_fusion.3), channel_id=1, source_target_pairs={{3,0},{4,1},{5,2},{6,3},{7,4},{8,5},{9,6},{10,7},{11,8},{12,9},{13... | collective-permute-start | bytes 393224 | tf_op jit(solution)/shard_map/ppermute | solution.py:77
  124.1 4.9 %collective-permute-done.3 = f32[8,64,128]{2,1,0:T(8,128)S(1)} collective-permute-done((f32[8,64,128]{2,1,0:T(8,128)}, f32[8,64,128]{2,1,0:T(8,128)S(1)}, u32[]{:S(2)}, u32[]{:S(2)}) %collective-permute-start.3) | collective-permute-done | bytes 262176 | tf_op jit(solution)/shard_map/ppermute | solution.py:77
  129.1 0.7 copy-done.8
  129.8 0.9 slice_dynamic-update-slice_fusion
  130.9 3.5 %collective-permute-start.1 = (f32[3,128,256]{1,2,0:T(8,128)S(1)}, f32[3,128,256]{1,2,0:T(8,128)S(1)}, u32[]{:S(2)}, u32[]{:S(2)}) collective-permute-start(f32[3,128,256]{1,2,0:T(8,128)S(1)} %pad_maximum_fusion), channel_id=1, source_target_pairs={{0,64},{1,65},{2,66},{3,67},{4,68},{5,69},{6,70},{7,71},{8,72},{9,... | collective-permute-start | bytes 1179656 | tf_op jit(solution)/shard_map/ppermute | solution.py:84
  134.5 8.8 %collective-permute-done.1 = f32[3,128,256]{1,2,0:T(8,128)S(1)} collective-permute-done((f32[3,128,256]{1,2,0:T(8,128)S(1)}, f32[3,128,256]{1,2,0:T(8,128)S(1)}, u32[]{:S(2)}, u32[]{:S(2)}) %collective-permute-start.1) | collective-permute-done | bytes 393248 | tf_op jit(solution)/shard_map/ppermute | solution.py:84
  145.1 1.9 collective-permute-start.5
  147.0 9.0 %collective-permute-start.6 = (f32[4,64,128]{2,1,0:T(8,128)S(1)}, f32[4,64,128]{2,1,0:T(8,128)S(1)}, u32[]{:S(2)}, u32[]{:S(2)}) collective-permute-start(f32[4,64,128]{2,1,0:T(8,128)S(1)} %get-tuple-element.18), channel_id=1, source_target_pairs={{2,64},{3,65},{4,66},{5,67},{6,68},{7,69},{8,70},{9,71},{10,72},{1... | collective-permute-start | bytes 393224 | tf_op jit(solution)/shard_map/ppermute | solution.py:84
  156.5 1.9 collective-permute-done.6
  159.4 1.9 collective-permute-start.7
  161.4 8.6 %collective-permute-start.8 = (f32[4,64,128]{2,1,0:T(8,128)S(1)}, f32[4,64,128]{2,1,0:T(8,128)S(1)}, u32[]{:S(2)}, u32[]{:S(2)}) collective-permute-start(f32[4,64,128]{2,1,0:T(8,128)S(1)} %fusion.117), channel_id=1, source_target_pairs={{2,64},{3,65},{4,66},{5,67},{6,68},{7,69},{8,70},{9,71},{10,72},{1... | collective-permute-start | bytes 393224 | tf_op jit(solution)/shard_map/ppermute | solution.py:84
  171.1 1.3 collective-permute-done.8
  173.2 0.8 fusion.122
  174.0 8.6 %collective-permute-start.10 = (f32[4,64,128]{2,1,0:T(8,128)}, f32[4,64,128]{2,1,0:T(8,128)}, u32[]{:S(2)}, u32[]{:S(2)}) collective-permute-start(f32[4,64,128]{2,1,0:T(8,128)} %fusion.122), channel_id=1, source_target_pairs={{2,64},{3,65},{4,66},{5,67},{6,68},{7,69},{8,70},{9,71},{10,72},{1... | collective-permute-start | bytes 393224 | tf_op jit(solution)/shard_map/ppermute | solution.py:84
  182.6 2.2 %collective-permute-start.9 = (f32[4,64,128]{2,1,0:T(8,128)}, f32[4,64,128]{2,1,0:T(8,128)}, u32[]{:S(2)}, u32[]{:S(2)}) collective-permute-start(f32[4,64,128]{2,1,0:T(8,128)} %fusion.122), channel_id=1, source_target_pairs={{62,64},{63,65},{0,66},{1,67},{2,68},{3,69},{4,70},{5,71},{6,72},{... | collective-permute-start | bytes 393224 | tf_op jit(solution)/shard_map/ppermute | solution.py:84
  185.4 1.0 copy.134
  186.4 0.9 slice.720
  187.5 6.6 %collective-permute-done.9 = f32[4,64,128]{2,1,0:T(8,128)} collective-permute-done((f32[4,64,128]{2,1,0:T(8,128)}, f32[4,64,128]{2,1,0:T(8,128)}, u32[]{:S(2)}, u32[]{:S(2)}) %collective-permute-start.9) | collective-permute-done | bytes 131104 | tf_op jit(solution)/shard_map/ppermute | solution.py:84
  194.0 1.0 maximum_select_fusion.2
  196.5 0.7 fusion.101
  197.2 1.4 convolution_bitcast_fusion
  198.9 1.1 copy.133
  (157 shorter events, 11.6 us)
Async XLA Ops:
  0.6 1.5 copy-start.5
  2.6 1.8 copy-start
  6.0 24.9 %all-to-all-start = ((f32[128,2,256]{2,1,0:T(2,128)}), f32[128,2,256]{2,1,0:T(2,128)S(1)}, u32[]{:S(2)}, u32[]{:S(2)}) async-start(f32[128,2,256]{2,1,0:T(2,128)} %copy.90), calls=%async_computation | async-start | bytes 524288 | tf_op jit(solution)/shard_map/all_to_all | solution.py:49
  33.4 17.9 %all-to-all-start.1 = ((f32[128,2,256]{2,1,0:T(2,128)}), f32[128,2,256]{2,1,0:T(2,128)S(1)}, u32[]{:S(2)}, u32[]{:S(2)}) async-start(f32[128,2,256]{2,1,0:T(2,128)} %copy.94), calls=%async_computation.1 | async-start | bytes 524288 | tf_op jit(solution)/shard_map/all_to_all | solution.py:52
  57.9 17.9 %all-to-all-start.2 = ((f32[128,2,256]{2,1,0:T(2,128)}), f32[128,2,256]{2,1,0:T(2,128)S(1)}, u32[]{:S(2)}, u32[]{:S(2)}) async-start(f32[128,2,256]{2,1,0:T(2,128)} %copy.101), calls=%async_computation.2 | async-start | bytes 524288 | tf_op jit(solution)/shard_map/all_to_all | solution.py:49
  78.2 17.9 %all-to-all-start.3 = ((f32[128,2,256]{2,1,0:T(2,128)}), f32[128,2,256]{2,1,0:T(2,128)S(1)}, u32[]{:S(2)}, u32[]{:S(2)}) async-start(f32[128,2,256]{2,1,0:T(2,128)} %copy.105), calls=%async_computation.3 | async-start | bytes 524288 | tf_op jit(solution)/shard_map/all_to_all | solution.py:52
  83.4 17.8 %copy-start.13 = (pred[256]{0:T(512)(128)(4,1)}, pred[256]{0:T(512)(128)(4,1)S(1)}, u32[]{:S(2)}) copy-start(pred[256]{0:T(512)(128)(4,1)S(1)} %compare_and_fusion.3) | copy-start | bytes 772
  84.0 18.5 %copy-start.9 = (pred[128]{0:T(512)(128)(4,1)}, pred[128]{0:T(512)(128)(4,1)S(1)}, u32[]{:S(2)}) copy-start(pred[128]{0:T(512)(128)(4,1)S(1)} %get-tuple-element.141) | copy-start | bytes 388
  98.5 0.7 copy-start.3
  99.4 1.5 copy-start.1
  99.4 1.5 copy-start.2
  101.1 16.8 %copy-start.4 = (f32[256,256]{1,0:T(8,128)S(1)}, f32[256,256]{1,0:T(8,128)}, u32[]{:S(2)}) copy-start(f32[256,256]{1,0:T(8,128)} %copy-done.3) | copy-start | bytes 786436
  102.9 7.8 %collective-permute-start.2 = (f32[4,64,128]{2,1,0:T(8,128)S(1)}, f32[4,64,128]{2,1,0:T(8,128)S(1)}, u32[]{:S(2)}, u32[]{:S(2)}) collective-permute-start(f32[4,64,128]{2,1,0:T(8,128)S(1)} %pad_maximum_fusion.2), channel_id=1, source_target_pairs={{63,0},{0,1},{1,2},{2,3},{3,4},{4,5},{5,6},{6,7},{7,8},{8,9},{9,10... | collective-permute-start | bytes 393224 | tf_op jit(solution)/shard_map/ppermute | solution.py:77
  111.9 2.9 %collective-permute-start = (f32[5,64,128]{2,1,0:T(8,128)S(1)}, f32[5,64,128]{2,1,0:T(8,128)S(1)}, u32[]{:S(2)}, u32[]{:S(2)}) collective-permute-start(f32[5,64,128]{2,1,0:T(8,128)S(1)} %constant_dynamic-update-slice_fusion.3), channel_id=1, source_target_pairs={{1,0},{2,1},{3,2},{4,3},{5,4},{6,5},{7,6},{8,7},{9,8},{10,9},{11,1... | collective-permute-start | bytes 491528 | tf_op jit(solution)/shard_map/ppermute | solution.py:77
  118.0 11.1 %collective-permute-start.3 = (f32[8,64,128]{2,1,0:T(8,128)}, f32[8,64,128]{2,1,0:T(8,128)S(1)}, u32[]{:S(2)}, u32[]{:S(2)}) collective-permute-start(f32[8,64,128]{2,1,0:T(8,128)} %constant_dynamic-update-slice_fusion.8), channel_id=1, source_target_pairs={{61,0},{62,1},{63,2},{0,3},{1,4},{2,5},{3,6},{4,7},{5,8},{6,9},{7,... | collective-permute-start | bytes 786440 | tf_op jit(solution)/shard_map/ppermute | solution.py:77
  118.8 15.7 %collective-permute-start.4 = (f32[4,64,128]{2,1,0:T(8,128)}, f32[4,64,128]{2,1,0:T(8,128)S(1)}, u32[]{:S(2)}, u32[]{:S(2)}) collective-permute-start(f32[4,64,128]{2,1,0:T(8,128)} %pad_maximum_fusion.3), channel_id=1, source_target_pairs={{3,0},{4,1},{5,2},{6,3},{7,4},{8,5},{9,6},{10,7},{11,8},{12,9},{13... | collective-permute-start | bytes 393224 | tf_op jit(solution)/shard_map/ppermute | solution.py:77
  129.1 0.7 copy-start.8
  129.8 4.7 %slice-start = ((f32[8,64,128]{2,1,0:T(8,128)}), f32[1,64,128]{2,1,0:T(8,128)S(1)}, s32[]{:S(2)}) async-start(f32[8,64,128]{2,1,0:T(8,128)} %copy-done.8), calls=%async_computation.4 | async-start | bytes 65536 | tf_op jit(solution)/shard_map/slice | solution.py:130
  130.9 12.4 %collective-permute-start.1 = (f32[3,128,256]{1,2,0:T(8,128)S(1)}, f32[3,128,256]{1,2,0:T(8,128)S(1)}, u32[]{:S(2)}, u32[]{:S(2)}) collective-permute-start(f32[3,128,256]{1,2,0:T(8,128)S(1)} %pad_maximum_fusion), channel_id=1, source_target_pairs={{0,64},{1,65},{2,66},{3,67},{4,68},{5,69},{6,70},{7,71},{8,72},{9,... | collective-permute-start | bytes 1179656 | tf_op jit(solution)/shard_map/ppermute | solution.py:84
  143.3 0.7 copy-start.6
  145.1 11.5 %collective-permute-start.5 = (f32[4,64,128]{2,1,0:T(8,128)S(1)}, f32[4,64,128]{2,1,0:T(8,128)S(1)}, u32[]{:S(2)}, u32[]{:S(2)}) collective-permute-start(f32[4,64,128]{2,1,0:T(8,128)S(1)} %get-tuple-element.18), channel_id=1, source_target_pairs={{62,64},{63,65},{0,66},{1,67},{2,68},{3,69},{4,70},{5,71},{6,72},{... | collective-permute-start | bytes 393224 | tf_op jit(solution)/shard_map/ppermute | solution.py:84
  147.0 11.5 %collective-permute-start.6 = (f32[4,64,128]{2,1,0:T(8,128)S(1)}, f32[4,64,128]{2,1,0:T(8,128)S(1)}, u32[]{:S(2)}, u32[]{:S(2)}) collective-permute-start(f32[4,64,128]{2,1,0:T(8,128)S(1)} %get-tuple-element.18), channel_id=1, source_target_pairs={{2,64},{3,65},{4,66},{5,67},{6,68},{7,69},{8,70},{9,71},{10,72},{1... | collective-permute-start | bytes 393224 | tf_op jit(solution)/shard_map/ppermute | solution.py:84
  159.4 11.7 %collective-permute-start.7 = (f32[4,64,128]{2,1,0:T(8,128)S(1)}, f32[4,64,128]{2,1,0:T(8,128)S(1)}, u32[]{:S(2)}, u32[]{:S(2)}) collective-permute-start(f32[4,64,128]{2,1,0:T(8,128)S(1)} %fusion.117), channel_id=1, source_target_pairs={{62,64},{63,65},{0,66},{1,67},{2,68},{3,69},{4,70},{5,71},{6,72},{... | collective-permute-start | bytes 393224 | tf_op jit(solution)/shard_map/ppermute | solution.py:84
  161.4 11.1 %collective-permute-start.8 = (f32[4,64,128]{2,1,0:T(8,128)S(1)}, f32[4,64,128]{2,1,0:T(8,128)S(1)}, u32[]{:S(2)}, u32[]{:S(2)}) collective-permute-start(f32[4,64,128]{2,1,0:T(8,128)S(1)} %fusion.117), channel_id=1, source_target_pairs={{2,64},{3,65},{4,66},{5,67},{6,68},{7,69},{8,70},{9,71},{10,72},{1... | collective-permute-start | bytes 393224 | tf_op jit(solution)/shard_map/ppermute | solution.py:84
  174.0 13.4 %collective-permute-start.10 = (f32[4,64,128]{2,1,0:T(8,128)}, f32[4,64,128]{2,1,0:T(8,128)}, u32[]{:S(2)}, u32[]{:S(2)}) collective-permute-start(f32[4,64,128]{2,1,0:T(8,128)} %fusion.122), channel_id=1, source_target_pairs={{2,64},{3,65},{4,66},{5,67},{6,68},{7,69},{8,70},{9,71},{10,72},{1... | collective-permute-start | bytes 393224 | tf_op jit(solution)/shard_map/ppermute | solution.py:84
  182.6 11.4 %collective-permute-start.9 = (f32[4,64,128]{2,1,0:T(8,128)}, f32[4,64,128]{2,1,0:T(8,128)}, u32[]{:S(2)}, u32[]{:S(2)}) collective-permute-start(f32[4,64,128]{2,1,0:T(8,128)} %fusion.122), channel_id=1, source_target_pairs={{62,64},{63,65},{0,66},{1,67},{2,68},{3,69},{4,70},{5,71},{6,72},{... | collective-permute-start | bytes 393224 | tf_op jit(solution)/shard_map/ppermute | solution.py:84
  195.8 0.6 copy-start.11
  195.8 0.7 copy-start.12
  195.8 0.7 copy-start.14
  195.8 0.7 copy-start.18
  195.9 1.3 copy-start.10
  195.9 1.3 copy-start.15
  195.9 1.3 copy-start.16
  195.9 1.3 copy-start.17
  197.2 1.5 copy-start.7

commit v4 on v1

--- a/solution.py
+++ b/solution.py
@@ -201,28 +201,28 @@
     slot = lax.axis_index("tm")
     slices = lax.axis_size("tm")
     local = planes // 2
-    near = gather_bands(
-        [(coarse[0], (0, 0), (1, 1)), (coarse[1], (0, 0), (1, 1)), (coarse[3], (0, 0), (1, 1)),
-         (coarse[4], (0, 0), (1, 1)), (coarse[2], (0, 0), (0, 1))]
+    wide = gather_bands(
+        [(coarse[0], (0, 0), (4, 3)), (coarse[1], (0, 0), (3, 2)), (coarse[3], (0, 0), (3, 2)),
+         (coarse[4], (0, 0), (2, 1)), (coarse[2], (0, 0), (2, 1))]
     )
     previous_two = fetch(values[2], 0, 1)
-    previous_two, near = lax.optimization_barrier((previous_two, near))
-    coarse_two = near[4]
-    wide = gather_bands(
-        [(near[0], (1, 1), (4, 3)), (near[1], (1, 1), (3, 2)), (near[2], (1, 1), (3, 2)),
-         (near[3], (1, 1), (2, 1))]
-    )
-    previous_coarse_two = fetch(coarse_two, 0, 1)
-    previous_coarse_two, wide = lax.optimization_barrier((previous_coarse_two, wide))
+    previous_two, wide = lax.optimization_barrier((previous_two, wide))
     start_c = wide[0]
     rates_c = (coarse_rate(start_c), coarse_rate(wide[1]))
     sums_c = (wide[2], wide[3])
     coarse_one = wide[1][3:4 + local]
+    coarse_two = wide[4][2:3 + local]
     start = start_c
+    previous_coarse_two = None
     for section in range(slices - 1):
         first, second = coarse_sweep(start, rates_c, sums_c)
-        received = gather_bands([(second, (2, 1), (4, 3))], back=1)[0]
-        start = jnp.where(slot == 0, start_c, received)
+        items = [(second, (2, 1), (4, 3))]
+        if previous_coarse_two is None:
+            items.append((wide[4], (2, 1), (0, 1)))
+        received = gather_bands(items, back=1)
+        if previous_coarse_two is None:
+            previous_coarse_two = received[1]
+        start = jnp.where(slot == 0, start_c, received[0])
     first, second = coarse_sweep(start, rates_c, sums_c)
     delta = jnp.stack(
         [first[2:3 + local] - coarse_one, second[2:3 + local] - coarse_two,

time: 180 us -> 185 us (1.028)
  starting transfers between devices: 69.2 us -> 60.9 us
  waiting for transfers between devices: 66 us -> 73.3 us
  local copies, waits for them, and re-layouts: 16.4 us -> 22.2 us
    ppermute x8 -> x7, waiting for transfers between devices: 8.2 us -> 19.3 us  [fetch(): return lax.ppermute(value, ('tm', 'space'), pairs)]
    ppermute x8 -> x7, starting transfers between devices: 38.7 us -> 27.9 us  [fetch(): return lax.ppermute(value, ('tm', 'space'), pairs)]
    unnamed x50 -> x57, local copies, waits for them, and re-layouts: 6.67 us -> 9.23 us
    ppermute x4 -> x7, starting transfers between devices: 3.46 us -> 5.91 us  [fetch(): return lax.ppermute(value, 'space', pairs)]
    ppermute x4 -> x7, waiting for transfers between devices: 10.8 us -> 8.57 us  [fetch(): return lax.ppermute(value, 'space', pairs)]
  transfers between devices with their start and end apart: 16 -> 18, of which waited for: 12 -> 12; matrix products, arithmetic and copies ran while one was open for 4% -> 5% of each run, Pallas kernels for 0% -> 0%
where the time goes in v4:
time: 185 us; the launch traced here: 183 us
  waiting for transfers between devices  73.3 us (40%)
  starting transfers between devices  60.9 us (33%)
  local copies, waits for them, and re-layouts  22.2 us (12%)
  matrix products  16.7 us (9%)
  other arithmetic  8.63 us (5%)
  between operations  1.85 us (1%)
    all_to_all x4, waiting for transfers between devices, spectral_solve(): lax.all_to_all(field, 'space', split_axis=0, concat_axis=1, tiled=True)  45.4 us
    ppermute x7, starting transfers between devices, fetch(): return lax.ppermute(value, ('tm', 'space'), pairs)  27.9 us
    all_to_all x4, starting transfers between devices, spectral_solve(): lax.all_to_all(field, 'space', split_axis=0, concat_axis=1, tiled=True)  27.1 us
    ppermute x7, waiting for transfers between devices, fetch(): return lax.ppermute(value, ('tm', 'space'), pairs)  19.3 us
    unnamed x57, local copies, waits for them, and re-layouts  9.23 us
    ppermute x7, waiting for transfers between devices, fetch(): return lax.ppermute(value, 'space', pairs)  8.57 us
    ppermute x7, starting transfers between devices, fetch(): return lax.ppermute(value, 'space', pairs)  5.91 us
    dot_general x2, matrix products, spectral_solve(): jnp.dot(field.reshape(planes * size_y, size_z), basis_z, precision=HIGHEST)  4.2 us
  transfers between devices with their start and end apart: 18, of which 12 were waited for; matrix products, arithmetic and copies ran while one was open for 5% of the time, Pallas kernels for 0%

profile of v4, /device:TPU:8, one launch (start us, length us, event | category | flops | bytes accessed | tf_op | source)
XLA Modules:
  0.0 183.5 jit_solution(8549527858991302403)
XLA Ops:
  0.7 1.4 copy.80
  2.6 1.8 fusion.14
  4.4 0.7 fusion.178
  5.1 0.9 copy.86
  6.0 11.9 %all-to-all-start = ((f32[128,2,256]{2,1,0:T(2,128)}), f32[128,2,256]{2,1,0:T(2,128)S(1)}, u32[]{:S(2)}, u32[]{:S(2)}) async-start(f32[128,2,256]{2,1,0:T(2,128)} %copy.86), calls=%async_computation | async-start | bytes 524288 | tf_op jit(solution)/shard_map/all_to_all | solution.py:49
  18.1 12.8 %all-to-all-done = f32[128,2,256]{2,1,0:T(2,128)S(1)} async-done(((f32[128,2,256]{2,1,0:T(2,128)}), f32[128,2,256]{2,1,0:T(2,128)S(1)}, u32[]{:S(2)}, u32[]{:S(2)}) %all-to-all-start) | async-done | bytes 262176 | tf_op jit(solution)/shard_map/all_to_all | solution.py:49
  31.1 0.7 convolution_multiply_fusion.1
  31.8 0.7 fusion.190
  32.4 0.9 copy.90
  33.3 5.1 %all-to-all-start.1 = ((f32[128,2,256]{2,1,0:T(2,128)}), f32[128,2,256]{2,1,0:T(2,128)S(1)}, u32[]{:S(2)}, u32[]{:S(2)}) async-start(f32[128,2,256]{2,1,0:T(2,128)} %copy.90), calls=%async_computation.1 | async-start | bytes 524288 | tf_op jit(solution)/shard_map/all_to_all | solution.py:52
  38.5 0.7 slice.743
  39.2 1.8 copy.92
  41.0 0.8 copy.95
  41.9 0.7 slice_bitcast_fusion.1
  42.6 0.8 copy.94
  43.4 7.8 %all-to-all-done.1 = f32[128,2,256]{2,1,0:T(2,128)S(1)} async-done(((f32[128,2,256]{2,1,0:T(2,128)}), f32[128,2,256]{2,1,0:T(2,128)S(1)}, u32[]{:S(2)}, u32[]{:S(2)}) %all-to-all-start.1) | async-done | bytes 262176 | tf_op jit(solution)/shard_map/all_to_all | solution.py:52
  51.5 0.7 fusion.188
  52.1 2.7 %fusion.23 = (f32[256,256]{1,0:T(8,128)S(1)}, f32[256,256]{1,0:T(8,128)S(1)}) fusion(f32[1,2,128,256]{3,2,1,0:T(8,128)} %copy.95, f32[1,1,2,128,256]{4,3,2,1,0:T(8,128)} %copy.94, f32[1,2,128,256]{3,2,1,0:T(8,128)} %copy.92, f32[256,256]{1,0:T(8,128)S(1)} %bitcast.222, f32[256]{0:T(256)S(1)} %fusion.246, s32[256]{0:T(256)S(1)} %iota_add_fusion, ...), kind=kOutput, calls=%fused_computation.47 | convolution fusion | flops 202964992 | bytes 1575168 | tf_op jit(solution)/shard_map/dot_general | solution.py:54
  54.8 1.5 fusion.48
  56.4 0.7 fusion.181
  57.1 0.9 copy.97
  58.0 4.9 %all-to-all-start.2 = ((f32[128,2,256]{2,1,0:T(2,128)}), f32[128,2,256]{2,1,0:T(2,128)S(1)}, u32[]{:S(2)}, u32[]{:S(2)}) async-start(f32[128,2,256]{2,1,0:T(2,128)} %copy.97), calls=%async_computation.2 | async-start | bytes 524288 | tf_op jit(solution)/shard_map/all_to_all | solution.py:49
  62.9 12.9 %all-to-all-done.2 = f32[128,2,256]{2,1,0:T(2,128)S(1)} async-done(((f32[128,2,256]{2,1,0:T(2,128)}), f32[128,2,256]{2,1,0:T(2,128)S(1)}, u32[]{:S(2)}, u32[]{:S(2)}) %all-to-all-start.2) | async-done | bytes 262176 | tf_op jit(solution)/shard_map/all_to_all | solution.py:49
  76.0 0.7 convolution_multiply_fusion
  76.7 0.7 fusion.186
  77.3 0.9 copy.101
  78.3 5.1 %all-to-all-start.3 = ((f32[128,2,256]{2,1,0:T(2,128)}), f32[128,2,256]{2,1,0:T(2,128)S(1)}, u32[]{:S(2)}, u32[]{:S(2)}) async-start(f32[128,2,256]{2,1,0:T(2,128)} %copy.101), calls=%async_computation.3 | async-start | bytes 524288 | tf_op jit(solution)/shard_map/all_to_all | solution.py:52
  83.4 0.7 slice_bitcast_fusion.2
  84.3 11.8 %all-to-all-done.3 = f32[128,2,256]{2,1,0:T(2,128)S(1)} async-done(((f32[128,2,256]{2,1,0:T(2,128)}), f32[128,2,256]{2,1,0:T(2,128)S(1)}, u32[]{:S(2)}, u32[]{:S(2)}) %all-to-all-start.3) | async-done | bytes 262176 | tf_op jit(solution)/shard_map/all_to_all | solution.py:52
  96.4 0.7 fusion.184
  97.0 1.5 fusion.161
  98.6 0.7 copy-done.5
  99.4 1.4 fusion.30
  101.7 1.3 fusion.3
  103.4 0.6 constant_dynamic-update-slice_fusion.7
  104.0 0.6 constant_dynamic-update-slice_fusion.6
  104.6 0.6 constant_dynamic-update-slice_fusion.5
  105.2 0.6 constant_dynamic-update-slice_fusion.4
  105.8 0.6 constant_dynamic-update-slice_fusion.3
  106.5 0.8 collective-permute-start.3
  107.3 5.1 %collective-permute-start.5 = (f32[5,64,128]{2,1,0:T(8,128)}, f32[5,64,128]{2,1,0:T(8,128)S(1)}, u32[]{:S(2)}, u32[]{:S(2)}) collective-permute-start(f32[5,64,128]{2,1,0:T(8,128)} %constant_dynamic-update-slice_fusion.3), channel_id=1, source_target_pairs={{1,0},{2,1},{3,2},{4,3},{5,4},{6,5},{7,6},{8,7},{9,8},{10,9},{11,1... | collective-permute-start | bytes 491528 | tf_op jit(solution)/shard_map/ppermute | solution.py:77
  112.4 0.6 pad_maximum_fusion.4
  113.1 7.0 %collective-permute-done.1 = f32[1,64,128]{2,1,0:T(8,128)S(1)} collective-permute-done((f32[1,64,128]{2,1,0:T(8,128)S(1)}, f32[1,64,128]{2,1,0:T(8,128)S(1)}, u32[]{:S(2)}, u32[]{:S(2)}) %collective-permute-start.1) | collective-permute-done | bytes 32800 | tf_op jit(solution)/shard_map/ppermute | solution.py:77
  120.2 1.3 collective-permute-done.2
  121.5 3.5 %collective-permute-start = (f32[2,128,256]{1,2,0:T(8,128)S(1)}, f32[2,128,256]{1,2,0:T(8,128)S(1)}, u32[]{:S(2)}, u32[]{:S(2)}) collective-permute-start(f32[2,128,256]{1,2,0:T(8,128)S(1)} %copy.103), channel_id=1, source_target_pairs={{0,64},{1,65},{2,66},{3,67},{4,68},{5,69},{6,70},{7,71},{8,72},{9,... | collective-permute-start | bytes 786440 | tf_op jit(solution)/shard_map/ppermute | solution.py:84
  125.4 7.1 %collective-permute-done = f32[2,128,256]{1,2,0:T(8,128)S(1)} collective-permute-done((f32[2,128,256]{1,2,0:T(8,128)S(1)}, f32[2,128,256]{1,2,0:T(8,128)S(1)}, u32[]{:S(2)}, u32[]{:S(2)}) %collective-permute-start) | collective-permute-done | bytes 262176 | tf_op jit(solution)/shard_map/ppermute | solution.py:84
  134.5 3.4 %collective-permute-start.9 = (f32[6,64,128]{2,1,0:T(8,128)S(1)}, f32[6,64,128]{2,1,0:T(8,128)S(1)}, u32[]{:S(2)}, u32[]{:S(2)}) collective-permute-start(f32[6,64,128]{2,1,0:T(8,128)S(1)} %pad_maximum_fusion.1), channel_id=1, source_target_pairs={{2,64},{3,65},{4,66},{5,67},{6,68},{7,69},{8,70},{9,71},{10,72},{1... | collective-permute-start | bytes 589832 | tf_op jit(solution)/shard_map/ppermute | solution.py:84
  138.0 4.4 %collective-permute-start.8 = (f32[4,64,128]{2,1,0:T(8,128)S(1)}, f32[4,64,128]{2,1,0:T(8,128)S(1)}, u32[]{:S(2)}, u32[]{:S(2)}) collective-permute-start(f32[4,64,128]{2,1,0:T(8,128)S(1)} %get-tuple-element.20), channel_id=1, source_target_pairs={{62,64},{63,65},{0,66},{1,67},{2,68},{3,69},{4,70},{5,71},{6,72},{... | collective-permute-start | bytes 393224 | tf_op jit(solution)/shard_map/ppermute | solution.py:84
  142.9 1.2 collective-permute-done.9
  144.2 6.0 %collective-permute-done.8 = f32[4,64,128]{2,1,0:T(8,128)S(1)} collective-permute-done((f32[4,64,128]{2,1,0:T(8,128)S(1)}, f32[4,64,128]{2,1,0:T(8,128)S(1)}, u32[]{:S(2)}, u32[]{:S(2)}) %collective-permute-start.8) | collective-permute-done | bytes 131104 | tf_op jit(solution)/shard_map/ppermute | solution.py:84
  151.1 1.9 %collective-permute-start.10 = (f32[4,64,128]{2,1,0:T(8,128)S(1)}, f32[4,64,128]{2,1,0:T(8,128)S(1)}, u32[]{:S(2)}, u32[]{:S(2)}) collective-permute-start(f32[4,64,128]{2,1,0:T(8,128)S(1)} %fusion.117), channel_id=1, source_target_pairs={{62,64},{63,65},{0,66},{1,67},{2,68},{3,69},{4,70},{5,71},{6,72},{... | collective-permute-start | bytes 393224 | tf_op jit(solution)/shard_map/ppermute | solution.py:84
  153.0 6.2 %collective-permute-start.11 = (f32[4,64,128]{2,1,0:T(8,128)S(1)}, f32[4,64,128]{2,1,0:T(8,128)S(1)}, u32[]{:S(2)}, u32[]{:S(2)}) collective-permute-start(f32[4,64,128]{2,1,0:T(8,128)S(1)} %fusion.117), channel_id=1, source_target_pairs={{2,64},{3,65},{4,66},{5,67},{6,68},{7,69},{8,70},{9,71},{10,72},{1... | collective-permute-start | bytes 393224 | tf_op jit(solution)/shard_map/ppermute | solution.py:84
  159.3 0.6 compare_and_fusion.1
  159.8 0.5 iota_and_fusion
  160.4 3.4 %collective-permute-done.10 = f32[4,64,128]{2,1,0:T(8,128)S(1)} collective-permute-done((f32[4,64,128]{2,1,0:T(8,128)S(1)}, f32[4,64,128]{2,1,0:T(8,128)S(1)}, u32[]{:S(2)}, u32[]{:S(2)}) %collective-permute-start.10) | collective-permute-done | bytes 131104 | tf_op jit(solution)/shard_map/ppermute | solution.py:84
  164.8 1.9 %collective-permute-start.12 = (f32[4,64,128]{2,1,0:T(8,128)S(1)}, f32[4,64,128]{2,1,0:T(8,128)}, u32[]{:S(2)}, u32[]{:S(2)}) collective-permute-start(f32[4,64,128]{2,1,0:T(8,128)S(1)} %fusion.122), channel_id=1, source_target_pairs={{62,64},{63,65},{0,66},{1,67},{2,68},{3,69},{4,70},{5,71},{6,72},{... | collective-permute-start | bytes 393224 | tf_op jit(solution)/shard_map/ppermute | solution.py:84
  166.7 6.5 %collective-permute-start.13 = (f32[4,64,128]{2,1,0:T(8,128)S(1)}, f32[4,64,128]{2,1,0:T(8,128)}, u32[]{:S(2)}, u32[]{:S(2)}) collective-permute-start(f32[4,64,128]{2,1,0:T(8,128)S(1)} %fusion.122), channel_id=1, source_target_pairs={{2,64},{3,65},{4,66},{5,67},{6,68},{7,69},{8,70},{9,71},{10,72},{1... | collective-permute-start | bytes 393224 | tf_op jit(solution)/shard_map/ppermute | solution.py:84
  173.8 1.0 copy.128
  174.8 1.6 collective-permute-done.12
  176.3 1.0 maximum_select_fusion.2
  179.0 0.7 fusion.101
  179.7 1.4 convolution_bitcast_fusion
  181.3 0.9 copy-done.11
  182.3 1.1 copy.127
  (158 shorter events, 9.7 us)
Async XLA Ops:
  0.6 1.5 copy-start.7
  2.6 35.8 %copy-start = (f32[3,2,128,256]{2,3,1,0:T(8,128)}, f32[3,2,128,256]{2,3,1,0:T(8,128)S(1)}, u32[]{:S(2)}) copy-start(f32[3,2,128,256]{2,3,1,0:T(8,128)S(1)} %get-tuple-element.34) | copy-start | bytes 2359300
  6.0 24.9 %all-to-all-start = ((f32[128,2,256]{2,1,0:T(2,128)}), f32[128,2,256]{2,1,0:T(2,128)S(1)}, u32[]{:S(2)}, u32[]{:S(2)}) async-start(f32[128,2,256]{2,1,0:T(2,128)} %copy.86), calls=%async_computation | async-start | bytes 524288 | tf_op jit(solution)/shard_map/all_to_all | solution.py:49
  33.3 17.9 %all-to-all-start.1 = ((f32[128,2,256]{2,1,0:T(2,128)}), f32[128,2,256]{2,1,0:T(2,128)S(1)}, u32[]{:S(2)}, u32[]{:S(2)}) async-start(f32[128,2,256]{2,1,0:T(2,128)} %copy.90), calls=%async_computation.1 | async-start | bytes 524288 | tf_op jit(solution)/shard_map/all_to_all | solution.py:52
  58.0 17.9 %all-to-all-start.2 = ((f32[128,2,256]{2,1,0:T(2,128)}), f32[128,2,256]{2,1,0:T(2,128)S(1)}, u32[]{:S(2)}, u32[]{:S(2)}) async-start(f32[128,2,256]{2,1,0:T(2,128)} %copy.97), calls=%async_computation.2 | async-start | bytes 524288 | tf_op jit(solution)/shard_map/all_to_all | solution.py:49
  62.9 38.8 %copy-start.16 = (pred[256]{0:T(512)(128)(4,1)}, pred[256]{0:T(512)(128)(4,1)S(1)}, u32[]{:S(2)}) copy-start(pred[256]{0:T(512)(128)(4,1)S(1)} %compare_and_fusion.3) | copy-start | bytes 772
  78.3 17.9 %all-to-all-start.3 = ((f32[128,2,256]{2,1,0:T(2,128)}), f32[128,2,256]{2,1,0:T(2,128)S(1)}, u32[]{:S(2)}, u32[]{:S(2)}) async-start(f32[128,2,256]{2,1,0:T(2,128)} %copy.101), calls=%async_computation.3 | async-start | bytes 524288 | tf_op jit(solution)/shard_map/all_to_all | solution.py:52
  83.4 19.6 %copy-start.12 = (s32[128]{0:T(128)}, s32[128]{0:T(128)S(1)}, u32[]{:S(2)}) copy-start(s32[128]{0:T(128)S(1)} %get-tuple-element.143) | copy-start | bytes 1540
  98.6 0.7 copy-start.5
  99.4 1.5 copy-start.3
  99.4 1.5 copy-start.4
  100.8 0.7 copy-start.1
  101.7 11.4 %copy-start.6 = (f32[256,256]{1,0:T(8,128)S(1)}, f32[256,256]{1,0:T(8,128)}, u32[]{:S(2)}) copy-start(f32[256,256]{1,0:T(8,128)} %copy-done.5) | copy-start | bytes 786436
  106.5 15.0 %collective-permute-start.3 = (f32[5,64,128]{2,1,0:T(8,128)}, f32[5,64,128]{2,1,0:T(8,128)S(1)}, u32[]{:S(2)}, u32[]{:S(2)}) collective-permute-start(f32[5,64,128]{2,1,0:T(8,128)} %constant_dynamic-update-slice_fusion.3), channel_id=1, source_target_pairs={{62,0},{63,1},{0,2},{1,3},{2,4},{3,5},{4,6},{5,7},{6,8},{7,9},{8,1... | collective-permute-start | bytes 491528 | tf_op jit(solution)/shard_map/ppermute | solution.py:77
  107.3 17.7 %collective-permute-start.4 = (f32[5,64,128]{2,1,0:T(8,128)}, f32[5,64,128]{2,1,0:T(8,128)S(1)}, u32[]{:S(2)}, u32[]{:S(2)}) collective-permute-start(f32[5,64,128]{2,1,0:T(8,128)} %constant_dynamic-update-slice_fusion.3), channel_id=1, source_target_pairs={{63,0},{0,1},{1,2},{2,3},{3,4},{4,5},{5,6},{6,7},{7,8},{8,9},{9,10... | collective-permute-start | bytes 491528 | tf_op jit(solution)/shard_map/ppermute | solution.py:77
  107.3 17.8 %collective-permute-start.5 = (f32[5,64,128]{2,1,0:T(8,128)}, f32[5,64,128]{2,1,0:T(8,128)S(1)}, u32[]{:S(2)}, u32[]{:S(2)}) collective-permute-start(f32[5,64,128]{2,1,0:T(8,128)} %constant_dynamic-update-slice_fusion.3), channel_id=1, source_target_pairs={{1,0},{2,1},{3,2},{4,3},{5,4},{6,5},{7,6},{8,7},{9,8},{10,9},{11,1... | collective-permute-start | bytes 491528 | tf_op jit(solution)/shard_map/ppermute | solution.py:77
  112.4 7.8 %collective-permute-start.1 = (f32[1,64,128]{2,1,0:T(8,128)S(1)}, f32[1,64,128]{2,1,0:T(8,128)S(1)}, u32[]{:S(2)}, u32[]{:S(2)}) collective-permute-start(f32[1,64,128]{2,1,0:T(8,128)S(1)} %get-tuple-element.128), channel_id=1, source_target_pairs={{60,0},{61,1},{62,2},{63,3},{0,4},{1,5},{2,6},{3,7},{4,8},{5,9},{6... | collective-permute-start | bytes 98312 | tf_op jit(solution)/shard_map/ppermute | solution.py:77
  113.0 8.5 %collective-permute-start.2 = (f32[3,64,128]{2,1,0:T(8,128)}, f32[3,64,128]{2,1,0:T(8,128)S(1)}, u32[]{:S(2)}, u32[]{:S(2)}) collective-permute-start(f32[3,64,128]{2,1,0:T(8,128)} %pad_maximum_fusion.4), channel_id=1, source_target_pairs={{61,0},{62,1},{63,2},{0,3},{1,4},{2,5},{3,6},{4,7},{5,8},{6,9},{7,... | collective-permute-start | bytes 294920 | tf_op jit(solution)/shard_map/ppermute | solution.py:77
  120.2 5.2 %collective-permute-start.6 = (f32[3,64,128]{2,1,0:T(8,128)}, f32[3,64,128]{2,1,0:T(8,128)S(1)}, u32[]{:S(2)}, u32[]{:S(2)}) collective-permute-start(f32[3,64,128]{2,1,0:T(8,128)} %pad_maximum_fusion.4), channel_id=1, source_target_pairs={{2,0},{3,1},{4,2},{5,3},{6,4},{7,5},{8,6},{9,7},{10,8},{11,9},{12,... | collective-permute-start | bytes 294920 | tf_op jit(solution)/shard_map/ppermute | solution.py:77
  121.5 3.9 %collective-permute-start.7 = (f32[1,64,128]{2,1,0:T(8,128)S(1)}, f32[1,64,128]{2,1,0:T(8,128)S(1)}, u32[]{:S(2)}, u32[]{:S(2)}) collective-permute-start(f32[1,64,128]{2,1,0:T(8,128)S(1)} %get-tuple-element.128), channel_id=1, source_target_pairs={{3,0},{4,1},{5,2},{6,3},{7,4},{8,5},{9,6},{10,7},{11,8},{12,9},{13... | collective-permute-start | bytes 98312 | tf_op jit(solution)/shard_map/ppermute | solution.py:77
  121.5 11.0 %collective-permute-start = (f32[2,128,256]{1,2,0:T(8,128)S(1)}, f32[2,128,256]{1,2,0:T(8,128)S(1)}, u32[]{:S(2)}, u32[]{:S(2)}) collective-permute-start(f32[2,128,256]{1,2,0:T(8,128)S(1)} %copy.103), channel_id=1, source_target_pairs={{0,64},{1,65},{2,66},{3,67},{4,68},{5,69},{6,70},{7,71},{8,72},{9,... | collective-permute-start | bytes 786440 | tf_op jit(solution)/shard_map/ppermute | solution.py:84
  125.4 8.3 %copy-start.8 = (f32[4,64,128]{2,1,0:T(8,128)}, f32[4,64,128]{2,1,0:T(8,128)S(1)}, u32[]{:S(2)}) copy-start(f32[4,64,128]{2,1,0:T(8,128)S(1)} %pad_maximum_fusion.3) | copy-start | bytes 393220
  132.5 0.7 copy-start.10
  133.7 0.8 slice-start
  134.5 9.6 %collective-permute-start.9 = (f32[6,64,128]{2,1,0:T(8,128)S(1)}, f32[6,64,128]{2,1,0:T(8,128)S(1)}, u32[]{:S(2)}, u32[]{:S(2)}) collective-permute-start(f32[6,64,128]{2,1,0:T(8,128)S(1)} %pad_maximum_fusion.1), channel_id=1, source_target_pairs={{2,64},{3,65},{4,66},{5,67},{6,68},{7,69},{8,70},{9,71},{10,72},{1... | collective-permute-start | bytes 589832 | tf_op jit(solution)/shard_map/ppermute | solution.py:84
  138.0 12.2 %collective-permute-start.8 = (f32[4,64,128]{2,1,0:T(8,128)S(1)}, f32[4,64,128]{2,1,0:T(8,128)S(1)}, u32[]{:S(2)}, u32[]{:S(2)}) collective-permute-start(f32[4,64,128]{2,1,0:T(8,128)S(1)} %get-tuple-element.20), channel_id=1, source_target_pairs={{62,64},{63,65},{0,66},{1,67},{2,68},{3,69},{4,70},{5,71},{6,72},{... | collective-permute-start | bytes 393224 | tf_op jit(solution)/shard_map/ppermute | solution.py:84
  151.1 12.7 %collective-permute-start.10 = (f32[4,64,128]{2,1,0:T(8,128)S(1)}, f32[4,64,128]{2,1,0:T(8,128)S(1)}, u32[]{:S(2)}, u32[]{:S(2)}) collective-permute-start(f32[4,64,128]{2,1,0:T(8,128)S(1)} %fusion.117), channel_id=1, source_target_pairs={{62,64},{63,65},{0,66},{1,67},{2,68},{3,69},{4,70},{5,71},{6,72},{... | collective-permute-start | bytes 393224 | tf_op jit(solution)/shard_map/ppermute | solution.py:84
  153.0 10.8 %collective-permute-start.11 = (f32[4,64,128]{2,1,0:T(8,128)S(1)}, f32[4,64,128]{2,1,0:T(8,128)S(1)}, u32[]{:S(2)}, u32[]{:S(2)}) collective-permute-start(f32[4,64,128]{2,1,0:T(8,128)S(1)} %fusion.117), channel_id=1, source_target_pairs={{2,64},{3,65},{4,66},{5,67},{6,68},{7,69},{8,70},{9,71},{10,72},{1... | collective-permute-start | bytes 393224 | tf_op jit(solution)/shard_map/ppermute | solution.py:84
  164.5 9.3 %copy-start.2 = (f32[1,2,128,256]{2,3,1,0:T(8,128)S(1)}, f32[1,2,128,256]{2,3,1,0:T(8,128)}, u32[]{:S(2)}) copy-start(f32[1,2,128,256]{2,3,1,0:T(8,128)} %copy-done.1) | copy-start | bytes 786436
  164.8 11.6 %collective-permute-start.12 = (f32[4,64,128]{2,1,0:T(8,128)S(1)}, f32[4,64,128]{2,1,0:T(8,128)}, u32[]{:S(2)}, u32[]{:S(2)}) collective-permute-start(f32[4,64,128]{2,1,0:T(8,128)S(1)} %fusion.122), channel_id=1, source_target_pairs={{62,64},{63,65},{0,66},{1,67},{2,68},{3,69},{4,70},{5,71},{6,72},{... | collective-permute-start | bytes 393224 | tf_op jit(solution)/shard_map/ppermute | solution.py:84
  166.7 9.6 %collective-permute-start.13 = (f32[4,64,128]{2,1,0:T(8,128)S(1)}, f32[4,64,128]{2,1,0:T(8,128)}, u32[]{:S(2)}, u32[]{:S(2)}) collective-permute-start(f32[4,64,128]{2,1,0:T(8,128)S(1)} %fusion.122), channel_id=1, source_target_pairs={{2,64},{3,65},{4,66},{5,67},{6,68},{7,69},{8,70},{9,71},{10,72},{1... | collective-permute-start | bytes 393224 | tf_op jit(solution)/shard_map/ppermute | solution.py:84
  178.0 0.9 copy-start.9
  178.1 0.9 copy-start.14
  178.1 0.9 copy-start.15
  178.1 0.9 copy-start.17
  178.1 0.9 copy-start.21
  178.3 1.4 copy-start.13
  178.3 1.4 copy-start.18
  178.3 1.4 copy-start.19
  178.3 1.4 copy-start.20
  181.2 1.0 copy-start.11

commit v5 on v1

--- a/solution.py
+++ b/solution.py
@@ -98,6 +98,8 @@
             offset = (at + have[0]) // local
             best = (offset, offset * local - have[0], offset * local + local + have[1])
         upto = min(best[2], high)
+        if best[0] != 0 and 0 in allowed and at < -have[0] < upto:
+            upto = -have[0]
         plan.append((best[0], at - best[1], upto - best[1]))
         at = upto
     return plan
@@ -160,9 +162,10 @@
     return spread(both[:, :planes], both[:, 1:], 1)
 
 
-def coarse_sweep(start, rates, sums):
-    first = start[1:-1] + 0.25 * (coarse_rate(start) - rates[0]) + sums[0]
-    second = first[1:-1] + 0.25 * (coarse_rate(first) - rates[1]) + sums[1]
+def coarse_sweep(start, rates, sums, trim):
+    inner = lambda band: band[trim:band.shape[0] - trim]
+    first = start[1:-1] + 0.25 * (coarse_rate(start) - inner(rates[0])) + inner(sums[0])
+    second = first[1:-1] + 0.25 * (coarse_rate(first) - inner(rates[1])) + inner(sums[1])
     return (first[1:-1], second)
 
 
@@ -208,26 +211,30 @@
     previous_two = fetch(values[2], 0, 1)
     previous_two, near = lax.optimization_barrier((previous_two, near))
     coarse_two = near[4]
+    reach = 2 * slices
+    mid = gather_bands([(band, (1, 1), (4, 4)) for band in near[:4]])
     wide = gather_bands(
-        [(near[0], (1, 1), (4, 3)), (near[1], (1, 1), (3, 2)), (near[2], (1, 1), (3, 2)),
-         (near[3], (1, 1), (2, 1))]
+        [(mid[0], (4, 4), (reach, reach + 1)), (mid[1], (4, 4), (reach - 1, reach)),
+         (mid[2], (4, 4), (reach - 1, reach)), (mid[3], (4, 4), (reach - 2, reach - 1))]
     )
-    previous_coarse_two = fetch(coarse_two, 0, 1)
-    previous_coarse_two, wide = lax.optimization_barrier((previous_coarse_two, wide))
     start_c = wide[0]
     rates_c = (coarse_rate(start_c), coarse_rate(wide[1]))
     sums_c = (wide[2], wide[3])
-    coarse_one = wide[1][3:4 + local]
+    coarse_one = wide[1][reach - 1:reach + local]
     start = start_c
+    previous_coarse_two = None
     for section in range(slices - 1):
-        first, second = coarse_sweep(start, rates_c, sums_c)
-        received = gather_bands([(second, (2, 1), (4, 3))], back=1)[0]
-        start = jnp.where(slot == 0, start_c, received)
-    first, second = coarse_sweep(start, rates_c, sums_c)
-    delta = jnp.stack(
-        [first[2:3 + local] - coarse_one, second[2:3 + local] - coarse_two,
-         start[4:5 + local] - previous_coarse_two]
-    )
+        first, second = coarse_sweep(start, rates_c, sums_c, 2 * section)
+        if previous_coarse_two is None:
+            sent = fetch(jnp.concatenate([second, coarse_two]), 0, 1)
+            received = sent[:second.shape[0]]
+            previous_coarse_two = sent[second.shape[0]:]
+        else:
+            received = fetch(second, 0, 1)
+        trim = 2 * (section + 1)
+        start = jnp.where(slot == 0, start_c[trim:start_c.shape[0] - trim], received)
+    first, second = coarse_sweep(start, rates_c, sums_c, 2 * (slices - 1))
+    delta = jnp.stack([first - coarse_one, second - coarse_two, start[2:3 + local] - previous_coarse_two])
     corr = refine(delta)
     fixed_one = values[1] + corr[0]
     fixed_two = values[2] + corr[1]

time: 180 us -> 209 us (1.16)
  the two profiles are of different devices: /device:TPU:8 before, /device:TPU:10 now
where the time goes in v5:
time: 209 us; the launch traced here: 208 us
  waiting for transfers between devices  101 us (48%)
  starting transfers between devices  51.7 us (25%)
  local copies, waits for them, and re-layouts  25.8 us (12%)
  matrix products  18 us (9%)
  other arithmetic  10 us (5%)
    all_to_all x4, waiting for transfers between devices, spectral_solve(): lax.all_to_all(field, 'space', split_axis=0, concat_axis=1, tiled=True)  44 us
    ppermute x6, waiting for transfers between devices, fetch(): return lax.ppermute(value, 'space', pairs)  31.8 us
    all_to_all x4, starting transfers between devices, spectral_solve(): lax.all_to_all(field, 'space', split_axis=0, concat_axis=1, tiled=True)  29 us
    ppermute x4, waiting for transfers between devices, fetch(): return lax.ppermute(value, ('tm', 'space'), pairs)  24.9 us
    ppermute x4, starting transfers between devices, fetch(): return lax.ppermute(value, ('tm', 'space'), pairs)  15.5 us
    unnamed x65, local copies, waits for them, and re-layouts  8.55 us
    ppermute x6, starting transfers between devices, fetch(): return lax.ppermute(value, 'space', pairs)  7.2 us
    dot_general x2, matrix products, spectral_solve(): jnp.dot(field.reshape(planes * size_y, size_z), basis_z, precision=HIGHEST)  5.55 us
  transfers between devices with their start and end apart: 14, of which 11 were waited for; matrix products, arithmetic and copies ran while one was open for 3% of the time, Pallas kernels for 0%

profile of v5, /device:TPU:10, one launch (start us, length us, event | category | flops | bytes accessed | tf_op | source)
XLA Modules:
  0.0 208.0 jit_solution(7192651224825318216)
XLA Ops:
  0.7 1.4 copy.82
  2.6 1.8 fusion.67
  4.4 0.7 fusion.192
  5.1 0.9 copy.86
  6.0 12.0 %all-to-all-start = ((f32[128,2,256]{2,1,0:T(2,128)}), f32[128,2,256]{2,1,0:T(2,128)S(1)}, u32[]{:S(2)}, u32[]{:S(2)}) async-start(f32[128,2,256]{2,1,0:T(2,128)} %copy.86), calls=%async_computation | async-start | bytes 524288 | tf_op jit(solution)/shard_map/all_to_all | solution.py:49
  18.2 12.1 %all-to-all-done = f32[128,2,256]{2,1,0:T(2,128)S(1)} async-done(((f32[128,2,256]{2,1,0:T(2,128)}), f32[128,2,256]{2,1,0:T(2,128)S(1)}, u32[]{:S(2)}, u32[]{:S(2)}) %all-to-all-start) | async-done | bytes 262176 | tf_op jit(solution)/shard_map/all_to_all | solution.py:49
  30.4 0.7 convolution_multiply_fusion.1
  31.1 0.7 fusion.204
  31.8 0.9 copy.90
  32.7 5.7 %all-to-all-start.1 = ((f32[128,2,256]{2,1,0:T(2,128)}), f32[128,2,256]{2,1,0:T(2,128)S(1)}, u32[]{:S(2)}, u32[]{:S(2)}) async-start(f32[128,2,256]{2,1,0:T(2,128)} %copy.90), calls=%async_computation.1 | async-start | bytes 524288 | tf_op jit(solution)/shard_map/all_to_all | solution.py:52
  38.4 1.0 slice.888
  39.4 0.8 copy.95
  40.3 0.8 copy.94
  41.1 0.8 copy.92
  42.0 8.6 %all-to-all-done.1 = f32[128,2,256]{2,1,0:T(2,128)S(1)} async-done(((f32[128,2,256]{2,1,0:T(2,128)}), f32[128,2,256]{2,1,0:T(2,128)S(1)}, u32[]{:S(2)}, u32[]{:S(2)}) %all-to-all-start.1) | async-done | bytes 262176 | tf_op jit(solution)/shard_map/all_to_all | solution.py:52
  50.8 0.7 fusion.202
  51.5 3.3 %fusion.76 = (f32[256,256]{1,0:T(8,128)S(1)}, f32[256,256]{1,0:T(8,128)}) fusion(f32[1,2,128,256]{3,2,1,0:T(8,128)S(1)} %copy-done.19, f32[1,1,2,128,256]{4,3,2,1,0:T(8,128)} %copy.94, f32[1,2,128,256]{3,2,1,0:T(8,128)} %copy.92, f32[256,256]{1,0:T(8,128)S(1)} %bitcast.215, f32[256]{0:T(256)S(1)} %fusion.260, s32[256]{0:T(256)S(1)} %iota_add_fusion, ...), kind=kOutput, calls=%fused_computation.128 | convolution fusion | flops 202964992 | bytes 1575168 | tf_op jit(solution)/shard_map/dot_general | solution.py:54
  54.8 1.5 fusion.112
  56.4 0.7 fusion.195
  57.1 0.9 copy.97
  58.0 5.6 %all-to-all-start.2 = ((f32[128,2,256]{2,1,0:T(2,128)}), f32[128,2,256]{2,1,0:T(2,128)S(1)}, u32[]{:S(2)}, u32[]{:S(2)}) async-start(f32[128,2,256]{2,1,0:T(2,128)} %copy.97), calls=%async_computation.2 | async-start | bytes 524288 | tf_op jit(solution)/shard_map/all_to_all | solution.py:49
  63.6 12.2 %all-to-all-done.2 = f32[128,2,256]{2,1,0:T(2,128)S(1)} async-done(((f32[128,2,256]{2,1,0:T(2,128)}), f32[128,2,256]{2,1,0:T(2,128)S(1)}, u32[]{:S(2)}, u32[]{:S(2)}) %all-to-all-start.2) | async-done | bytes 262176 | tf_op jit(solution)/shard_map/all_to_all | solution.py:49
  76.0 0.7 convolution_multiply_fusion
  76.7 0.7 fusion.200
  77.4 0.9 copy.101
  78.3 5.7 %all-to-all-start.3 = ((f32[128,2,256]{2,1,0:T(2,128)}), f32[128,2,256]{2,1,0:T(2,128)S(1)}, u32[]{:S(2)}, u32[]{:S(2)}) async-start(f32[128,2,256]{2,1,0:T(2,128)} %copy.101), calls=%async_computation.3 | async-start | bytes 524288 | tf_op jit(solution)/shard_map/all_to_all | solution.py:52
  84.0 1.1 copy.114
  85.1 11.1 %all-to-all-done.3 = f32[128,2,256]{2,1,0:T(2,128)S(1)} async-done(((f32[128,2,256]{2,1,0:T(2,128)}), f32[128,2,256]{2,1,0:T(2,128)S(1)}, u32[]{:S(2)}, u32[]{:S(2)}) %all-to-all-start.3) | async-done | bytes 262176 | tf_op jit(solution)/shard_map/all_to_all | solution.py:52
  96.1 0.7 copy.150
  96.9 1.1 all_to_all.67
  98.0 0.7 fusion.198
  98.7 2.2 %fusion.168 = f32[256,256]{1,0:T(8,128)} fusion(f32[256,256]{1,0:T(8,128)S(1)} %bitcast.214, f32[256]{0:T(256)S(1)} %fusion.260, s32[256]{0:T(256)S(1)} %iota_add_fusion, pred[256]{0:T(512)(128)(4,1)S(1)} %iota_compare_fusion.12), kind=kOutput, calls=%fused_computation.264 | convolution fusion | flops 202440704 | bytes 526592 | tf_op jit(solution)/shard_map/dot_general | solution.py:54
  100.9 1.1 copy.115
  102.0 1.3 fusion.83
  104.3 1.3 fusion.3
  106.1 3.5 %collective-permute-start = (f32[2,128,256]{1,2,0:T(8,128)S(1)}, f32[2,128,256]{1,2,0:T(8,128)S(1)}, u32[]{:S(2)}, u32[]{:S(2)}) collective-permute-start(f32[2,128,256]{1,2,0:T(8,128)S(1)} %copy.103), channel_id=1, source_target_pairs={{0,64},{1,65},{2,66},{3,67},{4,68},{5,69},{6,70},{7,71},{8,72},{9,... | collective-permute-start | bytes 786440 | tf_op jit(solution)/shard_map/ppermute | solution.py:84
  109.7 0.8 collective-permute-start.2
  110.6 4.4 %collective-permute-done.1 = f32[4,64,128]{2,1,0:T(8,128)S(1)} collective-permute-done((f32[4,64,128]{2,1,0:T(8,128)S(1)}, f32[4,64,128]{2,1,0:T(8,128)S(1)}, u32[]{:S(2)}, u32[]{:S(2)}) %collective-permute-start.1) | collective-permute-done | bytes 131104 | tf_op jit(solution)/shard_map/ppermute | solution.py:77
  115.1 1.2 collective-permute-done
  116.5 5.3 %collective-permute-start.4 = (f32[12,64,128]{2,1,0:T(8,128)S(1)}, f32[12,64,128]{2,1,0:T(8,128)S(1)}, u32[]{:S(2)}, u32[]{:S(2)}) collective-permute-start(f32[12,64,128]{2,1,0:T(8,128)S(1)} %constant_dynamic-update-slice_fusion.8), channel_id=1, source_target_pairs={{3,0},{4,1},{5,2},{6,3},{7,4},{8,5},{9,6},{10,7},{11,8},{12,9},{13... | collective-permute-start | bytes 1179656 | tf_op jit(solution)/shard_map/ppermute | solution.py:77
  121.8 9.2 %collective-permute-done.3 = f32[12,64,128]{2,1,0:T(8,128)S(1)} collective-permute-done((f32[12,64,128]{2,1,0:T(8,128)S(1)}, f32[12,64,128]{2,1,0:T(8,128)S(1)}, u32[]{:S(2)}, u32[]{:S(2)}) %collective-permute-start.3) | collective-permute-done | bytes 393248 | tf_op jit(solution)/shard_map/ppermute | solution.py:77
  131.7 0.8 collective-permute-start.5
  132.5 18.2 %collective-permute-done.6 = f32[12,64,128]{2,1,0:T(8,128)S(1)} collective-permute-done((f32[12,64,128]{2,1,0:T(8,128)S(1)}, f32[12,64,128]{2,1,0:T(8,128)S(1)}, u32[]{:S(2)}, u32[]{:S(2)}) %collective-permute-start.6) | collective-permute-done | bytes 393248 | tf_op jit(solution)/shard_map/ppermute | solution.py:77
  150.8 0.7 fusion.354
  151.6 0.7 fusion.340
  154.6 0.7 fusion.341
  155.3 0.8 fusion.17
  156.1 0.8 pad_maximum_fusion.1
  157.0 3.9 %collective-permute-start.7 = (f32[16,64,128]{2,1,0:T(8,128)}, f32[16,64,128]{2,1,0:T(8,128)}, u32[]{:S(2)}, u32[]{:S(2)}) collective-permute-start(f32[16,64,128]{2,1,0:T(8,128)} %pad_maximum_fusion.1), channel_id=1, source_target_pairs={{0,64},{1,65},{2,66},{3,67},{4,68},{5,69},{6,70},{7,71},{8,72},{9,... | collective-permute-start | bytes 1572872 | tf_op jit(solution)/shard_map/ppermute | solution.py:84
  160.9 12.7 %collective-permute-done.7 = f32[16,64,128]{2,1,0:T(8,128)} collective-permute-done((f32[16,64,128]{2,1,0:T(8,128)}, f32[16,64,128]{2,1,0:T(8,128)}, u32[]{:S(2)}, u32[]{:S(2)}) %collective-permute-start.7) | collective-permute-done | bytes 524320 | tf_op jit(solution)/shard_map/ppermute | solution.py:84
  173.6 1.1 slice_select_fusion
  175.1 0.7 copy-done.6
  177.7 4.1 %collective-permute-start.8 = (f32[10,64,128]{2,1,0:T(8,128)S(1)}, f32[10,64,128]{2,1,0:T(8,128)S(1)}, u32[]{:S(2)}, u32[]{:S(2)}) collective-permute-start(f32[10,64,128]{2,1,0:T(8,128)S(1)} %fusion.53), channel_id=1, source_target_pairs={{0,64},{1,65},{2,66},{3,67},{4,68},{5,69},{6,70},{7,71},{8,72},{9,... | collective-permute-start | bytes 983048 | tf_op jit(solution)/shard_map/ppermute | solution.py:84
  181.8 7.5 %collective-permute-done.8 = f32[10,64,128]{2,1,0:T(8,128)S(1)} collective-permute-done((f32[10,64,128]{2,1,0:T(8,128)S(1)}, f32[10,64,128]{2,1,0:T(8,128)S(1)}, u32[]{:S(2)}, u32[]{:S(2)}) %collective-permute-start.8) | collective-permute-done | bytes 327712 | tf_op jit(solution)/shard_map/ppermute | solution.py:84
  191.1 0.9 fusion.130
  192.0 3.9 %collective-permute-start.9 = (f32[6,64,128]{2,1,0:T(8,128)}, f32[6,64,128]{2,1,0:T(8,128)}, u32[]{:S(2)}, u32[]{:S(2)}) collective-permute-start(f32[6,64,128]{2,1,0:T(8,128)} %fusion.130), channel_id=1, source_target_pairs={{0,64},{1,65},{2,66},{3,67},{4,68},{5,69},{6,70},{7,71},{8,72},{9,... | collective-permute-start | bytes 589832 | tf_op jit(solution)/shard_map/ppermute | solution.py:84
  196.1 1.0 copy.128
  197.0 3.5 %collective-permute-done.9 = f32[6,64,128]{2,1,0:T(8,128)} collective-permute-done((f32[6,64,128]{2,1,0:T(8,128)}, f32[6,64,128]{2,1,0:T(8,128)}, u32[]{:S(2)}, u32[]{:S(2)}) %collective-permute-start.9) | collective-permute-done | bytes 196640 | tf_op jit(solution)/shard_map/ppermute | solution.py:84
  200.5 1.0 fusion.137
  202.7 0.8 fusion.185
  203.6 0.7 fusion.138
  204.3 1.4 convolution_bitcast_fusion
  205.8 0.9 copy-done.21
  206.9 1.1 copy.127
  (164 shorter events, 11.2 us)
Async XLA Ops:
  0.6 1.5 copy-start.14
  2.6 1.8 copy-start
  6.0 24.2 %all-to-all-start = ((f32[128,2,256]{2,1,0:T(2,128)}), f32[128,2,256]{2,1,0:T(2,128)S(1)}, u32[]{:S(2)}, u32[]{:S(2)}) async-start(f32[128,2,256]{2,1,0:T(2,128)} %copy.86), calls=%async_computation | async-start | bytes 524288 | tf_op jit(solution)/shard_map/all_to_all | solution.py:49
  32.7 17.9 %all-to-all-start.1 = ((f32[128,2,256]{2,1,0:T(2,128)}), f32[128,2,256]{2,1,0:T(2,128)S(1)}, u32[]{:S(2)}, u32[]{:S(2)}) async-start(f32[128,2,256]{2,1,0:T(2,128)} %copy.90), calls=%async_computation.1 | async-start | bytes 524288 | tf_op jit(solution)/shard_map/all_to_all | solution.py:52
  41.1 10.4 %copy-start.19 = (f32[1,2,128,256]{3,2,1,0:T(8,128)S(1)}, f32[1,2,128,256]{3,2,1,0:T(8,128)}, u32[]{:S(2)}) copy-start(f32[1,2,128,256]{3,2,1,0:T(8,128)} %copy.95) | copy-start | bytes 786436
  58.0 17.9 %all-to-all-start.2 = ((f32[128,2,256]{2,1,0:T(2,128)}), f32[128,2,256]{2,1,0:T(2,128)S(1)}, u32[]{:S(2)}, u32[]{:S(2)}) async-start(f32[128,2,256]{2,1,0:T(2,128)} %copy.97), calls=%async_computation.2 | async-start | bytes 524288 | tf_op jit(solution)/shard_map/all_to_all | solution.py:49
  78.3 17.9 %all-to-all-start.3 = ((f32[128,2,256]{2,1,0:T(2,128)}), f32[128,2,256]{2,1,0:T(2,128)S(1)}, u32[]{:S(2)}, u32[]{:S(2)}) async-start(f32[128,2,256]{2,1,0:T(2,128)} %copy.101), calls=%async_computation.3 | async-start | bytes 524288 | tf_op jit(solution)/shard_map/all_to_all | solution.py:52
  103.3 0.7 copy-start.1
  103.3 0.8 copy-start.3
  104.2 1.8 copy-start.9
  106.1 10.2 %collective-permute-start = (f32[2,128,256]{1,2,0:T(8,128)S(1)}, f32[2,128,256]{1,2,0:T(8,128)S(1)}, u32[]{:S(2)}, u32[]{:S(2)}) collective-permute-start(f32[2,128,256]{1,2,0:T(8,128)S(1)} %copy.103), channel_id=1, source_target_pairs={{0,64},{1,65},{2,66},{3,67},{4,68},{5,69},{6,70},{7,71},{8,72},{9,... | collective-permute-start | bytes 786440 | tf_op jit(solution)/shard_map/ppermute | solution.py:84
  109.7 5.3 %collective-permute-start.2 = (f32[5,64,128]{2,1,0:T(8,128)S(1)}, f32[5,64,128]{2,1,0:T(8,128)S(1)}, u32[]{:S(2)}, u32[]{:S(2)}) collective-permute-start(f32[5,64,128]{2,1,0:T(8,128)S(1)} %constant_dynamic-update-slice_fusion.3), channel_id=1, source_target_pairs={{1,0},{2,1},{3,2},{4,3},{5,4},{6,5},{7,6},{8,7},{9,8},{10,9},{11,1... | collective-permute-start | bytes 491528 | tf_op jit(solution)/shard_map/ppermute | solution.py:77
  110.5 4.5 %collective-permute-start.1 = (f32[4,64,128]{2,1,0:T(8,128)S(1)}, f32[4,64,128]{2,1,0:T(8,128)S(1)}, u32[]{:S(2)}, u32[]{:S(2)}) collective-permute-start(f32[4,64,128]{2,1,0:T(8,128)S(1)} %pad_maximum_fusion.17), channel_id=1, source_target_pairs={{63,0},{0,1},{1,2},{2,3},{3,4},{4,5},{5,6},{6,7},{7,8},{8,9},{9,10... | collective-permute-start | bytes 393224 | tf_op jit(solution)/shard_map/ppermute | solution.py:77
  115.1 41.1 %copy-start.16 = (f32[2,64,128]{2,1,0:T(8,128)}, f32[2,64,128]{2,1,0:T(8,128)S(1)}, u32[]{:S(2)}) copy-start(f32[2,64,128]{2,1,0:T(8,128)S(1)} %pad_maximum_fusion.22) | copy-start | bytes 196612
  116.3 14.8 %copy-start.20 = (f32[2,128,256]{1,2,0:T(8,128)}, f32[2,128,256]{1,2,0:T(8,128)S(1)}, u32[]{:S(2)}) copy-start(f32[2,128,256]{1,2,0:T(8,128)S(1)} %collective-permute-done) | copy-start | bytes 786436
  116.4 14.6 %collective-permute-start.3 = (f32[12,64,128]{2,1,0:T(8,128)S(1)}, f32[12,64,128]{2,1,0:T(8,128)S(1)}, u32[]{:S(2)}, u32[]{:S(2)}) collective-permute-start(f32[12,64,128]{2,1,0:T(8,128)S(1)} %constant_dynamic-update-slice_fusion.8), channel_id=1, source_target_pairs={{61,0},{62,1},{63,2},{0,3},{1,4},{2,5},{3,6},{4,7},{5,8},{6,9},{7,... | collective-permute-start | bytes 1179656 | tf_op jit(solution)/shard_map/ppermute | solution.py:77
  116.5 34.3 %collective-permute-start.4 = (f32[12,64,128]{2,1,0:T(8,128)S(1)}, f32[12,64,128]{2,1,0:T(8,128)S(1)}, u32[]{:S(2)}, u32[]{:S(2)}) collective-permute-start(f32[12,64,128]{2,1,0:T(8,128)S(1)} %constant_dynamic-update-slice_fusion.8), channel_id=1, source_target_pairs={{3,0},{4,1},{5,2},{6,3},{7,4},{8,5},{9,6},{10,7},{11,8},{12,9},{13... | collective-permute-start | bytes 1179656 | tf_op jit(solution)/shard_map/ppermute | solution.py:77
  131.1 0.6 copy-start.7
  131.1 19.6 %collective-permute-start.6 = (f32[12,64,128]{2,1,0:T(8,128)S(1)}, f32[12,64,128]{2,1,0:T(8,128)S(1)}, u32[]{:S(2)}, u32[]{:S(2)}) collective-permute-start(f32[12,64,128]{2,1,0:T(8,128)S(1)} %fusion.44), channel_id=1, source_target_pairs={{60,0},{61,1},{62,2},{63,3},{0,4},{1,5},{2,6},{3,7},{4,8},{5,9},{6... | collective-permute-start | bytes 1179656 | tf_op jit(solution)/shard_map/ppermute | solution.py:77
  131.7 19.9 %collective-permute-start.5 = (f32[16,64,128]{2,1,0:T(8,128)S(1)}, f32[16,64,128]{2,1,0:T(8,128)S(1)}, u32[]{:S(2)}, u32[]{:S(2)}) collective-permute-start(f32[16,64,128]{2,1,0:T(8,128)S(1)} %pad_maximum_fusion), channel_id=1, source_target_pairs={{9,0},{10,1},{11,2},{12,3},{13,4},{14,5},{15,6},{16,7},{17,8},{18,... | collective-permute-start | bytes 1572872 | tf_op jit(solution)/shard_map/ppermute | solution.py:77
  152.9 0.8 copy-start.5
  157.0 16.6 %collective-permute-start.7 = (f32[16,64,128]{2,1,0:T(8,128)}, f32[16,64,128]{2,1,0:T(8,128)}, u32[]{:S(2)}, u32[]{:S(2)}) collective-permute-start(f32[16,64,128]{2,1,0:T(8,128)} %pad_maximum_fusion.1), channel_id=1, source_target_pairs={{0,64},{1,65},{2,66},{3,67},{4,68},{5,69},{6,70},{7,71},{8,72},{9,... | collective-permute-start | bytes 1572872 | tf_op jit(solution)/shard_map/ppermute | solution.py:84
  174.7 1.0 copy-start.6
  176.3 0.9 copy-start.11
  176.3 0.9 copy-start.18
  177.3 12.1 %copy-start.12 = (f32[3,64,128]{2,1,0:T(8,128)S(1)}, f32[3,64,128]{2,1,0:T(8,128)}, u32[]{:S(2)}) copy-start(f32[3,64,128]{2,1,0:T(8,128)} %get-tuple-element.73) | copy-start | bytes 294916
  177.3 12.1 %copy-start.15 = (f32[5,64,128]{2,1,0:T(8,128)S(1)}, f32[5,64,128]{2,1,0:T(8,128)}, u32[]{:S(2)}) copy-start(f32[5,64,128]{2,1,0:T(8,128)} %get-tuple-element.43) | copy-start | bytes 491524
  177.7 11.7 %collective-permute-start.8 = (f32[10,64,128]{2,1,0:T(8,128)S(1)}, f32[10,64,128]{2,1,0:T(8,128)S(1)}, u32[]{:S(2)}, u32[]{:S(2)}) collective-permute-start(f32[10,64,128]{2,1,0:T(8,128)S(1)} %fusion.53), channel_id=1, source_target_pairs={{0,64},{1,65},{2,66},{3,67},{4,68},{5,69},{6,70},{7,71},{8,72},{9,... | collective-permute-start | bytes 983048 | tf_op jit(solution)/shard_map/ppermute | solution.py:84
  189.5 0.9 copy-start.8
  189.5 0.9 copy-start.10
  191.1 4.9 %copy-start.2 = (f32[1,2,128,256]{2,3,1,0:T(8,128)S(1)}, f32[1,2,128,256]{2,3,1,0:T(8,128)}, u32[]{:S(2)}) copy-start(f32[1,2,128,256]{2,3,1,0:T(8,128)} %copy-done.1) | copy-start | bytes 786436
  191.1 4.9 %copy-start.4 = (f32[1,2,128,256]{2,3,1,0:T(8,128)S(1)}, f32[1,2,128,256]{2,3,1,0:T(8,128)}, u32[]{:S(2)}) copy-start(f32[1,2,128,256]{2,3,1,0:T(8,128)} %copy-done.3) | copy-start | bytes 786436
  192.0 8.5 %copy-start.13 = (f32[3,64,128]{2,1,0:T(8,128)S(1)}, f32[3,64,128]{2,1,0:T(8,128)}, u32[]{:S(2)}) copy-start(f32[3,64,128]{2,1,0:T(8,128)} %get-tuple-element.73) | copy-start | bytes 294916
  192.0 8.5 %collective-permute-start.9 = (f32[6,64,128]{2,1,0:T(8,128)}, f32[6,64,128]{2,1,0:T(8,128)}, u32[]{:S(2)}, u32[]{:S(2)}) collective-permute-start(f32[6,64,128]{2,1,0:T(8,128)} %fusion.130), channel_id=1, source_target_pairs={{0,64},{1,65},{2,66},{3,67},{4,68},{5,69},{6,70},{7,71},{8,72},{9,... | collective-permute-start | bytes 589832 | tf_op jit(solution)/shard_map/ppermute | solution.py:84
  201.7 0.8 copy-start.17
  205.8 1.0 copy-start.21

commit v6 on v1

--- a/solution.py
+++ b/solution.py
@@ -8,6 +8,7 @@
 WEIGHTS = ((5.0 / 24.0, 1.0 / 3.0, -1.0 / 24.0), (-1.0 / 24.0, 1.0 / 3.0, 5.0 / 24.0))
 EPS2 = 2.0
 HIGHEST = lax.Precision.HIGHEST
+TRANSFORM = lax.Precision.HIGH
 
 
 def react(u):
@@ -43,15 +44,15 @@
 
 def spectral_solve(rhs, basis_x, basis_y, basis_z, factor):
     planes, size_y, size_z = rhs.shape
-    flat = jnp.dot(rhs.reshape(planes * size_y, size_z), basis_z.T, precision=HIGHEST)
+    flat = jnp.dot(rhs.reshape(planes * size_y, size_z), basis_z.T, precision=TRANSFORM)
     field = flat.reshape(planes, size_y, size_z)
-    field = jnp.einsum("ky,xyz->kxz", basis_y, field, precision=HIGHEST)
+    field = jnp.einsum("ky,xyz->kxz", basis_y, field, precision=TRANSFORM)
     field = lax.all_to_all(field, "space", split_axis=0, concat_axis=1, tiled=True)
-    field = jnp.einsum("kx,yxz->kyz", basis_x, field, precision=HIGHEST) * factor
-    field = jnp.einsum("kx,kyz->xyz", basis_x, field, precision=HIGHEST)
+    field = jnp.einsum("kx,yxz->kyz", basis_x, field, precision=TRANSFORM) * factor
+    field = jnp.einsum("kx,kyz->xyz", basis_x, field, precision=TRANSFORM)
     field = lax.all_to_all(field, "space", split_axis=0, concat_axis=1, tiled=True)
-    field = jnp.matmul(basis_y.T, field, precision=HIGHEST)
-    flat = jnp.dot(field.reshape(planes * size_y, size_z), basis_z, precision=HIGHEST)
+    field = jnp.matmul(basis_y.T, field, precision=TRANSFORM)
+    flat = jnp.dot(field.reshape(planes * size_y, size_z), basis_z, precision=TRANSFORM)
     return flat.reshape(planes, size_y, size_z)
 
 

time: 180 us -> 178 us (0.989)
  no operation moved by 1% of the time
where the time goes in v6:
time: 178 us; the launch traced here: 177 us
  starting transfers between devices  68.9 us (39%)
  waiting for transfers between devices  66.2 us (37%)
  local copies, waits for them, and re-layouts  16.4 us (9%)
  matrix products  15.1 us (8%)
  other arithmetic  8.8 us (5%)
  between operations  1.95 us (1%)
    all_to_all x4, waiting for transfers between devices, spectral_solve(): lax.all_to_all(field, 'space', split_axis=0, concat_axis=1, tiled=True)  47.2 us
    ppermute x8, starting transfers between devices, fetch(): return lax.ppermute(value, ('tm', 'space'), pairs)  38.6 us
    all_to_all x4, starting transfers between devices, spectral_solve(): lax.all_to_all(field, 'space', split_axis=0, concat_axis=1, tiled=True)  26.8 us
    ppermute x4, waiting for transfers between devices, fetch(): return lax.ppermute(value, 'space', pairs)  10.8 us
    ppermute x8, waiting for transfers between devices, fetch(): return lax.ppermute(value, ('tm', 'space'), pairs)  8.24 us
    unnamed x50, local copies, waits for them, and re-layouts  6.67 us
    dot_general x2, matrix products, spectral_solve(): jnp.dot(field.reshape(planes * size_y, size_z), basis_z, precision=TRANSF...  3.86 us
  transfers between devices with their start and end apart: 16, of which 12 were waited for; matrix products, arithmetic and copies ran while one was open for 4% of the time, Pallas kernels for 0%

profile of v6, /device:TPU:8, one launch (start us, length us, event | category | flops | bytes accessed | tf_op | source)
XLA Modules:
  0.0 177.4 jit_solution(1826681500024249425)
XLA Ops:
  0.7 1.4 copy.80
  2.6 1.6 fusion.14
  4.3 0.6 fusion.178
  4.8 0.9 copy.86
  5.7 11.9 %all-to-all-start = ((f32[128,2,256]{2,1,0:T(2,128)}), f32[128,2,256]{2,1,0:T(2,128)S(1)}, u32[]{:S(2)}, u32[]{:S(2)}) async-start(f32[128,2,256]{2,1,0:T(2,128)} %copy.86), calls=%async_computation | async-start | bytes 524288 | tf_op jit(solution)/shard_map/all_to_all | solution.py:50
  17.8 12.8 %all-to-all-done = f32[128,2,256]{2,1,0:T(2,128)S(1)} async-done(((f32[128,2,256]{2,1,0:T(2,128)}), f32[128,2,256]{2,1,0:T(2,128)S(1)}, u32[]{:S(2)}, u32[]{:S(2)}) %all-to-all-start) | async-done | bytes 262176 | tf_op jit(solution)/shard_map/all_to_all | solution.py:50
  30.8 0.6 convolution_multiply_fusion.1
  31.4 0.5 fusion.190
  31.9 0.9 copy.90
  32.8 4.9 %all-to-all-start.1 = ((f32[128,2,256]{2,1,0:T(2,128)}), f32[128,2,256]{2,1,0:T(2,128)S(1)}, u32[]{:S(2)}, u32[]{:S(2)}) async-start(f32[128,2,256]{2,1,0:T(2,128)} %copy.90), calls=%async_computation.1 | async-start | bytes 524288 | tf_op jit(solution)/shard_map/all_to_all | solution.py:53
  37.7 1.0 slice.731
  39.1 0.7 slice_bitcast_fusion.1
  39.8 0.8 copy.94
  40.6 10.1 %all-to-all-done.1 = f32[128,2,256]{2,1,0:T(2,128)S(1)} async-done(((f32[128,2,256]{2,1,0:T(2,128)}), f32[128,2,256]{2,1,0:T(2,128)S(1)}, u32[]{:S(2)}, u32[]{:S(2)}) %all-to-all-start.1) | async-done | bytes 262176 | tf_op jit(solution)/shard_map/all_to_all | solution.py:53
  50.9 0.5 fusion.188
  51.5 2.4 %fusion.23 = (f32[256,256]{1,0:T(8,128)S(1)}, f32[256,256]{1,0:T(8,128)S(1)}) fusion(f32[1,2,128,256]{3,2,1,0:T(8,128)S(1)} %copy.95, f32[1,1,2,128,256]{4,3,2,1,0:T(8,128)} %copy.94, f32[1,2,128,256]{3,2,1,0:T(8,128)S(1)} %copy.92, f32[256,256]{1,0:T(8,128)S(1)} %bitcast.215, f32[256]{0:T(256)S(1)} %fusion.246, s32[256]{0:T(256)S(1)} %iota_add_fusion, ...), kind=kOutput, calls=%fused_computation.47 | convolution fusion | flops 102301696 | bytes 1575168 | tf_op jit(solution)/shard_map/dot_general | solution.py:55
  53.9 1.5 fusion.48
  55.4 0.6 fusion.181
  56.0 0.9 copy.97
  56.9 5.1 %all-to-all-start.2 = ((f32[128,2,256]{2,1,0:T(2,128)}), f32[128,2,256]{2,1,0:T(2,128)S(1)}, u32[]{:S(2)}, u32[]{:S(2)}) async-start(f32[128,2,256]{2,1,0:T(2,128)} %copy.97), calls=%async_computation.2 | async-start | bytes 524288 | tf_op jit(solution)/shard_map/all_to_all | solution.py:50
  62.0 12.8 %all-to-all-done.2 = f32[128,2,256]{2,1,0:T(2,128)S(1)} async-done(((f32[128,2,256]{2,1,0:T(2,128)}), f32[128,2,256]{2,1,0:T(2,128)S(1)}, u32[]{:S(2)}, u32[]{:S(2)}) %all-to-all-start.2) | async-done | bytes 262176 | tf_op jit(solution)/shard_map/all_to_all | solution.py:50
  74.9 0.6 convolution_multiply_fusion
  75.5 0.5 fusion.186
  76.0 0.9 copy.101
  76.9 4.9 %all-to-all-start.3 = ((f32[128,2,256]{2,1,0:T(2,128)}), f32[128,2,256]{2,1,0:T(2,128)S(1)}, u32[]{:S(2)}, u32[]{:S(2)}) async-start(f32[128,2,256]{2,1,0:T(2,128)} %copy.101), calls=%async_computation.3 | async-start | bytes 524288 | tf_op jit(solution)/shard_map/all_to_all | solution.py:53
  81.9 0.5 compare_and_fusion
  82.4 0.7 slice_bitcast_fusion.2
  83.2 11.6 %all-to-all-done.3 = f32[128,2,256]{2,1,0:T(2,128)S(1)} async-done(((f32[128,2,256]{2,1,0:T(2,128)}), f32[128,2,256]{2,1,0:T(2,128)S(1)}, u32[]{:S(2)}, u32[]{:S(2)}) %all-to-all-start.3) | async-done | bytes 262176 | tf_op jit(solution)/shard_map/all_to_all | solution.py:53
  95.0 0.5 fusion.184
  95.6 1.4 fusion.161
  97.0 0.7 copy-done.3
  97.9 1.4 fusion.30
  99.6 1.3 fusion.3
  101.0 0.3 fusion.215
  101.4 1.5 collective-permute-start.2
  103.1 3.5 %collective-permute-start = (f32[2,128,256]{1,2,0:T(8,128)S(1)}, f32[2,128,256]{1,2,0:T(8,128)S(1)}, u32[]{:S(2)}, u32[]{:S(2)}) collective-permute-start(f32[2,128,256]{1,2,0:T(8,128)S(1)} %copy.103), channel_id=1, source_target_pairs={{0,64},{1,65},{2,66},{3,67},{4,68},{5,69},{6,70},{7,71},{8,72},{9,... | collective-permute-start | bytes 786440 | tf_op jit(solution)/shard_map/ppermute | solution.py:85
  106.6 4.1 %collective-permute-done.1 = f32[4,64,128]{2,1,0:T(8,128)S(1)} collective-permute-done((f32[4,64,128]{2,1,0:T(8,128)S(1)}, f32[4,64,128]{2,1,0:T(8,128)S(1)}, u32[]{:S(2)}, u32[]{:S(2)}) %collective-permute-start.1) | collective-permute-done | bytes 131104 | tf_op jit(solution)/shard_map/ppermute | solution.py:78
  110.8 3.0 %collective-permute-done = f32[2,128,256]{1,2,0:T(8,128)S(1)} collective-permute-done((f32[2,128,256]{1,2,0:T(8,128)S(1)}, f32[2,128,256]{1,2,0:T(8,128)S(1)}, u32[]{:S(2)}, u32[]{:S(2)}) %collective-permute-start) | collective-permute-done | bytes 262176 | tf_op jit(solution)/shard_map/ppermute | solution.py:85
  113.8 0.7 copy-done.8
  114.7 1.7 collective-permute-start.4
  116.5 3.5 %collective-permute-start.3 = (f32[2,64,128]{2,1,0:T(8,128)S(1)}, f32[2,64,128]{2,1,0:T(8,128)S(1)}, u32[]{:S(2)}, u32[]{:S(2)}) collective-permute-start(f32[2,64,128]{2,1,0:T(8,128)S(1)} %pad_maximum_fusion.12), channel_id=1, source_target_pairs={{0,64},{1,65},{2,66},{3,67},{4,68},{5,69},{6,70},{7,71},{8,72},{9,... | collective-permute-start | bytes 196616 | tf_op jit(solution)/shard_map/ppermute | solution.py:85
  119.9 0.5 collective-permute-done.5
  120.4 6.2 %collective-permute-done.4 = f32[8,64,128]{2,1,0:T(8,128)S(1)} collective-permute-done((f32[8,64,128]{2,1,0:T(8,128)S(1)}, f32[8,64,128]{2,1,0:T(8,128)S(1)}, u32[]{:S(2)}, u32[]{:S(2)}) %collective-permute-start.4) | collective-permute-done | bytes 262176 | tf_op jit(solution)/shard_map/ppermute | solution.py:78
  128.1 3.8 %collective-permute-start.6 = (f32[4,64,128]{2,1,0:T(8,128)S(1)}, f32[4,64,128]{2,1,0:T(8,128)S(1)}, u32[]{:S(2)}, u32[]{:S(2)}) collective-permute-start(f32[4,64,128]{2,1,0:T(8,128)S(1)} %get-tuple-element.30), channel_id=1, source_target_pairs={{62,64},{63,65},{0,66},{1,67},{2,68},{3,69},{4,70},{5,71},{6,72},{... | collective-permute-start | bytes 393224 | tf_op jit(solution)/shard_map/ppermute | solution.py:85
  131.9 7.3 %collective-permute-start.7 = (f32[4,64,128]{2,1,0:T(8,128)S(1)}, f32[4,64,128]{2,1,0:T(8,128)S(1)}, u32[]{:S(2)}, u32[]{:S(2)}) collective-permute-start(f32[4,64,128]{2,1,0:T(8,128)S(1)} %get-tuple-element.30), channel_id=1, source_target_pairs={{2,64},{3,65},{4,66},{5,67},{6,68},{7,69},{8,70},{9,71},{10,72},{1... | collective-permute-start | bytes 393224 | tf_op jit(solution)/shard_map/ppermute | solution.py:85
  139.2 2.0 %collective-permute-done.6 = f32[4,64,128]{2,1,0:T(8,128)S(1)} collective-permute-done((f32[4,64,128]{2,1,0:T(8,128)S(1)}, f32[4,64,128]{2,1,0:T(8,128)S(1)}, u32[]{:S(2)}, u32[]{:S(2)}) %collective-permute-start.6) | collective-permute-done | bytes 131104 | tf_op jit(solution)/shard_map/ppermute | solution.py:85
  141.2 0.7 collective-permute-done.7
  142.9 1.9 %collective-permute-start.8 = (f32[4,64,128]{2,1,0:T(8,128)S(1)}, f32[4,64,128]{2,1,0:T(8,128)S(1)}, u32[]{:S(2)}, u32[]{:S(2)}) collective-permute-start(f32[4,64,128]{2,1,0:T(8,128)S(1)} %fusion.117), channel_id=1, source_target_pairs={{62,64},{63,65},{0,66},{1,67},{2,68},{3,69},{4,70},{5,71},{6,72},{... | collective-permute-start | bytes 393224 | tf_op jit(solution)/shard_map/ppermute | solution.py:85
  144.8 8.2 %collective-permute-start.9 = (f32[4,64,128]{2,1,0:T(8,128)S(1)}, f32[4,64,128]{2,1,0:T(8,128)S(1)}, u32[]{:S(2)}, u32[]{:S(2)}) collective-permute-start(f32[4,64,128]{2,1,0:T(8,128)S(1)} %fusion.117), channel_id=1, source_target_pairs={{2,64},{3,65},{4,66},{5,67},{6,68},{7,69},{8,70},{9,71},{10,72},{1... | collective-permute-start | bytes 393224 | tf_op jit(solution)/shard_map/ppermute | solution.py:85
  153.0 0.6 iota_and_fusion.1
  153.6 0.6 iota_and_fusion
  154.2 1.3 collective-permute-done.9
  156.3 0.8 fusion.122
  157.1 1.9 %collective-permute-start.10 = (f32[4,64,128]{2,1,0:T(8,128)}, f32[4,64,128]{2,1,0:T(8,128)}, u32[]{:S(2)}, u32[]{:S(2)}) collective-permute-start(f32[4,64,128]{2,1,0:T(8,128)} %fusion.122), channel_id=1, source_target_pairs={{62,64},{63,65},{0,66},{1,67},{2,68},{3,69},{4,70},{5,71},{6,72},{... | collective-permute-start | bytes 393224 | tf_op jit(solution)/shard_map/ppermute | solution.py:85
  159.0 8.6 %collective-permute-start.11 = (f32[4,64,128]{2,1,0:T(8,128)}, f32[4,64,128]{2,1,0:T(8,128)}, u32[]{:S(2)}, u32[]{:S(2)}) collective-permute-start(f32[4,64,128]{2,1,0:T(8,128)} %fusion.122), channel_id=1, source_target_pairs={{2,64},{3,65},{4,66},{5,67},{6,68},{7,69},{8,70},{9,71},{10,72},{1... | collective-permute-start | bytes 393224 | tf_op jit(solution)/shard_map/ppermute | solution.py:85
  167.6 0.5 compare_and_fusion.1
  168.1 1.0 copy.128
  169.1 1.3 collective-permute-done.11
  170.4 1.0 maximum_select_fusion.2
  172.4 0.5 copy-done.7
  172.9 0.7 fusion.101
  173.7 1.4 convolution_bitcast_fusion
  175.3 0.9 copy-done.9
  176.3 1.1 copy.127
  (159 shorter events, 6.9 us)
Async XLA Ops:
  0.6 1.5 copy-start.5
  2.6 1.6 copy-start
  5.7 24.9 %all-to-all-start = ((f32[128,2,256]{2,1,0:T(2,128)}), f32[128,2,256]{2,1,0:T(2,128)S(1)}, u32[]{:S(2)}, u32[]{:S(2)}) async-start(f32[128,2,256]{2,1,0:T(2,128)} %copy.86), calls=%async_computation | async-start | bytes 524288 | tf_op jit(solution)/shard_map/all_to_all | solution.py:50
  32.8 17.9 %all-to-all-start.1 = ((f32[128,2,256]{2,1,0:T(2,128)}), f32[128,2,256]{2,1,0:T(2,128)S(1)}, u32[]{:S(2)}, u32[]{:S(2)}) async-start(f32[128,2,256]{2,1,0:T(2,128)} %copy.90), calls=%async_computation.1 | async-start | bytes 524288 | tf_op jit(solution)/shard_map/all_to_all | solution.py:53
  56.9 17.9 %all-to-all-start.2 = ((f32[128,2,256]{2,1,0:T(2,128)}), f32[128,2,256]{2,1,0:T(2,128)S(1)}, u32[]{:S(2)}, u32[]{:S(2)}) async-start(f32[128,2,256]{2,1,0:T(2,128)} %copy.97), calls=%async_computation.2 | async-start | bytes 524288 | tf_op jit(solution)/shard_map/all_to_all | solution.py:50
  76.9 17.9 %all-to-all-start.3 = ((f32[128,2,256]{2,1,0:T(2,128)}), f32[128,2,256]{2,1,0:T(2,128)S(1)}, u32[]{:S(2)}, u32[]{:S(2)}) async-start(f32[128,2,256]{2,1,0:T(2,128)} %copy.101), calls=%async_computation.3 | async-start | bytes 524288 | tf_op jit(solution)/shard_map/all_to_all | solution.py:53
  81.9 17.8 %copy-start.14 = (pred[256]{0:T(512)(128)(4,1)}, pred[256]{0:T(512)(128)(4,1)S(1)}, u32[]{:S(2)}) copy-start(pred[256]{0:T(512)(128)(4,1)S(1)} %compare_and_fusion.3) | copy-start | bytes 772
  82.4 18.6 %copy-start.10 = (pred[128]{0:T(512)(128)(4,1)}, pred[128]{0:T(512)(128)(4,1)S(1)}, u32[]{:S(2)}) copy-start(pred[128]{0:T(512)(128)(4,1)S(1)} %get-tuple-element.146) | copy-start | bytes 388
  97.0 0.7 copy-start.3
  97.8 1.5 copy-start.1
  97.9 1.5 copy-start.2
  99.6 3.4 %copy-start.4 = (f32[256,256]{1,0:T(8,128)S(1)}, f32[256,256]{1,0:T(8,128)}, u32[]{:S(2)}) copy-start(f32[256,256]{1,0:T(8,128)} %copy-done.3) | copy-start | bytes 786436
  101.4 9.3 %collective-permute-start.2 = (f32[5,64,128]{2,1,0:T(8,128)S(1)}, f32[5,64,128]{2,1,0:T(8,128)S(1)}, u32[]{:S(2)}, u32[]{:S(2)}) collective-permute-start(f32[5,64,128]{2,1,0:T(8,128)S(1)} %constant_dynamic-update-slice_fusion.3), channel_id=1, source_target_pairs={{1,0},{2,1},{3,2},{4,3},{5,4},{6,5},{7,6},{8,7},{9,8},{10,9},{11,1... | collective-permute-start | bytes 491528 | tf_op jit(solution)/shard_map/ppermute | solution.py:78
  102.9 7.8 %collective-permute-start.1 = (f32[4,64,128]{2,1,0:T(8,128)S(1)}, f32[4,64,128]{2,1,0:T(8,128)S(1)}, u32[]{:S(2)}, u32[]{:S(2)}) collective-permute-start(f32[4,64,128]{2,1,0:T(8,128)S(1)} %pad_maximum_fusion.5), channel_id=1, source_target_pairs={{63,0},{0,1},{1,2},{2,3},{3,4},{4,5},{5,6},{6,7},{7,8},{8,9},{9,10... | collective-permute-start | bytes 393224 | tf_op jit(solution)/shard_map/ppermute | solution.py:78
  103.1 10.7 %collective-permute-start = (f32[2,128,256]{1,2,0:T(8,128)S(1)}, f32[2,128,256]{1,2,0:T(8,128)S(1)}, u32[]{:S(2)}, u32[]{:S(2)}) collective-permute-start(f32[2,128,256]{1,2,0:T(8,128)S(1)} %copy.103), channel_id=1, source_target_pairs={{0,64},{1,65},{2,66},{3,67},{4,68},{5,69},{6,70},{7,71},{8,72},{9,... | collective-permute-start | bytes 786440 | tf_op jit(solution)/shard_map/ppermute | solution.py:85
  110.8 15.9 %copy-start.6 = (f32[2,64,128]{2,1,0:T(8,128)}, f32[2,64,128]{2,1,0:T(8,128)S(1)}, u32[]{:S(2)}) copy-start(f32[2,64,128]{2,1,0:T(8,128)S(1)} %pad_maximum_fusion.12) | copy-start | bytes 196612
  113.8 0.7 copy-start.8
  114.5 5.9 %collective-permute-start.5 = (f32[4,64,128]{2,1,0:T(8,128)S(1)}, f32[4,64,128]{2,1,0:T(8,128)S(1)}, u32[]{:S(2)}, u32[]{:S(2)}) collective-permute-start(f32[4,64,128]{2,1,0:T(8,128)S(1)} %pad_maximum_fusion.6), channel_id=1, source_target_pairs={{3,0},{4,1},{5,2},{6,3},{7,4},{8,5},{9,6},{10,7},{11,8},{12,9},{13... | collective-permute-start | bytes 393224 | tf_op jit(solution)/shard_map/ppermute | solution.py:78
  114.7 11.9 %collective-permute-start.4 = (f32[8,64,128]{2,1,0:T(8,128)S(1)}, f32[8,64,128]{2,1,0:T(8,128)S(1)}, u32[]{:S(2)}, u32[]{:S(2)}) collective-permute-start(f32[8,64,128]{2,1,0:T(8,128)S(1)} %pad_maximum_fusion.1), channel_id=1, source_target_pairs={{61,0},{62,1},{63,2},{0,3},{1,4},{2,5},{3,6},{4,7},{5,8},{6,9},{7,... | collective-permute-start | bytes 786440 | tf_op jit(solution)/shard_map/ppermute | solution.py:78
  116.5 10.3 %collective-permute-start.3 = (f32[2,64,128]{2,1,0:T(8,128)S(1)}, f32[2,64,128]{2,1,0:T(8,128)S(1)}, u32[]{:S(2)}, u32[]{:S(2)}) collective-permute-start(f32[2,64,128]{2,1,0:T(8,128)S(1)} %pad_maximum_fusion.12), channel_id=1, source_target_pairs={{0,64},{1,65},{2,66},{3,67},{4,68},{5,69},{6,70},{7,71},{8,72},{9,... | collective-permute-start | bytes 196616 | tf_op jit(solution)/shard_map/ppermute | solution.py:85
  128.1 13.1 %collective-permute-start.6 = (f32[4,64,128]{2,1,0:T(8,128)S(1)}, f32[4,64,128]{2,1,0:T(8,128)S(1)}, u32[]{:S(2)}, u32[]{:S(2)}) collective-permute-start(f32[4,64,128]{2,1,0:T(8,128)S(1)} %get-tuple-element.30), channel_id=1, source_target_pairs={{62,64},{63,65},{0,66},{1,67},{2,68},{3,69},{4,70},{5,71},{6,72},{... | collective-permute-start | bytes 393224 | tf_op jit(solution)/shard_map/ppermute | solution.py:85
  131.9 10.0 %collective-permute-start.7 = (f32[4,64,128]{2,1,0:T(8,128)S(1)}, f32[4,64,128]{2,1,0:T(8,128)S(1)}, u32[]{:S(2)}, u32[]{:S(2)}) collective-permute-start(f32[4,64,128]{2,1,0:T(8,128)S(1)} %get-tuple-element.30), channel_id=1, source_target_pairs={{2,64},{3,65},{4,66},{5,67},{6,68},{7,69},{8,70},{9,71},{10,72},{1... | collective-permute-start | bytes 393224 | tf_op jit(solution)/shard_map/ppermute | solution.py:85
  142.9 11.3 %collective-permute-start.8 = (f32[4,64,128]{2,1,0:T(8,128)S(1)}, f32[4,64,128]{2,1,0:T(8,128)S(1)}, u32[]{:S(2)}, u32[]{:S(2)}) collective-permute-start(f32[4,64,128]{2,1,0:T(8,128)S(1)} %fusion.117), channel_id=1, source_target_pairs={{62,64},{63,65},{0,66},{1,67},{2,68},{3,69},{4,70},{5,71},{6,72},{... | collective-permute-start | bytes 393224 | tf_op jit(solution)/shard_map/ppermute | solution.py:85
  144.8 10.7 %collective-permute-start.9 = (f32[4,64,128]{2,1,0:T(8,128)S(1)}, f32[4,64,128]{2,1,0:T(8,128)S(1)}, u32[]{:S(2)}, u32[]{:S(2)}) collective-permute-start(f32[4,64,128]{2,1,0:T(8,128)S(1)} %fusion.117), channel_id=1, source_target_pairs={{2,64},{3,65},{4,66},{5,67},{6,68},{7,69},{8,70},{9,71},{10,72},{1... | collective-permute-start | bytes 393224 | tf_op jit(solution)/shard_map/ppermute | solution.py:85
  157.1 12.1 %collective-permute-start.10 = (f32[4,64,128]{2,1,0:T(8,128)}, f32[4,64,128]{2,1,0:T(8,128)}, u32[]{:S(2)}, u32[]{:S(2)}) collective-permute-start(f32[4,64,128]{2,1,0:T(8,128)} %fusion.122), channel_id=1, source_target_pairs={{62,64},{63,65},{0,66},{1,67},{2,68},{3,69},{4,70},{5,71},{6,72},{... | collective-permute-start | bytes 393224 | tf_op jit(solution)/shard_map/ppermute | solution.py:85
  159.0 11.4 %collective-permute-start.11 = (f32[4,64,128]{2,1,0:T(8,128)}, f32[4,64,128]{2,1,0:T(8,128)}, u32[]{:S(2)}, u32[]{:S(2)}) collective-permute-start(f32[4,64,128]{2,1,0:T(8,128)} %fusion.122), channel_id=1, source_target_pairs={{2,64},{3,65},{4,66},{5,67},{6,68},{7,69},{8,70},{9,71},{10,72},{1... | collective-permute-start | bytes 393224 | tf_op jit(solution)/shard_map/ppermute | solution.py:85
  172.0 0.8 copy-start.7
  172.1 0.8 copy-start.12
  172.2 0.8 copy-start.13
  172.2 0.8 copy-start.15
  172.2 0.8 copy-start.19
  172.2 1.4 copy-start.11
  172.3 1.4 copy-start.16
  172.3 1.4 copy-start.17
  172.3 1.4 copy-start.18
  175.2 1.0 copy-start.9

commit v7 on v4

--- a/solution.py
+++ b/solution.py
@@ -8,6 +8,7 @@
 WEIGHTS = ((5.0 / 24.0, 1.0 / 3.0, -1.0 / 24.0), (-1.0 / 24.0, 1.0 / 3.0, 5.0 / 24.0))
 EPS2 = 2.0
 HIGHEST = lax.Precision.HIGHEST
+TRANSFORM = lax.Precision.HIGH
 
 
 def react(u):
@@ -43,15 +44,15 @@
 
 def spectral_solve(rhs, basis_x, basis_y, basis_z, factor):
     planes, size_y, size_z = rhs.shape
-    flat = jnp.dot(rhs.reshape(planes * size_y, size_z), basis_z.T, precision=HIGHEST)
+    flat = jnp.dot(rhs.reshape(planes * size_y, size_z), basis_z.T, precision=TRANSFORM)
     field = flat.reshape(planes, size_y, size_z)
-    field = jnp.einsum("ky,xyz->kxz", basis_y, field, precision=HIGHEST)
+    field = jnp.einsum("ky,xyz->kxz", basis_y, field, precision=TRANSFORM)
     field = lax.all_to_all(field, "space", split_axis=0, concat_axis=1, tiled=True)
-    field = jnp.einsum("kx,yxz->kyz", basis_x, field, precision=HIGHEST) * factor
-    field = jnp.einsum("kx,kyz->xyz", basis_x, field, precision=HIGHEST)
+    field = jnp.einsum("kx,yxz->kyz", basis_x, field, precision=TRANSFORM) * factor
+    field = jnp.einsum("kx,kyz->xyz", basis_x, field, precision=TRANSFORM)
     field = lax.all_to_all(field, "space", split_axis=0, concat_axis=1, tiled=True)
-    field = jnp.matmul(basis_y.T, field, precision=HIGHEST)
-    flat = jnp.dot(field.reshape(planes * size_y, size_z), basis_z, precision=HIGHEST)
+    field = jnp.matmul(basis_y.T, field, precision=TRANSFORM)
+    flat = jnp.dot(field.reshape(planes * size_y, size_z), basis_z, precision=TRANSFORM)
     return flat.reshape(planes, size_y, size_z)
 
 
@@ -202,31 +203,31 @@
     slices = lax.axis_size("tm")
     local = planes // 2
     wide = gather_bands(
-        [(coarse[0], (0, 0), (4, 3)), (coarse[1], (0, 0), (3, 2)), (coarse[3], (0, 0), (3, 2)),
-         (coarse[4], (0, 0), (2, 1)), (coarse[2], (0, 0), (2, 1))]
+        [(coarse[0], (0, 0), (2, 3)), (coarse[1], (0, 0), (1, 2)), (coarse[3], (0, 0), (1, 2)),
+         (coarse[4], (0, 0), (0, 1)), (coarse[2], (0, 0), (0, 1))]
     )
     previous_two = fetch(values[2], 0, 1)
     previous_two, wide = lax.optimization_barrier((previous_two, wide))
     start_c = wide[0]
     rates_c = (coarse_rate(start_c), coarse_rate(wide[1]))
     sums_c = (wide[2], wide[3])
-    coarse_one = wide[1][3:4 + local]
-    coarse_two = wide[4][2:3 + local]
+    coarse_one = wide[1][1:2 + local]
+    coarse_two = wide[4]
     start = start_c
     previous_coarse_two = None
     for section in range(slices - 1):
         first, second = coarse_sweep(start, rates_c, sums_c)
-        items = [(second, (2, 1), (4, 3))]
+        items = [(second, (0, 1), (2, 3))]
         if previous_coarse_two is None:
-            items.append((wide[4], (2, 1), (0, 1)))
+            items.append((coarse_two, (0, 1), (0, 1)))
         received = gather_bands(items, back=1)
         if previous_coarse_two is None:
             previous_coarse_two = received[1]
         start = jnp.where(slot == 0, start_c, received[0])
     first, second = coarse_sweep(start, rates_c, sums_c)
     delta = jnp.stack(
-        [first[2:3 + local] - coarse_one, second[2:3 + local] - coarse_two,
-         start[4:5 + local] - previous_coarse_two]
+        [first - coarse_one, second - coarse_two,
+         start[2:3 + local] - previous_coarse_two]
     )
     corr = refine(delta)
     fixed_one = values[1] + corr[0]

time: 185 us -> 174 us (0.941)
  waiting for transfers between devices: 73.3 us -> 66.1 us
  local copies, waits for them, and re-layouts: 22.2 us -> 15.5 us
  starting transfers between devices: 60.9 us -> 66.8 us
    ppermute x7 -> x5, waiting for transfers between devices: 8.57 us -> 3.16 us  [fetch(): return lax.ppermute(value, 'space', pairs)]
    ppermute x7 -> x10, starting transfers between devices: 27.9 us -> 33.3 us  [fetch(): return lax.ppermute(value, ('tm', 'space'), pairs)]
    unnamed x57 -> x45, local copies, waits for them, and re-layouts: 9.23 us -> 5.54 us
    ppermute x7 -> x10, waiting for transfers between devices: 19.3 us -> 15.7 us  [fetch(): return lax.ppermute(value, ('tm', 'space'), pairs)]
    ppermute x7 -> x5, starting transfers between devices: 5.91 us -> 6.68 us  [fetch(): return lax.ppermute(value, 'space', pairs)]
  transfers between devices with their start and end apart: 18 -> 19, of which waited for: 12 -> 11; matrix products, arithmetic and copies ran while one was open for 5% -> 5% of each run, Pallas kernels for 0% -> 0%
where the time goes in v7:
time: 174 us; the launch traced here: 173 us
  starting transfers between devices  66.8 us (38%)
  waiting for transfers between devices  66.1 us (38%)
  local copies, waits for them, and re-layouts  15.5 us (9%)
  matrix products  15.1 us (9%)
  other arithmetic  8.12 us (5%)
  between operations  1.78 us (1%)
    all_to_all x4, waiting for transfers between devices, spectral_solve(): lax.all_to_all(field, 'space', split_axis=0, concat_axis=1, tiled=True)  47.2 us
    ppermute x10, starting transfers between devices, fetch(): return lax.ppermute(value, ('tm', 'space'), pairs)  33.3 us
    all_to_all x4, starting transfers between devices, spectral_solve(): lax.all_to_all(field, 'space', split_axis=0, concat_axis=1, tiled=True)  26.8 us
    ppermute x10, waiting for transfers between devices, fetch(): return lax.ppermute(value, ('tm', 'space'), pairs)  15.7 us
    ppermute x5, starting transfers between devices, fetch(): return lax.ppermute(value, 'space', pairs)  6.68 us
    unnamed x45, local copies, waits for them, and re-layouts  5.54 us
    dot_general x2, matrix products, spectral_solve(): jnp.dot(field.reshape(planes * size_y, size_z), basis_z, precision=TRANSF...  3.86 us
  transfers between devices with their start and end apart: 19, of which 11 were waited for; matrix products, arithmetic and copies ran while one was open for 5% of the time, Pallas kernels for 0%

profile of v7, /device:TPU:8, one launch (start us, length us, event | category | flops | bytes accessed | tf_op | source)
XLA Modules:
  0.0 173.3 jit_solution(11142252176459712026)
XLA Ops:
  0.7 1.4 copy.80
  2.6 1.6 fusion.14
  4.3 0.6 fusion.180
  4.8 0.9 copy.86
  5.7 11.9 %all-to-all-start = ((f32[128,2,256]{2,1,0:T(2,128)}), f32[128,2,256]{2,1,0:T(2,128)S(1)}, u32[]{:S(2)}, u32[]{:S(2)}) async-start(f32[128,2,256]{2,1,0:T(2,128)} %copy.86), calls=%async_computation | async-start | bytes 524288 | tf_op jit(solution)/shard_map/all_to_all | solution.py:50
  17.8 12.8 %all-to-all-done = f32[128,2,256]{2,1,0:T(2,128)S(1)} async-done(((f32[128,2,256]{2,1,0:T(2,128)}), f32[128,2,256]{2,1,0:T(2,128)S(1)}, u32[]{:S(2)}, u32[]{:S(2)}) %all-to-all-start) | async-done | bytes 262176 | tf_op jit(solution)/shard_map/all_to_all | solution.py:50
  30.8 0.6 convolution_multiply_fusion.1
  31.4 0.5 fusion.192
  31.9 0.9 copy.90
  32.8 4.9 %all-to-all-start.1 = ((f32[128,2,256]{2,1,0:T(2,128)}), f32[128,2,256]{2,1,0:T(2,128)S(1)}, u32[]{:S(2)}, u32[]{:S(2)}) async-start(f32[128,2,256]{2,1,0:T(2,128)} %copy.90), calls=%async_computation.1 | async-start | bytes 524288 | tf_op jit(solution)/shard_map/all_to_all | solution.py:53
  37.7 1.0 slice.683
  39.1 0.7 slice_bitcast_fusion.1
  39.8 0.8 copy.94
  40.6 10.1 %all-to-all-done.1 = f32[128,2,256]{2,1,0:T(2,128)S(1)} async-done(((f32[128,2,256]{2,1,0:T(2,128)}), f32[128,2,256]{2,1,0:T(2,128)S(1)}, u32[]{:S(2)}, u32[]{:S(2)}) %all-to-all-start.1) | async-done | bytes 262176 | tf_op jit(solution)/shard_map/all_to_all | solution.py:53
  50.9 0.5 fusion.190
  51.5 2.4 %fusion.23 = (f32[256,256]{1,0:T(8,128)S(1)}, f32[256,256]{1,0:T(8,128)S(1)}) fusion(f32[1,2,128,256]{3,2,1,0:T(8,128)S(1)} %copy.95, f32[1,1,2,128,256]{4,3,2,1,0:T(8,128)} %copy.94, f32[1,2,128,256]{3,2,1,0:T(8,128)S(1)} %copy.92, f32[256,256]{1,0:T(8,128)S(1)} %bitcast.217, f32[256]{0:T(256)S(1)} %fusion.248, s32[256]{0:T(256)S(1)} %iota_add_fusion, ...), kind=kOutput, calls=%fused_computation.43 | convolution fusion | flops 102301696 | bytes 1575168 | tf_op jit(solution)/shard_map/dot_general | solution.py:55
  53.9 1.5 fusion.48
  55.4 0.6 fusion.183
  56.0 0.9 copy.97
  56.9 5.1 %all-to-all-start.2 = ((f32[128,2,256]{2,1,0:T(2,128)}), f32[128,2,256]{2,1,0:T(2,128)S(1)}, u32[]{:S(2)}, u32[]{:S(2)}) async-start(f32[128,2,256]{2,1,0:T(2,128)} %copy.97), calls=%async_computation.2 | async-start | bytes 524288 | tf_op jit(solution)/shard_map/all_to_all | solution.py:50
  62.0 12.7 %all-to-all-done.2 = f32[128,2,256]{2,1,0:T(2,128)S(1)} async-done(((f32[128,2,256]{2,1,0:T(2,128)}), f32[128,2,256]{2,1,0:T(2,128)S(1)}, u32[]{:S(2)}, u32[]{:S(2)}) %all-to-all-start.2) | async-done | bytes 262176 | tf_op jit(solution)/shard_map/all_to_all | solution.py:50
  74.9 0.6 convolution_multiply_fusion
  75.5 0.5 fusion.188
  76.0 0.9 copy.101
  76.9 4.9 %all-to-all-start.3 = ((f32[128,2,256]{2,1,0:T(2,128)}), f32[128,2,256]{2,1,0:T(2,128)S(1)}, u32[]{:S(2)}, u32[]{:S(2)}) async-start(f32[128,2,256]{2,1,0:T(2,128)} %copy.101), calls=%async_computation.3 | async-start | bytes 524288 | tf_op jit(solution)/shard_map/all_to_all | solution.py:53
  81.8 0.6 iota_and_fusion
  82.4 0.7 slice_bitcast_fusion.2
  83.3 11.5 %all-to-all-done.3 = f32[128,2,256]{2,1,0:T(2,128)S(1)} async-done(((f32[128,2,256]{2,1,0:T(2,128)}), f32[128,2,256]{2,1,0:T(2,128)S(1)}, u32[]{:S(2)}, u32[]{:S(2)}) %all-to-all-start.3) | async-done | bytes 262176 | tf_op jit(solution)/shard_map/all_to_all | solution.py:53
  95.0 0.5 fusion.186
  95.5 1.4 fusion.117
  97.0 0.7 copy-done.3
  97.8 1.4 fusion.30
  99.6 1.3 fusion.3
  101.3 0.9 collective-permute-start.1
  102.3 4.6 %collective-permute-start.4 = (f32[3,64,128]{2,1,0:T(8,128)S(1)}, f32[3,64,128]{2,1,0:T(8,128)S(1)}, u32[]{:S(2)}, u32[]{:S(2)}) collective-permute-start(f32[3,64,128]{2,1,0:T(8,128)S(1)} %pad_maximum_fusion.4), channel_id=1, source_target_pairs={{2,0},{3,1},{4,2},{5,3},{6,4},{7,5},{8,6},{9,7},{10,8},{11,9},{12,... | collective-permute-start | bytes 294920 | tf_op jit(solution)/shard_map/ppermute | solution.py:78
  106.9 1.1 collective-permute-start.5
  108.1 3.5 %collective-permute-start = (f32[2,128,256]{1,2,0:T(8,128)S(1)}, f32[2,128,256]{1,2,0:T(8,128)S(1)}, u32[]{:S(2)}, u32[]{:S(2)}) collective-permute-start(f32[2,128,256]{1,2,0:T(8,128)S(1)} %copy.103), channel_id=1, source_target_pairs={{0,64},{1,65},{2,66},{3,67},{4,68},{5,69},{6,70},{7,71},{8,72},{9,... | collective-permute-start | bytes 786440 | tf_op jit(solution)/shard_map/ppermute | solution.py:85
  111.7 0.6 constant_dynamic-update-slice_fusion.4
  112.3 0.6 constant_dynamic-update-slice_fusion.3
  112.9 3.1 %collective-permute-done.3 = f32[5,64,128]{2,1,0:T(8,128)S(1)} collective-permute-done((f32[5,64,128]{2,1,0:T(8,128)}, f32[5,64,128]{2,1,0:T(8,128)S(1)}, u32[]{:S(2)}, u32[]{:S(2)}) %collective-permute-start.3) | collective-permute-done | bytes 163872 | tf_op jit(solution)/shard_map/ppermute | solution.py:78
  116.2 1.5 collective-permute-done
  118.7 3.5 %collective-permute-start.7 = (f32[4,64,128]{2,1,0:T(8,128)S(1)}, f32[4,64,128]{2,1,0:T(8,128)S(1)}, u32[]{:S(2)}, u32[]{:S(2)}) collective-permute-start(f32[4,64,128]{2,1,0:T(8,128)S(1)} %pad_maximum_fusion.3), channel_id=1, source_target_pairs={{0,64},{1,65},{2,66},{3,67},{4,68},{5,69},{6,70},{7,71},{8,72},{9,... | collective-permute-start | bytes 393224 | tf_op jit(solution)/shard_map/ppermute | solution.py:85
  122.2 0.6 iota_and_fusion.1
  122.8 4.2 %collective-permute-start.6 = (f32[2,64,128]{2,1,0:T(8,128)S(1)}, f32[2,64,128]{2,1,0:T(8,128)S(1)}, u32[]{:S(2)}, u32[]{:S(2)}) collective-permute-start(f32[2,64,128]{2,1,0:T(8,128)S(1)} %get-tuple-element.20), channel_id=1, source_target_pairs={{62,64},{63,65},{0,66},{1,67},{2,68},{3,69},{4,70},{5,71},{6,72},{... | collective-permute-start | bytes 196616 | tf_op jit(solution)/shard_map/ppermute | solution.py:85
  127.0 4.7 %collective-permute-start.8 = (f32[2,64,128]{2,1,0:T(8,128)S(1)}, f32[2,64,128]{2,1,0:T(8,128)S(1)}, u32[]{:S(2)}, u32[]{:S(2)}) collective-permute-start(f32[2,64,128]{2,1,0:T(8,128)S(1)} %get-tuple-element.20), channel_id=1, source_target_pairs={{2,64},{3,65},{4,66},{5,67},{6,68},{7,69},{8,70},{9,71},{10,72},{1... | collective-permute-start | bytes 196616 | tf_op jit(solution)/shard_map/ppermute | solution.py:85
  131.7 0.5 compare_and_fusion.1
  132.3 0.9 collective-permute-done.6
  133.2 0.9 collective-permute-done.8
  134.8 2.3 %collective-permute-start.10 = (f32[2,64,128]{2,1,0:T(8,128)S(1)}, f32[2,64,128]{2,1,0:T(8,128)S(1)}, u32[]{:S(2)}, u32[]{:S(2)}) collective-permute-start(f32[2,64,128]{2,1,0:T(8,128)S(1)} %fusion.137), channel_id=1, source_target_pairs={{0,64},{1,65},{2,66},{3,67},{4,68},{5,69},{6,70},{7,71},{8,72},{9,... | collective-permute-start | bytes 196616 | tf_op jit(solution)/shard_map/ppermute | solution.py:85
  137.1 7.4 %collective-permute-start.11 = (f32[2,64,128]{2,1,0:T(8,128)S(1)}, f32[2,64,128]{2,1,0:T(8,128)S(1)}, u32[]{:S(2)}, u32[]{:S(2)}) collective-permute-start(f32[2,64,128]{2,1,0:T(8,128)S(1)} %fusion.137), channel_id=1, source_target_pairs={{2,64},{3,65},{4,66},{5,67},{6,68},{7,69},{8,70},{9,71},{10,72},{1... | collective-permute-start | bytes 196616 | tf_op jit(solution)/shard_map/ppermute | solution.py:85
  144.6 1.9 %collective-permute-start.9 = (f32[2,64,128]{2,1,0:T(8,128)S(1)}, f32[2,64,128]{2,1,0:T(8,128)S(1)}, u32[]{:S(2)}, u32[]{:S(2)}) collective-permute-start(f32[2,64,128]{2,1,0:T(8,128)S(1)} %fusion.137), channel_id=1, source_target_pairs={{62,64},{63,65},{0,66},{1,67},{2,68},{3,69},{4,70},{5,71},{6,72},{... | collective-permute-start | bytes 196616 | tf_op jit(solution)/shard_map/ppermute | solution.py:85
  146.5 0.5 compare_and_fusion
  147.0 7.9 %collective-permute-done.9 = f32[2,64,128]{2,1,0:T(8,128)S(1)} collective-permute-done((f32[2,64,128]{2,1,0:T(8,128)S(1)}, f32[2,64,128]{2,1,0:T(8,128)S(1)}, u32[]{:S(2)}, u32[]{:S(2)}) %collective-permute-start.9) | collective-permute-done | bytes 65568 | tf_op jit(solution)/shard_map/ppermute | solution.py:85
  155.6 0.8 fusion.142
  156.3 1.9 %collective-permute-start.12 = (f32[2,64,128]{2,1,0:T(8,128)}, f32[2,64,128]{2,1,0:T(8,128)}, u32[]{:S(2)}, u32[]{:S(2)}) collective-permute-start(f32[2,64,128]{2,1,0:T(8,128)} %fusion.142), channel_id=1, source_target_pairs={{62,64},{63,65},{0,66},{1,67},{2,68},{3,69},{4,70},{5,71},{6,72},{... | collective-permute-start | bytes 196616 | tf_op jit(solution)/shard_map/ppermute | solution.py:85
  158.2 1.9 %collective-permute-start.13 = (f32[2,64,128]{2,1,0:T(8,128)}, f32[2,64,128]{2,1,0:T(8,128)}, u32[]{:S(2)}, u32[]{:S(2)}) collective-permute-start(f32[2,64,128]{2,1,0:T(8,128)} %fusion.142), channel_id=1, source_target_pairs={{0,64},{1,65},{2,66},{3,67},{4,68},{5,69},{6,70},{7,71},{8,72},{9,... | collective-permute-start | bytes 196616 | tf_op jit(solution)/shard_map/ppermute | solution.py:85
  160.2 1.9 %collective-permute-start.14 = (f32[2,64,128]{2,1,0:T(8,128)}, f32[2,64,128]{2,1,0:T(8,128)}, u32[]{:S(2)}, u32[]{:S(2)}) collective-permute-start(f32[2,64,128]{2,1,0:T(8,128)} %fusion.142), channel_id=1, source_target_pairs={{2,64},{3,65},{4,66},{5,67},{6,68},{7,69},{8,70},{9,71},{10,72},{1... | collective-permute-start | bytes 196616 | tf_op jit(solution)/shard_map/ppermute | solution.py:85
  162.2 1.0 copy.128
  163.2 4.0 %collective-permute-done.12 = f32[2,64,128]{2,1,0:T(8,128)} collective-permute-done((f32[2,64,128]{2,1,0:T(8,128)}, f32[2,64,128]{2,1,0:T(8,128)}, u32[]{:S(2)}, u32[]{:S(2)}) %collective-permute-start.12) | collective-permute-done | bytes 65568 | tf_op jit(solution)/shard_map/ppermute | solution.py:85
  167.2 0.5 collective-permute-done.14
  167.7 0.9 maximum_select_fusion.2
  169.7 0.7 fusion.62
  170.5 1.4 convolution_bitcast_fusion
  172.2 1.1 copy.127
  (145 shorter events, 6.3 us)
Async XLA Ops:
  0.6 1.5 copy-start.5
  2.6 1.6 copy-start
  5.7 24.9 %all-to-all-start = ((f32[128,2,256]{2,1,0:T(2,128)}), f32[128,2,256]{2,1,0:T(2,128)S(1)}, u32[]{:S(2)}, u32[]{:S(2)}) async-start(f32[128,2,256]{2,1,0:T(2,128)} %copy.86), calls=%async_computation | async-start | bytes 524288 | tf_op jit(solution)/shard_map/all_to_all | solution.py:50
  32.8 17.9 %all-to-all-start.1 = ((f32[128,2,256]{2,1,0:T(2,128)}), f32[128,2,256]{2,1,0:T(2,128)S(1)}, u32[]{:S(2)}, u32[]{:S(2)}) async-start(f32[128,2,256]{2,1,0:T(2,128)} %copy.90), calls=%async_computation.1 | async-start | bytes 524288 | tf_op jit(solution)/shard_map/all_to_all | solution.py:53
  56.9 17.9 %all-to-all-start.2 = ((f32[128,2,256]{2,1,0:T(2,128)}), f32[128,2,256]{2,1,0:T(2,128)S(1)}, u32[]{:S(2)}, u32[]{:S(2)}) async-start(f32[128,2,256]{2,1,0:T(2,128)} %copy.97), calls=%async_computation.2 | async-start | bytes 524288 | tf_op jit(solution)/shard_map/all_to_all | solution.py:50
  62.0 37.6 %copy-start.11 = (pred[256]{0:T(512)(128)(4,1)}, pred[256]{0:T(512)(128)(4,1)S(1)}, u32[]{:S(2)}) copy-start(pred[256]{0:T(512)(128)(4,1)S(1)} %compare_and_fusion.3) | copy-start | bytes 772
  76.9 17.9 %all-to-all-start.3 = ((f32[128,2,256]{2,1,0:T(2,128)}), f32[128,2,256]{2,1,0:T(2,128)S(1)}, u32[]{:S(2)}, u32[]{:S(2)}) async-start(f32[128,2,256]{2,1,0:T(2,128)} %copy.101), calls=%async_computation.3 | async-start | bytes 524288 | tf_op jit(solution)/shard_map/all_to_all | solution.py:53
  81.8 19.1 %copy-start.7 = (pred[128]{0:T(512)(128)(4,1)}, pred[128]{0:T(512)(128)(4,1)S(1)}, u32[]{:S(2)}) copy-start(pred[128]{0:T(512)(128)(4,1)S(1)} %compare_and_fusion.2) | copy-start | bytes 388
  97.0 0.7 copy-start.3
  97.8 1.5 copy-start.1
  97.8 1.5 copy-start.2
  99.6 8.4 %copy-start.4 = (f32[256,256]{1,0:T(8,128)S(1)}, f32[256,256]{1,0:T(8,128)}, u32[]{:S(2)}) copy-start(f32[256,256]{1,0:T(8,128)} %copy-done.3) | copy-start | bytes 786436
  101.3 10.3 %collective-permute-start.1 = (f32[1,64,128]{2,1,0:T(8,128)S(1)}, f32[1,64,128]{2,1,0:T(8,128)S(1)}, u32[]{:S(2)}, u32[]{:S(2)}) collective-permute-start(f32[1,64,128]{2,1,0:T(8,128)S(1)} %get-tuple-element.75), channel_id=1, source_target_pairs={{62,0},{63,1},{0,2},{1,3},{2,4},{3,5},{4,6},{5,7},{6,8},{7,9},{8,1... | collective-permute-start | bytes 98312 | tf_op jit(solution)/shard_map/ppermute | solution.py:78
  102.2 9.5 %collective-permute-start.2 = (f32[3,64,128]{2,1,0:T(8,128)S(1)}, f32[3,64,128]{2,1,0:T(8,128)S(1)}, u32[]{:S(2)}, u32[]{:S(2)}) collective-permute-start(f32[3,64,128]{2,1,0:T(8,128)S(1)} %pad_maximum_fusion.4), channel_id=1, source_target_pairs={{63,0},{0,1},{1,2},{2,3},{3,4},{4,5},{5,6},{6,7},{7,8},{8,9},{9,10... | collective-permute-start | bytes 294920 | tf_op jit(solution)/shard_map/ppermute | solution.py:78
  102.3 13.8 %collective-permute-start.4 = (f32[3,64,128]{2,1,0:T(8,128)S(1)}, f32[3,64,128]{2,1,0:T(8,128)S(1)}, u32[]{:S(2)}, u32[]{:S(2)}) collective-permute-start(f32[3,64,128]{2,1,0:T(8,128)S(1)} %pad_maximum_fusion.4), channel_id=1, source_target_pairs={{2,0},{3,1},{4,2},{5,3},{6,4},{7,5},{8,6},{9,7},{10,8},{11,9},{12,... | collective-permute-start | bytes 294920 | tf_op jit(solution)/shard_map/ppermute | solution.py:78
  106.9 9.3 %collective-permute-start.5 = (f32[1,64,128]{2,1,0:T(8,128)S(1)}, f32[1,64,128]{2,1,0:T(8,128)S(1)}, u32[]{:S(2)}, u32[]{:S(2)}) collective-permute-start(f32[1,64,128]{2,1,0:T(8,128)S(1)} %get-tuple-element.75), channel_id=1, source_target_pairs={{3,0},{4,1},{5,2},{6,3},{7,4},{8,5},{9,6},{10,7},{11,8},{12,9},{13... | collective-permute-start | bytes 98312 | tf_op jit(solution)/shard_map/ppermute | solution.py:78
  108.0 3.7 %copy-start.6 = (f32[5,64,128]{2,1,0:T(8,128)}, f32[5,64,128]{2,1,0:T(8,128)S(1)}, u32[]{:S(2)}) copy-start(f32[5,64,128]{2,1,0:T(8,128)S(1)} %constant_dynamic-update-slice_fusion.5) | copy-start | bytes 491524
  108.1 9.6 %collective-permute-start = (f32[2,128,256]{1,2,0:T(8,128)S(1)}, f32[2,128,256]{1,2,0:T(8,128)S(1)}, u32[]{:S(2)}, u32[]{:S(2)}) collective-permute-start(f32[2,128,256]{1,2,0:T(8,128)S(1)} %copy.103), channel_id=1, source_target_pairs={{0,64},{1,65},{2,66},{3,67},{4,68},{5,69},{6,70},{7,71},{8,72},{9,... | collective-permute-start | bytes 786440 | tf_op jit(solution)/shard_map/ppermute | solution.py:85
  112.9 3.2 %collective-permute-start.3 = (f32[5,64,128]{2,1,0:T(8,128)}, f32[5,64,128]{2,1,0:T(8,128)S(1)}, u32[]{:S(2)}, u32[]{:S(2)}) collective-permute-start(f32[5,64,128]{2,1,0:T(8,128)} %constant_dynamic-update-slice_fusion.3), channel_id=1, source_target_pairs={{1,0},{2,1},{3,2},{4,3},{5,4},{6,5},{7,6},{8,7},{9,8},{10,9},{11,1... | collective-permute-start | bytes 491528 | tf_op jit(solution)/shard_map/ppermute | solution.py:78
  118.7 13.5 %collective-permute-start.7 = (f32[4,64,128]{2,1,0:T(8,128)S(1)}, f32[4,64,128]{2,1,0:T(8,128)S(1)}, u32[]{:S(2)}, u32[]{:S(2)}) collective-permute-start(f32[4,64,128]{2,1,0:T(8,128)S(1)} %pad_maximum_fusion.3), channel_id=1, source_target_pairs={{0,64},{1,65},{2,66},{3,67},{4,68},{5,69},{6,70},{7,71},{8,72},{9,... | collective-permute-start | bytes 393224 | tf_op jit(solution)/shard_map/ppermute | solution.py:85
  122.8 10.4 %collective-permute-start.6 = (f32[2,64,128]{2,1,0:T(8,128)S(1)}, f32[2,64,128]{2,1,0:T(8,128)S(1)}, u32[]{:S(2)}, u32[]{:S(2)}) collective-permute-start(f32[2,64,128]{2,1,0:T(8,128)S(1)} %get-tuple-element.20), channel_id=1, source_target_pairs={{62,64},{63,65},{0,66},{1,67},{2,68},{3,69},{4,70},{5,71},{6,72},{... | collective-permute-start | bytes 196616 | tf_op jit(solution)/shard_map/ppermute | solution.py:85
  127.0 7.1 %collective-permute-start.8 = (f32[2,64,128]{2,1,0:T(8,128)S(1)}, f32[2,64,128]{2,1,0:T(8,128)S(1)}, u32[]{:S(2)}, u32[]{:S(2)}) collective-permute-start(f32[2,64,128]{2,1,0:T(8,128)S(1)} %get-tuple-element.20), channel_id=1, source_target_pairs={{2,64},{3,65},{4,66},{5,67},{6,68},{7,69},{8,70},{9,71},{10,72},{1... | collective-permute-start | bytes 196616 | tf_op jit(solution)/shard_map/ppermute | solution.py:85
  134.8 12.2 %collective-permute-start.10 = (f32[2,64,128]{2,1,0:T(8,128)S(1)}, f32[2,64,128]{2,1,0:T(8,128)S(1)}, u32[]{:S(2)}, u32[]{:S(2)}) collective-permute-start(f32[2,64,128]{2,1,0:T(8,128)S(1)} %fusion.137), channel_id=1, source_target_pairs={{0,64},{1,65},{2,66},{3,67},{4,68},{5,69},{6,70},{7,71},{8,72},{9,... | collective-permute-start | bytes 196616 | tf_op jit(solution)/shard_map/ppermute | solution.py:85
  137.1 9.9 %collective-permute-start.11 = (f32[2,64,128]{2,1,0:T(8,128)S(1)}, f32[2,64,128]{2,1,0:T(8,128)S(1)}, u32[]{:S(2)}, u32[]{:S(2)}) collective-permute-start(f32[2,64,128]{2,1,0:T(8,128)S(1)} %fusion.137), channel_id=1, source_target_pairs={{2,64},{3,65},{4,66},{5,67},{6,68},{7,69},{8,70},{9,71},{10,72},{1... | collective-permute-start | bytes 196616 | tf_op jit(solution)/shard_map/ppermute | solution.py:85
  144.6 10.4 %collective-permute-start.9 = (f32[2,64,128]{2,1,0:T(8,128)S(1)}, f32[2,64,128]{2,1,0:T(8,128)S(1)}, u32[]{:S(2)}, u32[]{:S(2)}) collective-permute-start(f32[2,64,128]{2,1,0:T(8,128)S(1)} %fusion.137), channel_id=1, source_target_pairs={{62,64},{63,65},{0,66},{1,67},{2,68},{3,69},{4,70},{5,71},{6,72},{... | collective-permute-start | bytes 196616 | tf_op jit(solution)/shard_map/ppermute | solution.py:85
  156.3 10.8 %collective-permute-start.12 = (f32[2,64,128]{2,1,0:T(8,128)}, f32[2,64,128]{2,1,0:T(8,128)}, u32[]{:S(2)}, u32[]{:S(2)}) collective-permute-start(f32[2,64,128]{2,1,0:T(8,128)} %fusion.142), channel_id=1, source_target_pairs={{62,64},{63,65},{0,66},{1,67},{2,68},{3,69},{4,70},{5,71},{6,72},{... | collective-permute-start | bytes 196616 | tf_op jit(solution)/shard_map/ppermute | solution.py:85
  158.2 8.9 %collective-permute-start.13 = (f32[2,64,128]{2,1,0:T(8,128)}, f32[2,64,128]{2,1,0:T(8,128)}, u32[]{:S(2)}, u32[]{:S(2)}) collective-permute-start(f32[2,64,128]{2,1,0:T(8,128)} %fusion.142), channel_id=1, source_target_pairs={{0,64},{1,65},{2,66},{3,67},{4,68},{5,69},{6,70},{7,71},{8,72},{9,... | collective-permute-start | bytes 196616 | tf_op jit(solution)/shard_map/ppermute | solution.py:85
  160.2 7.5 %collective-permute-start.14 = (f32[2,64,128]{2,1,0:T(8,128)}, f32[2,64,128]{2,1,0:T(8,128)}, u32[]{:S(2)}, u32[]{:S(2)}) collective-permute-start(f32[2,64,128]{2,1,0:T(8,128)} %fusion.142), channel_id=1, source_target_pairs={{2,64},{3,65},{4,66},{5,67},{6,68},{7,69},{8,70},{9,71},{10,72},{1... | collective-permute-start | bytes 196616 | tf_op jit(solution)/shard_map/ppermute | solution.py:85
  169.1 0.7 copy-start.9
  169.1 0.7 copy-start.10
  169.1 0.7 copy-start.12
  169.1 0.7 copy-start.16
  169.3 1.2 copy-start.8
  169.3 1.2 copy-start.13
  169.3 1.2 copy-start.14
  169.3 1.2 copy-start.15

commit v8 on v7

--- a/solution.py
+++ b/solution.py
@@ -184,6 +184,8 @@
     factor = 1.0 / (1.0 + 0.5 * lam)
     explicit_old = react(nodes)
     rates_old = explicit_old + implicit
+    start_c = gather_bands([(restrict(nodes[0:1])[0], (0, 0), (2, 3))])[0]
+    rate_start = coarse_rate(start_c)
     values = [nodes[0]]
     terms = [implicit[0]]
     for m in range(2):
@@ -198,21 +200,20 @@
     fresh = jnp.stack(values)
     rates_new = react(fresh) + jnp.stack(terms)
     sums = [0.5 * (w[0] * rates_new[0] + w[1] * rates_new[1] + w[2] * rates_new[2]) for w in WEIGHTS]
-    coarse = restrict(jnp.stack([values[0], values[1], values[2], sums[0], sums[1]]))
+    coarse = restrict(jnp.stack([values[1], values[2], sums[0], sums[1]]))
     slot = lax.axis_index("tm")
     slices = lax.axis_size("tm")
     local = planes // 2
     wide = gather_bands(
-        [(coarse[0], (0, 0), (2, 3)), (coarse[1], (0, 0), (1, 2)), (coarse[3], (0, 0), (1, 2)),
-         (coarse[4], (0, 0), (0, 1)), (coarse[2], (0, 0), (0, 1))]
+        [(coarse[0], (0, 0), (1, 2)), (coarse[2], (0, 0), (1, 2)), (coarse[3], (0, 0), (0, 1)),
+         (coarse[1], (0, 0), (0, 1))]
     )
     previous_two = fetch(values[2], 0, 1)
     previous_two, wide = lax.optimization_barrier((previous_two, wide))
-    start_c = wide[0]
-    rates_c = (coarse_rate(start_c), coarse_rate(wide[1]))
-    sums_c = (wide[2], wide[3])
-    coarse_one = wide[1][1:2 + local]
-    coarse_two = wide[4]
+    rates_c = (rate_start, coarse_rate(wide[0]))
+    sums_c = (wide[1], wide[2])
+    coarse_one = wide[0][1:2 + local]
+    coarse_two = wide[3]
     start = start_c
     previous_coarse_two = None
     for section in range(slices - 1):

time: 174 us -> 187 us (1.075)
  local copies, waits for them, and re-layouts: 15.5 us -> 27.8 us
  waiting for transfers between devices: 66.1 us -> 55.6 us
  starting transfers between devices: 66.8 us -> 74.8 us
  matrix products: 15.1 us -> 17.1 us
    ppermute x5 -> x8, starting transfers between devices: 6.68 us -> 16 us  [fetch(): return lax.ppermute(value, 'space', pairs)]
    unnamed x45 -> x121, local copies, waits for them, and re-layouts: 5.54 us -> 12.9 us
    all_to_all x4, waiting for transfers between devices: 47.2 us -> 40 us  [spectral_solve(): lax.all_to_all(field, 'space', split_axis=0, concat_axis=1, tiled=True)]
    ppermute x5 -> x8, waiting for transfers between devices: 3.16 us -> 0.02 us  [fetch(): return lax.ppermute(value, 'space', pairs)]
    all_to_all x4, starting transfers between devices: 26.8 us -> 24.1 us  [spectral_solve(): lax.all_to_all(field, 'space', split_axis=0, concat_axis=1, tiled=True)]
  transfers between devices with their start and end apart: 19 -> 22, of which waited for: 11 -> 10; matrix products, arithmetic and copies ran while one was open for 5% -> 19% of each run, Pallas kernels for 0% -> 0%
where the time goes in v8:
time: 187 us; the launch traced here: 185 us
  starting transfers between devices  74.8 us (40%)
  waiting for transfers between devices  55.6 us (30%)
  local copies, waits for them, and re-layouts  27.8 us (15%)
  matrix products  17.1 us (9%)
  other arithmetic  7.4 us (4%)
  between operations  2.07 us (1%)
    all_to_all x4, waiting for transfers between devices, spectral_solve(): lax.all_to_all(field, 'space', split_axis=0, concat_axis=1, tiled=True)  40 us
    ppermute x10, starting transfers between devices, fetch(): return lax.ppermute(value, ('tm', 'space'), pairs)  34.8 us
    all_to_all x4, starting transfers between devices, spectral_solve(): lax.all_to_all(field, 'space', split_axis=0, concat_axis=1, tiled=True)  24.1 us
    ppermute x8, starting transfers between devices, fetch(): return lax.ppermute(value, 'space', pairs)  16 us
    ppermute x10, waiting for transfers between devices, fetch(): return lax.ppermute(value, ('tm', 'space'), pairs)  15.6 us
    unnamed x121, local copies, waits for them, and re-layouts  12.9 us
    dot_general x2, matrix products, spectral_solve(): jnp.dot(field.reshape(planes * size_y, size_z), basis_z, precision=TRANSF...  4.55 us
  transfers between devices with their start and end apart: 22, of which 10 were waited for; matrix products, arithmetic and copies ran while one was open for 19% of the time, Pallas kernels for 0%

profile of v8, /device:TPU:8, one launch (start us, length us, event | category | flops | bytes accessed | tf_op | source)
XLA Modules:
  0.0 184.8 jit_solution(1828099523912056545)
XLA Ops:
  1.2 1.4 fusion.68
  3.0 7.6 %collective-permute-start.6 = (f32[1,64,128]{2,1,0:T(8,128)S(1)}, f32[1,64,128]{2,1,0:T(8,128)S(1)}, u32[]{:S(2)}, u32[]{:S(2)}) collective-permute-start(f32[1,64,128]{2,1,0:T(8,128)S(1)} %convolution_bitcast_fusion.1), channel_id=1, source_target_pairs={{1,0},{2,1},{3,2},{4,3},{5,4},{6,5},{7,6},{8,7},{9,8},{10,9},{11,1... | collective-permute-start | bytes 98312 | tf_op jit(solution)/shard_map/ppermute | solution.py:78
  10.5 2.2 %collective-permute-start.7 = (f32[1,64,128]{2,1,0:T(8,128)S(1)}, f32[1,64,128]{2,1,0:T(8,128)S(1)}, u32[]{:S(2)}, u32[]{:S(2)}) collective-permute-start(f32[1,64,128]{2,1,0:T(8,128)S(1)} %convolution_bitcast_fusion.1), channel_id=1, source_target_pairs={{2,0},{3,1},{4,2},{5,3},{6,4},{7,5},{8,6},{9,7},{10,8},{11,9},{12,... | collective-permute-start | bytes 98312 | tf_op jit(solution)/shard_map/ppermute | solution.py:78
  12.7 0.9 collective-permute-start.8
  13.7 1.4 copy.78
  15.7 1.6 fusion.13
  17.9 0.9 copy.84
  18.8 8.9 %all-to-all-start = ((f32[128,2,256]{2,1,0:T(2,128)}), f32[128,2,256]{2,1,0:T(2,128)S(1)}, u32[]{:S(2)}, u32[]{:S(2)}) async-start(f32[128,2,256]{2,1,0:T(2,128)} %copy.84), calls=%async_computation | async-start | bytes 524288 | tf_op jit(solution)/shard_map/all_to_all | solution.py:50
  27.8 0.6 iota_and_fusion
  29.0 0.7 slice_bitcast_fusion.1
  29.8 0.7 slice_bitcast_fusion.2
  30.5 10.2 %all-to-all-done = f32[128,2,256]{2,1,0:T(2,128)S(1)} async-done(((f32[128,2,256]{2,1,0:T(2,128)}), f32[128,2,256]{2,1,0:T(2,128)S(1)}, u32[]{:S(2)}, u32[]{:S(2)}) %all-to-all-start) | async-done | bytes 262176 | tf_op jit(solution)/shard_map/all_to_all | solution.py:50
  42.5 0.9 copy.88
  43.5 5.1 %all-to-all-start.1 = ((f32[128,2,256]{2,1,0:T(2,128)}), f32[128,2,256]{2,1,0:T(2,128)S(1)}, u32[]{:S(2)}, u32[]{:S(2)}) async-start(f32[128,2,256]{2,1,0:T(2,128)} %copy.88), calls=%async_computation.1 | async-start | bytes 524288 | tf_op jit(solution)/shard_map/all_to_all | solution.py:53
  48.6 0.6 iota_and_fusion.1
  49.7 1.0 slice.664
  50.7 0.8 copy.90
  51.5 0.8 copy.93
  52.4 0.8 copy.92
  53.2 0.8 constant_dynamic-update-slice_fusion.5
  54.0 7.3 %all-to-all-done.1 = f32[128,2,256]{2,1,0:T(2,128)S(1)} async-done(((f32[128,2,256]{2,1,0:T(2,128)}), f32[128,2,256]{2,1,0:T(2,128)S(1)}, u32[]{:S(2)}, u32[]{:S(2)}) %all-to-all-start.1) | async-done | bytes 262176 | tf_op jit(solution)/shard_map/all_to_all | solution.py:53
  62.9 3.1 %fusion.22 = (f32[256,256]{1,0:T(8,128)S(1)}, f32[256,256]{1,0:T(8,128)}) fusion(f32[1,2,128,256]{3,2,1,0:T(8,128)S(1)} %copy-done.16, f32[1,1,2,128,256]{4,3,2,1,0:T(8,128)} %copy.92, f32[1,2,128,256]{3,2,1,0:T(8,128)S(1)} %copy-done.15, f32[256,256]{1,0:T(8,128)S(1)} %bitcast.205, f32[256]{0:T(256)S(1)} %copy-done.45, s32[256]{0:T(256)S(1)} %copy-done.48, ...), kind=kOutput, calls=%fused_computation.44 | convolution fusion | flops 102301696 | bytes 1575168 | tf_op jit(solution)/shard_map/dot_general | solution.py:55
  66.0 1.5 fusion.47
  68.0 0.9 copy.95
  68.9 4.9 %all-to-all-start.2 = ((f32[128,2,256]{2,1,0:T(2,128)}), f32[128,2,256]{2,1,0:T(2,128)S(1)}, u32[]{:S(2)}, u32[]{:S(2)}) async-start(f32[128,2,256]{2,1,0:T(2,128)} %copy.95), calls=%async_computation.2 | async-start | bytes 524288 | tf_op jit(solution)/shard_map/all_to_all | solution.py:50
  73.9 0.6 fusion.381
  74.5 0.7 fusion.380
  75.2 11.6 %all-to-all-done.2 = f32[128,2,256]{2,1,0:T(2,128)S(1)} async-done(((f32[128,2,256]{2,1,0:T(2,128)}), f32[128,2,256]{2,1,0:T(2,128)S(1)}, u32[]{:S(2)}, u32[]{:S(2)}) %all-to-all-start.2) | async-done | bytes 262176 | tf_op jit(solution)/shard_map/all_to_all | solution.py:50
  88.7 0.9 copy.99
  89.6 5.1 %all-to-all-start.3 = ((f32[128,2,256]{2,1,0:T(2,128)}), f32[128,2,256]{2,1,0:T(2,128)S(1)}, u32[]{:S(2)}, u32[]{:S(2)}) async-start(f32[128,2,256]{2,1,0:T(2,128)} %copy.99), calls=%async_computation.3 | async-start | bytes 524288 | tf_op jit(solution)/shard_map/all_to_all | solution.py:53
  94.8 0.8 fusion.382
  95.5 0.8 fusion.383
  96.7 10.8 %all-to-all-done.3 = f32[128,2,256]{2,1,0:T(2,128)S(1)} async-done(((f32[128,2,256]{2,1,0:T(2,128)}), f32[128,2,256]{2,1,0:T(2,128)S(1)}, u32[]{:S(2)}, u32[]{:S(2)}) %all-to-all-start.3) | async-done | bytes 262176 | tf_op jit(solution)/shard_map/all_to_all | solution.py:53
  108.9 1.4 fusion.127
  110.4 0.7 copy-done.5
  111.2 1.4 fusion.29
  113.5 1.1 fusion.3
  115.4 1.5 collective-permute-start.3
  116.9 3.4 %collective-permute-start.2 = (f32[4,64,128]{2,1,0:T(8,128)S(1)}, f32[4,64,128]{2,1,0:T(8,128)S(1)}, u32[]{:S(2)}, u32[]{:S(2)}) collective-permute-start(f32[4,64,128]{2,1,0:T(8,128)S(1)} %fusion.71), channel_id=1, source_target_pairs={{1,0},{2,1},{3,2},{4,3},{5,4},{6,5},{7,6},{8,7},{9,8},{10,9},{11,1... | collective-permute-start | bytes 393224 | tf_op jit(solution)/shard_map/ppermute | solution.py:78
  120.3 0.8 copy.101
  121.1 3.5 %collective-permute-start = (f32[2,128,256]{1,2,0:T(8,128)}, f32[2,128,256]{1,2,0:T(8,128)S(1)}, u32[]{:S(2)}, u32[]{:S(2)}) collective-permute-start(f32[2,128,256]{1,2,0:T(8,128)} %copy.101), channel_id=1, source_target_pairs={{0,64},{1,65},{2,66},{3,67},{4,68},{5,69},{6,70},{7,71},{8,72},{9,... | collective-permute-start | bytes 786440 | tf_op jit(solution)/shard_map/ppermute | solution.py:85
  124.8 6.8 %collective-permute-done = f32[2,128,256]{1,2,0:T(8,128)S(1)} collective-permute-done((f32[2,128,256]{1,2,0:T(8,128)}, f32[2,128,256]{1,2,0:T(8,128)S(1)}, u32[]{:S(2)}, u32[]{:S(2)}) %collective-permute-start) | collective-permute-done | bytes 262176 | tf_op jit(solution)/shard_map/ppermute | solution.py:85
  131.6 0.7 copy-done.17
  132.3 0.9 add_add_fusion
  133.8 3.6 %collective-permute-start.10 = (f32[4,64,128]{2,1,0:T(8,128)S(1)}, f32[4,64,128]{2,1,0:T(8,128)S(1)}, u32[]{:S(2)}, u32[]{:S(2)}) collective-permute-start(f32[4,64,128]{2,1,0:T(8,128)S(1)} %pad_maximum_fusion.5), channel_id=1, source_target_pairs={{0,64},{1,65},{2,66},{3,67},{4,68},{5,69},{6,70},{7,71},{8,72},{9,... | collective-permute-start | bytes 393224 | tf_op jit(solution)/shard_map/ppermute | solution.py:85
  137.5 1.9 %collective-permute-start.11 = (f32[2,64,128]{2,1,0:T(8,128)S(1)}, f32[2,64,128]{2,1,0:T(8,128)S(1)}, u32[]{:S(2)}, u32[]{:S(2)}) collective-permute-start(f32[2,64,128]{2,1,0:T(8,128)S(1)} %get-tuple-element.18), channel_id=1, source_target_pairs={{2,64},{3,65},{4,66},{5,67},{6,68},{7,69},{8,70},{9,71},{10,72},{1... | collective-permute-start | bytes 196616 | tf_op jit(solution)/shard_map/ppermute | solution.py:85
  139.4 3.5 %collective-permute-start.9 = (f32[2,64,128]{2,1,0:T(8,128)S(1)}, f32[2,64,128]{2,1,0:T(8,128)S(1)}, u32[]{:S(2)}, u32[]{:S(2)}) collective-permute-start(f32[2,64,128]{2,1,0:T(8,128)S(1)} %get-tuple-element.18), channel_id=1, source_target_pairs={{62,64},{63,65},{0,66},{1,67},{2,68},{3,69},{4,70},{5,71},{6,72},{... | collective-permute-start | bytes 196616 | tf_op jit(solution)/shard_map/ppermute | solution.py:85
  142.9 0.8 constant_dynamic-update-slice_fusion
  143.7 0.9 collective-permute-done.11
  144.5 5.2 %collective-permute-done.9 = f32[2,64,128]{2,1,0:T(8,128)S(1)} collective-permute-done((f32[2,64,128]{2,1,0:T(8,128)S(1)}, f32[2,64,128]{2,1,0:T(8,128)S(1)}, u32[]{:S(2)}, u32[]{:S(2)}) %collective-permute-start.9) | collective-permute-done | bytes 65568 | tf_op jit(solution)/shard_map/ppermute | solution.py:85
  150.5 1.9 %collective-permute-start.12 = (f32[2,64,128]{2,1,0:T(8,128)S(1)}, f32[2,64,128]{2,1,0:T(8,128)S(1)}, u32[]{:S(2)}, u32[]{:S(2)}) collective-permute-start(f32[2,64,128]{2,1,0:T(8,128)S(1)} %fusion.147), channel_id=1, source_target_pairs={{62,64},{63,65},{0,66},{1,67},{2,68},{3,69},{4,70},{5,71},{6,72},{... | collective-permute-start | bytes 196616 | tf_op jit(solution)/shard_map/ppermute | solution.py:85
  152.5 3.2 %collective-permute-start.13 = (f32[2,64,128]{2,1,0:T(8,128)S(1)}, f32[2,64,128]{2,1,0:T(8,128)S(1)}, u32[]{:S(2)}, u32[]{:S(2)}) collective-permute-start(f32[2,64,128]{2,1,0:T(8,128)S(1)} %fusion.147), channel_id=1, source_target_pairs={{0,64},{1,65},{2,66},{3,67},{4,68},{5,69},{6,70},{7,71},{8,72},{9,... | collective-permute-start | bytes 196616 | tf_op jit(solution)/shard_map/ppermute | solution.py:85
  155.7 4.9 %collective-permute-start.14 = (f32[2,64,128]{2,1,0:T(8,128)S(1)}, f32[2,64,128]{2,1,0:T(8,128)S(1)}, u32[]{:S(2)}, u32[]{:S(2)}) collective-permute-start(f32[2,64,128]{2,1,0:T(8,128)S(1)} %fusion.147), channel_id=1, source_target_pairs={{2,64},{3,65},{4,66},{5,67},{6,68},{7,69},{8,70},{9,71},{10,72},{1... | collective-permute-start | bytes 196616 | tf_op jit(solution)/shard_map/ppermute | solution.py:85
  160.9 1.8 collective-permute-done.14
  163.5 1.9 %collective-permute-start.15 = (f32[2,64,128]{2,1,0:T(8,128)S(1)}, f32[2,64,128]{2,1,0:T(8,128)S(1)}, u32[]{:S(2)}, u32[]{:S(2)}) collective-permute-start(f32[2,64,128]{2,1,0:T(8,128)S(1)} %fusion.152), channel_id=1, source_target_pairs={{62,64},{63,65},{0,66},{1,67},{2,68},{3,69},{4,70},{5,71},{6,72},{... | collective-permute-start | bytes 196616 | tf_op jit(solution)/shard_map/ppermute | solution.py:85
  165.4 2.1 %collective-permute-start.16 = (f32[2,64,128]{2,1,0:T(8,128)S(1)}, f32[2,64,128]{2,1,0:T(8,128)S(1)}, u32[]{:S(2)}, u32[]{:S(2)}) collective-permute-start(f32[2,64,128]{2,1,0:T(8,128)S(1)} %fusion.152), channel_id=1, source_target_pairs={{0,64},{1,65},{2,66},{3,67},{4,68},{5,69},{6,70},{7,71},{8,72},{9,... | collective-permute-start | bytes 196616 | tf_op jit(solution)/shard_map/ppermute | solution.py:85
  167.5 8.3 %collective-permute-start.17 = (f32[2,64,128]{2,1,0:T(8,128)S(1)}, f32[2,64,128]{2,1,0:T(8,128)S(1)}, u32[]{:S(2)}, u32[]{:S(2)}) collective-permute-start(f32[2,64,128]{2,1,0:T(8,128)S(1)} %fusion.152), channel_id=1, source_target_pairs={{2,64},{3,65},{4,66},{5,67},{6,68},{7,69},{8,70},{9,71},{10,72},{1... | collective-permute-start | bytes 196616 | tf_op jit(solution)/shard_map/ppermute | solution.py:85
  175.9 1.0 copy.125
  178.3 0.7 copy-done.20
  179.1 0.6 copy-done.31
  179.7 0.7 fusion.62
  181.1 1.4 convolution_bitcast_fusion
  182.6 0.9 copy-done.18
  183.6 1.1 copy.124
  (230 shorter events, 17.0 us)
Async XLA Ops:
  0.7 1.9 %copy-start.22 = (s32[128]{0:T(128)}, s32[128]{0:T(128)S(1)}, u32[]{:S(2)}) copy-start(s32[128]{0:T(128)S(1)} %get-tuple-element.123) | copy-start | bytes 1540
  0.7 1.9 %copy-start.24 = (s32[128]{0:T(128)}, s32[128]{0:T(128)S(1)}, u32[]{:S(2)}) copy-start(s32[128]{0:T(128)S(1)} %get-tuple-element.124) | copy-start | bytes 1540
  0.7 1.9 %copy-start.26 = (pred[128]{0:T(512)(128)(4,1)}, pred[128]{0:T(512)(128)(4,1)S(1)}, u32[]{:S(2)}) copy-start(pred[128]{0:T(512)(128)(4,1)S(1)} %compare_and_fusion.2) | copy-start | bytes 388
  2.9 12.3 %copy-start.7 = (f32[1,3,2,128,256]{4,3,2,1,0:T(8,128)S(1)}, f32[1,3,2,128,256]{4,3,2,1,0:T(8,128)}, u32[]{:S(2)}) copy-start(f32[1,3,2,128,256]{4,3,2,1,0:T(8,128)} %param.3) | copy-start | bytes 2359300
  2.9 51.1 %collective-permute-start.5 = (f32[1,64,128]{2,1,0:T(8,128)S(1)}, f32[1,64,128]{2,1,0:T(8,128)S(1)}, u32[]{:S(2)}, u32[]{:S(2)}) collective-permute-start(f32[1,64,128]{2,1,0:T(8,128)S(1)} %convolution_bitcast_fusion.1), channel_id=1, source_target_pairs={{63,0},{0,1},{1,2},{2,3},{3,4},{4,5},{5,6},{6,7},{7,8},{8,9},{9,10... | collective-permute-start | bytes 98312 | tf_op jit(solution)/shard_map/ppermute | solution.py:78
  3.0 51.0 %collective-permute-start.6 = (f32[1,64,128]{2,1,0:T(8,128)S(1)}, f32[1,64,128]{2,1,0:T(8,128)S(1)}, u32[]{:S(2)}, u32[]{:S(2)}) collective-permute-start(f32[1,64,128]{2,1,0:T(8,128)S(1)} %convolution_bitcast_fusion.1), channel_id=1, source_target_pairs={{1,0},{2,1},{3,2},{4,3},{5,4},{6,5},{7,6},{8,7},{9,8},{10,9},{11,1... | collective-permute-start | bytes 98312 | tf_op jit(solution)/shard_map/ppermute | solution.py:78
  10.5 43.5 %collective-permute-start.7 = (f32[1,64,128]{2,1,0:T(8,128)S(1)}, f32[1,64,128]{2,1,0:T(8,128)S(1)}, u32[]{:S(2)}, u32[]{:S(2)}) collective-permute-start(f32[1,64,128]{2,1,0:T(8,128)S(1)} %convolution_bitcast_fusion.1), channel_id=1, source_target_pairs={{2,0},{3,1},{4,2},{5,3},{6,4},{7,5},{8,6},{9,7},{10,8},{11,9},{12,... | collective-permute-start | bytes 98312 | tf_op jit(solution)/shard_map/ppermute | solution.py:78
  12.7 40.5 %collective-permute-start.4 = (f32[1,64,128]{2,1,0:T(8,128)S(1)}, f32[1,64,128]{2,1,0:T(8,128)}, u32[]{:S(2)}, u32[]{:S(2)}) collective-permute-start(f32[1,64,128]{2,1,0:T(8,128)S(1)} %convolution_bitcast_fusion.1), channel_id=1, source_target_pairs={{62,0},{63,1},{0,2},{1,3},{2,4},{3,5},{4,6},{5,7},{6,8},{7,9},{8,1... | collective-permute-start | bytes 98312 | tf_op jit(solution)/shard_map/ppermute | solution.py:78
  12.7 118.8 %collective-permute-start.8 = (f32[1,64,128]{2,1,0:T(8,128)S(1)}, f32[1,64,128]{2,1,0:T(8,128)}, u32[]{:S(2)}, u32[]{:S(2)}) collective-permute-start(f32[1,64,128]{2,1,0:T(8,128)S(1)} %convolution_bitcast_fusion.1), channel_id=1, source_target_pairs={{3,0},{4,1},{5,2},{6,3},{7,4},{8,5},{9,6},{10,7},{11,8},{12,9},{13... | collective-permute-start | bytes 98312 | tf_op jit(solution)/shard_map/ppermute | solution.py:78
  15.6 1.7 copy-start
  18.8 21.9 %all-to-all-start = ((f32[128,2,256]{2,1,0:T(2,128)}), f32[128,2,256]{2,1,0:T(2,128)S(1)}, u32[]{:S(2)}, u32[]{:S(2)}) async-start(f32[128,2,256]{2,1,0:T(2,128)} %copy.84), calls=%async_computation | async-start | bytes 524288 | tf_op jit(solution)/shard_map/all_to_all | solution.py:50
  28.5 12.3 %copy-start.37 = (f32[128,2]{0,1:T(2,128)}, f32[128,2]{0,1:T(2,128)S(1)}, u32[]{:S(2)}) copy-start(f32[128,2]{0,1:T(2,128)S(1)} %broadcast_add_fusion.1) | copy-start | bytes 3076
  43.5 17.9 %all-to-all-start.1 = ((f32[128,2,256]{2,1,0:T(2,128)}), f32[128,2,256]{2,1,0:T(2,128)S(1)}, u32[]{:S(2)}, u32[]{:S(2)}) async-start(f32[128,2,256]{2,1,0:T(2,128)} %copy.88), calls=%async_computation.1 | async-start | bytes 524288 | tf_op jit(solution)/shard_map/all_to_all | solution.py:53
  61.6 1.0 copy-start.15
  61.6 1.0 copy-start.16
  61.6 1.0 copy-start.48
  62.1 0.7 copy-start.45
  62.1 0.7 copy-start.54
  68.9 17.9 %all-to-all-start.2 = ((f32[128,2,256]{2,1,0:T(2,128)}), f32[128,2,256]{2,1,0:T(2,128)S(1)}, u32[]{:S(2)}, u32[]{:S(2)}) async-start(f32[128,2,256]{2,1,0:T(2,128)} %copy.95), calls=%async_computation.2 | async-start | bytes 524288 | tf_op jit(solution)/shard_map/all_to_all | solution.py:50
  89.6 17.9 %all-to-all-start.3 = ((f32[128,2,256]{2,1,0:T(2,128)}), f32[128,2,256]{2,1,0:T(2,128)S(1)}, u32[]{:S(2)}, u32[]{:S(2)}) async-start(f32[128,2,256]{2,1,0:T(2,128)} %copy.99), calls=%async_computation.3 | async-start | bytes 524288 | tf_op jit(solution)/shard_map/all_to_all | solution.py:53
  94.7 0.8 copy-start.1
  95.5 1.0 copy-start.14
  108.3 0.7 copy-start.46
  110.4 0.7 copy-start.5
  111.2 1.4 copy-start.3
  111.2 1.4 copy-start.4
  112.8 0.7 copy-start.30
  112.8 0.7 copy-start.33
  112.9 0.7 copy-start.42
  113.5 1.1 copy-start.23
  113.5 1.1 copy-start.25
  113.5 1.2 copy-start.27
  115.0 5.3 %copy-start.6 = (f32[256,256]{1,0:T(8,128)S(1)}, f32[256,256]{1,0:T(8,128)}, u32[]{:S(2)}) copy-start(f32[256,256]{1,0:T(8,128)} %copy-done.5) | copy-start | bytes 786436
  115.0 9.6 %collective-permute-start.1 = (f32[2,64,128]{2,1,0:T(8,128)S(1)}, f32[2,64,128]{2,1,0:T(8,128)S(1)}, u32[]{:S(2)}, u32[]{:S(2)}) collective-permute-start(f32[2,64,128]{2,1,0:T(8,128)S(1)} %pad_maximum_fusion.6), channel_id=1, source_target_pairs={{63,0},{0,1},{1,2},{2,3},{3,4},{4,5},{5,6},{6,7},{7,8},{8,9},{9,10... | collective-permute-start | bytes 196616 | tf_op jit(solution)/shard_map/ppermute | solution.py:78
  115.4 9.3 %collective-permute-start.3 = (f32[2,64,128]{2,1,0:T(8,128)S(1)}, f32[2,64,128]{2,1,0:T(8,128)S(1)}, u32[]{:S(2)}, u32[]{:S(2)}) collective-permute-start(f32[2,64,128]{2,1,0:T(8,128)S(1)} %pad_maximum_fusion.6), channel_id=1, source_target_pairs={{2,0},{3,1},{4,2},{5,3},{6,4},{7,5},{8,6},{9,7},{10,8},{11,9},{12,... | collective-permute-start | bytes 196616 | tf_op jit(solution)/shard_map/ppermute | solution.py:78
  116.9 7.7 %collective-permute-start.2 = (f32[4,64,128]{2,1,0:T(8,128)S(1)}, f32[4,64,128]{2,1,0:T(8,128)S(1)}, u32[]{:S(2)}, u32[]{:S(2)}) collective-permute-start(f32[4,64,128]{2,1,0:T(8,128)S(1)} %fusion.71), channel_id=1, source_target_pairs={{1,0},{2,1},{3,2},{4,3},{5,4},{6,5},{7,6},{8,7},{9,8},{10,9},{11,1... | collective-permute-start | bytes 393224 | tf_op jit(solution)/shard_map/ppermute | solution.py:78
  121.1 10.4 %collective-permute-start = (f32[2,128,256]{1,2,0:T(8,128)}, f32[2,128,256]{1,2,0:T(8,128)S(1)}, u32[]{:S(2)}, u32[]{:S(2)}) collective-permute-start(f32[2,128,256]{1,2,0:T(8,128)} %copy.101), channel_id=1, source_target_pairs={{0,64},{1,65},{2,66},{3,67},{4,68},{5,69},{6,70},{7,71},{8,72},{9,... | collective-permute-start | bytes 786440 | tf_op jit(solution)/shard_map/ppermute | solution.py:85
  124.7 7.6 %copy-start.11 = (f32[4,64,127]{2,1,0:T(8,128)S(1)}, f32[4,64,127]{2,1,0:T(8,128)}, u32[]{:S(2)}) copy-start(f32[4,64,127]{2,1,0:T(8,128)} %get-tuple-element.105) | copy-start | bytes 390148
  124.7 7.6 %copy-start.12 = (f32[4,64,1]{2,1,0:T(8,128)S(1)}, f32[4,64,1]{2,1,0:T(8,128)}, u32[]{:S(2)}) copy-start(f32[4,64,1]{2,1,0:T(8,128)} %get-tuple-element.106) | copy-start | bytes 3076
  124.7 7.6 %copy-start.13 = (f32[4,64,1]{2,1,0:T(8,128)S(1)}, f32[4,64,1]{2,1,0:T(8,128)}, u32[]{:S(2)}) copy-start(f32[4,64,1]{2,1,0:T(8,128)} %get-tuple-element.107) | copy-start | bytes 3076
  124.7 7.5 %copy-start.9 = (f32[4,63,128]{2,1,0:T(8,128)S(1)}, f32[4,63,128]{2,1,0:T(8,128)}, u32[]{:S(2)}) copy-start(f32[4,63,128]{2,1,0:T(8,128)} %get-tuple-element.101) | copy-start | bytes 387076
  124.7 7.5 %copy-start.10 = (f32[4,64,127]{2,1,0:T(8,128)S(1)}, f32[4,64,127]{2,1,0:T(8,128)}, u32[]{:S(2)}) copy-start(f32[4,64,127]{2,1,0:T(8,128)} %get-tuple-element.104) | copy-start | bytes 390148
  124.8 7.5 %copy-start.8 = (f32[4,63,128]{2,1,0:T(8,128)S(1)}, f32[4,63,128]{2,1,0:T(8,128)}, u32[]{:S(2)}) copy-start(f32[4,63,128]{2,1,0:T(8,128)} %get-tuple-element.100) | copy-start | bytes 387076
  131.6 0.7 copy-start.17
  131.6 0.7 copy-start.21
  133.8 3.7 %copy-start.2 = (f32[6,64,128]{2,1,0:T(8,128)S(1)}, f32[6,64,128]{2,1,0:T(8,128)}, u32[]{:S(2)}) copy-start(f32[6,64,128]{2,1,0:T(8,128)} %copy-done.1) | copy-start | bytes 589828
  133.8 9.8 %collective-permute-start.10 = (f32[4,64,128]{2,1,0:T(8,128)S(1)}, f32[4,64,128]{2,1,0:T(8,128)S(1)}, u32[]{:S(2)}, u32[]{:S(2)}) collective-permute-start(f32[4,64,128]{2,1,0:T(8,128)S(1)} %pad_maximum_fusion.5), channel_id=1, source_target_pairs={{0,64},{1,65},{2,66},{3,67},{4,68},{5,69},{6,70},{7,71},{8,72},{9,... | collective-permute-start | bytes 393224 | tf_op jit(solution)/shard_map/ppermute | solution.py:85
  137.5 7.1 %collective-permute-start.11 = (f32[2,64,128]{2,1,0:T(8,128)S(1)}, f32[2,64,128]{2,1,0:T(8,128)S(1)}, u32[]{:S(2)}, u32[]{:S(2)}) collective-permute-start(f32[2,64,128]{2,1,0:T(8,128)S(1)} %get-tuple-element.18), channel_id=1, source_target_pairs={{2,64},{3,65},{4,66},{5,67},{6,68},{7,69},{8,70},{9,71},{10,72},{1... | collective-permute-start | bytes 196616 | tf_op jit(solution)/shard_map/ppermute | solution.py:85
  139.4 10.4 %collective-permute-start.9 = (f32[2,64,128]{2,1,0:T(8,128)S(1)}, f32[2,64,128]{2,1,0:T(8,128)S(1)}, u32[]{:S(2)}, u32[]{:S(2)}) collective-permute-start(f32[2,64,128]{2,1,0:T(8,128)S(1)} %get-tuple-element.18), channel_id=1, source_target_pairs={{62,64},{63,65},{0,66},{1,67},{2,68},{3,69},{4,70},{5,71},{6,72},{... | collective-permute-start | bytes 196616 | tf_op jit(solution)/shard_map/ppermute | solution.py:85
  143.6 6.1 %copy-start.19 = (f32[4,64,128]{2,1,0:T(8,128)}, f32[4,64,128]{2,1,0:T(8,128)S(1)}, u32[]{:S(2)}) copy-start(f32[4,64,128]{2,1,0:T(8,128)S(1)} %collective-permute-done.10) | copy-start | bytes 393220
  150.5 10.4 %collective-permute-start.12 = (f32[2,64,128]{2,1,0:T(8,128)S(1)}, f32[2,64,128]{2,1,0:T(8,128)S(1)}, u32[]{:S(2)}, u32[]{:S(2)}) collective-permute-start(f32[2,64,128]{2,1,0:T(8,128)S(1)} %fusion.147), channel_id=1, source_target_pairs={{62,64},{63,65},{0,66},{1,67},{2,68},{3,69},{4,70},{5,71},{6,72},{... | collective-permute-start | bytes 196616 | tf_op jit(solution)/shard_map/ppermute | solution.py:85
  152.5 8.5 %collective-permute-start.13 = (f32[2,64,128]{2,1,0:T(8,128)S(1)}, f32[2,64,128]{2,1,0:T(8,128)S(1)}, u32[]{:S(2)}, u32[]{:S(2)}) collective-permute-start(f32[2,64,128]{2,1,0:T(8,128)S(1)} %fusion.147), channel_id=1, source_target_pairs={{0,64},{1,65},{2,66},{3,67},{4,68},{5,69},{6,70},{7,71},{8,72},{9,... | collective-permute-start | bytes 196616 | tf_op jit(solution)/shard_map/ppermute | solution.py:85
  155.7 7.1 %collective-permute-start.14 = (f32[2,64,128]{2,1,0:T(8,128)S(1)}, f32[2,64,128]{2,1,0:T(8,128)S(1)}, u32[]{:S(2)}, u32[]{:S(2)}) collective-permute-start(f32[2,64,128]{2,1,0:T(8,128)S(1)} %fusion.147), channel_id=1, source_target_pairs={{2,64},{3,65},{4,66},{5,67},{6,68},{7,69},{8,70},{9,71},{10,72},{1... | collective-permute-start | bytes 196616 | tf_op jit(solution)/shard_map/ppermute | solution.py:85
  163.5 13.4 %collective-permute-start.15 = (f32[2,64,128]{2,1,0:T(8,128)S(1)}, f32[2,64,128]{2,1,0:T(8,128)S(1)}, u32[]{:S(2)}, u32[]{:S(2)}) collective-permute-start(f32[2,64,128]{2,1,0:T(8,128)S(1)} %fusion.152), channel_id=1, source_target_pairs={{62,64},{63,65},{0,66},{1,67},{2,68},{3,69},{4,70},{5,71},{6,72},{... | collective-permute-start | bytes 196616 | tf_op jit(solution)/shard_map/ppermute | solution.py:85
  165.4 11.4 %collective-permute-start.16 = (f32[2,64,128]{2,1,0:T(8,128)S(1)}, f32[2,64,128]{2,1,0:T(8,128)S(1)}, u32[]{:S(2)}, u32[]{:S(2)}) collective-permute-start(f32[2,64,128]{2,1,0:T(8,128)S(1)} %fusion.152), channel_id=1, source_target_pairs={{0,64},{1,65},{2,66},{3,67},{4,68},{5,69},{6,70},{7,71},{8,72},{9,... | collective-permute-start | bytes 196616 | tf_op jit(solution)/shard_map/ppermute | solution.py:85
  167.5 9.9 %collective-permute-start.17 = (f32[2,64,128]{2,1,0:T(8,128)S(1)}, f32[2,64,128]{2,1,0:T(8,128)S(1)}, u32[]{:S(2)}, u32[]{:S(2)}) collective-permute-start(f32[2,64,128]{2,1,0:T(8,128)S(1)} %fusion.152), channel_id=1, source_target_pairs={{2,64},{3,65},{4,66},{5,67},{6,68},{7,69},{8,70},{9,71},{10,72},{1... | collective-permute-start | bytes 196616 | tf_op jit(solution)/shard_map/ppermute | solution.py:85
  178.1 0.9 copy-start.20
  178.1 0.9 copy-start.34
  178.1 0.9 copy-start.35
  178.1 0.9 copy-start.36
  178.1 0.9 copy-start.52
  179.0 0.7 copy-start.31
  180.4 0.7 copy-start.40
  182.6 1.0 copy-start.18
  (14 other events, 8.5 us)

commit v9 on v7

--- a/solution.py
+++ b/solution.py
@@ -66,9 +66,9 @@
     count, planes, size_y, size_z = fields.shape
     pairs = fields.reshape(count, planes // 2, 2, size_y, size_z)
     summed = (pairs[:, :, 0] + pairs[:, :, 1]) * 0.5
-    flat = jnp.dot(summed.reshape(-1, size_z), pair_average(size_z), precision=HIGHEST)
+    flat = jnp.dot(summed.reshape(-1, size_z), pair_average(size_z), precision=TRANSFORM)
     field = flat.reshape(count, planes // 2, size_y, size_z // 2)
-    return jnp.einsum("ya,kpyz->kpaz", pair_average(size_y), field, precision=HIGHEST)
+    return jnp.einsum("ya,kpyz->kpaz", pair_average(size_y), field, precision=TRANSFORM)
 
 
 def fetch(value, offset, back):
@@ -155,8 +155,8 @@
 def refine(stacked):
     matrix_y = interp_matrix(stacked.shape[2])
     matrix_z = interp_matrix(stacked.shape[3])
-    both = jnp.einsum("kayc,zc->kayz", stacked, matrix_z, precision=HIGHEST)
-    both = jnp.einsum("Yy,kayz->kaYz", matrix_y, both, precision=HIGHEST)
+    both = jnp.einsum("kayc,zc->kayz", stacked, matrix_z, precision=TRANSFORM)
+    both = jnp.einsum("Yy,kayz->kaYz", matrix_y, both, precision=TRANSFORM)
     planes = stacked.shape[1] - 1
     return spread(both[:, :planes], both[:, 1:], 1)
 

time: 174 us -> 173 us (level)
  no operation moved by 1% of the time
where the time goes in v9:
time: 173 us; the launch traced here: 172 us
  starting transfers between devices  66.8 us (39%)
  waiting for transfers between devices  66 us (38%)
  local copies, waits for them, and re-layouts  15.5 us (9%)
  matrix products  13.7 us (8%)
  other arithmetic  8.12 us (5%)
  between operations  1.78 us (1%)
    all_to_all x4, waiting for transfers between devices, spectral_solve(): lax.all_to_all(field, 'space', split_axis=0, concat_axis=1, tiled=True)  47.2 us
    ppermute x10, starting transfers between devices, fetch(): return lax.ppermute(value, ('tm', 'space'), pairs)  33.3 us
    all_to_all x4, starting transfers between devices, spectral_solve(): lax.all_to_all(field, 'space', split_axis=0, concat_axis=1, tiled=True)  26.8 us
    ppermute x10, waiting for transfers between devices, fetch(): return lax.ppermute(value, ('tm', 'space'), pairs)  15.7 us
    ppermute x5, starting transfers between devices, fetch(): return lax.ppermute(value, 'space', pairs)  6.68 us
    unnamed x45, local copies, waits for them, and re-layouts  5.54 us
    dot_general x2, matrix products, spectral_solve(): jnp.dot(field.reshape(planes * size_y, size_z), basis_z, precision=TRANSF...  3.86 us
  transfers between devices with their start and end apart: 19, of which 11 were waited for; matrix products, arithmetic and copies ran while one was open for 5% of the time, Pallas kernels for 0%

profile of v9, /device:TPU:8, one launch (start us, length us, event | category | flops | bytes accessed | tf_op | source)
XLA Modules:
  0.0 172.0 jit_solution(3012435994479205619)
XLA Ops:
  0.7 1.4 copy.80
  2.6 1.6 fusion.14
  4.3 0.6 fusion.180
  4.8 0.9 copy.86
  5.7 11.9 %all-to-all-start = ((f32[128,2,256]{2,1,0:T(2,128)}), f32[128,2,256]{2,1,0:T(2,128)S(1)}, u32[]{:S(2)}, u32[]{:S(2)}) async-start(f32[128,2,256]{2,1,0:T(2,128)} %copy.86), calls=%async_computation | async-start | bytes 524288 | tf_op jit(solution)/shard_map/all_to_all | solution.py:50
  17.8 12.8 %all-to-all-done = f32[128,2,256]{2,1,0:T(2,128)S(1)} async-done(((f32[128,2,256]{2,1,0:T(2,128)}), f32[128,2,256]{2,1,0:T(2,128)S(1)}, u32[]{:S(2)}, u32[]{:S(2)}) %all-to-all-start) | async-done | bytes 262176 | tf_op jit(solution)/shard_map/all_to_all | solution.py:50
  30.8 0.6 convolution_multiply_fusion.1
  31.4 0.5 fusion.192
  31.9 0.9 copy.90
  32.8 4.9 %all-to-all-start.1 = ((f32[128,2,256]{2,1,0:T(2,128)}), f32[128,2,256]{2,1,0:T(2,128)S(1)}, u32[]{:S(2)}, u32[]{:S(2)}) async-start(f32[128,2,256]{2,1,0:T(2,128)} %copy.90), calls=%async_computation.1 | async-start | bytes 524288 | tf_op jit(solution)/shard_map/all_to_all | solution.py:53
  37.7 1.0 slice.683
  39.1 0.7 slice_bitcast_fusion.1
  39.8 0.8 copy.94
  40.6 10.1 %all-to-all-done.1 = f32[128,2,256]{2,1,0:T(2,128)S(1)} async-done(((f32[128,2,256]{2,1,0:T(2,128)}), f32[128,2,256]{2,1,0:T(2,128)S(1)}, u32[]{:S(2)}, u32[]{:S(2)}) %all-to-all-start.1) | async-done | bytes 262176 | tf_op jit(solution)/shard_map/all_to_all | solution.py:53
  50.9 0.5 fusion.190
  51.5 2.4 %fusion.23 = (f32[256,256]{1,0:T(8,128)S(1)}, f32[256,256]{1,0:T(8,128)S(1)}) fusion(f32[1,2,128,256]{3,2,1,0:T(8,128)S(1)} %copy.95, f32[1,1,2,128,256]{4,3,2,1,0:T(8,128)} %copy.94, f32[1,2,128,256]{3,2,1,0:T(8,128)S(1)} %copy.92, f32[256,256]{1,0:T(8,128)S(1)} %bitcast.217, f32[256]{0:T(256)S(1)} %fusion.248, s32[256]{0:T(256)S(1)} %iota_add_fusion, ...), kind=kOutput, calls=%fused_computation.43 | convolution fusion | flops 102301696 | bytes 1575168 | tf_op jit(solution)/shard_map/dot_general | solution.py:55
  53.9 1.5 fusion.48
  55.4 0.6 fusion.183
  56.0 0.9 copy.97
  56.9 5.1 %all-to-all-start.2 = ((f32[128,2,256]{2,1,0:T(2,128)}), f32[128,2,256]{2,1,0:T(2,128)S(1)}, u32[]{:S(2)}, u32[]{:S(2)}) async-start(f32[128,2,256]{2,1,0:T(2,128)} %copy.97), calls=%async_computation.2 | async-start | bytes 524288 | tf_op jit(solution)/shard_map/all_to_all | solution.py:50
  62.0 12.7 %all-to-all-done.2 = f32[128,2,256]{2,1,0:T(2,128)S(1)} async-done(((f32[128,2,256]{2,1,0:T(2,128)}), f32[128,2,256]{2,1,0:T(2,128)S(1)}, u32[]{:S(2)}, u32[]{:S(2)}) %all-to-all-start.2) | async-done | bytes 262176 | tf_op jit(solution)/shard_map/all_to_all | solution.py:50
  74.9 0.6 convolution_multiply_fusion
  75.5 0.5 fusion.188
  76.0 0.9 copy.101
  76.9 4.9 %all-to-all-start.3 = ((f32[128,2,256]{2,1,0:T(2,128)}), f32[128,2,256]{2,1,0:T(2,128)S(1)}, u32[]{:S(2)}, u32[]{:S(2)}) async-start(f32[128,2,256]{2,1,0:T(2,128)} %copy.101), calls=%async_computation.3 | async-start | bytes 524288 | tf_op jit(solution)/shard_map/all_to_all | solution.py:53
  81.8 0.6 iota_and_fusion
  82.4 0.7 slice_bitcast_fusion.2
  83.3 11.5 %all-to-all-done.3 = f32[128,2,256]{2,1,0:T(2,128)S(1)} async-done(((f32[128,2,256]{2,1,0:T(2,128)}), f32[128,2,256]{2,1,0:T(2,128)S(1)}, u32[]{:S(2)}, u32[]{:S(2)}) %all-to-all-start.3) | async-done | bytes 262176 | tf_op jit(solution)/shard_map/all_to_all | solution.py:53
  95.0 0.5 fusion.186
  95.5 1.4 fusion.117
  97.0 0.7 copy-done.3
  97.8 1.4 fusion.30
  99.6 0.8 fusion.3
  100.7 0.9 collective-permute-start.1
  101.7 4.6 %collective-permute-start.4 = (f32[3,64,128]{2,1,0:T(8,128)S(1)}, f32[3,64,128]{2,1,0:T(8,128)S(1)}, u32[]{:S(2)}, u32[]{:S(2)}) collective-permute-start(f32[3,64,128]{2,1,0:T(8,128)S(1)} %pad_maximum_fusion.4), channel_id=1, source_target_pairs={{2,0},{3,1},{4,2},{5,3},{6,4},{7,5},{8,6},{9,7},{10,8},{11,9},{12,... | collective-permute-start | bytes 294920 | tf_op jit(solution)/shard_map/ppermute | solution.py:78
  106.3 1.1 collective-permute-start.5
  107.6 3.5 %collective-permute-start = (f32[2,128,256]{1,2,0:T(8,128)S(1)}, f32[2,128,256]{1,2,0:T(8,128)S(1)}, u32[]{:S(2)}, u32[]{:S(2)}) collective-permute-start(f32[2,128,256]{1,2,0:T(8,128)S(1)} %copy.103), channel_id=1, source_target_pairs={{0,64},{1,65},{2,66},{3,67},{4,68},{5,69},{6,70},{7,71},{8,72},{9,... | collective-permute-start | bytes 786440 | tf_op jit(solution)/shard_map/ppermute | solution.py:85
  111.1 0.6 constant_dynamic-update-slice_fusion.4
  111.7 0.6 constant_dynamic-update-slice_fusion.3
  112.4 3.1 %collective-permute-done.3 = f32[5,64,128]{2,1,0:T(8,128)S(1)} collective-permute-done((f32[5,64,128]{2,1,0:T(8,128)}, f32[5,64,128]{2,1,0:T(8,128)S(1)}, u32[]{:S(2)}, u32[]{:S(2)}) %collective-permute-start.3) | collective-permute-done | bytes 163872 | tf_op jit(solution)/shard_map/ppermute | solution.py:78
  115.6 1.5 collective-permute-done
  118.1 3.5 %collective-permute-start.7 = (f32[4,64,128]{2,1,0:T(8,128)S(1)}, f32[4,64,128]{2,1,0:T(8,128)S(1)}, u32[]{:S(2)}, u32[]{:S(2)}) collective-permute-start(f32[4,64,128]{2,1,0:T(8,128)S(1)} %pad_maximum_fusion.3), channel_id=1, source_target_pairs={{0,64},{1,65},{2,66},{3,67},{4,68},{5,69},{6,70},{7,71},{8,72},{9,... | collective-permute-start | bytes 393224 | tf_op jit(solution)/shard_map/ppermute | solution.py:85
  121.6 0.6 iota_and_fusion.1
  122.2 4.2 %collective-permute-start.6 = (f32[2,64,128]{2,1,0:T(8,128)S(1)}, f32[2,64,128]{2,1,0:T(8,128)S(1)}, u32[]{:S(2)}, u32[]{:S(2)}) collective-permute-start(f32[2,64,128]{2,1,0:T(8,128)S(1)} %get-tuple-element.20), channel_id=1, source_target_pairs={{62,64},{63,65},{0,66},{1,67},{2,68},{3,69},{4,70},{5,71},{6,72},{... | collective-permute-start | bytes 196616 | tf_op jit(solution)/shard_map/ppermute | solution.py:85
  126.4 4.5 %collective-permute-start.8 = (f32[2,64,128]{2,1,0:T(8,128)S(1)}, f32[2,64,128]{2,1,0:T(8,128)S(1)}, u32[]{:S(2)}, u32[]{:S(2)}) collective-permute-start(f32[2,64,128]{2,1,0:T(8,128)S(1)} %get-tuple-element.20), channel_id=1, source_target_pairs={{2,64},{3,65},{4,66},{5,67},{6,68},{7,69},{8,70},{9,71},{10,72},{1... | collective-permute-start | bytes 196616 | tf_op jit(solution)/shard_map/ppermute | solution.py:85
  130.9 0.5 compare_and_fusion.1
  131.5 1.1 collective-permute-done.6
  132.6 0.9 collective-permute-done.8
  134.2 2.3 %collective-permute-start.10 = (f32[2,64,128]{2,1,0:T(8,128)S(1)}, f32[2,64,128]{2,1,0:T(8,128)S(1)}, u32[]{:S(2)}, u32[]{:S(2)}) collective-permute-start(f32[2,64,128]{2,1,0:T(8,128)S(1)} %fusion.137), channel_id=1, source_target_pairs={{0,64},{1,65},{2,66},{3,67},{4,68},{5,69},{6,70},{7,71},{8,72},{9,... | collective-permute-start | bytes 196616 | tf_op jit(solution)/shard_map/ppermute | solution.py:85
  136.5 7.4 %collective-permute-start.11 = (f32[2,64,128]{2,1,0:T(8,128)S(1)}, f32[2,64,128]{2,1,0:T(8,128)S(1)}, u32[]{:S(2)}, u32[]{:S(2)}) collective-permute-start(f32[2,64,128]{2,1,0:T(8,128)S(1)} %fusion.137), channel_id=1, source_target_pairs={{2,64},{3,65},{4,66},{5,67},{6,68},{7,69},{8,70},{9,71},{10,72},{1... | collective-permute-start | bytes 196616 | tf_op jit(solution)/shard_map/ppermute | solution.py:85
  144.0 2.1 %collective-permute-start.9 = (f32[2,64,128]{2,1,0:T(8,128)S(1)}, f32[2,64,128]{2,1,0:T(8,128)S(1)}, u32[]{:S(2)}, u32[]{:S(2)}) collective-permute-start(f32[2,64,128]{2,1,0:T(8,128)S(1)} %fusion.137), channel_id=1, source_target_pairs={{62,64},{63,65},{0,66},{1,67},{2,68},{3,69},{4,70},{5,71},{6,72},{... | collective-permute-start | bytes 196616 | tf_op jit(solution)/shard_map/ppermute | solution.py:85
  146.1 0.5 compare_and_fusion
  146.7 7.7 %collective-permute-done.9 = f32[2,64,128]{2,1,0:T(8,128)S(1)} collective-permute-done((f32[2,64,128]{2,1,0:T(8,128)S(1)}, f32[2,64,128]{2,1,0:T(8,128)S(1)}, u32[]{:S(2)}, u32[]{:S(2)}) %collective-permute-start.9) | collective-permute-done | bytes 65568 | tf_op jit(solution)/shard_map/ppermute | solution.py:85
  155.0 0.8 fusion.142
  155.7 1.9 %collective-permute-start.12 = (f32[2,64,128]{2,1,0:T(8,128)}, f32[2,64,128]{2,1,0:T(8,128)}, u32[]{:S(2)}, u32[]{:S(2)}) collective-permute-start(f32[2,64,128]{2,1,0:T(8,128)} %fusion.142), channel_id=1, source_target_pairs={{62,64},{63,65},{0,66},{1,67},{2,68},{3,69},{4,70},{5,71},{6,72},{... | collective-permute-start | bytes 196616 | tf_op jit(solution)/shard_map/ppermute | solution.py:85
  157.7 1.9 %collective-permute-start.13 = (f32[2,64,128]{2,1,0:T(8,128)}, f32[2,64,128]{2,1,0:T(8,128)}, u32[]{:S(2)}, u32[]{:S(2)}) collective-permute-start(f32[2,64,128]{2,1,0:T(8,128)} %fusion.142), channel_id=1, source_target_pairs={{0,64},{1,65},{2,66},{3,67},{4,68},{5,69},{6,70},{7,71},{8,72},{9,... | collective-permute-start | bytes 196616 | tf_op jit(solution)/shard_map/ppermute | solution.py:85
  159.6 1.9 %collective-permute-start.14 = (f32[2,64,128]{2,1,0:T(8,128)}, f32[2,64,128]{2,1,0:T(8,128)}, u32[]{:S(2)}, u32[]{:S(2)}) collective-permute-start(f32[2,64,128]{2,1,0:T(8,128)} %fusion.142), channel_id=1, source_target_pairs={{2,64},{3,65},{4,66},{5,67},{6,68},{7,69},{8,70},{9,71},{10,72},{1... | collective-permute-start | bytes 196616 | tf_op jit(solution)/shard_map/ppermute | solution.py:85
  161.6 1.0 copy.128
  162.6 4.0 %collective-permute-done.12 = f32[2,64,128]{2,1,0:T(8,128)} collective-permute-done((f32[2,64,128]{2,1,0:T(8,128)}, f32[2,64,128]{2,1,0:T(8,128)}, u32[]{:S(2)}, u32[]{:S(2)}) %collective-permute-start.12) | collective-permute-done | bytes 65568 | tf_op jit(solution)/shard_map/ppermute | solution.py:85
  166.6 0.5 collective-permute-done.14
  167.1 0.9 maximum_select_fusion.2
  169.2 0.6 fusion.62
  169.8 0.8 convolution_bitcast_fusion
  170.8 1.1 copy.127
  (145 shorter events, 6.2 us)
Async XLA Ops:
  0.6 1.5 copy-start.5
  2.6 1.6 copy-start
  5.7 24.9 %all-to-all-start = ((f32[128,2,256]{2,1,0:T(2,128)}), f32[128,2,256]{2,1,0:T(2,128)S(1)}, u32[]{:S(2)}, u32[]{:S(2)}) async-start(f32[128,2,256]{2,1,0:T(2,128)} %copy.86), calls=%async_computation | async-start | bytes 524288 | tf_op jit(solution)/shard_map/all_to_all | solution.py:50
  32.8 17.9 %all-to-all-start.1 = ((f32[128,2,256]{2,1,0:T(2,128)}), f32[128,2,256]{2,1,0:T(2,128)S(1)}, u32[]{:S(2)}, u32[]{:S(2)}) async-start(f32[128,2,256]{2,1,0:T(2,128)} %copy.90), calls=%async_computation.1 | async-start | bytes 524288 | tf_op jit(solution)/shard_map/all_to_all | solution.py:53
  56.9 17.9 %all-to-all-start.2 = ((f32[128,2,256]{2,1,0:T(2,128)}), f32[128,2,256]{2,1,0:T(2,128)S(1)}, u32[]{:S(2)}, u32[]{:S(2)}) async-start(f32[128,2,256]{2,1,0:T(2,128)} %copy.97), calls=%async_computation.2 | async-start | bytes 524288 | tf_op jit(solution)/shard_map/all_to_all | solution.py:50
  62.0 37.6 %copy-start.11 = (pred[256]{0:T(512)(128)(4,1)}, pred[256]{0:T(512)(128)(4,1)S(1)}, u32[]{:S(2)}) copy-start(pred[256]{0:T(512)(128)(4,1)S(1)} %compare_and_fusion.3) | copy-start | bytes 772
  76.9 17.9 %all-to-all-start.3 = ((f32[128,2,256]{2,1,0:T(2,128)}), f32[128,2,256]{2,1,0:T(2,128)S(1)}, u32[]{:S(2)}, u32[]{:S(2)}) async-start(f32[128,2,256]{2,1,0:T(2,128)} %copy.101), calls=%async_computation.3 | async-start | bytes 524288 | tf_op jit(solution)/shard_map/all_to_all | solution.py:53
  81.8 18.6 %copy-start.7 = (pred[128]{0:T(512)(128)(4,1)}, pred[128]{0:T(512)(128)(4,1)S(1)}, u32[]{:S(2)}) copy-start(pred[128]{0:T(512)(128)(4,1)S(1)} %compare_and_fusion.2) | copy-start | bytes 388
  97.0 0.7 copy-start.3
  97.8 1.5 copy-start.1
  97.8 1.5 copy-start.2
  99.6 7.8 %copy-start.4 = (f32[256,256]{1,0:T(8,128)S(1)}, f32[256,256]{1,0:T(8,128)}, u32[]{:S(2)}) copy-start(f32[256,256]{1,0:T(8,128)} %copy-done.3) | copy-start | bytes 786436
  100.7 10.3 %collective-permute-start.1 = (f32[1,64,128]{2,1,0:T(8,128)S(1)}, f32[1,64,128]{2,1,0:T(8,128)S(1)}, u32[]{:S(2)}, u32[]{:S(2)}) collective-permute-start(f32[1,64,128]{2,1,0:T(8,128)S(1)} %get-tuple-element.75), channel_id=1, source_target_pairs={{62,0},{63,1},{0,2},{1,3},{2,4},{3,5},{4,6},{5,7},{6,8},{7,9},{8,1... | collective-permute-start | bytes 98312 | tf_op jit(solution)/shard_map/ppermute | solution.py:78
  101.6 9.5 %collective-permute-start.2 = (f32[3,64,128]{2,1,0:T(8,128)S(1)}, f32[3,64,128]{2,1,0:T(8,128)S(1)}, u32[]{:S(2)}, u32[]{:S(2)}) collective-permute-start(f32[3,64,128]{2,1,0:T(8,128)S(1)} %pad_maximum_fusion.4), channel_id=1, source_target_pairs={{63,0},{0,1},{1,2},{2,3},{3,4},{4,5},{5,6},{6,7},{7,8},{8,9},{9,10... | collective-permute-start | bytes 294920 | tf_op jit(solution)/shard_map/ppermute | solution.py:78
  101.7 13.8 %collective-permute-start.4 = (f32[3,64,128]{2,1,0:T(8,128)S(1)}, f32[3,64,128]{2,1,0:T(8,128)S(1)}, u32[]{:S(2)}, u32[]{:S(2)}) collective-permute-start(f32[3,64,128]{2,1,0:T(8,128)S(1)} %pad_maximum_fusion.4), channel_id=1, source_target_pairs={{2,0},{3,1},{4,2},{5,3},{6,4},{7,5},{8,6},{9,7},{10,8},{11,9},{12,... | collective-permute-start | bytes 294920 | tf_op jit(solution)/shard_map/ppermute | solution.py:78
  106.3 9.3 %collective-permute-start.5 = (f32[1,64,128]{2,1,0:T(8,128)S(1)}, f32[1,64,128]{2,1,0:T(8,128)S(1)}, u32[]{:S(2)}, u32[]{:S(2)}) collective-permute-start(f32[1,64,128]{2,1,0:T(8,128)S(1)} %get-tuple-element.75), channel_id=1, source_target_pairs={{3,0},{4,1},{5,2},{6,3},{7,4},{8,5},{9,6},{10,7},{11,8},{12,9},{13... | collective-permute-start | bytes 98312 | tf_op jit(solution)/shard_map/ppermute | solution.py:78
  107.4 3.7 %copy-start.6 = (f32[5,64,128]{2,1,0:T(8,128)}, f32[5,64,128]{2,1,0:T(8,128)S(1)}, u32[]{:S(2)}) copy-start(f32[5,64,128]{2,1,0:T(8,128)S(1)} %constant_dynamic-update-slice_fusion.5) | copy-start | bytes 491524
  107.6 9.6 %collective-permute-start = (f32[2,128,256]{1,2,0:T(8,128)S(1)}, f32[2,128,256]{1,2,0:T(8,128)S(1)}, u32[]{:S(2)}, u32[]{:S(2)}) collective-permute-start(f32[2,128,256]{1,2,0:T(8,128)S(1)} %copy.103), channel_id=1, source_target_pairs={{0,64},{1,65},{2,66},{3,67},{4,68},{5,69},{6,70},{7,71},{8,72},{9,... | collective-permute-start | bytes 786440 | tf_op jit(solution)/shard_map/ppermute | solution.py:85
  112.3 3.2 %collective-permute-start.3 = (f32[5,64,128]{2,1,0:T(8,128)}, f32[5,64,128]{2,1,0:T(8,128)S(1)}, u32[]{:S(2)}, u32[]{:S(2)}) collective-permute-start(f32[5,64,128]{2,1,0:T(8,128)} %constant_dynamic-update-slice_fusion.3), channel_id=1, source_target_pairs={{1,0},{2,1},{3,2},{4,3},{5,4},{6,5},{7,6},{8,7},{9,8},{10,9},{11,1... | collective-permute-start | bytes 491528 | tf_op jit(solution)/shard_map/ppermute | solution.py:78
  118.1 13.3 %collective-permute-start.7 = (f32[4,64,128]{2,1,0:T(8,128)S(1)}, f32[4,64,128]{2,1,0:T(8,128)S(1)}, u32[]{:S(2)}, u32[]{:S(2)}) collective-permute-start(f32[4,64,128]{2,1,0:T(8,128)S(1)} %pad_maximum_fusion.3), channel_id=1, source_target_pairs={{0,64},{1,65},{2,66},{3,67},{4,68},{5,69},{6,70},{7,71},{8,72},{9,... | collective-permute-start | bytes 393224 | tf_op jit(solution)/shard_map/ppermute | solution.py:85
  122.2 10.4 %collective-permute-start.6 = (f32[2,64,128]{2,1,0:T(8,128)S(1)}, f32[2,64,128]{2,1,0:T(8,128)S(1)}, u32[]{:S(2)}, u32[]{:S(2)}) collective-permute-start(f32[2,64,128]{2,1,0:T(8,128)S(1)} %get-tuple-element.20), channel_id=1, source_target_pairs={{62,64},{63,65},{0,66},{1,67},{2,68},{3,69},{4,70},{5,71},{6,72},{... | collective-permute-start | bytes 196616 | tf_op jit(solution)/shard_map/ppermute | solution.py:85
  126.4 7.1 %collective-permute-start.8 = (f32[2,64,128]{2,1,0:T(8,128)S(1)}, f32[2,64,128]{2,1,0:T(8,128)S(1)}, u32[]{:S(2)}, u32[]{:S(2)}) collective-permute-start(f32[2,64,128]{2,1,0:T(8,128)S(1)} %get-tuple-element.20), channel_id=1, source_target_pairs={{2,64},{3,65},{4,66},{5,67},{6,68},{7,69},{8,70},{9,71},{10,72},{1... | collective-permute-start | bytes 196616 | tf_op jit(solution)/shard_map/ppermute | solution.py:85
  134.2 12.5 %collective-permute-start.10 = (f32[2,64,128]{2,1,0:T(8,128)S(1)}, f32[2,64,128]{2,1,0:T(8,128)S(1)}, u32[]{:S(2)}, u32[]{:S(2)}) collective-permute-start(f32[2,64,128]{2,1,0:T(8,128)S(1)} %fusion.137), channel_id=1, source_target_pairs={{0,64},{1,65},{2,66},{3,67},{4,68},{5,69},{6,70},{7,71},{8,72},{9,... | collective-permute-start | bytes 196616 | tf_op jit(solution)/shard_map/ppermute | solution.py:85
  136.5 10.1 %collective-permute-start.11 = (f32[2,64,128]{2,1,0:T(8,128)S(1)}, f32[2,64,128]{2,1,0:T(8,128)S(1)}, u32[]{:S(2)}, u32[]{:S(2)}) collective-permute-start(f32[2,64,128]{2,1,0:T(8,128)S(1)} %fusion.137), channel_id=1, source_target_pairs={{2,64},{3,65},{4,66},{5,67},{6,68},{7,69},{8,70},{9,71},{10,72},{1... | collective-permute-start | bytes 196616 | tf_op jit(solution)/shard_map/ppermute | solution.py:85
  144.0 10.4 %collective-permute-start.9 = (f32[2,64,128]{2,1,0:T(8,128)S(1)}, f32[2,64,128]{2,1,0:T(8,128)S(1)}, u32[]{:S(2)}, u32[]{:S(2)}) collective-permute-start(f32[2,64,128]{2,1,0:T(8,128)S(1)} %fusion.137), channel_id=1, source_target_pairs={{62,64},{63,65},{0,66},{1,67},{2,68},{3,69},{4,70},{5,71},{6,72},{... | collective-permute-start | bytes 196616 | tf_op jit(solution)/shard_map/ppermute | solution.py:85
  155.7 10.8 %collective-permute-start.12 = (f32[2,64,128]{2,1,0:T(8,128)}, f32[2,64,128]{2,1,0:T(8,128)}, u32[]{:S(2)}, u32[]{:S(2)}) collective-permute-start(f32[2,64,128]{2,1,0:T(8,128)} %fusion.142), channel_id=1, source_target_pairs={{62,64},{63,65},{0,66},{1,67},{2,68},{3,69},{4,70},{5,71},{6,72},{... | collective-permute-start | bytes 196616 | tf_op jit(solution)/shard_map/ppermute | solution.py:85
  157.7 8.9 %collective-permute-start.13 = (f32[2,64,128]{2,1,0:T(8,128)}, f32[2,64,128]{2,1,0:T(8,128)}, u32[]{:S(2)}, u32[]{:S(2)}) collective-permute-start(f32[2,64,128]{2,1,0:T(8,128)} %fusion.142), channel_id=1, source_target_pairs={{0,64},{1,65},{2,66},{3,67},{4,68},{5,69},{6,70},{7,71},{8,72},{9,... | collective-permute-start | bytes 196616 | tf_op jit(solution)/shard_map/ppermute | solution.py:85
  159.6 7.5 %collective-permute-start.14 = (f32[2,64,128]{2,1,0:T(8,128)}, f32[2,64,128]{2,1,0:T(8,128)}, u32[]{:S(2)}, u32[]{:S(2)}) collective-permute-start(f32[2,64,128]{2,1,0:T(8,128)} %fusion.142), channel_id=1, source_target_pairs={{2,64},{3,65},{4,66},{5,67},{6,68},{7,69},{8,70},{9,71},{10,72},{1... | collective-permute-start | bytes 196616 | tf_op jit(solution)/shard_map/ppermute | solution.py:85
  168.5 0.7 copy-start.9
  168.5 0.7 copy-start.10
  168.5 0.7 copy-start.12
  168.5 0.7 copy-start.16
  168.7 1.0 copy-start.8
  168.7 1.0 copy-start.13
  168.7 1.0 copy-start.14
  168.7 1.0 copy-start.15

commit v10 on v9

--- a/solution.py
+++ b/solution.py
@@ -195,10 +195,12 @@
         solved = spectral_solve(rhs, basis_x, basis_y, basis_z, factor)
         values.append(solved)
         terms.append((solved - rhs) * 4.0)
-    fresh = jnp.stack(values)
-    rates_new = react(fresh) + jnp.stack(terms)
-    sums = [0.5 * (w[0] * rates_new[0] + w[1] * rates_new[1] + w[2] * rates_new[2]) for w in WEIGHTS]
-    coarse = restrict(jnp.stack([values[0], values[1], values[2], sums[0], sums[1]]))
+    rates_new = [react(values[j]) + terms[j] for j in range(3)]
+    known = [0.5 * (w[0] * rates_new[0] + w[1] * rates_new[1]) for w in WEIGHTS]
+    known = restrict(jnp.stack([values[0], values[1], known[0], known[1]]))
+    last = [0.5 * (w[2] * rates_new[2]) for w in WEIGHTS]
+    last = restrict(jnp.stack([values[2], last[0], last[1]]))
+    coarse = [known[0], known[1], last[0], known[2] + last[1], known[3] + last[2]]
     slot = lax.axis_index("tm")
     slices = lax.axis_size("tm")
     local = planes // 2

time: 173 us -> 179 us (1.035)
  local copies, waits for them, and re-layouts: 15.5 us -> 21.5 us
    unnamed x45 -> x46, local copies, waits for them, and re-layouts: 5.54 us -> 10 us
    ppermute x10, waiting for transfers between devices: 15.7 us -> 19.8 us  [fetch(): return lax.ppermute(value, ('tm', 'space'), pairs)]
    ppermute x5, waiting for transfers between devices: 3.16 us -> 0.01 us  [fetch(): return lax.ppermute(value, 'space', pairs)]
  transfers between devices with their start and end apart: 19 -> 19, of which waited for: 11 -> 10; matrix products, arithmetic and copies ran while one was open for 5% -> 5% of each run, Pallas kernels for 0% -> 0%
where the time goes in v10:
time: 179 us
  starting transfers between devices  67.2 us (38%)
  waiting for transfers between devices  67 us (37%)
  local copies, waits for them, and re-layouts  21.5 us (12%)
  matrix products  13.4 us (7%)
  other arithmetic  7.83 us (4%)
    all_to_all x4, waiting for transfers between devices, spectral_solve(): lax.all_to_all(field, 'space', split_axis=0, concat_axis=1, tiled=True)  47.2 us
    ppermute x10, starting transfers between devices, fetch(): return lax.ppermute(value, ('tm', 'space'), pairs)  33.5 us
    all_to_all x4, starting transfers between devices, spectral_solve(): lax.all_to_all(field, 'space', split_axis=0, concat_axis=1, tiled=True)  26.8 us
    ppermute x10, waiting for transfers between devices, fetch(): return lax.ppermute(value, ('tm', 'space'), pairs)  19.8 us
    unnamed x46, local copies, waits for them, and re-layouts  10 us
    ppermute x5, starting transfers between devices, fetch(): return lax.ppermute(value, 'space', pairs)  6.88 us
  transfers between devices with their start and end apart: 19, of which 10 were waited for; matrix products, arithmetic and copies ran while one was open for 5% of the time, Pallas kernels for 0%

profile of v10, /device:TPU:8, one launch (start us, length us, event | category | flops | bytes accessed | tf_op | source)
XLA Modules:
  0.0 178.6 jit_solution(5709486564939396408)
XLA Ops:
  0.7 1.5 copy.84
  2.6 1.6 fusion.17
  4.3 0.6 fusion.181
  4.9 0.9 copy.90
  5.8 11.9 %all-to-all-start = ((f32[128,2,256]{2,1,0:T(2,128)}), f32[128,2,256]{2,1,0:T(2,128)S(1)}, u32[]{:S(2)}, u32[]{:S(2)}) async-start(f32[128,2,256]{2,1,0:T(2,128)} %copy.90), calls=%async_computation | async-start | bytes 524288 | tf_op jit(solution)/shard_map/all_to_all | solution.py:50
  17.8 12.8 %all-to-all-done = f32[128,2,256]{2,1,0:T(2,128)S(1)} async-done(((f32[128,2,256]{2,1,0:T(2,128)}), f32[128,2,256]{2,1,0:T(2,128)S(1)}, u32[]{:S(2)}, u32[]{:S(2)}) %all-to-all-start) | async-done | bytes 262176 | tf_op jit(solution)/shard_map/all_to_all | solution.py:50
  30.8 0.6 convolution_multiply_fusion.1
  31.9 0.9 copy.94
  32.8 4.9 %all-to-all-start.1 = ((f32[128,2,256]{2,1,0:T(2,128)}), f32[128,2,256]{2,1,0:T(2,128)S(1)}, u32[]{:S(2)}, u32[]{:S(2)}) async-start(f32[128,2,256]{2,1,0:T(2,128)} %copy.94), calls=%async_computation.1 | async-start | bytes 524288 | tf_op jit(solution)/shard_map/all_to_all | solution.py:53
  37.7 1.0 slice.681
  38.9 0.8 copy.99
  39.8 0.8 copy.98
  40.6 10.1 %all-to-all-done.1 = f32[128,2,256]{2,1,0:T(2,128)S(1)} async-done(((f32[128,2,256]{2,1,0:T(2,128)}), f32[128,2,256]{2,1,0:T(2,128)S(1)}, u32[]{:S(2)}, u32[]{:S(2)}) %all-to-all-start.1) | async-done | bytes 262176 | tf_op jit(solution)/shard_map/all_to_all | solution.py:53
  52.0 1.5 fusion.26
  53.4 1.5 fusion.45
  54.9 0.6 fusion.184
  55.5 0.9 copy.101
  56.4 5.1 %all-to-all-start.2 = ((f32[128,2,256]{2,1,0:T(2,128)}), f32[128,2,256]{2,1,0:T(2,128)S(1)}, u32[]{:S(2)}, u32[]{:S(2)}) async-start(f32[128,2,256]{2,1,0:T(2,128)} %copy.101), calls=%async_computation.2 | async-start | bytes 524288 | tf_op jit(solution)/shard_map/all_to_all | solution.py:50
  61.5 12.7 %all-to-all-done.2 = f32[128,2,256]{2,1,0:T(2,128)S(1)} async-done(((f32[128,2,256]{2,1,0:T(2,128)}), f32[128,2,256]{2,1,0:T(2,128)S(1)}, u32[]{:S(2)}, u32[]{:S(2)}) %all-to-all-start.2) | async-done | bytes 262176 | tf_op jit(solution)/shard_map/all_to_all | solution.py:50
  74.4 0.6 convolution_multiply_fusion
  75.5 0.9 copy.105
  76.4 4.9 %all-to-all-start.3 = ((f32[128,2,256]{2,1,0:T(2,128)}), f32[128,2,256]{2,1,0:T(2,128)S(1)}, u32[]{:S(2)}, u32[]{:S(2)}) async-start(f32[128,2,256]{2,1,0:T(2,128)} %copy.105), calls=%async_computation.3 | async-start | bytes 524288 | tf_op jit(solution)/shard_map/all_to_all | solution.py:53
  81.4 0.6 iota_and_fusion
  82.0 0.7 slice_bitcast_fusion.2
  82.8 11.5 %all-to-all-done.3 = f32[128,2,256]{2,1,0:T(2,128)S(1)} async-done(((f32[128,2,256]{2,1,0:T(2,128)}), f32[128,2,256]{2,1,0:T(2,128)S(1)}, u32[]{:S(2)}, u32[]{:S(2)}) %all-to-all-start.3) | async-done | bytes 262176 | tf_op jit(solution)/shard_map/all_to_all | solution.py:53
  95.1 1.4 fusion.118
  96.5 0.7 copy-done.1
  97.3 1.4 broadcast_multiply_fusion.1
  98.9 0.8 copy-done.3
  99.8 0.7 fusion.2
  100.7 0.6 constant_dynamic-update-slice_fusion.4
  101.5 0.6 fusion.9
  102.3 0.6 constant_dynamic-update-slice_fusion.3
  102.9 0.6 constant_dynamic-update-slice_fusion.2
  103.5 0.8 collective-permute-start.1
  104.4 4.6 %collective-permute-start.4 = (f32[3,64,128]{2,1,0:T(8,128)S(1)}, f32[3,64,128]{2,1,0:T(8,128)}, u32[]{:S(2)}, u32[]{:S(2)}) collective-permute-start(f32[3,64,128]{2,1,0:T(8,128)S(1)} %pad_maximum_fusion.4), channel_id=1, source_target_pairs={{2,0},{3,1},{4,2},{5,3},{6,4},{7,5},{8,6},{9,7},{10,8},{11,9},{12,... | collective-permute-start | bytes 294920 | tf_op jit(solution)/shard_map/ppermute | solution.py:78
  109.0 1.1 collective-permute-start.5
  110.1 0.6 constant_dynamic-update-slice_fusion.1
  110.8 0.6 constant_dynamic-update-slice_fusion
  111.8 3.5 %collective-permute-start = (f32[2,128,256]{1,2,0:T(8,128)S(1)}, f32[2,128,256]{1,2,0:T(8,128)S(1)}, u32[]{:S(2)}, u32[]{:S(2)}) collective-permute-start(f32[2,128,256]{1,2,0:T(8,128)S(1)} %copy.107), channel_id=1, source_target_pairs={{0,64},{1,65},{2,66},{3,67},{4,68},{5,69},{6,70},{7,71},{8,72},{9,... | collective-permute-start | bytes 786440 | tf_op jit(solution)/shard_map/ppermute | solution.py:85
  115.4 0.8 fusion.386
  116.3 5.9 %collective-permute-done = f32[2,128,256]{1,2,0:T(8,128)S(1)} collective-permute-done((f32[2,128,256]{1,2,0:T(8,128)S(1)}, f32[2,128,256]{1,2,0:T(8,128)S(1)}, u32[]{:S(2)}, u32[]{:S(2)}) %collective-permute-start) | collective-permute-done | bytes 262176 | tf_op jit(solution)/shard_map/ppermute | solution.py:85
  122.1 0.7 copy-done.7
  123.8 3.5 %collective-permute-start.7 = (f32[4,64,128]{2,1,0:T(8,128)S(1)}, f32[4,64,128]{2,1,0:T(8,128)S(1)}, u32[]{:S(2)}, u32[]{:S(2)}) collective-permute-start(f32[4,64,128]{2,1,0:T(8,128)S(1)} %pad_maximum_fusion.3), channel_id=1, source_target_pairs={{0,64},{1,65},{2,66},{3,67},{4,68},{5,69},{6,70},{7,71},{8,72},{9,... | collective-permute-start | bytes 393224 | tf_op jit(solution)/shard_map/ppermute | solution.py:85
  127.3 0.6 iota_and_fusion.1
  127.9 3.8 %collective-permute-start.6 = (f32[2,64,128]{2,1,0:T(8,128)S(1)}, f32[2,64,128]{2,1,0:T(8,128)S(1)}, u32[]{:S(2)}, u32[]{:S(2)}) collective-permute-start(f32[2,64,128]{2,1,0:T(8,128)S(1)} %get-tuple-element.20), channel_id=1, source_target_pairs={{62,64},{63,65},{0,66},{1,67},{2,68},{3,69},{4,70},{5,71},{6,72},{... | collective-permute-start | bytes 196616 | tf_op jit(solution)/shard_map/ppermute | solution.py:85
  131.7 5.2 %collective-permute-start.8 = (f32[2,64,128]{2,1,0:T(8,128)S(1)}, f32[2,64,128]{2,1,0:T(8,128)S(1)}, u32[]{:S(2)}, u32[]{:S(2)}) collective-permute-start(f32[2,64,128]{2,1,0:T(8,128)S(1)} %get-tuple-element.20), channel_id=1, source_target_pairs={{2,64},{3,65},{4,66},{5,67},{6,68},{7,69},{8,70},{9,71},{10,72},{1... | collective-permute-start | bytes 196616 | tf_op jit(solution)/shard_map/ppermute | solution.py:85
  137.4 1.1 collective-permute-done.6
  139.7 2.5 %collective-permute-start.10 = (f32[2,64,128]{2,1,0:T(8,128)S(1)}, f32[2,64,128]{2,1,0:T(8,128)S(1)}, u32[]{:S(2)}, u32[]{:S(2)}) collective-permute-start(f32[2,64,128]{2,1,0:T(8,128)S(1)} %fusion.138), channel_id=1, source_target_pairs={{0,64},{1,65},{2,66},{3,67},{4,68},{5,69},{6,70},{7,71},{8,72},{9,... | collective-permute-start | bytes 196616 | tf_op jit(solution)/shard_map/ppermute | solution.py:85
  142.2 7.4 %collective-permute-start.11 = (f32[2,64,128]{2,1,0:T(8,128)S(1)}, f32[2,64,128]{2,1,0:T(8,128)S(1)}, u32[]{:S(2)}, u32[]{:S(2)}) collective-permute-start(f32[2,64,128]{2,1,0:T(8,128)S(1)} %fusion.138), channel_id=1, source_target_pairs={{2,64},{3,65},{4,66},{5,67},{6,68},{7,69},{8,70},{9,71},{10,72},{1... | collective-permute-start | bytes 196616 | tf_op jit(solution)/shard_map/ppermute | solution.py:85
  149.7 1.9 %collective-permute-start.9 = (f32[2,64,128]{2,1,0:T(8,128)S(1)}, f32[2,64,128]{2,1,0:T(8,128)S(1)}, u32[]{:S(2)}, u32[]{:S(2)}) collective-permute-start(f32[2,64,128]{2,1,0:T(8,128)S(1)} %fusion.138), channel_id=1, source_target_pairs={{62,64},{63,65},{0,66},{1,67},{2,68},{3,69},{4,70},{5,71},{6,72},{... | collective-permute-start | bytes 196616 | tf_op jit(solution)/shard_map/ppermute | solution.py:85
  151.6 0.6 compare_and_fusion
  152.2 7.9 %collective-permute-done.9 = f32[2,64,128]{2,1,0:T(8,128)S(1)} collective-permute-done((f32[2,64,128]{2,1,0:T(8,128)S(1)}, f32[2,64,128]{2,1,0:T(8,128)S(1)}, u32[]{:S(2)}, u32[]{:S(2)}) %collective-permute-start.9) | collective-permute-done | bytes 65568 | tf_op jit(solution)/shard_map/ppermute | solution.py:85
  160.7 0.7 fusion.143
  161.4 1.9 %collective-permute-start.12 = (f32[2,64,128]{2,1,0:T(8,128)}, f32[2,64,128]{2,1,0:T(8,128)S(1)}, u32[]{:S(2)}, u32[]{:S(2)}) collective-permute-start(f32[2,64,128]{2,1,0:T(8,128)} %fusion.143), channel_id=1, source_target_pairs={{62,64},{63,65},{0,66},{1,67},{2,68},{3,69},{4,70},{5,71},{6,72},{... | collective-permute-start | bytes 196616 | tf_op jit(solution)/shard_map/ppermute | solution.py:85
  163.4 1.9 %collective-permute-start.13 = (f32[2,64,128]{2,1,0:T(8,128)}, f32[2,64,128]{2,1,0:T(8,128)S(1)}, u32[]{:S(2)}, u32[]{:S(2)}) collective-permute-start(f32[2,64,128]{2,1,0:T(8,128)} %fusion.143), channel_id=1, source_target_pairs={{0,64},{1,65},{2,66},{3,67},{4,68},{5,69},{6,70},{7,71},{8,72},{9,... | collective-permute-start | bytes 196616 | tf_op jit(solution)/shard_map/ppermute | solution.py:85
  165.3 1.9 %collective-permute-start.14 = (f32[2,64,128]{2,1,0:T(8,128)}, f32[2,64,128]{2,1,0:T(8,128)S(1)}, u32[]{:S(2)}, u32[]{:S(2)}) collective-permute-start(f32[2,64,128]{2,1,0:T(8,128)} %fusion.143), channel_id=1, source_target_pairs={{2,64},{3,65},{4,66},{5,67},{6,68},{7,69},{8,70},{9,71},{10,72},{1... | collective-permute-start | bytes 196616 | tf_op jit(solution)/shard_map/ppermute | solution.py:85
  167.3 1.0 copy.135
  168.3 3.9 %collective-permute-done.12 = f32[2,64,128]{2,1,0:T(8,128)S(1)} collective-permute-done((f32[2,64,128]{2,1,0:T(8,128)}, f32[2,64,128]{2,1,0:T(8,128)S(1)}, u32[]{:S(2)}, u32[]{:S(2)}) %collective-permute-start.12) | collective-permute-done | bytes 65568 | tf_op jit(solution)/shard_map/ppermute | solution.py:85
  174.2 0.6 fusion.60
  174.8 0.7 copy-done.13
  175.5 0.8 convolution_bitcast_fusion
  176.4 0.9 copy-done.8
  177.4 1.1 copy.134
  (150 shorter events, 11.0 us)
Async XLA Ops:
  0.7 1.5 copy-start.4
  2.6 1.6 copy-start
  5.8 24.9 %all-to-all-start = ((f32[128,2,256]{2,1,0:T(2,128)}), f32[128,2,256]{2,1,0:T(2,128)S(1)}, u32[]{:S(2)}, u32[]{:S(2)}) async-start(f32[128,2,256]{2,1,0:T(2,128)} %copy.90), calls=%async_computation | async-start | bytes 524288 | tf_op jit(solution)/shard_map/all_to_all | solution.py:50
  32.8 17.9 %all-to-all-start.1 = ((f32[128,2,256]{2,1,0:T(2,128)}), f32[128,2,256]{2,1,0:T(2,128)S(1)}, u32[]{:S(2)}, u32[]{:S(2)}) async-start(f32[128,2,256]{2,1,0:T(2,128)} %copy.94), calls=%async_computation.1 | async-start | bytes 524288 | tf_op jit(solution)/shard_map/all_to_all | solution.py:53
  50.9 1.0 copy-start.5
  51.0 1.0 copy-start.6
  56.4 17.9 %all-to-all-start.2 = ((f32[128,2,256]{2,1,0:T(2,128)}), f32[128,2,256]{2,1,0:T(2,128)S(1)}, u32[]{:S(2)}, u32[]{:S(2)}) async-start(f32[128,2,256]{2,1,0:T(2,128)} %copy.101), calls=%async_computation.2 | async-start | bytes 524288 | tf_op jit(solution)/shard_map/all_to_all | solution.py:50
  61.5 39.9 %copy-start.16 = (pred[256]{0:T(512)(128)(4,1)}, pred[256]{0:T(512)(128)(4,1)S(1)}, u32[]{:S(2)}) copy-start(pred[256]{0:T(512)(128)(4,1)S(1)} %compare_and_fusion.3) | copy-start | bytes 772
  76.4 17.9 %all-to-all-start.3 = ((f32[128,2,256]{2,1,0:T(2,128)}), f32[128,2,256]{2,1,0:T(2,128)S(1)}, u32[]{:S(2)}, u32[]{:S(2)}) async-start(f32[128,2,256]{2,1,0:T(2,128)} %copy.105), calls=%async_computation.3 | async-start | bytes 524288 | tf_op jit(solution)/shard_map/all_to_all | solution.py:53
  81.4 20.1 %copy-start.9 = (s32[256]{0:T(256)}, s32[256]{0:T(256)S(1)}, u32[]{:S(2)}) copy-start(s32[256]{0:T(256)S(1)} %get-tuple-element.132) | copy-start | bytes 3076
  96.5 0.7 copy-start.1
  98.8 1.0 copy-start.3
  102.9 8.8 %copy-start.2 = (f32[256,256]{1,0:T(8,128)S(1)}, f32[256,256]{1,0:T(8,128)}, u32[]{:S(2)}) copy-start(f32[256,256]{1,0:T(8,128)} %copy-done.1) | copy-start | bytes 786436
  103.5 8.3 %collective-permute-start.1 = (f32[1,64,128]{2,1,0:T(8,128)S(1)}, f32[1,64,128]{2,1,0:T(8,128)S(1)}, u32[]{:S(2)}, u32[]{:S(2)}) collective-permute-start(f32[1,64,128]{2,1,0:T(8,128)S(1)} %get-tuple-element.120), channel_id=1, source_target_pairs={{62,0},{63,1},{0,2},{1,3},{2,4},{3,5},{4,6},{5,7},{6,8},{7,9},{8,1... | collective-permute-start | bytes 98312 | tf_op jit(solution)/shard_map/ppermute | solution.py:78
  104.4 10.9 %collective-permute-start.2 = (f32[3,64,128]{2,1,0:T(8,128)S(1)}, f32[3,64,128]{2,1,0:T(8,128)S(1)}, u32[]{:S(2)}, u32[]{:S(2)}) collective-permute-start(f32[3,64,128]{2,1,0:T(8,128)S(1)} %pad_maximum_fusion.4), channel_id=1, source_target_pairs={{63,0},{0,1},{1,2},{2,3},{3,4},{4,5},{5,6},{6,7},{7,8},{8,9},{9,10... | collective-permute-start | bytes 294920 | tf_op jit(solution)/shard_map/ppermute | solution.py:78
  104.4 10.9 %collective-permute-start.4 = (f32[3,64,128]{2,1,0:T(8,128)S(1)}, f32[3,64,128]{2,1,0:T(8,128)}, u32[]{:S(2)}, u32[]{:S(2)}) collective-permute-start(f32[3,64,128]{2,1,0:T(8,128)S(1)} %pad_maximum_fusion.4), channel_id=1, source_target_pairs={{2,0},{3,1},{4,2},{5,3},{6,4},{7,5},{8,6},{9,7},{10,8},{11,9},{12,... | collective-permute-start | bytes 294920 | tf_op jit(solution)/shard_map/ppermute | solution.py:78
  109.0 7.2 %collective-permute-start.5 = (f32[1,64,128]{2,1,0:T(8,128)S(1)}, f32[1,64,128]{2,1,0:T(8,128)S(1)}, u32[]{:S(2)}, u32[]{:S(2)}) collective-permute-start(f32[1,64,128]{2,1,0:T(8,128)S(1)} %get-tuple-element.120), channel_id=1, source_target_pairs={{3,0},{4,1},{5,2},{6,3},{7,4},{8,5},{9,6},{10,7},{11,8},{12,9},{13... | collective-permute-start | bytes 98312 | tf_op jit(solution)/shard_map/ppermute | solution.py:78
  111.4 4.0 %collective-permute-start.3 = (f32[5,64,128]{2,1,0:T(8,128)}, f32[5,64,128]{2,1,0:T(8,128)S(1)}, u32[]{:S(2)}, u32[]{:S(2)}) collective-permute-start(f32[5,64,128]{2,1,0:T(8,128)} %constant_dynamic-update-slice_fusion), channel_id=1, source_target_pairs={{1,0},{2,1},{3,2},{4,3},{5,4},{6,5},{7,6},{8,7},{9,8},{10,9},{11,1... | collective-permute-start | bytes 491528 | tf_op jit(solution)/shard_map/ppermute | solution.py:78
  111.8 10.3 %collective-permute-start = (f32[2,128,256]{1,2,0:T(8,128)S(1)}, f32[2,128,256]{1,2,0:T(8,128)S(1)}, u32[]{:S(2)}, u32[]{:S(2)}) collective-permute-start(f32[2,128,256]{1,2,0:T(8,128)S(1)} %copy.107), channel_id=1, source_target_pairs={{0,64},{1,65},{2,66},{3,67},{4,68},{5,69},{6,70},{7,71},{8,72},{9,... | collective-permute-start | bytes 786440 | tf_op jit(solution)/shard_map/ppermute | solution.py:85
  122.1 0.7 copy-start.7
  123.8 13.6 %collective-permute-start.7 = (f32[4,64,128]{2,1,0:T(8,128)S(1)}, f32[4,64,128]{2,1,0:T(8,128)S(1)}, u32[]{:S(2)}, u32[]{:S(2)}) collective-permute-start(f32[4,64,128]{2,1,0:T(8,128)S(1)} %pad_maximum_fusion.3), channel_id=1, source_target_pairs={{0,64},{1,65},{2,66},{3,67},{4,68},{5,69},{6,70},{7,71},{8,72},{9,... | collective-permute-start | bytes 393224 | tf_op jit(solution)/shard_map/ppermute | solution.py:85
  127.9 10.6 %collective-permute-start.6 = (f32[2,64,128]{2,1,0:T(8,128)S(1)}, f32[2,64,128]{2,1,0:T(8,128)S(1)}, u32[]{:S(2)}, u32[]{:S(2)}) collective-permute-start(f32[2,64,128]{2,1,0:T(8,128)S(1)} %get-tuple-element.20), channel_id=1, source_target_pairs={{62,64},{63,65},{0,66},{1,67},{2,68},{3,69},{4,70},{5,71},{6,72},{... | collective-permute-start | bytes 196616 | tf_op jit(solution)/shard_map/ppermute | solution.py:85
  131.7 7.3 %collective-permute-start.8 = (f32[2,64,128]{2,1,0:T(8,128)S(1)}, f32[2,64,128]{2,1,0:T(8,128)S(1)}, u32[]{:S(2)}, u32[]{:S(2)}) collective-permute-start(f32[2,64,128]{2,1,0:T(8,128)S(1)} %get-tuple-element.20), channel_id=1, source_target_pairs={{2,64},{3,65},{4,66},{5,67},{6,68},{7,69},{8,70},{9,71},{10,72},{1... | collective-permute-start | bytes 196616 | tf_op jit(solution)/shard_map/ppermute | solution.py:85
  139.7 12.5 %collective-permute-start.10 = (f32[2,64,128]{2,1,0:T(8,128)S(1)}, f32[2,64,128]{2,1,0:T(8,128)S(1)}, u32[]{:S(2)}, u32[]{:S(2)}) collective-permute-start(f32[2,64,128]{2,1,0:T(8,128)S(1)} %fusion.138), channel_id=1, source_target_pairs={{0,64},{1,65},{2,66},{3,67},{4,68},{5,69},{6,70},{7,71},{8,72},{9,... | collective-permute-start | bytes 196616 | tf_op jit(solution)/shard_map/ppermute | solution.py:85
  142.2 10.0 %collective-permute-start.11 = (f32[2,64,128]{2,1,0:T(8,128)S(1)}, f32[2,64,128]{2,1,0:T(8,128)S(1)}, u32[]{:S(2)}, u32[]{:S(2)}) collective-permute-start(f32[2,64,128]{2,1,0:T(8,128)S(1)} %fusion.138), channel_id=1, source_target_pairs={{2,64},{3,65},{4,66},{5,67},{6,68},{7,69},{8,70},{9,71},{10,72},{1... | collective-permute-start | bytes 196616 | tf_op jit(solution)/shard_map/ppermute | solution.py:85
  149.7 10.4 %collective-permute-start.9 = (f32[2,64,128]{2,1,0:T(8,128)S(1)}, f32[2,64,128]{2,1,0:T(8,128)S(1)}, u32[]{:S(2)}, u32[]{:S(2)}) collective-permute-start(f32[2,64,128]{2,1,0:T(8,128)S(1)} %fusion.138), channel_id=1, source_target_pairs={{62,64},{63,65},{0,66},{1,67},{2,68},{3,69},{4,70},{5,71},{6,72},{... | collective-permute-start | bytes 196616 | tf_op jit(solution)/shard_map/ppermute | solution.py:85
  161.4 10.7 %collective-permute-start.12 = (f32[2,64,128]{2,1,0:T(8,128)}, f32[2,64,128]{2,1,0:T(8,128)S(1)}, u32[]{:S(2)}, u32[]{:S(2)}) collective-permute-start(f32[2,64,128]{2,1,0:T(8,128)} %fusion.143), channel_id=1, source_target_pairs={{62,64},{63,65},{0,66},{1,67},{2,68},{3,69},{4,70},{5,71},{6,72},{... | collective-permute-start | bytes 196616 | tf_op jit(solution)/shard_map/ppermute | solution.py:85
  163.4 8.8 %collective-permute-start.13 = (f32[2,64,128]{2,1,0:T(8,128)}, f32[2,64,128]{2,1,0:T(8,128)S(1)}, u32[]{:S(2)}, u32[]{:S(2)}) collective-permute-start(f32[2,64,128]{2,1,0:T(8,128)} %fusion.143), channel_id=1, source_target_pairs={{0,64},{1,65},{2,66},{3,67},{4,68},{5,69},{6,70},{7,71},{8,72},{9,... | collective-permute-start | bytes 196616 | tf_op jit(solution)/shard_map/ppermute | solution.py:85
  165.3 7.4 %collective-permute-start.14 = (f32[2,64,128]{2,1,0:T(8,128)}, f32[2,64,128]{2,1,0:T(8,128)S(1)}, u32[]{:S(2)}, u32[]{:S(2)}) collective-permute-start(f32[2,64,128]{2,1,0:T(8,128)} %fusion.143), channel_id=1, source_target_pairs={{2,64},{3,65},{4,66},{5,67},{6,68},{7,69},{8,70},{9,71},{10,72},{1... | collective-permute-start | bytes 196616 | tf_op jit(solution)/shard_map/ppermute | solution.py:85
  173.4 0.7 copy-start.11
  173.4 0.7 copy-start.12
  173.5 0.6 copy-start.18
  173.5 0.7 copy-start.10
  173.5 0.7 copy-start.17
  174.8 0.7 copy-start.13
  174.8 0.7 copy-start.14
  174.8 0.7 copy-start.15
  176.3 1.0 copy-start.8

commit v11 on v9

--- a/solution.py
+++ b/solution.py
@@ -78,8 +78,8 @@
         return lax.ppermute(value, "space", pairs)
     slices = lax.axis_size("tm")
     pairs = [
-        ((slot - back) * count + (target + offset) % count, slot * count + target)
-        for slot in range(back, slices)
+        (((slot - back) % slices) * count + (target + offset) % count, slot * count + target)
+        for slot in range(slices)
         for target in range(count)
     ]
     return lax.ppermute(value, ("tm", "space"), pairs)

time: 173 us -> 163 us (0.942)
  starting transfers between devices: 66.8 us -> 60.8 us
  waiting for transfers between devices: 66 us -> 62.3 us
    ppermute x10, starting transfers between devices: 33.3 us -> 27.3 us  [fetch(): return lax.ppermute(value, ('tm', 'space'), pairs)]
    ppermute x10, waiting for transfers between devices: 15.7 us -> 12 us  [fetch(): return lax.ppermute(value, ('tm', 'space'), pairs)]
where the time goes in v11:
time: 163 us; the launch traced here: 162 us
  waiting for transfers between devices  62.3 us (38%)
  starting transfers between devices  60.8 us (37%)
  local copies, waits for them, and re-layouts  15.5 us (10%)
  matrix products  13.7 us (8%)
  other arithmetic  8.11 us (5%)
  between operations  1.68 us (1%)
    all_to_all x4, waiting for transfers between devices, spectral_solve(): lax.all_to_all(field, 'space', split_axis=0, concat_axis=1, tiled=True)  47.2 us
    ppermute x10, starting transfers between devices, fetch(): return lax.ppermute(value, ('tm', 'space'), pairs)  27.3 us
    all_to_all x4, starting transfers between devices, spectral_solve(): lax.all_to_all(field, 'space', split_axis=0, concat_axis=1, tiled=True)  26.8 us
    ppermute x10, waiting for transfers between devices, fetch(): return lax.ppermute(value, ('tm', 'space'), pairs)  12 us
    ppermute x5, starting transfers between devices, fetch(): return lax.ppermute(value, 'space', pairs)  6.68 us
    unnamed x45, local copies, waits for them, and re-layouts  5.54 us
    dot_general x2, matrix products, spectral_solve(): jnp.dot(field.reshape(planes * size_y, size_z), basis_z, precision=TRANSF...  3.86 us
  transfers between devices with their start and end apart: 19, of which 11 were waited for; matrix products, arithmetic and copies ran while one was open for 5% of the time, Pallas kernels for 0%

profile of v11, /device:TPU:8, one launch (start us, length us, event | category | flops | bytes accessed | tf_op | source)
XLA Modules:
  0.0 162.1 jit_solution(1606545798222097910)
XLA Ops:
  0.7 1.4 copy.80
  2.2 0.3 copy.82
  2.6 1.6 fusion.14
  4.3 0.6 fusion.180
  4.8 0.9 copy.86
  5.7 11.9 %all-to-all-start = ((f32[128,2,256]{2,1,0:T(2,128)}), f32[128,2,256]{2,1,0:T(2,128)S(1)}, u32[]{:S(2)}, u32[]{:S(2)}) async-start(f32[128,2,256]{2,1,0:T(2,128)} %copy.86), calls=%async_computation | async-start | bytes 524288 | tf_op jit(solution)/shard_map/all_to_all | solution.py:50
  17.8 12.8 %all-to-all-done = f32[128,2,256]{2,1,0:T(2,128)S(1)} async-done(((f32[128,2,256]{2,1,0:T(2,128)}), f32[128,2,256]{2,1,0:T(2,128)S(1)}, u32[]{:S(2)}, u32[]{:S(2)}) %all-to-all-start) | async-done | bytes 262176 | tf_op jit(solution)/shard_map/all_to_all | solution.py:50
  30.8 0.6 convolution_multiply_fusion.1
  31.4 0.5 fusion.192
  31.9 0.9 copy.90
  32.8 4.9 %all-to-all-start.1 = ((f32[128,2,256]{2,1,0:T(2,128)}), f32[128,2,256]{2,1,0:T(2,128)S(1)}, u32[]{:S(2)}, u32[]{:S(2)}) async-start(f32[128,2,256]{2,1,0:T(2,128)} %copy.90), calls=%async_computation.1 | async-start | bytes 524288 | tf_op jit(solution)/shard_map/all_to_all | solution.py:53
  37.7 1.0 slice.683
  39.1 0.7 slice_bitcast_fusion.1
  39.8 0.8 copy.94
  40.6 10.1 %all-to-all-done.1 = f32[128,2,256]{2,1,0:T(2,128)S(1)} async-done(((f32[128,2,256]{2,1,0:T(2,128)}), f32[128,2,256]{2,1,0:T(2,128)S(1)}, u32[]{:S(2)}, u32[]{:S(2)}) %all-to-all-start.1) | async-done | bytes 262176 | tf_op jit(solution)/shard_map/all_to_all | solution.py:53
  50.9 0.5 fusion.190
  51.5 2.4 %fusion.23 = (f32[256,256]{1,0:T(8,128)S(1)}, f32[256,256]{1,0:T(8,128)S(1)}) fusion(f32[1,2,128,256]{3,2,1,0:T(8,128)S(1)} %copy.95, f32[1,1,2,128,256]{4,3,2,1,0:T(8,128)} %copy.94, f32[1,2,128,256]{3,2,1,0:T(8,128)S(1)} %copy.92, f32[256,256]{1,0:T(8,128)S(1)} %bitcast.217, f32[256]{0:T(256)S(1)} %fusion.248, s32[256]{0:T(256)S(1)} %iota_add_fusion, ...), kind=kOutput, calls=%fused_computation.43 | convolution fusion | flops 102301696 | bytes 1575168 | tf_op jit(solution)/shard_map/dot_general | solution.py:55
  53.9 1.5 fusion.48
  55.4 0.6 fusion.183
  56.0 0.9 copy.97
  56.9 5.1 %all-to-all-start.2 = ((f32[128,2,256]{2,1,0:T(2,128)}), f32[128,2,256]{2,1,0:T(2,128)S(1)}, u32[]{:S(2)}, u32[]{:S(2)}) async-start(f32[128,2,256]{2,1,0:T(2,128)} %copy.97), calls=%async_computation.2 | async-start | bytes 524288 | tf_op jit(solution)/shard_map/all_to_all | solution.py:50
  62.0 12.7 %all-to-all-done.2 = f32[128,2,256]{2,1,0:T(2,128)S(1)} async-done(((f32[128,2,256]{2,1,0:T(2,128)}), f32[128,2,256]{2,1,0:T(2,128)S(1)}, u32[]{:S(2)}, u32[]{:S(2)}) %all-to-all-start.2) | async-done | bytes 262176 | tf_op jit(solution)/shard_map/all_to_all | solution.py:50
  74.9 0.6 convolution_multiply_fusion
  75.5 0.5 fusion.188
  76.0 0.9 copy.101
  76.9 4.9 %all-to-all-start.3 = ((f32[128,2,256]{2,1,0:T(2,128)}), f32[128,2,256]{2,1,0:T(2,128)S(1)}, u32[]{:S(2)}, u32[]{:S(2)}) async-start(f32[128,2,256]{2,1,0:T(2,128)} %copy.101), calls=%async_computation.3 | async-start | bytes 524288 | tf_op jit(solution)/shard_map/all_to_all | solution.py:53
  81.8 0.6 iota_and_fusion
  82.4 0.7 slice_bitcast_fusion.2
  83.3 11.5 %all-to-all-done.3 = f32[128,2,256]{2,1,0:T(2,128)S(1)} async-done(((f32[128,2,256]{2,1,0:T(2,128)}), f32[128,2,256]{2,1,0:T(2,128)S(1)}, u32[]{:S(2)}, u32[]{:S(2)}) %all-to-all-start.3) | async-done | bytes 262176 | tf_op jit(solution)/shard_map/all_to_all | solution.py:53
  95.0 0.5 fusion.186
  95.5 1.4 fusion.117
  97.0 0.7 copy-done.3
  97.8 1.4 fusion.30
  99.6 0.8 fusion.3
  100.7 0.9 collective-permute-start.1
  101.7 4.6 %collective-permute-start.4 = (f32[3,64,128]{2,1,0:T(8,128)S(1)}, f32[3,64,128]{2,1,0:T(8,128)S(1)}, u32[]{:S(2)}, u32[]{:S(2)}) collective-permute-start(f32[3,64,128]{2,1,0:T(8,128)S(1)} %pad_maximum_fusion.4), channel_id=1, source_target_pairs={{2,0},{3,1},{4,2},{5,3},{6,4},{7,5},{8,6},{9,7},{10,8},{11,9},{12,... | collective-permute-start | bytes 294920 | tf_op jit(solution)/shard_map/ppermute | solution.py:78
  106.3 1.1 collective-permute-start.5
  107.6 1.6 %collective-permute-start = (f32[2,128,256]{1,2,0:T(8,128)S(1)}, f32[2,128,256]{1,2,0:T(8,128)S(1)}, u32[]{:S(2)}, u32[]{:S(2)}) collective-permute-start(f32[2,128,256]{1,2,0:T(8,128)S(1)} %copy.103), channel_id=1, source_target_pairs={{192,0},{193,1},{194,2},{195,3},{196,4},{197,5},{198,6},{199,7},{2... | collective-permute-start | bytes 786440 | tf_op jit(solution)/shard_map/ppermute | solution.py:85
  109.2 0.6 constant_dynamic-update-slice_fusion.4
  109.9 0.6 constant_dynamic-update-slice_fusion.3
  110.5 3.1 %collective-permute-done.3 = f32[5,64,128]{2,1,0:T(8,128)S(1)} collective-permute-done((f32[5,64,128]{2,1,0:T(8,128)}, f32[5,64,128]{2,1,0:T(8,128)S(1)}, u32[]{:S(2)}, u32[]{:S(2)}) %collective-permute-start.3) | collective-permute-done | bytes 163872 | tf_op jit(solution)/shard_map/ppermute | solution.py:78
  113.8 1.5 collective-permute-done
  116.3 1.9 %collective-permute-start.7 = (f32[4,64,128]{2,1,0:T(8,128)S(1)}, f32[4,64,128]{2,1,0:T(8,128)S(1)}, u32[]{:S(2)}, u32[]{:S(2)}) collective-permute-start(f32[4,64,128]{2,1,0:T(8,128)S(1)} %pad_maximum_fusion.3), channel_id=1, source_target_pairs={{192,0},{193,1},{194,2},{195,3},{196,4},{197,5},{198,6},{199,7},{2... | collective-permute-start | bytes 393224 | tf_op jit(solution)/shard_map/ppermute | solution.py:85
  118.2 0.6 iota_and_fusion.1
  118.8 2.3 %collective-permute-start.6 = (f32[2,64,128]{2,1,0:T(8,128)S(1)}, f32[2,64,128]{2,1,0:T(8,128)S(1)}, u32[]{:S(2)}, u32[]{:S(2)}) collective-permute-start(f32[2,64,128]{2,1,0:T(8,128)S(1)} %get-tuple-element.20), channel_id=1, source_target_pairs={{254,0},{255,1},{192,2},{193,3},{194,4},{195,5},{196,6},{197,7},{1... | collective-permute-start | bytes 196616 | tf_op jit(solution)/shard_map/ppermute | solution.py:85
  121.0 4.7 %collective-permute-start.8 = (f32[2,64,128]{2,1,0:T(8,128)S(1)}, f32[2,64,128]{2,1,0:T(8,128)S(1)}, u32[]{:S(2)}, u32[]{:S(2)}) collective-permute-start(f32[2,64,128]{2,1,0:T(8,128)S(1)} %get-tuple-element.20), channel_id=1, source_target_pairs={{194,0},{195,1},{196,2},{197,3},{198,4},{199,5},{200,6},{201,7},{2... | collective-permute-start | bytes 196616 | tf_op jit(solution)/shard_map/ppermute | solution.py:85
  125.8 0.5 compare_and_fusion.1
  126.3 0.9 collective-permute-done.6
  127.3 0.4 collective-permute-done.8
  128.4 0.9 collective-permute-start.10
  129.4 6.0 %collective-permute-start.11 = (f32[2,64,128]{2,1,0:T(8,128)S(1)}, f32[2,64,128]{2,1,0:T(8,128)S(1)}, u32[]{:S(2)}, u32[]{:S(2)}) collective-permute-start(f32[2,64,128]{2,1,0:T(8,128)S(1)} %fusion.137), channel_id=1, source_target_pairs={{194,0},{195,1},{196,2},{197,3},{198,4},{199,5},{200,6},{201,7},{2... | collective-permute-start | bytes 196616 | tf_op jit(solution)/shard_map/ppermute | solution.py:85
  135.4 0.5 compare_and_fusion
  135.9 1.4 collective-permute-done.11
  137.3 6.6 %collective-permute-done.9 = f32[2,64,128]{2,1,0:T(8,128)S(1)} collective-permute-done((f32[2,64,128]{2,1,0:T(8,128)S(1)}, f32[2,64,128]{2,1,0:T(8,128)S(1)}, u32[]{:S(2)}, u32[]{:S(2)}) %collective-permute-start.9) | collective-permute-done | bytes 65568 | tf_op jit(solution)/shard_map/ppermute | solution.py:85
  144.5 0.8 fusion.142
  145.3 2.8 %collective-permute-start.13 = (f32[2,64,128]{2,1,0:T(8,128)}, f32[2,64,128]{2,1,0:T(8,128)}, u32[]{:S(2)}, u32[]{:S(2)}) collective-permute-start(f32[2,64,128]{2,1,0:T(8,128)} %fusion.142), channel_id=1, source_target_pairs={{192,0},{193,1},{194,2},{195,3},{196,4},{197,5},{198,6},{199,7},{2... | collective-permute-start | bytes 196616 | tf_op jit(solution)/shard_map/ppermute | solution.py:85
  148.1 7.0 %collective-permute-start.14 = (f32[2,64,128]{2,1,0:T(8,128)}, f32[2,64,128]{2,1,0:T(8,128)}, u32[]{:S(2)}, u32[]{:S(2)}) collective-permute-start(f32[2,64,128]{2,1,0:T(8,128)} %fusion.142), channel_id=1, source_target_pairs={{194,0},{195,1},{196,2},{197,3},{198,4},{199,5},{200,6},{201,7},{2... | collective-permute-start | bytes 196616 | tf_op jit(solution)/shard_map/ppermute | solution.py:85
  155.1 1.0 copy.128
  156.1 1.2 collective-permute-done.14
  157.3 0.9 maximum_select_fusion.2
  159.0 0.2 copy-done.9
  159.3 0.6 fusion.62
  159.9 0.8 convolution_bitcast_fusion
  161.0 1.1 copy.127
  (145 shorter events, 5.7 us)
Async XLA Ops:
  0.6 1.5 copy-start.5
  2.6 1.6 %copy-start = (f32[3,2,128,256]{2,3,1,0:T(8,128)}, f32[3,2,128,256]{2,3,1,0:T(8,128)S(1)}, u32[]{:S(2)}) copy-start(f32[3,2,128,256]{2,3,1,0:T(8,128)S(1)} %get-tuple-element.34) | copy-start | bytes 2359300
  5.7 24.9 %all-to-all-start = ((f32[128,2,256]{2,1,0:T(2,128)}), f32[128,2,256]{2,1,0:T(2,128)S(1)}, u32[]{:S(2)}, u32[]{:S(2)}) async-start(f32[128,2,256]{2,1,0:T(2,128)} %copy.86), calls=%async_computation | async-start | bytes 524288 | tf_op jit(solution)/shard_map/all_to_all | solution.py:50
  32.8 17.9 %all-to-all-start.1 = ((f32[128,2,256]{2,1,0:T(2,128)}), f32[128,2,256]{2,1,0:T(2,128)S(1)}, u32[]{:S(2)}, u32[]{:S(2)}) async-start(f32[128,2,256]{2,1,0:T(2,128)} %copy.90), calls=%async_computation.1 | async-start | bytes 524288 | tf_op jit(solution)/shard_map/all_to_all | solution.py:53
  56.9 17.9 %all-to-all-start.2 = ((f32[128,2,256]{2,1,0:T(2,128)}), f32[128,2,256]{2,1,0:T(2,128)S(1)}, u32[]{:S(2)}, u32[]{:S(2)}) async-start(f32[128,2,256]{2,1,0:T(2,128)} %copy.97), calls=%async_computation.2 | async-start | bytes 524288 | tf_op jit(solution)/shard_map/all_to_all | solution.py:50
  62.0 37.6 %copy-start.11 = (pred[256]{0:T(512)(128)(4,1)}, pred[256]{0:T(512)(128)(4,1)S(1)}, u32[]{:S(2)}) copy-start(pred[256]{0:T(512)(128)(4,1)S(1)} %compare_and_fusion.3) | copy-start | bytes 772
  76.9 17.9 %all-to-all-start.3 = ((f32[128,2,256]{2,1,0:T(2,128)}), f32[128,2,256]{2,1,0:T(2,128)S(1)}, u32[]{:S(2)}, u32[]{:S(2)}) async-start(f32[128,2,256]{2,1,0:T(2,128)} %copy.101), calls=%async_computation.3 | async-start | bytes 524288 | tf_op jit(solution)/shard_map/all_to_all | solution.py:53
  81.8 18.6 %copy-start.7 = (pred[128]{0:T(512)(128)(4,1)}, pred[128]{0:T(512)(128)(4,1)S(1)}, u32[]{:S(2)}) copy-start(pred[128]{0:T(512)(128)(4,1)S(1)} %compare_and_fusion.2) | copy-start | bytes 388
  97.0 0.7 copy-start.3
  97.8 1.5 copy-start.1
  97.8 1.5 copy-start.2
  99.6 7.8 %copy-start.4 = (f32[256,256]{1,0:T(8,128)S(1)}, f32[256,256]{1,0:T(8,128)}, u32[]{:S(2)}) copy-start(f32[256,256]{1,0:T(8,128)} %copy-done.3) | copy-start | bytes 786436
  100.7 8.5 %collective-permute-start.1 = (f32[1,64,128]{2,1,0:T(8,128)S(1)}, f32[1,64,128]{2,1,0:T(8,128)S(1)}, u32[]{:S(2)}, u32[]{:S(2)}) collective-permute-start(f32[1,64,128]{2,1,0:T(8,128)S(1)} %get-tuple-element.75), channel_id=1, source_target_pairs={{62,0},{63,1},{0,2},{1,3},{2,4},{3,5},{4,6},{5,7},{6,8},{7,9},{8,1... | collective-permute-start | bytes 98312 | tf_op jit(solution)/shard_map/ppermute | solution.py:78
  101.6 7.6 %collective-permute-start.2 = (f32[3,64,128]{2,1,0:T(8,128)S(1)}, f32[3,64,128]{2,1,0:T(8,128)S(1)}, u32[]{:S(2)}, u32[]{:S(2)}) collective-permute-start(f32[3,64,128]{2,1,0:T(8,128)S(1)} %pad_maximum_fusion.4), channel_id=1, source_target_pairs={{63,0},{0,1},{1,2},{2,3},{3,4},{4,5},{5,6},{6,7},{7,8},{8,9},{9,10... | collective-permute-start | bytes 294920 | tf_op jit(solution)/shard_map/ppermute | solution.py:78
  101.7 12.0 %collective-permute-start.4 = (f32[3,64,128]{2,1,0:T(8,128)S(1)}, f32[3,64,128]{2,1,0:T(8,128)S(1)}, u32[]{:S(2)}, u32[]{:S(2)}) collective-permute-start(f32[3,64,128]{2,1,0:T(8,128)S(1)} %pad_maximum_fusion.4), channel_id=1, source_target_pairs={{2,0},{3,1},{4,2},{5,3},{6,4},{7,5},{8,6},{9,7},{10,8},{11,9},{12,... | collective-permute-start | bytes 294920 | tf_op jit(solution)/shard_map/ppermute | solution.py:78
  106.3 7.4 %collective-permute-start.5 = (f32[1,64,128]{2,1,0:T(8,128)S(1)}, f32[1,64,128]{2,1,0:T(8,128)S(1)}, u32[]{:S(2)}, u32[]{:S(2)}) collective-permute-start(f32[1,64,128]{2,1,0:T(8,128)S(1)} %get-tuple-element.75), channel_id=1, source_target_pairs={{3,0},{4,1},{5,2},{6,3},{7,4},{8,5},{9,6},{10,7},{11,8},{12,9},{13... | collective-permute-start | bytes 98312 | tf_op jit(solution)/shard_map/ppermute | solution.py:78
  107.4 1.8 %copy-start.6 = (f32[5,64,128]{2,1,0:T(8,128)}, f32[5,64,128]{2,1,0:T(8,128)S(1)}, u32[]{:S(2)}) copy-start(f32[5,64,128]{2,1,0:T(8,128)S(1)} %constant_dynamic-update-slice_fusion.5) | copy-start | bytes 491524
  107.6 7.8 %collective-permute-start = (f32[2,128,256]{1,2,0:T(8,128)S(1)}, f32[2,128,256]{1,2,0:T(8,128)S(1)}, u32[]{:S(2)}, u32[]{:S(2)}) collective-permute-start(f32[2,128,256]{1,2,0:T(8,128)S(1)} %copy.103), channel_id=1, source_target_pairs={{192,0},{193,1},{194,2},{195,3},{196,4},{197,5},{198,6},{199,7},{2... | collective-permute-start | bytes 786440 | tf_op jit(solution)/shard_map/ppermute | solution.py:85
  110.5 3.2 %collective-permute-start.3 = (f32[5,64,128]{2,1,0:T(8,128)}, f32[5,64,128]{2,1,0:T(8,128)S(1)}, u32[]{:S(2)}, u32[]{:S(2)}) collective-permute-start(f32[5,64,128]{2,1,0:T(8,128)} %constant_dynamic-update-slice_fusion.3), channel_id=1, source_target_pairs={{1,0},{2,1},{3,2},{4,3},{5,4},{6,5},{7,6},{8,7},{9,8},{10,9},{11,1... | collective-permute-start | bytes 491528 | tf_op jit(solution)/shard_map/ppermute | solution.py:78
  116.3 10.0 %collective-permute-start.7 = (f32[4,64,128]{2,1,0:T(8,128)S(1)}, f32[4,64,128]{2,1,0:T(8,128)S(1)}, u32[]{:S(2)}, u32[]{:S(2)}) collective-permute-start(f32[4,64,128]{2,1,0:T(8,128)S(1)} %pad_maximum_fusion.3), channel_id=1, source_target_pairs={{192,0},{193,1},{194,2},{195,3},{196,4},{197,5},{198,6},{199,7},{2... | collective-permute-start | bytes 393224 | tf_op jit(solution)/shard_map/ppermute | solution.py:85
  118.8 8.5 %collective-permute-start.6 = (f32[2,64,128]{2,1,0:T(8,128)S(1)}, f32[2,64,128]{2,1,0:T(8,128)S(1)}, u32[]{:S(2)}, u32[]{:S(2)}) collective-permute-start(f32[2,64,128]{2,1,0:T(8,128)S(1)} %get-tuple-element.20), channel_id=1, source_target_pairs={{254,0},{255,1},{192,2},{193,3},{194,4},{195,5},{196,6},{197,7},{1... | collective-permute-start | bytes 196616 | tf_op jit(solution)/shard_map/ppermute | solution.py:85
  121.0 6.6 %collective-permute-start.8 = (f32[2,64,128]{2,1,0:T(8,128)S(1)}, f32[2,64,128]{2,1,0:T(8,128)S(1)}, u32[]{:S(2)}, u32[]{:S(2)}) collective-permute-start(f32[2,64,128]{2,1,0:T(8,128)S(1)} %get-tuple-element.20), channel_id=1, source_target_pairs={{194,0},{195,1},{196,2},{197,3},{198,4},{199,5},{200,6},{201,7},{2... | collective-permute-start | bytes 196616 | tf_op jit(solution)/shard_map/ppermute | solution.py:85
  128.4 7.5 %collective-permute-start.10 = (f32[2,64,128]{2,1,0:T(8,128)S(1)}, f32[2,64,128]{2,1,0:T(8,128)S(1)}, u32[]{:S(2)}, u32[]{:S(2)}) collective-permute-start(f32[2,64,128]{2,1,0:T(8,128)S(1)} %fusion.137), channel_id=1, source_target_pairs={{192,0},{193,1},{194,2},{195,3},{196,4},{197,5},{198,6},{199,7},{2... | collective-permute-start | bytes 196616 | tf_op jit(solution)/shard_map/ppermute | solution.py:85
  129.4 7.9 %collective-permute-start.11 = (f32[2,64,128]{2,1,0:T(8,128)S(1)}, f32[2,64,128]{2,1,0:T(8,128)S(1)}, u32[]{:S(2)}, u32[]{:S(2)}) collective-permute-start(f32[2,64,128]{2,1,0:T(8,128)S(1)} %fusion.137), channel_id=1, source_target_pairs={{194,0},{195,1},{196,2},{197,3},{198,4},{199,5},{200,6},{201,7},{2... | collective-permute-start | bytes 196616 | tf_op jit(solution)/shard_map/ppermute | solution.py:85
  135.4 8.5 %collective-permute-start.9 = (f32[2,64,128]{2,1,0:T(8,128)S(1)}, f32[2,64,128]{2,1,0:T(8,128)S(1)}, u32[]{:S(2)}, u32[]{:S(2)}) collective-permute-start(f32[2,64,128]{2,1,0:T(8,128)S(1)} %fusion.137), channel_id=1, source_target_pairs={{254,0},{255,1},{192,2},{193,3},{194,4},{195,5},{196,6},{197,7},{1... | collective-permute-start | bytes 196616 | tf_op jit(solution)/shard_map/ppermute | solution.py:85
  145.3 10.8 %collective-permute-start.12 = (f32[2,64,128]{2,1,0:T(8,128)}, f32[2,64,128]{2,1,0:T(8,128)}, u32[]{:S(2)}, u32[]{:S(2)}) collective-permute-start(f32[2,64,128]{2,1,0:T(8,128)} %fusion.142), channel_id=1, source_target_pairs={{254,0},{255,1},{192,2},{193,3},{194,4},{195,5},{196,6},{197,7},{1... | collective-permute-start | bytes 196616 | tf_op jit(solution)/shard_map/ppermute | solution.py:85
  145.3 10.8 %collective-permute-start.13 = (f32[2,64,128]{2,1,0:T(8,128)}, f32[2,64,128]{2,1,0:T(8,128)}, u32[]{:S(2)}, u32[]{:S(2)}) collective-permute-start(f32[2,64,128]{2,1,0:T(8,128)} %fusion.142), channel_id=1, source_target_pairs={{192,0},{193,1},{194,2},{195,3},{196,4},{197,5},{198,6},{199,7},{2... | collective-permute-start | bytes 196616 | tf_op jit(solution)/shard_map/ppermute | solution.py:85
  148.1 9.2 %collective-permute-start.14 = (f32[2,64,128]{2,1,0:T(8,128)}, f32[2,64,128]{2,1,0:T(8,128)}, u32[]{:S(2)}, u32[]{:S(2)}) collective-permute-start(f32[2,64,128]{2,1,0:T(8,128)} %fusion.142), channel_id=1, source_target_pairs={{194,0},{195,1},{196,2},{197,3},{198,4},{199,5},{200,6},{201,7},{2... | collective-permute-start | bytes 196616 | tf_op jit(solution)/shard_map/ppermute | solution.py:85
  158.6 0.7 copy-start.9
  158.6 0.7 copy-start.10
  158.6 0.7 copy-start.12
  158.6 0.7 copy-start.16
  158.8 1.0 copy-start.8
  158.9 1.0 copy-start.13
  158.9 1.0 copy-start.14
  158.9 1.0 copy-start.15

commit v12 on v11

--- a/solution.py
+++ b/solution.py
@@ -206,8 +206,6 @@
         [(coarse[0], (0, 0), (2, 3)), (coarse[1], (0, 0), (1, 2)), (coarse[3], (0, 0), (1, 2)),
          (coarse[4], (0, 0), (0, 1)), (coarse[2], (0, 0), (0, 1))]
     )
-    previous_two = fetch(values[2], 0, 1)
-    previous_two, wide = lax.optimization_barrier((previous_two, wide))
     start_c = wide[0]
     rates_c = (coarse_rate(start_c), coarse_rate(wide[1]))
     sums_c = (wide[2], wide[3])
@@ -222,6 +220,8 @@
             items.append((coarse_two, (0, 1), (0, 1)))
         received = gather_bands(items, back=1)
         if previous_coarse_two is None:
+            previous_two = fetch(values[2], 0, 1)
+            previous_two, received = lax.optimization_barrier((previous_two, received))
             previous_coarse_two = received[1]
         start = jnp.where(slot == 0, start_c, received[0])
     first, second = coarse_sweep(start, rates_c, sums_c)

time: 163 us -> 160 us (0.982)
  starting transfers between devices: 60.8 us -> 57.6 us
    ppermute x10, starting transfers between devices: 27.3 us -> 24 us  [fetch(): return lax.ppermute(value, ('tm', 'space'), pairs)]
    unnamed x45 -> x46, local copies, waits for them, and re-layouts: 5.54 us -> 4.99 us
  transfers between devices with their start and end apart: 19 -> 19, of which waited for: 11 -> 12; matrix products, arithmetic and copies ran while one was open for 5% -> 5% of each run, Pallas kernels for 0% -> 0%
where the time goes in v12:
time: 160 us; the launch traced here: 159 us
  waiting for transfers between devices  63.1 us (39%)
  starting transfers between devices  57.6 us (36%)
  local copies, waits for them, and re-layouts  15 us (9%)
  matrix products  13.7 us (9%)
  other arithmetic  8.24 us (5%)
  between operations  1.66 us (1%)
    all_to_all x4, waiting for transfers between devices, spectral_solve(): lax.all_to_all(field, 'space', split_axis=0, concat_axis=1, tiled=True)  46.6 us
    all_to_all x4, starting transfers between devices, spectral_solve(): lax.all_to_all(field, 'space', split_axis=0, concat_axis=1, tiled=True)  26.9 us
    ppermute x10, starting transfers between devices, fetch(): return lax.ppermute(value, ('tm', 'space'), pairs)  24 us
    ppermute x10, waiting for transfers between devices, fetch(): return lax.ppermute(value, ('tm', 'space'), pairs)  12 us
    ppermute x5, starting transfers between devices, fetch(): return lax.ppermute(value, 'space', pairs)  6.76 us
    unnamed x46, local copies, waits for them, and re-layouts  4.99 us
    ppermute x5, waiting for transfers between devices, fetch(): return lax.ppermute(value, 'space', pairs)  4.5 us
    dot_general x2, matrix products, spectral_solve(): jnp.dot(field.reshape(planes * size_y, size_z), basis_z, precision=TRANSF...  3.85 us
  transfers between devices with their start and end apart: 19, of which 12 were waited for; matrix products, arithmetic and copies ran while one was open for 5% of the time, Pallas kernels for 0%

profile of v12, /device:TPU:8, one launch (start us, length us, event | category | flops | bytes accessed | tf_op | source)
XLA Modules:
  0.0 159.4 jit_solution(6874471782073992205)
XLA Ops:
  0.7 1.4 copy.80
  2.2 0.3 copy.82
  2.6 1.6 %fusion.14 = f32[2,128,256]{2,1,0:T(8,128)S(1)} fusion(f32[3,2,128,256]{2,3,1,0:T(8,128)S(1)} %get-tuple-element.28, f32[1,3,2,128,256]{3,4,2,1,0:T(8,128)S(1)} %copy.82, f32[1,3,2,128,256]{3,4,2,1,0:T(8,128)S(1)} %copy.80, f32[256]{0:T(256)S(1)} %fusion.256, s32[256]{0:T(256)S(1)} %iota_add_fusion, pred[256]{0:T(512)(128)(4,1)S(1)} %iota_compare_fusion.6, ...), kind=kOutput, calls=%fused_computation.35 | convolution fusion | flops 102760448 | bytes 1837568 | tf_op jit(solution)/shard_map/dot_general | solution.py:47
  4.3 0.6 fusion.188
  4.8 0.9 copy.86
  5.7 11.9 %all-to-all-start = ((f32[128,2,256]{2,1,0:T(2,128)}), f32[128,2,256]{2,1,0:T(2,128)S(1)}, u32[]{:S(2)}, u32[]{:S(2)}) async-start(f32[128,2,256]{2,1,0:T(2,128)} %copy.86), calls=%async_computation | async-start | bytes 524288 | tf_op jit(solution)/shard_map/all_to_all | solution.py:50
  17.8 12.8 %all-to-all-done = f32[128,2,256]{2,1,0:T(2,128)S(1)} async-done(((f32[128,2,256]{2,1,0:T(2,128)}), f32[128,2,256]{2,1,0:T(2,128)S(1)}, u32[]{:S(2)}, u32[]{:S(2)}) %all-to-all-start) | async-done | bytes 262176 | tf_op jit(solution)/shard_map/all_to_all | solution.py:50
  30.8 0.6 convolution_multiply_fusion.1
  31.4 0.5 fusion.200
  31.9 0.9 copy.90
  32.8 4.9 %all-to-all-start.1 = ((f32[128,2,256]{2,1,0:T(2,128)}), f32[128,2,256]{2,1,0:T(2,128)S(1)}, u32[]{:S(2)}, u32[]{:S(2)}) async-start(f32[128,2,256]{2,1,0:T(2,128)} %copy.90), calls=%async_computation.1 | async-start | bytes 524288 | tf_op jit(solution)/shard_map/all_to_all | solution.py:53
  37.7 1.0 slice.656
  39.1 0.7 slice_bitcast_fusion.1
  39.8 0.8 copy.94
  40.6 10.1 %all-to-all-done.1 = f32[128,2,256]{2,1,0:T(2,128)S(1)} async-done(((f32[128,2,256]{2,1,0:T(2,128)}), f32[128,2,256]{2,1,0:T(2,128)S(1)}, u32[]{:S(2)}, u32[]{:S(2)}) %all-to-all-start.1) | async-done | bytes 262176 | tf_op jit(solution)/shard_map/all_to_all | solution.py:53
  50.9 0.5 fusion.198
  51.5 2.4 %fusion.23 = (f32[256,256]{1,0:T(8,128)S(1)}, f32[256,256]{1,0:T(8,128)S(1)}) fusion(f32[1,2,128,256]{3,2,1,0:T(8,128)S(1)} %copy.95, f32[1,1,2,128,256]{4,3,2,1,0:T(8,128)} %copy.94, f32[1,2,128,256]{3,2,1,0:T(8,128)S(1)} %copy.92, f32[256,256]{1,0:T(8,128)S(1)} %bitcast.217, f32[256]{0:T(256)S(1)} %fusion.256, s32[256]{0:T(256)S(1)} %iota_add_fusion, ...), kind=kOutput, calls=%fused_computation.43 | convolution fusion | flops 102301696 | bytes 1575168 | tf_op jit(solution)/shard_map/dot_general | solution.py:55
  53.9 1.5 fusion.48
  55.4 0.6 fusion.191
  56.0 0.9 copy.97
  56.9 5.1 %all-to-all-start.2 = ((f32[128,2,256]{2,1,0:T(2,128)}), f32[128,2,256]{2,1,0:T(2,128)S(1)}, u32[]{:S(2)}, u32[]{:S(2)}) async-start(f32[128,2,256]{2,1,0:T(2,128)} %copy.97), calls=%async_computation.2 | async-start | bytes 524288 | tf_op jit(solution)/shard_map/all_to_all | solution.py:50
  62.0 0.5 compare_and_fusion
  62.5 12.2 %all-to-all-done.2 = f32[128,2,256]{2,1,0:T(2,128)S(1)} async-done(((f32[128,2,256]{2,1,0:T(2,128)}), f32[128,2,256]{2,1,0:T(2,128)S(1)}, u32[]{:S(2)}, u32[]{:S(2)}) %all-to-all-start.2) | async-done | bytes 262176 | tf_op jit(solution)/shard_map/all_to_all | solution.py:50
  74.9 0.6 convolution_multiply_fusion
  75.5 0.5 fusion.196
  76.0 0.9 copy.101
  76.9 4.9 %all-to-all-start.3 = ((f32[128,2,256]{2,1,0:T(2,128)}), f32[128,2,256]{2,1,0:T(2,128)S(1)}, u32[]{:S(2)}, u32[]{:S(2)}) async-start(f32[128,2,256]{2,1,0:T(2,128)} %copy.101), calls=%async_computation.3 | async-start | bytes 524288 | tf_op jit(solution)/shard_map/all_to_all | solution.py:53
  81.9 0.6 iota_and_fusion
  82.5 0.7 slice_bitcast_fusion.2
  83.3 11.5 %all-to-all-done.3 = f32[128,2,256]{2,1,0:T(2,128)S(1)} async-done(((f32[128,2,256]{2,1,0:T(2,128)}), f32[128,2,256]{2,1,0:T(2,128)S(1)}, u32[]{:S(2)}, u32[]{:S(2)}) %all-to-all-start.3) | async-done | bytes 262176 | tf_op jit(solution)/shard_map/all_to_all | solution.py:53
  95.1 0.5 fusion.194
  95.6 1.4 fusion.118
  97.0 0.7 copy-done.2
  97.9 1.4 fusion.30
  99.6 0.8 fusion.3
  100.5 0.2 fusion.225
  100.7 0.9 collective-permute-start.5
  101.7 4.6 %collective-permute-start.3 = (f32[3,64,128]{2,1,0:T(8,128)S(1)}, f32[3,64,128]{2,1,0:T(8,128)S(1)}, u32[]{:S(2)}, u32[]{:S(2)}) collective-permute-start(f32[3,64,128]{2,1,0:T(8,128)S(1)} %pad_maximum_fusion.6), channel_id=1, source_target_pairs={{2,0},{3,1},{4,2},{5,3},{6,4},{7,5},{8,6},{9,7},{10,8},{11,9},{12,... | collective-permute-start | bytes 294920 | tf_op jit(solution)/shard_map/ppermute | solution.py:78
  106.3 1.1 collective-permute-start.4
  107.4 0.6 collective-permute-done.5
  108.1 1.0 collective-permute-done.1
  109.3 2.8 %collective-permute-done.2 = f32[5,64,128]{2,1,0:T(8,128)S(1)} collective-permute-done((f32[5,64,128]{2,1,0:T(8,128)S(1)}, f32[5,64,128]{2,1,0:T(8,128)S(1)}, u32[]{:S(2)}, u32[]{:S(2)}) %collective-permute-start.2) | collective-permute-done | bytes 163872 | tf_op jit(solution)/shard_map/ppermute | solution.py:78
  113.2 0.7 pad_maximum_fusion.5
  113.8 1.6 collective-permute-start.7
  115.4 0.6 iota_and_fusion.1
  116.1 1.6 collective-permute-start
  117.7 6.0 %collective-permute-start.8 = (f32[2,64,128]{2,1,0:T(8,128)S(1)}, f32[2,64,128]{2,1,0:T(8,128)S(1)}, u32[]{:S(2)}, u32[]{:S(2)}) collective-permute-start(f32[2,64,128]{2,1,0:T(8,128)S(1)} %get-tuple-element.14), channel_id=1, source_target_pairs={{194,0},{195,1},{196,2},{197,3},{198,4},{199,5},{200,6},{201,7},{2... | collective-permute-start | bytes 196616 | tf_op jit(solution)/shard_map/ppermute | solution.py:85
  123.7 0.9 fusion.358
  124.6 1.7 %collective-permute-done.6 = f32[2,64,128]{2,1,0:T(8,128)S(1)} collective-permute-done((f32[2,64,128]{2,1,0:T(8,128)S(1)}, f32[2,64,128]{2,1,0:T(8,128)S(1)}, u32[]{:S(2)}, u32[]{:S(2)}) %collective-permute-start.6) | collective-permute-done | bytes 65568 | tf_op jit(solution)/shard_map/ppermute | solution.py:85
  126.3 1.5 collective-permute-done
  128.6 1.7 %collective-permute-start.10 = (f32[2,64,128]{2,1,0:T(8,128)S(1)}, f32[2,64,128]{2,1,0:T(8,128)S(1)}, u32[]{:S(2)}, u32[]{:S(2)}) collective-permute-start(f32[2,64,128]{2,1,0:T(8,128)S(1)} %fusion.138), channel_id=1, source_target_pairs={{192,0},{193,1},{194,2},{195,3},{196,4},{197,5},{198,6},{199,7},{2... | collective-permute-start | bytes 196616 | tf_op jit(solution)/shard_map/ppermute | solution.py:85
  130.2 4.5 %collective-permute-start.11 = (f32[2,64,128]{2,1,0:T(8,128)S(1)}, f32[2,64,128]{2,1,0:T(8,128)S(1)}, u32[]{:S(2)}, u32[]{:S(2)}) collective-permute-start(f32[2,64,128]{2,1,0:T(8,128)S(1)} %fusion.138), channel_id=1, source_target_pairs={{194,0},{195,1},{196,2},{197,3},{198,4},{199,5},{200,6},{201,7},{2... | collective-permute-start | bytes 196616 | tf_op jit(solution)/shard_map/ppermute | solution.py:85
  134.8 0.5 compare_and_fusion.1
  135.3 1.4 collective-permute-done.11
  136.7 6.6 %collective-permute-done.9 = f32[2,64,128]{2,1,0:T(8,128)S(1)} collective-permute-done((f32[2,64,128]{2,1,0:T(8,128)S(1)}, f32[2,64,128]{2,1,0:T(8,128)S(1)}, u32[]{:S(2)}, u32[]{:S(2)}) %collective-permute-start.9) | collective-permute-done | bytes 65568 | tf_op jit(solution)/shard_map/ppermute | solution.py:85
  144.1 2.4 %collective-permute-start.13 = (f32[2,64,128]{2,1,0:T(8,128)S(1)}, f32[2,64,128]{2,1,0:T(8,128)}, u32[]{:S(2)}, u32[]{:S(2)}) collective-permute-start(f32[2,64,128]{2,1,0:T(8,128)S(1)} %fusion.143), channel_id=1, source_target_pairs={{192,0},{193,1},{194,2},{195,3},{196,4},{197,5},{198,6},{199,7},{2... | collective-permute-start | bytes 196616 | tf_op jit(solution)/shard_map/ppermute | solution.py:85
  146.6 6.1 %collective-permute-start.14 = (f32[2,64,128]{2,1,0:T(8,128)S(1)}, f32[2,64,128]{2,1,0:T(8,128)}, u32[]{:S(2)}, u32[]{:S(2)}) collective-permute-start(f32[2,64,128]{2,1,0:T(8,128)S(1)} %fusion.143), channel_id=1, source_target_pairs={{194,0},{195,1},{196,2},{197,3},{198,4},{199,5},{200,6},{201,7},{2... | collective-permute-start | bytes 196616 | tf_op jit(solution)/shard_map/ppermute | solution.py:85
  152.7 1.0 copy.128
  153.7 0.9 collective-permute-done.14
  154.6 0.9 maximum_select_fusion.1
  156.3 0.2 copy-done.8
  156.6 0.6 fusion.62
  157.2 0.8 convolution_bitcast_fusion
  158.3 1.1 copy.127
  (140 shorter events, 5.7 us)
Async XLA Ops:
  0.6 1.5 copy-start.5
  2.6 1.6 %copy-start = (f32[3,2,128,256]{2,3,1,0:T(8,128)}, f32[3,2,128,256]{2,3,1,0:T(8,128)S(1)}, u32[]{:S(2)}) copy-start(f32[3,2,128,256]{2,3,1,0:T(8,128)S(1)} %get-tuple-element.28) | copy-start | bytes 2359300
  5.7 24.9 %all-to-all-start = ((f32[128,2,256]{2,1,0:T(2,128)}), f32[128,2,256]{2,1,0:T(2,128)S(1)}, u32[]{:S(2)}, u32[]{:S(2)}) async-start(f32[128,2,256]{2,1,0:T(2,128)} %copy.86), calls=%async_computation | async-start | bytes 524288 | tf_op jit(solution)/shard_map/all_to_all | solution.py:50
  32.8 17.9 %all-to-all-start.1 = ((f32[128,2,256]{2,1,0:T(2,128)}), f32[128,2,256]{2,1,0:T(2,128)S(1)}, u32[]{:S(2)}, u32[]{:S(2)}) async-start(f32[128,2,256]{2,1,0:T(2,128)} %copy.90), calls=%async_computation.1 | async-start | bytes 524288 | tf_op jit(solution)/shard_map/all_to_all | solution.py:53
  56.9 17.9 %all-to-all-start.2 = ((f32[128,2,256]{2,1,0:T(2,128)}), f32[128,2,256]{2,1,0:T(2,128)S(1)}, u32[]{:S(2)}, u32[]{:S(2)}) async-start(f32[128,2,256]{2,1,0:T(2,128)} %copy.97), calls=%async_computation.2 | async-start | bytes 524288 | tf_op jit(solution)/shard_map/all_to_all | solution.py:50
  62.5 37.9 %copy-start.6 = (pred[128]{0:T(512)(128)(4,1)}, pred[128]{0:T(512)(128)(4,1)S(1)}, u32[]{:S(2)}) copy-start(pred[128]{0:T(512)(128)(4,1)S(1)} %get-tuple-element.134) | copy-start | bytes 388
  76.9 17.9 %all-to-all-start.3 = ((f32[128,2,256]{2,1,0:T(2,128)}), f32[128,2,256]{2,1,0:T(2,128)S(1)}, u32[]{:S(2)}, u32[]{:S(2)}) async-start(f32[128,2,256]{2,1,0:T(2,128)} %copy.101), calls=%async_computation.3 | async-start | bytes 524288 | tf_op jit(solution)/shard_map/all_to_all | solution.py:53
  81.9 17.8 %copy-start.10 = (pred[256]{0:T(512)(128)(4,1)}, pred[256]{0:T(512)(128)(4,1)S(1)}, u32[]{:S(2)}) copy-start(pred[256]{0:T(512)(128)(4,1)S(1)} %compare_and_fusion.3) | copy-start | bytes 772
  97.0 0.7 copy-start.2
  97.8 1.5 copy-start.1
  97.9 1.5 copy-start.4
  100.7 7.3 %collective-permute-start.5 = (f32[1,64,128]{2,1,0:T(8,128)S(1)}, f32[1,64,128]{2,1,0:T(8,128)S(1)}, u32[]{:S(2)}, u32[]{:S(2)}) collective-permute-start(f32[1,64,128]{2,1,0:T(8,128)S(1)} %get-tuple-element.64), channel_id=1, source_target_pairs={{62,0},{63,1},{0,2},{1,3},{2,4},{3,5},{4,6},{5,7},{6,8},{7,9},{8,1... | collective-permute-start | bytes 98312 | tf_op jit(solution)/shard_map/ppermute | solution.py:78
  101.7 7.4 %collective-permute-start.1 = (f32[3,64,128]{2,1,0:T(8,128)S(1)}, f32[3,64,128]{2,1,0:T(8,128)S(1)}, u32[]{:S(2)}, u32[]{:S(2)}) collective-permute-start(f32[3,64,128]{2,1,0:T(8,128)S(1)} %pad_maximum_fusion.6), channel_id=1, source_target_pairs={{63,0},{0,1},{1,2},{2,3},{3,4},{4,5},{5,6},{6,7},{7,8},{8,9},{9,10... | collective-permute-start | bytes 294920 | tf_op jit(solution)/shard_map/ppermute | solution.py:78
  101.7 10.6 %collective-permute-start.3 = (f32[3,64,128]{2,1,0:T(8,128)S(1)}, f32[3,64,128]{2,1,0:T(8,128)S(1)}, u32[]{:S(2)}, u32[]{:S(2)}) collective-permute-start(f32[3,64,128]{2,1,0:T(8,128)S(1)} %pad_maximum_fusion.6), channel_id=1, source_target_pairs={{2,0},{3,1},{4,2},{5,3},{6,4},{7,5},{8,6},{9,7},{10,8},{11,9},{12,... | collective-permute-start | bytes 294920 | tf_op jit(solution)/shard_map/ppermute | solution.py:78
  106.3 6.3 %collective-permute-start.4 = (f32[1,64,128]{2,1,0:T(8,128)S(1)}, f32[1,64,128]{2,1,0:T(8,128)S(1)}, u32[]{:S(2)}, u32[]{:S(2)}) collective-permute-start(f32[1,64,128]{2,1,0:T(8,128)S(1)} %get-tuple-element.64), channel_id=1, source_target_pairs={{3,0},{4,1},{5,2},{6,3},{7,4},{8,5},{9,6},{10,7},{11,8},{12,9},{13... | collective-permute-start | bytes 98312 | tf_op jit(solution)/shard_map/ppermute | solution.py:78
  109.2 2.9 %collective-permute-start.2 = (f32[5,64,128]{2,1,0:T(8,128)S(1)}, f32[5,64,128]{2,1,0:T(8,128)S(1)}, u32[]{:S(2)}, u32[]{:S(2)}) collective-permute-start(f32[5,64,128]{2,1,0:T(8,128)S(1)} %constant_dynamic-update-slice_fusion.3), channel_id=1, source_target_pairs={{1,0},{2,1},{3,2},{4,3},{5,4},{6,5},{7,6},{8,7},{9,8},{10,9},{11,1... | collective-permute-start | bytes 491528 | tf_op jit(solution)/shard_map/ppermute | solution.py:78
  112.8 3.2 %copy-start.3 = (f32[256,256]{1,0:T(8,128)S(1)}, f32[256,256]{1,0:T(8,128)}, u32[]{:S(2)}) copy-start(f32[256,256]{1,0:T(8,128)} %copy-done.2) | copy-start | bytes 786436
  113.8 9.9 %collective-permute-start.7 = (f32[4,64,128]{2,1,0:T(8,128)}, f32[4,64,128]{2,1,0:T(8,128)}, u32[]{:S(2)}, u32[]{:S(2)}) collective-permute-start(f32[4,64,128]{2,1,0:T(8,128)} %pad_maximum_fusion.5), channel_id=1, source_target_pairs={{192,0},{193,1},{194,2},{195,3},{196,4},{197,5},{198,6},{199,7},{2... | collective-permute-start | bytes 393224 | tf_op jit(solution)/shard_map/ppermute | solution.py:85
  116.1 11.7 %collective-permute-start = (f32[2,128,256]{1,2,0:T(8,128)S(1)}, f32[2,128,256]{1,2,0:T(8,128)S(1)}, u32[]{:S(2)}, u32[]{:S(2)}) collective-permute-start(f32[2,128,256]{1,2,0:T(8,128)S(1)} %copy.103), channel_id=1, source_target_pairs={{192,0},{193,1},{194,2},{195,3},{196,4},{197,5},{198,6},{199,7},{2... | collective-permute-start | bytes 786440 | tf_op jit(solution)/shard_map/ppermute | solution.py:85
  117.7 8.6 %collective-permute-start.6 = (f32[2,64,128]{2,1,0:T(8,128)S(1)}, f32[2,64,128]{2,1,0:T(8,128)S(1)}, u32[]{:S(2)}, u32[]{:S(2)}) collective-permute-start(f32[2,64,128]{2,1,0:T(8,128)S(1)} %get-tuple-element.14), channel_id=1, source_target_pairs={{254,0},{255,1},{192,2},{193,3},{194,4},{195,5},{196,6},{197,7},{1... | collective-permute-start | bytes 196616 | tf_op jit(solution)/shard_map/ppermute | solution.py:85
  117.7 8.6 %collective-permute-start.8 = (f32[2,64,128]{2,1,0:T(8,128)S(1)}, f32[2,64,128]{2,1,0:T(8,128)S(1)}, u32[]{:S(2)}, u32[]{:S(2)}) collective-permute-start(f32[2,64,128]{2,1,0:T(8,128)S(1)} %get-tuple-element.14), channel_id=1, source_target_pairs={{194,0},{195,1},{196,2},{197,3},{198,4},{199,5},{200,6},{201,7},{2... | collective-permute-start | bytes 196616 | tf_op jit(solution)/shard_map/ppermute | solution.py:85
  128.6 6.7 %collective-permute-start.10 = (f32[2,64,128]{2,1,0:T(8,128)S(1)}, f32[2,64,128]{2,1,0:T(8,128)S(1)}, u32[]{:S(2)}, u32[]{:S(2)}) collective-permute-start(f32[2,64,128]{2,1,0:T(8,128)S(1)} %fusion.138), channel_id=1, source_target_pairs={{192,0},{193,1},{194,2},{195,3},{196,4},{197,5},{198,6},{199,7},{2... | collective-permute-start | bytes 196616 | tf_op jit(solution)/shard_map/ppermute | solution.py:85
  130.2 6.4 %collective-permute-start.11 = (f32[2,64,128]{2,1,0:T(8,128)S(1)}, f32[2,64,128]{2,1,0:T(8,128)S(1)}, u32[]{:S(2)}, u32[]{:S(2)}) collective-permute-start(f32[2,64,128]{2,1,0:T(8,128)S(1)} %fusion.138), channel_id=1, source_target_pairs={{194,0},{195,1},{196,2},{197,3},{198,4},{199,5},{200,6},{201,7},{2... | collective-permute-start | bytes 196616 | tf_op jit(solution)/shard_map/ppermute | solution.py:85
  134.8 8.5 %collective-permute-start.9 = (f32[2,64,128]{2,1,0:T(8,128)S(1)}, f32[2,64,128]{2,1,0:T(8,128)S(1)}, u32[]{:S(2)}, u32[]{:S(2)}) collective-permute-start(f32[2,64,128]{2,1,0:T(8,128)S(1)} %fusion.138), channel_id=1, source_target_pairs={{254,0},{255,1},{192,2},{193,3},{194,4},{195,5},{196,6},{197,7},{1... | collective-permute-start | bytes 196616 | tf_op jit(solution)/shard_map/ppermute | solution.py:85
  144.0 9.7 %collective-permute-start.12 = (f32[2,64,128]{2,1,0:T(8,128)S(1)}, f32[2,64,128]{2,1,0:T(8,128)S(1)}, u32[]{:S(2)}, u32[]{:S(2)}) collective-permute-start(f32[2,64,128]{2,1,0:T(8,128)S(1)} %fusion.143), channel_id=1, source_target_pairs={{254,0},{255,1},{192,2},{193,3},{194,4},{195,5},{196,6},{197,7},{1... | collective-permute-start | bytes 196616 | tf_op jit(solution)/shard_map/ppermute | solution.py:85
  144.1 9.6 %collective-permute-start.13 = (f32[2,64,128]{2,1,0:T(8,128)S(1)}, f32[2,64,128]{2,1,0:T(8,128)}, u32[]{:S(2)}, u32[]{:S(2)}) collective-permute-start(f32[2,64,128]{2,1,0:T(8,128)S(1)} %fusion.143), channel_id=1, source_target_pairs={{192,0},{193,1},{194,2},{195,3},{196,4},{197,5},{198,6},{199,7},{2... | collective-permute-start | bytes 196616 | tf_op jit(solution)/shard_map/ppermute | solution.py:85
  146.6 8.0 %collective-permute-start.14 = (f32[2,64,128]{2,1,0:T(8,128)S(1)}, f32[2,64,128]{2,1,0:T(8,128)}, u32[]{:S(2)}, u32[]{:S(2)}) collective-permute-start(f32[2,64,128]{2,1,0:T(8,128)S(1)} %fusion.143), channel_id=1, source_target_pairs={{194,0},{195,1},{196,2},{197,3},{198,4},{199,5},{200,6},{201,7},{2... | collective-permute-start | bytes 196616 | tf_op jit(solution)/shard_map/ppermute | solution.py:85
  155.9 0.7 copy-start.8
  155.9 0.7 copy-start.9
  155.9 0.7 copy-start.11
  155.9 0.7 copy-start.15
  156.1 1.0 copy-start.7
  156.1 1.0 copy-start.12
  156.1 1.0 copy-start.13
  156.2 1.0 copy-start.14

commit v13 on v12

--- a/solution.py
+++ b/solution.py
@@ -220,9 +220,10 @@
             items.append((coarse_two, (0, 1), (0, 1)))
         received = gather_bands(items, back=1)
         if previous_coarse_two is None:
+            previous_coarse_two = received[1]
+        if section == slices - 2:
             previous_two = fetch(values[2], 0, 1)
             previous_two, received = lax.optimization_barrier((previous_two, received))
-            previous_coarse_two = received[1]
         start = jnp.where(slot == 0, start_c, received[0])
     first, second = coarse_sweep(start, rates_c, sums_c)
     delta = jnp.stack(

time: 160 us -> 158 us (0.988)
  waiting for transfers between devices: 63.1 us -> 58.3 us
  starting transfers between devices: 57.6 us -> 59.8 us
    ppermute x10, waiting for transfers between devices: 12 us -> 7.99 us  [fetch(): return lax.ppermute(value, ('tm', 'space'), pairs)]
    ppermute x10, starting transfers between devices: 24 us -> 26.2 us  [fetch(): return lax.ppermute(value, ('tm', 'space'), pairs)]
    unnamed x46 -> x50, local copies, waits for them, and re-layouts: 4.99 us -> 5.04 us
  transfers between devices with their start and end apart: 19 -> 19, of which waited for: 12 -> 10; matrix products, arithmetic and copies ran while one was open for 5% -> 6% of each run, Pallas kernels for 0% -> 0%
where the time goes in v13:
time: 158 us; the launch traced here: 157 us
  starting transfers between devices  59.8 us (38%)
  waiting for transfers between devices  58.3 us (37%)
  local copies, waits for them, and re-layouts  15.6 us (10%)
  matrix products  13.8 us (9%)
  other arithmetic  7.73 us (5%)
  between operations  1.72 us (1%)
    all_to_all x4, waiting for transfers between devices, spectral_solve(): lax.all_to_all(field, 'space', split_axis=0, concat_axis=1, tiled=True)  45.8 us
    all_to_all x4, starting transfers between devices, spectral_solve(): lax.all_to_all(field, 'space', split_axis=0, concat_axis=1, tiled=True)  26.8 us
    ppermute x10, starting transfers between devices, fetch(): return lax.ppermute(value, ('tm', 'space'), pairs)  26.2 us
    ppermute x10, waiting for transfers between devices, fetch(): return lax.ppermute(value, ('tm', 'space'), pairs)  7.99 us
    ppermute x5, starting transfers between devices, fetch(): return lax.ppermute(value, 'space', pairs)  6.76 us
    unnamed x50, local copies, waits for them, and re-layouts  5.04 us
    ppermute x5, waiting for transfers between devices, fetch(): return lax.ppermute(value, 'space', pairs)  4.5 us
    dot_general x2, matrix products, spectral_solve(): jnp.dot(field.reshape(planes * size_y, size_z), basis_z, precision=TRANSF...  3.91 us
  transfers between devices with their start and end apart: 19, of which 10 were waited for; matrix products, arithmetic and copies ran while one was open for 6% of the time, Pallas kernels for 0%

profile of v13, /device:TPU:8, one launch (start us, length us, event | category | flops | bytes accessed | tf_op | source)
XLA Modules:
  0.0 157.0 jit_solution(18421028715148218580)
XLA Ops:
  0.7 1.4 copy.80
  2.2 0.3 copy.82
  2.6 1.6 %fusion.14 = f32[2,128,256]{2,1,0:T(8,128)S(1)} fusion(f32[3,2,128,256]{2,3,1,0:T(8,128)S(1)} %get-tuple-element.26, f32[1,3,2,128,256]{3,4,2,1,0:T(8,128)S(1)} %copy.82, f32[1,3,2,128,256]{3,4,2,1,0:T(8,128)S(1)} %copy.80, f32[256]{0:T(256)S(1)} %fusion.256, s32[256]{0:T(256)S(1)} %iota_add_fusion, pred[256]{0:T(512)(128)(4,1)S(1)} %iota_compare_fusion.6, ...), kind=kOutput, calls=%fused_computation.35 | convolution fusion | flops 102760448 | bytes 1837568 | tf_op jit(solution)/shard_map/dot_general | solution.py:47
  4.3 0.6 fusion.188
  4.8 0.9 copy.86
  5.7 11.9 %all-to-all-start = ((f32[128,2,256]{2,1,0:T(2,128)}), f32[128,2,256]{2,1,0:T(2,128)S(1)}, u32[]{:S(2)}, u32[]{:S(2)}) async-start(f32[128,2,256]{2,1,0:T(2,128)} %copy.86), calls=%async_computation | async-start | bytes 524288 | tf_op jit(solution)/shard_map/all_to_all | solution.py:50
  17.8 12.8 %all-to-all-done = f32[128,2,256]{2,1,0:T(2,128)S(1)} async-done(((f32[128,2,256]{2,1,0:T(2,128)}), f32[128,2,256]{2,1,0:T(2,128)S(1)}, u32[]{:S(2)}, u32[]{:S(2)}) %all-to-all-start) | async-done | bytes 262176 | tf_op jit(solution)/shard_map/all_to_all | solution.py:50
  30.8 0.6 convolution_multiply_fusion.1
  31.4 0.5 fusion.200
  31.9 0.9 copy.90
  32.8 4.9 %all-to-all-start.1 = ((f32[128,2,256]{2,1,0:T(2,128)}), f32[128,2,256]{2,1,0:T(2,128)S(1)}, u32[]{:S(2)}, u32[]{:S(2)}) async-start(f32[128,2,256]{2,1,0:T(2,128)} %copy.90), calls=%async_computation.1 | async-start | bytes 524288 | tf_op jit(solution)/shard_map/all_to_all | solution.py:53
  37.7 1.0 slice.656
  38.9 0.8 copy.95
  39.8 0.7 slice_bitcast_fusion.1
  40.5 0.9 copy.94
  41.4 9.3 %all-to-all-done.1 = f32[128,2,256]{2,1,0:T(2,128)S(1)} async-done(((f32[128,2,256]{2,1,0:T(2,128)}), f32[128,2,256]{2,1,0:T(2,128)S(1)}, u32[]{:S(2)}, u32[]{:S(2)}) %all-to-all-start.1) | async-done | bytes 262176 | tf_op jit(solution)/shard_map/all_to_all | solution.py:53
  50.9 0.5 fusion.198
  51.5 2.5 %fusion.23 = (f32[256,256]{1,0:T(8,128)S(1)}, f32[256,256]{1,0:T(8,128)S(1)}) fusion(f32[1,2,128,256]{3,2,1,0:T(8,128)} %copy.95, f32[1,1,2,128,256]{4,3,2,1,0:T(8,128)} %copy.94, f32[1,2,128,256]{3,2,1,0:T(8,128)S(1)} %copy.92, f32[256,256]{1,0:T(8,128)S(1)} %bitcast.217, f32[256]{0:T(256)S(1)} %fusion.256, s32[256]{0:T(256)S(1)} %iota_add_fusion, ...), kind=kOutput, calls=%fused_computation.43 | convolution fusion | flops 102301696 | bytes 1575168 | tf_op jit(solution)/shard_map/dot_general | solution.py:55
  54.0 1.5 fusion.48
  55.4 0.6 fusion.191
  56.0 0.9 copy.97
  56.9 5.1 %all-to-all-start.2 = ((f32[128,2,256]{2,1,0:T(2,128)}), f32[128,2,256]{2,1,0:T(2,128)S(1)}, u32[]{:S(2)}, u32[]{:S(2)}) async-start(f32[128,2,256]{2,1,0:T(2,128)} %copy.97), calls=%async_computation.2 | async-start | bytes 524288 | tf_op jit(solution)/shard_map/all_to_all | solution.py:50
  62.1 0.5 iota_and_fusion.1
  62.6 12.2 %all-to-all-done.2 = f32[128,2,256]{2,1,0:T(2,128)S(1)} async-done(((f32[128,2,256]{2,1,0:T(2,128)}), f32[128,2,256]{2,1,0:T(2,128)S(1)}, u32[]{:S(2)}, u32[]{:S(2)}) %all-to-all-start.2) | async-done | bytes 262176 | tf_op jit(solution)/shard_map/all_to_all | solution.py:50
  74.9 0.6 convolution_multiply_fusion
  75.5 0.5 fusion.196
  76.1 0.9 copy.101
  77.0 4.9 %all-to-all-start.3 = ((f32[128,2,256]{2,1,0:T(2,128)}), f32[128,2,256]{2,1,0:T(2,128)S(1)}, u32[]{:S(2)}, u32[]{:S(2)}) async-start(f32[128,2,256]{2,1,0:T(2,128)} %copy.101), calls=%async_computation.3 | async-start | bytes 524288 | tf_op jit(solution)/shard_map/all_to_all | solution.py:53
  81.9 0.6 iota_and_fusion
  82.5 0.7 slice_bitcast_fusion.2
  83.4 11.5 %all-to-all-done.3 = f32[128,2,256]{2,1,0:T(2,128)S(1)} async-done(((f32[128,2,256]{2,1,0:T(2,128)}), f32[128,2,256]{2,1,0:T(2,128)S(1)}, u32[]{:S(2)}, u32[]{:S(2)}) %all-to-all-start.3) | async-done | bytes 262176 | tf_op jit(solution)/shard_map/all_to_all | solution.py:53
  94.9 0.2 all_to_all.67
  95.1 0.5 fusion.194
  95.6 1.4 fusion.118
  97.0 0.7 copy-done.2
  97.9 1.4 fusion.30
  99.7 0.8 fusion.3
  100.5 0.2 fusion.225
  100.8 0.9 collective-permute-start.1
  101.8 4.6 %collective-permute-start.4 = (f32[3,64,128]{2,1,0:T(8,128)S(1)}, f32[3,64,128]{2,1,0:T(8,128)S(1)}, u32[]{:S(2)}, u32[]{:S(2)}) collective-permute-start(f32[3,64,128]{2,1,0:T(8,128)S(1)} %pad_maximum_fusion.6), channel_id=1, source_target_pairs={{2,0},{3,1},{4,2},{5,3},{6,4},{7,5},{8,6},{9,7},{10,8},{11,9},{12,... | collective-permute-start | bytes 294920 | tf_op jit(solution)/shard_map/ppermute | solution.py:78
  106.3 1.1 collective-permute-start.5
  107.4 0.6 collective-permute-done.1
  108.1 1.0 collective-permute-done.2
  109.3 2.8 %collective-permute-done.3 = f32[5,64,128]{2,1,0:T(8,128)S(1)} collective-permute-done((f32[5,64,128]{2,1,0:T(8,128)S(1)}, f32[5,64,128]{2,1,0:T(8,128)S(1)}, u32[]{:S(2)}, u32[]{:S(2)}) %collective-permute-start.3) | collective-permute-done | bytes 163872 | tf_op jit(solution)/shard_map/ppermute | solution.py:78
  113.2 1.7 %collective-permute-start.7 = (f32[4,64,128]{2,1,0:T(8,128)S(1)}, f32[4,64,128]{2,1,0:T(8,128)S(1)}, u32[]{:S(2)}, u32[]{:S(2)}) collective-permute-start(f32[4,64,128]{2,1,0:T(8,128)S(1)} %pad_maximum_fusion.5), channel_id=1, source_target_pairs={{192,0},{193,1},{194,2},{195,3},{196,4},{197,5},{198,6},{199,7},{2... | collective-permute-start | bytes 393224 | tf_op jit(solution)/shard_map/ppermute | solution.py:85
  114.8 0.5 compare_and_fusion.1
  115.4 0.4 collective-permute-start.6
  115.8 5.3 %collective-permute-start.8 = (f32[2,64,128]{2,1,0:T(8,128)S(1)}, f32[2,64,128]{2,1,0:T(8,128)S(1)}, u32[]{:S(2)}, u32[]{:S(2)}) collective-permute-start(f32[2,64,128]{2,1,0:T(8,128)S(1)} %get-tuple-element.12), channel_id=1, source_target_pairs={{194,0},{195,1},{196,2},{197,3},{198,4},{199,5},{200,6},{201,7},{2... | collective-permute-start | bytes 196616 | tf_op jit(solution)/shard_map/ppermute | solution.py:85
  121.1 2.7 %collective-permute-done.6 = f32[2,64,128]{2,1,0:T(8,128)S(1)} collective-permute-done((f32[2,64,128]{2,1,0:T(8,128)S(1)}, f32[2,64,128]{2,1,0:T(8,128)S(1)}, u32[]{:S(2)}, u32[]{:S(2)}) %collective-permute-start.6) | collective-permute-done | bytes 65568 | tf_op jit(solution)/shard_map/ppermute | solution.py:85
  124.7 1.4 collective-permute-start.10
  126.0 6.0 %collective-permute-start.11 = (f32[2,64,128]{2,1,0:T(8,128)S(1)}, f32[2,64,128]{2,1,0:T(8,128)S(1)}, u32[]{:S(2)}, u32[]{:S(2)}) collective-permute-start(f32[2,64,128]{2,1,0:T(8,128)S(1)} %fusion.138), channel_id=1, source_target_pairs={{194,0},{195,1},{196,2},{197,3},{198,4},{199,5},{200,6},{201,7},{2... | collective-permute-start | bytes 196616 | tf_op jit(solution)/shard_map/ppermute | solution.py:85
  132.0 0.6 compare_and_fusion
  132.6 0.8 copy.103
  133.5 2.8 %collective-permute-start = (f32[2,128,256]{1,2,0:T(8,128)}, f32[2,128,256]{1,2,0:T(8,128)}, u32[]{:S(2)}, u32[]{:S(2)}) collective-permute-start(f32[2,128,256]{1,2,0:T(8,128)} %copy.103), channel_id=1, source_target_pairs={{192,0},{193,1},{194,2},{195,3},{196,4},{197,5},{198,6},{199,7},{2... | collective-permute-start | bytes 786440 | tf_op jit(solution)/shard_map/ppermute | solution.py:85
  136.2 4.4 %collective-permute-done.9 = f32[2,64,128]{2,1,0:T(8,128)S(1)} collective-permute-done((f32[2,64,128]{2,1,0:T(8,128)S(1)}, f32[2,64,128]{2,1,0:T(8,128)S(1)}, u32[]{:S(2)}, u32[]{:S(2)}) %collective-permute-start.9) | collective-permute-done | bytes 65568 | tf_op jit(solution)/shard_map/ppermute | solution.py:85
  141.5 2.9 %collective-permute-start.13 = (f32[2,64,128]{2,1,0:T(8,128)S(1)}, f32[2,64,128]{2,1,0:T(8,128)S(1)}, u32[]{:S(2)}, u32[]{:S(2)}) collective-permute-start(f32[2,64,128]{2,1,0:T(8,128)S(1)} %fusion.143), channel_id=1, source_target_pairs={{192,0},{193,1},{194,2},{195,3},{196,4},{197,5},{198,6},{199,7},{2... | collective-permute-start | bytes 196616 | tf_op jit(solution)/shard_map/ppermute | solution.py:85
  144.3 5.7 %collective-permute-start.14 = (f32[2,64,128]{2,1,0:T(8,128)S(1)}, f32[2,64,128]{2,1,0:T(8,128)S(1)}, u32[]{:S(2)}, u32[]{:S(2)}) collective-permute-start(f32[2,64,128]{2,1,0:T(8,128)S(1)} %fusion.143), channel_id=1, source_target_pairs={{194,0},{195,1},{196,2},{197,3},{198,4},{199,5},{200,6},{201,7},{2... | collective-permute-start | bytes 196616 | tf_op jit(solution)/shard_map/ppermute | solution.py:85
  150.1 1.0 copy.128
  151.1 0.9 collective-permute-done.14
  152.8 0.3 copy-done.7
  153.2 0.6 fusion.62
  153.8 0.8 convolution_bitcast_fusion
  154.8 1.0 fusion.45
  155.9 1.1 copy.127
  (145 shorter events, 5.3 us)
Async XLA Ops:
  0.6 1.5 copy-start.5
  2.6 1.6 %copy-start = (f32[3,2,128,256]{2,3,1,0:T(8,128)}, f32[3,2,128,256]{2,3,1,0:T(8,128)S(1)}, u32[]{:S(2)}) copy-start(f32[3,2,128,256]{2,3,1,0:T(8,128)S(1)} %get-tuple-element.26) | copy-start | bytes 2359300
  5.7 24.9 %all-to-all-start = ((f32[128,2,256]{2,1,0:T(2,128)}), f32[128,2,256]{2,1,0:T(2,128)S(1)}, u32[]{:S(2)}, u32[]{:S(2)}) async-start(f32[128,2,256]{2,1,0:T(2,128)} %copy.86), calls=%async_computation | async-start | bytes 524288 | tf_op jit(solution)/shard_map/all_to_all | solution.py:50
  32.8 17.9 %all-to-all-start.1 = ((f32[128,2,256]{2,1,0:T(2,128)}), f32[128,2,256]{2,1,0:T(2,128)S(1)}, u32[]{:S(2)}, u32[]{:S(2)}) async-start(f32[128,2,256]{2,1,0:T(2,128)} %copy.90), calls=%async_computation.1 | async-start | bytes 524288 | tf_op jit(solution)/shard_map/all_to_all | solution.py:53
  56.9 17.9 %all-to-all-start.2 = ((f32[128,2,256]{2,1,0:T(2,128)}), f32[128,2,256]{2,1,0:T(2,128)S(1)}, u32[]{:S(2)}, u32[]{:S(2)}) async-start(f32[128,2,256]{2,1,0:T(2,128)} %copy.97), calls=%async_computation.2 | async-start | bytes 524288 | tf_op jit(solution)/shard_map/all_to_all | solution.py:50
  62.0 37.6 %copy-start.12 = (pred[256]{0:T(512)(128)(4,1)}, pred[256]{0:T(512)(128)(4,1)S(1)}, u32[]{:S(2)}) copy-start(pred[256]{0:T(512)(128)(4,1)S(1)} %compare_and_fusion.3) | copy-start | bytes 772
  77.0 17.9 %all-to-all-start.3 = ((f32[128,2,256]{2,1,0:T(2,128)}), f32[128,2,256]{2,1,0:T(2,128)S(1)}, u32[]{:S(2)}, u32[]{:S(2)}) async-start(f32[128,2,256]{2,1,0:T(2,128)} %copy.101), calls=%async_computation.3 | async-start | bytes 524288 | tf_op jit(solution)/shard_map/all_to_all | solution.py:53
  81.9 18.6 %copy-start.8 = (pred[128]{0:T(512)(128)(4,1)}, pred[128]{0:T(512)(128)(4,1)S(1)}, u32[]{:S(2)}) copy-start(pred[128]{0:T(512)(128)(4,1)S(1)} %compare_and_fusion.2) | copy-start | bytes 388
  97.0 0.7 copy-start.2
  97.9 1.5 copy-start.1
  97.9 1.5 copy-start.4
  100.8 7.3 %collective-permute-start.1 = (f32[1,64,128]{2,1,0:T(8,128)S(1)}, f32[1,64,128]{2,1,0:T(8,128)S(1)}, u32[]{:S(2)}, u32[]{:S(2)}) collective-permute-start(f32[1,64,128]{2,1,0:T(8,128)S(1)} %get-tuple-element.62), channel_id=1, source_target_pairs={{62,0},{63,1},{0,2},{1,3},{2,4},{3,5},{4,6},{5,7},{6,8},{7,9},{8,1... | collective-permute-start | bytes 98312 | tf_op jit(solution)/shard_map/ppermute | solution.py:78
  101.7 7.4 %collective-permute-start.2 = (f32[3,64,128]{2,1,0:T(8,128)S(1)}, f32[3,64,128]{2,1,0:T(8,128)S(1)}, u32[]{:S(2)}, u32[]{:S(2)}) collective-permute-start(f32[3,64,128]{2,1,0:T(8,128)S(1)} %pad_maximum_fusion.6), channel_id=1, source_target_pairs={{63,0},{0,1},{1,2},{2,3},{3,4},{4,5},{5,6},{6,7},{7,8},{8,9},{9,10... | collective-permute-start | bytes 294920 | tf_op jit(solution)/shard_map/ppermute | solution.py:78
  101.8 10.6 %collective-permute-start.4 = (f32[3,64,128]{2,1,0:T(8,128)S(1)}, f32[3,64,128]{2,1,0:T(8,128)S(1)}, u32[]{:S(2)}, u32[]{:S(2)}) collective-permute-start(f32[3,64,128]{2,1,0:T(8,128)S(1)} %pad_maximum_fusion.6), channel_id=1, source_target_pairs={{2,0},{3,1},{4,2},{5,3},{6,4},{7,5},{8,6},{9,7},{10,8},{11,9},{12,... | collective-permute-start | bytes 294920 | tf_op jit(solution)/shard_map/ppermute | solution.py:78
  106.3 6.3 %collective-permute-start.5 = (f32[1,64,128]{2,1,0:T(8,128)S(1)}, f32[1,64,128]{2,1,0:T(8,128)S(1)}, u32[]{:S(2)}, u32[]{:S(2)}) collective-permute-start(f32[1,64,128]{2,1,0:T(8,128)S(1)} %get-tuple-element.62), channel_id=1, source_target_pairs={{3,0},{4,1},{5,2},{6,3},{7,4},{8,5},{9,6},{10,7},{11,8},{12,9},{13... | collective-permute-start | bytes 98312 | tf_op jit(solution)/shard_map/ppermute | solution.py:78
  109.2 2.9 %collective-permute-start.3 = (f32[5,64,128]{2,1,0:T(8,128)S(1)}, f32[5,64,128]{2,1,0:T(8,128)S(1)}, u32[]{:S(2)}, u32[]{:S(2)}) collective-permute-start(f32[5,64,128]{2,1,0:T(8,128)S(1)} %constant_dynamic-update-slice_fusion.3), channel_id=1, source_target_pairs={{1,0},{2,1},{3,2},{4,3},{5,4},{6,5},{7,6},{8,7},{9,8},{10,9},{11,1... | collective-permute-start | bytes 491528 | tf_op jit(solution)/shard_map/ppermute | solution.py:78
  113.2 7.9 %collective-permute-start.7 = (f32[4,64,128]{2,1,0:T(8,128)S(1)}, f32[4,64,128]{2,1,0:T(8,128)S(1)}, u32[]{:S(2)}, u32[]{:S(2)}) collective-permute-start(f32[4,64,128]{2,1,0:T(8,128)S(1)} %pad_maximum_fusion.5), channel_id=1, source_target_pairs={{192,0},{193,1},{194,2},{195,3},{196,4},{197,5},{198,6},{199,7},{2... | collective-permute-start | bytes 393224 | tf_op jit(solution)/shard_map/ppermute | solution.py:85
  115.4 8.5 %collective-permute-start.6 = (f32[2,64,128]{2,1,0:T(8,128)S(1)}, f32[2,64,128]{2,1,0:T(8,128)S(1)}, u32[]{:S(2)}, u32[]{:S(2)}) collective-permute-start(f32[2,64,128]{2,1,0:T(8,128)S(1)} %get-tuple-element.12), channel_id=1, source_target_pairs={{254,0},{255,1},{192,2},{193,3},{194,4},{195,5},{196,6},{197,7},{1... | collective-permute-start | bytes 196616 | tf_op jit(solution)/shard_map/ppermute | solution.py:85
  115.8 8.1 %collective-permute-start.8 = (f32[2,64,128]{2,1,0:T(8,128)S(1)}, f32[2,64,128]{2,1,0:T(8,128)S(1)}, u32[]{:S(2)}, u32[]{:S(2)}) collective-permute-start(f32[2,64,128]{2,1,0:T(8,128)S(1)} %get-tuple-element.12), channel_id=1, source_target_pairs={{194,0},{195,1},{196,2},{197,3},{198,4},{199,5},{200,6},{201,7},{2... | collective-permute-start | bytes 196616 | tf_op jit(solution)/shard_map/ppermute | solution.py:85
  121.1 3.0 %copy-start.6 = (f32[4,64,128]{2,1,0:T(8,128)}, f32[4,64,128]{2,1,0:T(8,128)S(1)}, u32[]{:S(2)}) copy-start(f32[4,64,128]{2,1,0:T(8,128)S(1)} %collective-permute-done.7) | copy-start | bytes 393220
  124.1 8.5 %copy-start.3 = (f32[256,256]{1,0:T(8,128)S(1)}, f32[256,256]{1,0:T(8,128)}, u32[]{:S(2)}) copy-start(f32[256,256]{1,0:T(8,128)} %copy-done.2) | copy-start | bytes 786436
  124.7 11.6 %collective-permute-start.10 = (f32[2,64,128]{2,1,0:T(8,128)S(1)}, f32[2,64,128]{2,1,0:T(8,128)S(1)}, u32[]{:S(2)}, u32[]{:S(2)}) collective-permute-start(f32[2,64,128]{2,1,0:T(8,128)S(1)} %fusion.138), channel_id=1, source_target_pairs={{192,0},{193,1},{194,2},{195,3},{196,4},{197,5},{198,6},{199,7},{2... | collective-permute-start | bytes 196616 | tf_op jit(solution)/shard_map/ppermute | solution.py:85
  126.0 10.2 %collective-permute-start.11 = (f32[2,64,128]{2,1,0:T(8,128)S(1)}, f32[2,64,128]{2,1,0:T(8,128)S(1)}, u32[]{:S(2)}, u32[]{:S(2)}) collective-permute-start(f32[2,64,128]{2,1,0:T(8,128)S(1)} %fusion.138), channel_id=1, source_target_pairs={{194,0},{195,1},{196,2},{197,3},{198,4},{199,5},{200,6},{201,7},{2... | collective-permute-start | bytes 196616 | tf_op jit(solution)/shard_map/ppermute | solution.py:85
  132.0 8.6 %collective-permute-start.9 = (f32[2,64,128]{2,1,0:T(8,128)S(1)}, f32[2,64,128]{2,1,0:T(8,128)S(1)}, u32[]{:S(2)}, u32[]{:S(2)}) collective-permute-start(f32[2,64,128]{2,1,0:T(8,128)S(1)} %fusion.138), channel_id=1, source_target_pairs={{254,0},{255,1},{192,2},{193,3},{194,4},{195,5},{196,6},{197,7},{1... | collective-permute-start | bytes 196616 | tf_op jit(solution)/shard_map/ppermute | solution.py:85
  133.5 18.5 %collective-permute-start = (f32[2,128,256]{1,2,0:T(8,128)}, f32[2,128,256]{1,2,0:T(8,128)}, u32[]{:S(2)}, u32[]{:S(2)}) collective-permute-start(f32[2,128,256]{1,2,0:T(8,128)} %copy.103), channel_id=1, source_target_pairs={{192,0},{193,1},{194,2},{195,3},{196,4},{197,5},{198,6},{199,7},{2... | collective-permute-start | bytes 786440 | tf_op jit(solution)/shard_map/ppermute | solution.py:85
  141.4 9.7 %collective-permute-start.12 = (f32[2,64,128]{2,1,0:T(8,128)S(1)}, f32[2,64,128]{2,1,0:T(8,128)S(1)}, u32[]{:S(2)}, u32[]{:S(2)}) collective-permute-start(f32[2,64,128]{2,1,0:T(8,128)S(1)} %fusion.143), channel_id=1, source_target_pairs={{254,0},{255,1},{192,2},{193,3},{194,4},{195,5},{196,6},{197,7},{1... | collective-permute-start | bytes 196616 | tf_op jit(solution)/shard_map/ppermute | solution.py:85
  141.5 9.6 %collective-permute-start.13 = (f32[2,64,128]{2,1,0:T(8,128)S(1)}, f32[2,64,128]{2,1,0:T(8,128)S(1)}, u32[]{:S(2)}, u32[]{:S(2)}) collective-permute-start(f32[2,64,128]{2,1,0:T(8,128)S(1)} %fusion.143), channel_id=1, source_target_pairs={{192,0},{193,1},{194,2},{195,3},{196,4},{197,5},{198,6},{199,7},{2... | collective-permute-start | bytes 196616 | tf_op jit(solution)/shard_map/ppermute | solution.py:85
  144.3 7.6 %collective-permute-start.14 = (f32[2,64,128]{2,1,0:T(8,128)S(1)}, f32[2,64,128]{2,1,0:T(8,128)S(1)}, u32[]{:S(2)}, u32[]{:S(2)}) collective-permute-start(f32[2,64,128]{2,1,0:T(8,128)S(1)} %fusion.143), channel_id=1, source_target_pairs={{194,0},{195,1},{196,2},{197,3},{198,4},{199,5},{200,6},{201,7},{2... | collective-permute-start | bytes 196616 | tf_op jit(solution)/shard_map/ppermute | solution.py:85
  152.3 0.9 copy-start.7
  152.4 0.7 copy-start.10
  152.4 0.7 copy-start.11
  152.5 0.7 copy-start.13
  152.5 0.7 copy-start.17
  152.7 1.1 copy-start.9
  152.7 1.1 copy-start.14
  152.7 1.1 copy-start.15
  152.7 1.1 copy-start.16

commit v14 on v13

--- a/solution.py
+++ b/solution.py
@@ -216,10 +216,10 @@
     for section in range(slices - 1):
         first, second = coarse_sweep(start, rates_c, sums_c)
         items = [(second, (0, 1), (2, 3))]
-        if previous_coarse_two is None:
+        if section == slices - 2:
             items.append((coarse_two, (0, 1), (0, 1)))
         received = gather_bands(items, back=1)
-        if previous_coarse_two is None:
+        if section == slices - 2:
             previous_coarse_two = received[1]
         if section == slices - 2:
             previous_two = fetch(values[2], 0, 1)

time: 158 us -> 161 us (1.019)
  waiting for transfers between devices: 58.3 us -> 67.1 us
  starting transfers between devices: 59.8 us -> 57 us
    ppermute x5, waiting for transfers between devices: 4.5 us -> 11.6 us  [fetch(): return lax.ppermute(value, 'space', pairs)]
    ppermute x5, starting transfers between devices: 6.76 us -> 2.33 us  [fetch(): return lax.ppermute(value, 'space', pairs)]
    all_to_all x4, waiting for transfers between devices: 45.8 us -> 47.7 us  [spectral_solve(): lax.all_to_all(field, 'space', split_axis=0, concat_axis=1, tiled=True)]
    ppermute x10, starting transfers between devices: 26.2 us -> 27.9 us  [fetch(): return lax.ppermute(value, ('tm', 'space'), pairs)]
    unnamed x50 -> x23, local copies, waits for them, and re-layouts: 5.04 us -> 4.63 us
  transfers between devices with their start and end apart: 19 -> 19, of which waited for: 10 -> 12; matrix products, arithmetic and copies ran while one was open for 6% -> 5% of each run, Pallas kernels for 0% -> 0%
where the time goes in v14:
time: 161 us; the launch traced here: 160 us
  waiting for transfers between devices  67.1 us (42%)
  starting transfers between devices  57 us (35%)
  local copies, waits for them, and re-layouts  14.5 us (9%)
  matrix products  13.7 us (9%)
  other arithmetic  6.3 us (4%)
    all_to_all x4, waiting for transfers between devices, spectral_solve(): lax.all_to_all(field, 'space', split_axis=0, concat_axis=1, tiled=True)  47.7 us
    ppermute x10, starting transfers between devices, fetch(): return lax.ppermute(value, ('tm', 'space'), pairs)  27.9 us
    all_to_all x4, starting transfers between devices, spectral_solve(): lax.all_to_all(field, 'space', split_axis=0, concat_axis=1, tiled=True)  26.8 us
    ppermute x5, waiting for transfers between devices, fetch(): return lax.ppermute(value, 'space', pairs)  11.6 us
    ppermute x10, waiting for transfers between devices, fetch(): return lax.ppermute(value, ('tm', 'space'), pairs)  7.72 us
    unnamed x23, local copies, waits for them, and re-layouts  4.63 us
    dot_general x2, matrix products, spectral_solve(): jnp.dot(field.reshape(planes * size_y, size_z), basis_z, precision=TRANSF...  3.86 us
  transfers between devices with their start and end apart: 19, of which 12 were waited for; matrix products, arithmetic and copies ran while one was open for 5% of the time, Pallas kernels for 0%

profile of v14, /device:TPU:8, one launch (start us, length us, event | category | flops | bytes accessed | tf_op | source)
XLA Modules:
  0.0 160.2 jit_solution(3481636959842830356)
XLA Ops:
  0.7 1.4 copy.80
  2.2 0.3 copy.82
  2.4 0.2 bitcast_add_fusion
  2.6 1.6 %fusion.14 = f32[2,128,256]{2,1,0:T(8,128)S(1)} fusion(f32[3,2,128,256]{2,3,1,0:T(8,128)S(1)} %get-tuple-element.26, f32[1,3,2,128,256]{3,4,2,1,0:T(8,128)S(1)} %copy.82, f32[1,3,2,128,256]{3,4,2,1,0:T(8,128)S(1)} %copy.80, f32[256]{0:T(256)S(1)} %fusion.256, s32[256]{0:T(256)S(1)} %iota_add_fusion, pred[256]{0:T(512)(128)(4,1)S(1)} %iota_compare_fusion.6, ...), kind=kOutput, calls=%fused_computation.35 | convolution fusion | flops 102760448 | bytes 1837568 | tf_op jit(solution)/shard_map/dot_general | solution.py:47
  4.3 0.6 fusion.188
  4.8 0.9 copy.86
  5.7 11.9 %all-to-all-start = ((f32[128,2,256]{2,1,0:T(2,128)}), f32[128,2,256]{2,1,0:T(2,128)S(1)}, u32[]{:S(2)}, u32[]{:S(2)}) async-start(f32[128,2,256]{2,1,0:T(2,128)} %copy.86), calls=%async_computation | async-start | bytes 524288 | tf_op jit(solution)/shard_map/all_to_all | solution.py:50
  17.8 12.8 %all-to-all-done = f32[128,2,256]{2,1,0:T(2,128)S(1)} async-done(((f32[128,2,256]{2,1,0:T(2,128)}), f32[128,2,256]{2,1,0:T(2,128)S(1)}, u32[]{:S(2)}, u32[]{:S(2)}) %all-to-all-start) | async-done | bytes 262176 | tf_op jit(solution)/shard_map/all_to_all | solution.py:50
  30.8 0.6 convolution_multiply_fusion.1
  31.4 0.5 fusion.200
  31.9 0.9 copy.90
  32.8 4.9 %all-to-all-start.1 = ((f32[128,2,256]{2,1,0:T(2,128)}), f32[128,2,256]{2,1,0:T(2,128)S(1)}, u32[]{:S(2)}, u32[]{:S(2)}) async-start(f32[128,2,256]{2,1,0:T(2,128)} %copy.90), calls=%async_computation.1 | async-start | bytes 524288 | tf_op jit(solution)/shard_map/all_to_all | solution.py:53
  37.7 1.0 slice.656
  39.1 0.7 slice_bitcast_fusion.1
  39.8 0.8 copy.94
  40.6 10.1 %all-to-all-done.1 = f32[128,2,256]{2,1,0:T(2,128)S(1)} async-done(((f32[128,2,256]{2,1,0:T(2,128)}), f32[128,2,256]{2,1,0:T(2,128)S(1)}, u32[]{:S(2)}, u32[]{:S(2)}) %all-to-all-start.1) | async-done | bytes 262176 | tf_op jit(solution)/shard_map/all_to_all | solution.py:53
  50.7 0.2 all_to_all.59
  50.9 0.5 fusion.198
  51.5 2.4 %fusion.23 = (f32[256,256]{1,0:T(8,128)S(1)}, f32[256,256]{1,0:T(8,128)S(1)}) fusion(f32[1,2,128,256]{3,2,1,0:T(8,128)S(1)} %copy.95, f32[1,1,2,128,256]{4,3,2,1,0:T(8,128)} %copy.94, f32[1,2,128,256]{3,2,1,0:T(8,128)S(1)} %copy.92, f32[256,256]{1,0:T(8,128)S(1)} %bitcast.217, f32[256]{0:T(256)S(1)} %fusion.256, s32[256]{0:T(256)S(1)} %iota_add_fusion, ...), kind=kOutput, calls=%fused_computation.43 | convolution fusion | flops 102301696 | bytes 1575168 | tf_op jit(solution)/shard_map/dot_general | solution.py:55
  53.9 1.5 fusion.48
  55.4 0.6 fusion.191
  56.0 0.9 copy.97
  56.9 5.1 %all-to-all-start.2 = ((f32[128,2,256]{2,1,0:T(2,128)}), f32[128,2,256]{2,1,0:T(2,128)S(1)}, u32[]{:S(2)}, u32[]{:S(2)}) async-start(f32[128,2,256]{2,1,0:T(2,128)} %copy.97), calls=%async_computation.2 | async-start | bytes 524288 | tf_op jit(solution)/shard_map/all_to_all | solution.py:50
  62.0 12.8 %all-to-all-done.2 = f32[128,2,256]{2,1,0:T(2,128)S(1)} async-done(((f32[128,2,256]{2,1,0:T(2,128)}), f32[128,2,256]{2,1,0:T(2,128)S(1)}, u32[]{:S(2)}, u32[]{:S(2)}) %all-to-all-start.2) | async-done | bytes 262176 | tf_op jit(solution)/shard_map/all_to_all | solution.py:50
  74.9 0.6 convolution_multiply_fusion
  75.5 0.5 fusion.196
  76.0 0.9 copy.101
  76.9 4.9 %all-to-all-start.3 = ((f32[128,2,256]{2,1,0:T(2,128)}), f32[128,2,256]{2,1,0:T(2,128)S(1)}, u32[]{:S(2)}, u32[]{:S(2)}) async-start(f32[128,2,256]{2,1,0:T(2,128)} %copy.101), calls=%async_computation.3 | async-start | bytes 524288 | tf_op jit(solution)/shard_map/all_to_all | solution.py:53
  81.9 0.7 slice_bitcast_fusion.2
  82.7 12.1 %all-to-all-done.3 = f32[128,2,256]{2,1,0:T(2,128)S(1)} async-done(((f32[128,2,256]{2,1,0:T(2,128)}), f32[128,2,256]{2,1,0:T(2,128)S(1)}, u32[]{:S(2)}, u32[]{:S(2)}) %all-to-all-start.3) | async-done | bytes 262176 | tf_op jit(solution)/shard_map/all_to_all | solution.py:53
  94.8 0.2 all_to_all.67
  95.0 0.5 fusion.194
  95.6 1.4 fusion.118
  97.0 0.7 copy-done.2
  97.8 1.4 fusion.30
  99.6 0.8 fusion.3
  100.4 0.2 fusion.225
  100.7 0.9 collective-permute-start.1
  101.7 6.3 %collective-permute-done.1 = f32[1,64,128]{2,1,0:T(8,128)S(1)} collective-permute-done((f32[1,64,128]{2,1,0:T(8,128)S(1)}, f32[1,64,128]{2,1,0:T(8,128)S(1)}, u32[]{:S(2)}, u32[]{:S(2)}) %collective-permute-start.1) | collective-permute-done | bytes 32800 | tf_op jit(solution)/shard_map/ppermute | solution.py:78
  108.0 1.0 collective-permute-done.2
  109.2 1.3 collective-permute-start.4
  110.5 2.6 %collective-permute-done.3 = f32[5,64,128]{2,1,0:T(8,128)S(1)} collective-permute-done((f32[5,64,128]{2,1,0:T(8,128)S(1)}, f32[5,64,128]{2,1,0:T(8,128)S(1)}, u32[]{:S(2)}, u32[]{:S(2)}) %collective-permute-start.3) | collective-permute-done | bytes 163872 | tf_op jit(solution)/shard_map/ppermute | solution.py:78
  113.3 1.7 %collective-permute-done.4 = f32[3,64,128]{2,1,0:T(8,128)S(1)} collective-permute-done((f32[3,64,128]{2,1,0:T(8,128)S(1)}, f32[3,64,128]{2,1,0:T(8,128)S(1)}, u32[]{:S(2)}, u32[]{:S(2)}) %collective-permute-start.4) | collective-permute-done | bytes 98336 | tf_op jit(solution)/shard_map/ppermute | solution.py:78
  115.3 0.2 add_add_fusion
  115.6 0.2 fusion.132
  115.8 0.6 collective-permute-start.6
  116.4 1.3 collective-permute-start.7
  117.8 6.4 %collective-permute-start.8 = (f32[2,64,128]{2,1,0:T(8,128)S(1)}, f32[2,64,128]{2,1,0:T(8,128)S(1)}, u32[]{:S(2)}, u32[]{:S(2)}) collective-permute-start(f32[2,64,128]{2,1,0:T(8,128)S(1)} %get-tuple-element.12), channel_id=1, source_target_pairs={{194,0},{195,1},{196,2},{197,3},{198,4},{199,5},{200,6},{201,7},{2... | collective-permute-start | bytes 196616 | tf_op jit(solution)/shard_map/ppermute | solution.py:85
  124.2 0.8 collective-permute-done.6
  125.0 1.1 collective-permute-done.8
  126.8 0.7 collective-permute-start.10
  127.5 6.6 %collective-permute-start.11 = (f32[2,64,128]{2,1,0:T(8,128)S(1)}, f32[2,64,128]{2,1,0:T(8,128)S(1)}, u32[]{:S(2)}, u32[]{:S(2)}) collective-permute-start(f32[2,64,128]{2,1,0:T(8,128)S(1)} %fusion.138), channel_id=1, source_target_pairs={{194,0},{195,1},{196,2},{197,3},{198,4},{199,5},{200,6},{201,7},{2... | collective-permute-start | bytes 196616 | tf_op jit(solution)/shard_map/ppermute | solution.py:85
  134.1 0.8 copy.103
  134.9 2.8 %collective-permute-start = (f32[2,128,256]{1,2,0:T(8,128)}, f32[2,128,256]{1,2,0:T(8,128)}, u32[]{:S(2)}, u32[]{:S(2)}) collective-permute-start(f32[2,128,256]{1,2,0:T(8,128)} %copy.103), channel_id=1, source_target_pairs={{192,0},{193,1},{194,2},{195,3},{196,4},{197,5},{198,6},{199,7},{2... | collective-permute-start | bytes 786440 | tf_op jit(solution)/shard_map/ppermute | solution.py:85
  137.7 4.9 %collective-permute-done.9 = f32[2,64,128]{2,1,0:T(8,128)S(1)} collective-permute-done((f32[2,64,128]{2,1,0:T(8,128)S(1)}, f32[2,64,128]{2,1,0:T(8,128)S(1)}, u32[]{:S(2)}, u32[]{:S(2)}) %collective-permute-start.9) | collective-permute-done | bytes 65568 | tf_op jit(solution)/shard_map/ppermute | solution.py:85
  143.5 2.9 %collective-permute-start.13 = (f32[4,64,128]{2,1,0:T(8,128)S(1)}, f32[4,64,128]{2,1,0:T(8,128)S(1)}, u32[]{:S(2)}, u32[]{:S(2)}) collective-permute-start(f32[4,64,128]{2,1,0:T(8,128)S(1)} %pad_maximum_fusion.5), channel_id=1, source_target_pairs={{192,0},{193,1},{194,2},{195,3},{196,4},{197,5},{198,6},{199,7},{2... | collective-permute-start | bytes 393224 | tf_op jit(solution)/shard_map/ppermute | solution.py:85
  146.3 6.6 %collective-permute-start.14 = (f32[2,64,128]{2,1,0:T(8,128)S(1)}, f32[2,64,128]{2,1,0:T(8,128)}, u32[]{:S(2)}, u32[]{:S(2)}) collective-permute-start(f32[2,64,128]{2,1,0:T(8,128)S(1)} %fusion.143), channel_id=1, source_target_pairs={{194,0},{195,1},{196,2},{197,3},{198,4},{199,5},{200,6},{201,7},{2... | collective-permute-start | bytes 196616 | tf_op jit(solution)/shard_map/ppermute | solution.py:85
  153.0 1.0 copy.128
  154.0 0.8 collective-permute-done.12
  154.8 0.9 pad_maximum_fusion.1
  156.5 0.6 fusion.62
  157.1 0.8 convolution_bitcast_fusion
  158.0 1.0 fusion.45
  159.1 1.1 copy.127
  (121 shorter events, 4.6 us)
Async XLA Ops:
  0.6 1.5 copy-start.5
  2.6 1.6 %copy-start = (f32[3,2,128,256]{2,3,1,0:T(8,128)}, f32[3,2,128,256]{2,3,1,0:T(8,128)S(1)}, u32[]{:S(2)}) copy-start(f32[3,2,128,256]{2,3,1,0:T(8,128)S(1)} %get-tuple-element.26) | copy-start | bytes 2359300
  5.7 24.9 %all-to-all-start = ((f32[128,2,256]{2,1,0:T(2,128)}), f32[128,2,256]{2,1,0:T(2,128)S(1)}, u32[]{:S(2)}, u32[]{:S(2)}) async-start(f32[128,2,256]{2,1,0:T(2,128)} %copy.86), calls=%async_computation | async-start | bytes 524288 | tf_op jit(solution)/shard_map/all_to_all | solution.py:50
  32.8 17.9 %all-to-all-start.1 = ((f32[128,2,256]{2,1,0:T(2,128)}), f32[128,2,256]{2,1,0:T(2,128)S(1)}, u32[]{:S(2)}, u32[]{:S(2)}) async-start(f32[128,2,256]{2,1,0:T(2,128)} %copy.90), calls=%async_computation.1 | async-start | bytes 524288 | tf_op jit(solution)/shard_map/all_to_all | solution.py:53
  56.9 17.9 %all-to-all-start.2 = ((f32[128,2,256]{2,1,0:T(2,128)}), f32[128,2,256]{2,1,0:T(2,128)S(1)}, u32[]{:S(2)}, u32[]{:S(2)}) async-start(f32[128,2,256]{2,1,0:T(2,128)} %copy.97), calls=%async_computation.2 | async-start | bytes 524288 | tf_op jit(solution)/shard_map/all_to_all | solution.py:50
  76.9 17.9 %all-to-all-start.3 = ((f32[128,2,256]{2,1,0:T(2,128)}), f32[128,2,256]{2,1,0:T(2,128)S(1)}, u32[]{:S(2)}, u32[]{:S(2)}) async-start(f32[128,2,256]{2,1,0:T(2,128)} %copy.101), calls=%async_computation.3 | async-start | bytes 524288 | tf_op jit(solution)/shard_map/all_to_all | solution.py:53
  97.0 0.7 copy-start.2
  97.8 1.5 copy-start.1
  97.8 1.5 copy-start.4
  100.7 7.3 %collective-permute-start.1 = (f32[1,64,128]{2,1,0:T(8,128)S(1)}, f32[1,64,128]{2,1,0:T(8,128)S(1)}, u32[]{:S(2)}, u32[]{:S(2)}) collective-permute-start(f32[1,64,128]{2,1,0:T(8,128)S(1)} %get-tuple-element.60), channel_id=1, source_target_pairs={{62,0},{63,1},{0,2},{1,3},{2,4},{3,5},{4,6},{5,7},{6,8},{7,9},{8,1... | collective-permute-start | bytes 98312 | tf_op jit(solution)/shard_map/ppermute | solution.py:78
  101.6 7.4 %collective-permute-start.2 = (f32[3,64,128]{2,1,0:T(8,128)S(1)}, f32[3,64,128]{2,1,0:T(8,128)S(1)}, u32[]{:S(2)}, u32[]{:S(2)}) collective-permute-start(f32[3,64,128]{2,1,0:T(8,128)S(1)} %pad_maximum_fusion.6), channel_id=1, source_target_pairs={{63,0},{0,1},{1,2},{2,3},{3,4},{4,5},{5,6},{6,7},{7,8},{8,9},{9,10... | collective-permute-start | bytes 294920 | tf_op jit(solution)/shard_map/ppermute | solution.py:78
  109.1 4.0 %collective-permute-start.3 = (f32[5,64,128]{2,1,0:T(8,128)S(1)}, f32[5,64,128]{2,1,0:T(8,128)S(1)}, u32[]{:S(2)}, u32[]{:S(2)}) collective-permute-start(f32[5,64,128]{2,1,0:T(8,128)S(1)} %constant_dynamic-update-slice_fusion.3), channel_id=1, source_target_pairs={{1,0},{2,1},{3,2},{4,3},{5,4},{6,5},{7,6},{8,7},{9,8},{10,9},{11,1... | collective-permute-start | bytes 491528 | tf_op jit(solution)/shard_map/ppermute | solution.py:78
  109.2 5.7 %collective-permute-start.4 = (f32[3,64,128]{2,1,0:T(8,128)S(1)}, f32[3,64,128]{2,1,0:T(8,128)S(1)}, u32[]{:S(2)}, u32[]{:S(2)}) collective-permute-start(f32[3,64,128]{2,1,0:T(8,128)S(1)} %pad_maximum_fusion.6), channel_id=1, source_target_pairs={{2,0},{3,1},{4,2},{5,3},{6,4},{7,5},{8,6},{9,7},{10,8},{11,9},{12,... | collective-permute-start | bytes 294920 | tf_op jit(solution)/shard_map/ppermute | solution.py:78
  110.5 4.8 %collective-permute-start.5 = (f32[1,64,128]{2,1,0:T(8,128)S(1)}, f32[1,64,128]{2,1,0:T(8,128)S(1)}, u32[]{:S(2)}, u32[]{:S(2)}) collective-permute-start(f32[1,64,128]{2,1,0:T(8,128)S(1)} %get-tuple-element.60), channel_id=1, source_target_pairs={{3,0},{4,1},{5,2},{6,3},{7,4},{8,5},{9,6},{10,7},{11,8},{12,9},{13... | collective-permute-start | bytes 98312 | tf_op jit(solution)/shard_map/ppermute | solution.py:78
  115.8 9.2 %collective-permute-start.6 = (f32[2,64,128]{2,1,0:T(8,128)S(1)}, f32[2,64,128]{2,1,0:T(8,128)S(1)}, u32[]{:S(2)}, u32[]{:S(2)}) collective-permute-start(f32[2,64,128]{2,1,0:T(8,128)S(1)} %get-tuple-element.12), channel_id=1, source_target_pairs={{254,0},{255,1},{192,2},{193,3},{194,4},{195,5},{196,6},{197,7},{1... | collective-permute-start | bytes 196616 | tf_op jit(solution)/shard_map/ppermute | solution.py:85
  116.4 8.5 %collective-permute-start.7 = (f32[2,64,128]{2,1,0:T(8,128)S(1)}, f32[2,64,128]{2,1,0:T(8,128)S(1)}, u32[]{:S(2)}, u32[]{:S(2)}) collective-permute-start(f32[2,64,128]{2,1,0:T(8,128)S(1)} %get-tuple-element.12), channel_id=1, source_target_pairs={{192,0},{193,1},{194,2},{195,3},{196,4},{197,5},{198,6},{199,7},{2... | collective-permute-start | bytes 196616 | tf_op jit(solution)/shard_map/ppermute | solution.py:85
  117.8 8.3 %collective-permute-start.8 = (f32[2,64,128]{2,1,0:T(8,128)S(1)}, f32[2,64,128]{2,1,0:T(8,128)S(1)}, u32[]{:S(2)}, u32[]{:S(2)}) collective-permute-start(f32[2,64,128]{2,1,0:T(8,128)S(1)} %get-tuple-element.12), channel_id=1, source_target_pairs={{194,0},{195,1},{196,2},{197,3},{198,4},{199,5},{200,6},{201,7},{2... | collective-permute-start | bytes 196616 | tf_op jit(solution)/shard_map/ppermute | solution.py:85
  126.3 7.8 %copy-start.3 = (f32[256,256]{1,0:T(8,128)S(1)}, f32[256,256]{1,0:T(8,128)}, u32[]{:S(2)}) copy-start(f32[256,256]{1,0:T(8,128)} %copy-done.2) | copy-start | bytes 786436
  126.8 10.9 %collective-permute-start.10 = (f32[2,64,128]{2,1,0:T(8,128)S(1)}, f32[2,64,128]{2,1,0:T(8,128)S(1)}, u32[]{:S(2)}, u32[]{:S(2)}) collective-permute-start(f32[2,64,128]{2,1,0:T(8,128)S(1)} %fusion.138), channel_id=1, source_target_pairs={{192,0},{193,1},{194,2},{195,3},{196,4},{197,5},{198,6},{199,7},{2... | collective-permute-start | bytes 196616 | tf_op jit(solution)/shard_map/ppermute | solution.py:85
  127.5 10.2 %collective-permute-start.11 = (f32[2,64,128]{2,1,0:T(8,128)S(1)}, f32[2,64,128]{2,1,0:T(8,128)S(1)}, u32[]{:S(2)}, u32[]{:S(2)}) collective-permute-start(f32[2,64,128]{2,1,0:T(8,128)S(1)} %fusion.138), channel_id=1, source_target_pairs={{194,0},{195,1},{196,2},{197,3},{198,4},{199,5},{200,6},{201,7},{2... | collective-permute-start | bytes 196616 | tf_op jit(solution)/shard_map/ppermute | solution.py:85
  134.1 8.6 %collective-permute-start.9 = (f32[2,64,128]{2,1,0:T(8,128)S(1)}, f32[2,64,128]{2,1,0:T(8,128)S(1)}, u32[]{:S(2)}, u32[]{:S(2)}) collective-permute-start(f32[2,64,128]{2,1,0:T(8,128)S(1)} %fusion.138), channel_id=1, source_target_pairs={{254,0},{255,1},{192,2},{193,3},{194,4},{195,5},{196,6},{197,7},{1... | collective-permute-start | bytes 196616 | tf_op jit(solution)/shard_map/ppermute | solution.py:85
  134.9 20.7 %collective-permute-start = (f32[2,128,256]{1,2,0:T(8,128)}, f32[2,128,256]{1,2,0:T(8,128)}, u32[]{:S(2)}, u32[]{:S(2)}) collective-permute-start(f32[2,128,256]{1,2,0:T(8,128)} %copy.103), channel_id=1, source_target_pairs={{192,0},{193,1},{194,2},{195,3},{196,4},{197,5},{198,6},{199,7},{2... | collective-permute-start | bytes 786440 | tf_op jit(solution)/shard_map/ppermute | solution.py:85
  143.5 10.5 %collective-permute-start.13 = (f32[4,64,128]{2,1,0:T(8,128)S(1)}, f32[4,64,128]{2,1,0:T(8,128)S(1)}, u32[]{:S(2)}, u32[]{:S(2)}) collective-permute-start(f32[4,64,128]{2,1,0:T(8,128)S(1)} %pad_maximum_fusion.5), channel_id=1, source_target_pairs={{192,0},{193,1},{194,2},{195,3},{196,4},{197,5},{198,6},{199,7},{2... | collective-permute-start | bytes 393224 | tf_op jit(solution)/shard_map/ppermute | solution.py:85
  146.3 8.5 %collective-permute-start.12 = (f32[2,64,128]{2,1,0:T(8,128)S(1)}, f32[2,64,128]{2,1,0:T(8,128)S(1)}, u32[]{:S(2)}, u32[]{:S(2)}) collective-permute-start(f32[2,64,128]{2,1,0:T(8,128)S(1)} %fusion.143), channel_id=1, source_target_pairs={{254,0},{255,1},{192,2},{193,3},{194,4},{195,5},{196,6},{197,7},{1... | collective-permute-start | bytes 196616 | tf_op jit(solution)/shard_map/ppermute | solution.py:85
  146.3 8.5 %collective-permute-start.14 = (f32[2,64,128]{2,1,0:T(8,128)S(1)}, f32[2,64,128]{2,1,0:T(8,128)}, u32[]{:S(2)}, u32[]{:S(2)}) collective-permute-start(f32[2,64,128]{2,1,0:T(8,128)S(1)} %fusion.143), channel_id=1, source_target_pairs={{194,0},{195,1},{196,2},{197,3},{198,4},{199,5},{200,6},{201,7},{2... | collective-permute-start | bytes 196616 | tf_op jit(solution)/shard_map/ppermute | solution.py:85

commit v15 on v13

--- a/solution.py
+++ b/solution.py
@@ -222,8 +222,8 @@
         if previous_coarse_two is None:
             previous_coarse_two = received[1]
         if section == slices - 2:
-            previous_two = fetch(values[2], 0, 1)
-            previous_two, received = lax.optimization_barrier((previous_two, received))
+            previous_two, second = lax.optimization_barrier((values[2], second))
+            previous_two = fetch(previous_two, 0, 1)
         start = jnp.where(slot == 0, start_c, received[0])
     first, second = coarse_sweep(start, rates_c, sums_c)
     delta = jnp.stack(

time: 158 us -> 159 us (level)
  waiting for transfers between devices: 58.3 us -> 62.2 us
    ppermute x10, waiting for transfers between devices: 7.99 us -> 11.9 us  [fetch(): return lax.ppermute(value, ('tm', 'space'), pairs)]
  transfers between devices with their start and end apart: 19 -> 19, of which waited for: 10 -> 11; matrix products, arithmetic and copies ran while one was open for 6% -> 7% of each run, Pallas kernels for 0% -> 0%
where the time goes in v15:
time: 159 us; the launch traced here: 158 us
  waiting for transfers between devices  62.2 us (39%)
  starting transfers between devices  58.3 us (37%)
  local copies, waits for them, and re-layouts  14.9 us (9%)
  matrix products  13.8 us (9%)
  other arithmetic  7.53 us (5%)
  between operations  1.73 us (1%)
    all_to_all x4, waiting for transfers between devices, spectral_solve(): lax.all_to_all(field, 'space', split_axis=0, concat_axis=1, tiled=True)  45.9 us
    all_to_all x4, starting transfers between devices, spectral_solve(): lax.all_to_all(field, 'space', split_axis=0, concat_axis=1, tiled=True)  26.8 us
    ppermute x10, starting transfers between devices, fetch(): return lax.ppermute(value, ('tm', 'space'), pairs)  24.7 us
    ppermute x10, waiting for transfers between devices, fetch(): return lax.ppermute(value, ('tm', 'space'), pairs)  11.9 us
    ppermute x5, starting transfers between devices, fetch(): return lax.ppermute(value, 'space', pairs)  6.76 us
    unnamed x50, local copies, waits for them, and re-layouts  5.06 us
    ppermute x5, waiting for transfers between devices, fetch(): return lax.ppermute(value, 'space', pairs)  4.5 us
    dot_general x2, matrix products, spectral_solve(): jnp.dot(field.reshape(planes * size_y, size_z), basis_z, precision=TRANSF...  3.91 us
  transfers between devices with their start and end apart: 19, of which 11 were waited for; matrix products, arithmetic and copies ran while one was open for 7% of the time, Pallas kernels for 0%

profile of v15, /device:TPU:8, one launch (start us, length us, event | category | flops | bytes accessed | tf_op | source)
XLA Modules:
  0.0 158.5 jit_solution(2119237808369596995)
XLA Ops:
  0.7 1.4 copy.80
  2.2 0.3 copy.82
  2.6 1.6 %fusion.14 = f32[2,128,256]{2,1,0:T(8,128)S(1)} fusion(f32[3,2,128,256]{2,3,1,0:T(8,128)S(1)} %get-tuple-element.24, f32[1,3,2,128,256]{3,4,2,1,0:T(8,128)S(1)} %copy.82, f32[1,3,2,128,256]{3,4,2,1,0:T(8,128)S(1)} %copy.80, f32[256]{0:T(256)S(1)} %fusion.256, s32[256]{0:T(256)S(1)} %iota_add_fusion, pred[256]{0:T(512)(128)(4,1)S(1)} %iota_compare_fusion.6, ...), kind=kOutput, calls=%fused_computation.35 | convolution fusion | flops 102760448 | bytes 1837568 | tf_op jit(solution)/shard_map/dot_general | solution.py:47
  4.3 0.6 fusion.188
  4.8 0.9 copy.86
  5.7 11.9 %all-to-all-start = ((f32[128,2,256]{2,1,0:T(2,128)}), f32[128,2,256]{2,1,0:T(2,128)S(1)}, u32[]{:S(2)}, u32[]{:S(2)}) async-start(f32[128,2,256]{2,1,0:T(2,128)} %copy.86), calls=%async_computation | async-start | bytes 524288 | tf_op jit(solution)/shard_map/all_to_all | solution.py:50
  17.8 12.8 %all-to-all-done = f32[128,2,256]{2,1,0:T(2,128)S(1)} async-done(((f32[128,2,256]{2,1,0:T(2,128)}), f32[128,2,256]{2,1,0:T(2,128)S(1)}, u32[]{:S(2)}, u32[]{:S(2)}) %all-to-all-start) | async-done | bytes 262176 | tf_op jit(solution)/shard_map/all_to_all | solution.py:50
  30.8 0.6 convolution_multiply_fusion.1
  31.4 0.5 fusion.200
  31.9 0.9 copy.90
  32.8 4.9 %all-to-all-start.1 = ((f32[128,2,256]{2,1,0:T(2,128)}), f32[128,2,256]{2,1,0:T(2,128)S(1)}, u32[]{:S(2)}, u32[]{:S(2)}) async-start(f32[128,2,256]{2,1,0:T(2,128)} %copy.90), calls=%async_computation.1 | async-start | bytes 524288 | tf_op jit(solution)/shard_map/all_to_all | solution.py:53
  37.7 1.0 slice.656
  38.9 0.8 copy.95
  39.8 0.7 slice_bitcast_fusion.1
  40.5 0.9 copy.94
  41.4 9.3 %all-to-all-done.1 = f32[128,2,256]{2,1,0:T(2,128)S(1)} async-done(((f32[128,2,256]{2,1,0:T(2,128)}), f32[128,2,256]{2,1,0:T(2,128)S(1)}, u32[]{:S(2)}, u32[]{:S(2)}) %all-to-all-start.1) | async-done | bytes 262176 | tf_op jit(solution)/shard_map/all_to_all | solution.py:53
  50.7 0.2 all_to_all.59
  50.9 0.5 fusion.198
  51.5 2.5 %fusion.23 = (f32[256,256]{1,0:T(8,128)S(1)}, f32[256,256]{1,0:T(8,128)S(1)}) fusion(f32[1,2,128,256]{3,2,1,0:T(8,128)} %copy.95, f32[1,1,2,128,256]{4,3,2,1,0:T(8,128)} %copy.94, f32[1,2,128,256]{3,2,1,0:T(8,128)S(1)} %copy.92, f32[256,256]{1,0:T(8,128)S(1)} %bitcast.217, f32[256]{0:T(256)S(1)} %fusion.256, s32[256]{0:T(256)S(1)} %iota_add_fusion, ...), kind=kOutput, calls=%fused_computation.43 | convolution fusion | flops 102301696 | bytes 1575168 | tf_op jit(solution)/shard_map/dot_general | solution.py:55
  54.0 1.5 fusion.48
  55.4 0.6 fusion.191
  56.0 0.9 copy.97
  56.9 5.1 %all-to-all-start.2 = ((f32[128,2,256]{2,1,0:T(2,128)}), f32[128,2,256]{2,1,0:T(2,128)S(1)}, u32[]{:S(2)}, u32[]{:S(2)}) async-start(f32[128,2,256]{2,1,0:T(2,128)} %copy.97), calls=%async_computation.2 | async-start | bytes 524288 | tf_op jit(solution)/shard_map/all_to_all | solution.py:50
  62.1 0.6 iota_and_fusion.1
  62.7 12.2 %all-to-all-done.2 = f32[128,2,256]{2,1,0:T(2,128)S(1)} async-done(((f32[128,2,256]{2,1,0:T(2,128)}), f32[128,2,256]{2,1,0:T(2,128)S(1)}, u32[]{:S(2)}, u32[]{:S(2)}) %all-to-all-start.2) | async-done | bytes 262176 | tf_op jit(solution)/shard_map/all_to_all | solution.py:50
  74.9 0.6 convolution_multiply_fusion
  75.5 0.5 fusion.196
  76.1 0.9 copy.101
  77.0 4.9 %all-to-all-start.3 = ((f32[128,2,256]{2,1,0:T(2,128)}), f32[128,2,256]{2,1,0:T(2,128)S(1)}, u32[]{:S(2)}, u32[]{:S(2)}) async-start(f32[128,2,256]{2,1,0:T(2,128)} %copy.101), calls=%async_computation.3 | async-start | bytes 524288 | tf_op jit(solution)/shard_map/all_to_all | solution.py:53
  81.9 0.5 iota_and_fusion
  82.5 0.7 slice_bitcast_fusion.2
  83.3 11.5 %all-to-all-done.3 = f32[128,2,256]{2,1,0:T(2,128)S(1)} async-done(((f32[128,2,256]{2,1,0:T(2,128)}), f32[128,2,256]{2,1,0:T(2,128)S(1)}, u32[]{:S(2)}, u32[]{:S(2)}) %all-to-all-start.3) | async-done | bytes 262176 | tf_op jit(solution)/shard_map/all_to_all | solution.py:53
  94.9 0.2 all_to_all.67
  95.1 0.5 fusion.194
  95.6 1.4 fusion.118
  97.0 0.7 copy-done.2
  97.9 1.4 fusion.30
  99.7 0.8 fusion.3
  100.5 0.2 fusion.225
  100.8 0.9 collective-permute-start
  101.8 4.6 %collective-permute-start.3 = (f32[3,64,128]{2,1,0:T(8,128)S(1)}, f32[3,64,128]{2,1,0:T(8,128)S(1)}, u32[]{:S(2)}, u32[]{:S(2)}) collective-permute-start(f32[3,64,128]{2,1,0:T(8,128)S(1)} %pad_maximum_fusion.5), channel_id=1, source_target_pairs={{2,0},{3,1},{4,2},{5,3},{6,4},{7,5},{8,6},{9,7},{10,8},{11,9},{12,... | collective-permute-start | bytes 294920 | tf_op jit(solution)/shard_map/ppermute | solution.py:78
  106.4 1.1 collective-permute-start.4
  107.5 0.6 collective-permute-done
  108.1 1.0 collective-permute-done.1
  109.3 2.8 %collective-permute-done.2 = f32[5,64,128]{2,1,0:T(8,128)S(1)} collective-permute-done((f32[5,64,128]{2,1,0:T(8,128)S(1)}, f32[5,64,128]{2,1,0:T(8,128)S(1)}, u32[]{:S(2)}, u32[]{:S(2)}) %collective-permute-start.2) | collective-permute-done | bytes 163872 | tf_op jit(solution)/shard_map/ppermute | solution.py:78
  113.2 1.7 %collective-permute-start.6 = (f32[4,64,128]{2,1,0:T(8,128)S(1)}, f32[4,64,128]{2,1,0:T(8,128)S(1)}, u32[]{:S(2)}, u32[]{:S(2)}) collective-permute-start(f32[4,64,128]{2,1,0:T(8,128)S(1)} %pad_maximum_fusion.4), channel_id=1, source_target_pairs={{192,0},{193,1},{194,2},{195,3},{196,4},{197,5},{198,6},{199,7},{2... | collective-permute-start | bytes 393224 | tf_op jit(solution)/shard_map/ppermute | solution.py:85
  114.9 0.5 compare_and_fusion.1
  115.3 0.4 collective-permute-start.5
  115.7 5.3 %collective-permute-start.7 = (f32[2,64,128]{2,1,0:T(8,128)S(1)}, f32[2,64,128]{2,1,0:T(8,128)S(1)}, u32[]{:S(2)}, u32[]{:S(2)}) collective-permute-start(f32[2,64,128]{2,1,0:T(8,128)S(1)} %get-tuple-element.10), channel_id=1, source_target_pairs={{194,0},{195,1},{196,2},{197,3},{198,4},{199,5},{200,6},{201,7},{2... | collective-permute-start | bytes 196616 | tf_op jit(solution)/shard_map/ppermute | solution.py:85
  121.1 2.7 %collective-permute-done.5 = f32[2,64,128]{2,1,0:T(8,128)S(1)} collective-permute-done((f32[2,64,128]{2,1,0:T(8,128)S(1)}, f32[2,64,128]{2,1,0:T(8,128)S(1)}, u32[]{:S(2)}, u32[]{:S(2)}) %collective-permute-start.5) | collective-permute-done | bytes 65568 | tf_op jit(solution)/shard_map/ppermute | solution.py:85
  124.6 5.9 %collective-permute-start.10 = (f32[2,64,128]{2,1,0:T(8,128)S(1)}, f32[2,64,128]{2,1,0:T(8,128)S(1)}, u32[]{:S(2)}, u32[]{:S(2)}) collective-permute-start(f32[2,64,128]{2,1,0:T(8,128)S(1)} %fusion.138), channel_id=1, source_target_pairs={{194,0},{195,1},{196,2},{197,3},{198,4},{199,5},{200,6},{201,7},{2... | collective-permute-start | bytes 196616 | tf_op jit(solution)/shard_map/ppermute | solution.py:85
  130.5 1.5 collective-permute-start.9
  132.0 0.6 compare_and_fusion
  132.5 6.4 %collective-permute-done.8 = f32[2,64,128]{2,1,0:T(8,128)S(1)} collective-permute-done((f32[2,64,128]{2,1,0:T(8,128)S(1)}, f32[2,64,128]{2,1,0:T(8,128)S(1)}, u32[]{:S(2)}, u32[]{:S(2)}) %collective-permute-start.8) | collective-permute-done | bytes 65568 | tf_op jit(solution)/shard_map/ppermute | solution.py:85
  139.8 1.6 collective-permute-start.13
  141.4 8.2 %collective-permute-start.14 = (f32[2,64,128]{2,1,0:T(8,128)S(1)}, f32[2,64,128]{2,1,0:T(8,128)}, u32[]{:S(2)}, u32[]{:S(2)}) collective-permute-start(f32[2,64,128]{2,1,0:T(8,128)S(1)} %fusion.143), channel_id=1, source_target_pairs={{194,0},{195,1},{196,2},{197,3},{198,4},{199,5},{200,6},{201,7},{2... | collective-permute-start | bytes 196616 | tf_op jit(solution)/shard_map/ppermute | solution.py:85
  149.6 1.0 copy.128
  150.9 0.6 collective-permute-done.14
  151.5 0.9 maximum_select_fusion.2
  153.2 0.3 copy-done.7
  153.6 0.6 fusion.62
  154.2 0.8 convolution_bitcast_fusion
  155.1 2.1 %collective-permute-done.11 = f32[2,128,256]{1,2,0:T(8,128)S(1)} collective-permute-done((f32[2,128,256]{1,2,0:T(8,128)S(1)}, f32[2,128,256]{1,2,0:T(8,128)S(1)}, u32[]{:S(2)}, u32[]{:S(2)}) %collective-permute-start.11) | collective-permute-done | bytes 262176 | tf_op jit(solution)/shard_map/ppermute | solution.py:85
  157.3 1.1 copy.127
  (144 shorter events, 5.4 us)
Async XLA Ops:
  0.6 1.5 copy-start.5
  2.6 1.6 %copy-start = (f32[3,2,128,256]{2,3,1,0:T(8,128)}, f32[3,2,128,256]{2,3,1,0:T(8,128)S(1)}, u32[]{:S(2)}) copy-start(f32[3,2,128,256]{2,3,1,0:T(8,128)S(1)} %get-tuple-element.24) | copy-start | bytes 2359300
  5.7 24.9 %all-to-all-start = ((f32[128,2,256]{2,1,0:T(2,128)}), f32[128,2,256]{2,1,0:T(2,128)S(1)}, u32[]{:S(2)}, u32[]{:S(2)}) async-start(f32[128,2,256]{2,1,0:T(2,128)} %copy.86), calls=%async_computation | async-start | bytes 524288 | tf_op jit(solution)/shard_map/all_to_all | solution.py:50
  32.8 17.9 %all-to-all-start.1 = ((f32[128,2,256]{2,1,0:T(2,128)}), f32[128,2,256]{2,1,0:T(2,128)S(1)}, u32[]{:S(2)}, u32[]{:S(2)}) async-start(f32[128,2,256]{2,1,0:T(2,128)} %copy.90), calls=%async_computation.1 | async-start | bytes 524288 | tf_op jit(solution)/shard_map/all_to_all | solution.py:53
  56.9 17.9 %all-to-all-start.2 = ((f32[128,2,256]{2,1,0:T(2,128)}), f32[128,2,256]{2,1,0:T(2,128)S(1)}, u32[]{:S(2)}, u32[]{:S(2)}) async-start(f32[128,2,256]{2,1,0:T(2,128)} %copy.97), calls=%async_computation.2 | async-start | bytes 524288 | tf_op jit(solution)/shard_map/all_to_all | solution.py:50
  62.0 37.6 %copy-start.12 = (pred[256]{0:T(512)(128)(4,1)}, pred[256]{0:T(512)(128)(4,1)S(1)}, u32[]{:S(2)}) copy-start(pred[256]{0:T(512)(128)(4,1)S(1)} %compare_and_fusion.3) | copy-start | bytes 772
  77.0 17.9 %all-to-all-start.3 = ((f32[128,2,256]{2,1,0:T(2,128)}), f32[128,2,256]{2,1,0:T(2,128)S(1)}, u32[]{:S(2)}, u32[]{:S(2)}) async-start(f32[128,2,256]{2,1,0:T(2,128)} %copy.101), calls=%async_computation.3 | async-start | bytes 524288 | tf_op jit(solution)/shard_map/all_to_all | solution.py:53
  81.9 18.6 %copy-start.8 = (pred[128]{0:T(512)(128)(4,1)}, pred[128]{0:T(512)(128)(4,1)S(1)}, u32[]{:S(2)}) copy-start(pred[128]{0:T(512)(128)(4,1)S(1)} %compare_and_fusion.2) | copy-start | bytes 388
  97.0 0.7 copy-start.2
  97.9 1.5 copy-start.1
  97.9 1.5 copy-start.4
  100.8 7.3 %collective-permute-start = (f32[1,64,128]{2,1,0:T(8,128)S(1)}, f32[1,64,128]{2,1,0:T(8,128)S(1)}, u32[]{:S(2)}, u32[]{:S(2)}) collective-permute-start(f32[1,64,128]{2,1,0:T(8,128)S(1)} %get-tuple-element.60), channel_id=1, source_target_pairs={{62,0},{63,1},{0,2},{1,3},{2,4},{3,5},{4,6},{5,7},{6,8},{7,9},{8,1... | collective-permute-start | bytes 98312 | tf_op jit(solution)/shard_map/ppermute | solution.py:78
  101.7 7.4 %collective-permute-start.1 = (f32[3,64,128]{2,1,0:T(8,128)S(1)}, f32[3,64,128]{2,1,0:T(8,128)S(1)}, u32[]{:S(2)}, u32[]{:S(2)}) collective-permute-start(f32[3,64,128]{2,1,0:T(8,128)S(1)} %pad_maximum_fusion.5), channel_id=1, source_target_pairs={{63,0},{0,1},{1,2},{2,3},{3,4},{4,5},{5,6},{6,7},{7,8},{8,9},{9,10... | collective-permute-start | bytes 294920 | tf_op jit(solution)/shard_map/ppermute | solution.py:78
  101.8 10.6 %collective-permute-start.3 = (f32[3,64,128]{2,1,0:T(8,128)S(1)}, f32[3,64,128]{2,1,0:T(8,128)S(1)}, u32[]{:S(2)}, u32[]{:S(2)}) collective-permute-start(f32[3,64,128]{2,1,0:T(8,128)S(1)} %pad_maximum_fusion.5), channel_id=1, source_target_pairs={{2,0},{3,1},{4,2},{5,3},{6,4},{7,5},{8,6},{9,7},{10,8},{11,9},{12,... | collective-permute-start | bytes 294920 | tf_op jit(solution)/shard_map/ppermute | solution.py:78
  106.4 6.3 %collective-permute-start.4 = (f32[1,64,128]{2,1,0:T(8,128)S(1)}, f32[1,64,128]{2,1,0:T(8,128)S(1)}, u32[]{:S(2)}, u32[]{:S(2)}) collective-permute-start(f32[1,64,128]{2,1,0:T(8,128)S(1)} %get-tuple-element.60), channel_id=1, source_target_pairs={{3,0},{4,1},{5,2},{6,3},{7,4},{8,5},{9,6},{10,7},{11,8},{12,9},{13... | collective-permute-start | bytes 98312 | tf_op jit(solution)/shard_map/ppermute | solution.py:78
  109.2 2.9 %collective-permute-start.2 = (f32[5,64,128]{2,1,0:T(8,128)S(1)}, f32[5,64,128]{2,1,0:T(8,128)S(1)}, u32[]{:S(2)}, u32[]{:S(2)}) collective-permute-start(f32[5,64,128]{2,1,0:T(8,128)S(1)} %constant_dynamic-update-slice_fusion.3), channel_id=1, source_target_pairs={{1,0},{2,1},{3,2},{4,3},{5,4},{6,5},{7,6},{8,7},{9,8},{10,9},{11,1... | collective-permute-start | bytes 491528 | tf_op jit(solution)/shard_map/ppermute | solution.py:78
  113.2 7.9 %collective-permute-start.6 = (f32[4,64,128]{2,1,0:T(8,128)S(1)}, f32[4,64,128]{2,1,0:T(8,128)S(1)}, u32[]{:S(2)}, u32[]{:S(2)}) collective-permute-start(f32[4,64,128]{2,1,0:T(8,128)S(1)} %pad_maximum_fusion.4), channel_id=1, source_target_pairs={{192,0},{193,1},{194,2},{195,3},{196,4},{197,5},{198,6},{199,7},{2... | collective-permute-start | bytes 393224 | tf_op jit(solution)/shard_map/ppermute | solution.py:85
  115.3 8.5 %collective-permute-start.5 = (f32[2,64,128]{2,1,0:T(8,128)S(1)}, f32[2,64,128]{2,1,0:T(8,128)S(1)}, u32[]{:S(2)}, u32[]{:S(2)}) collective-permute-start(f32[2,64,128]{2,1,0:T(8,128)S(1)} %get-tuple-element.10), channel_id=1, source_target_pairs={{254,0},{255,1},{192,2},{193,3},{194,4},{195,5},{196,6},{197,7},{1... | collective-permute-start | bytes 196616 | tf_op jit(solution)/shard_map/ppermute | solution.py:85
  115.7 8.1 %collective-permute-start.7 = (f32[2,64,128]{2,1,0:T(8,128)S(1)}, f32[2,64,128]{2,1,0:T(8,128)S(1)}, u32[]{:S(2)}, u32[]{:S(2)}) collective-permute-start(f32[2,64,128]{2,1,0:T(8,128)S(1)} %get-tuple-element.10), channel_id=1, source_target_pairs={{194,0},{195,1},{196,2},{197,3},{198,4},{199,5},{200,6},{201,7},{2... | collective-permute-start | bytes 196616 | tf_op jit(solution)/shard_map/ppermute | solution.py:85
  121.1 2.8 %copy-start.6 = (f32[4,64,128]{2,1,0:T(8,128)}, f32[4,64,128]{2,1,0:T(8,128)S(1)}, u32[]{:S(2)}) copy-start(f32[4,64,128]{2,1,0:T(8,128)S(1)} %collective-permute-done.6) | copy-start | bytes 393220
  124.6 8.0 %collective-permute-start.10 = (f32[2,64,128]{2,1,0:T(8,128)S(1)}, f32[2,64,128]{2,1,0:T(8,128)S(1)}, u32[]{:S(2)}, u32[]{:S(2)}) collective-permute-start(f32[2,64,128]{2,1,0:T(8,128)S(1)} %fusion.138), channel_id=1, source_target_pairs={{194,0},{195,1},{196,2},{197,3},{198,4},{199,5},{200,6},{201,7},{2... | collective-permute-start | bytes 196616 | tf_op jit(solution)/shard_map/ppermute | solution.py:85
  130.5 8.5 %collective-permute-start.8 = (f32[2,64,128]{2,1,0:T(8,128)S(1)}, f32[2,64,128]{2,1,0:T(8,128)S(1)}, u32[]{:S(2)}, u32[]{:S(2)}) collective-permute-start(f32[2,64,128]{2,1,0:T(8,128)S(1)} %fusion.138), channel_id=1, source_target_pairs={{254,0},{255,1},{192,2},{193,3},{194,4},{195,5},{196,6},{197,7},{1... | collective-permute-start | bytes 196616 | tf_op jit(solution)/shard_map/ppermute | solution.py:85
  130.5 8.5 %collective-permute-start.9 = (f32[2,64,128]{2,1,0:T(8,128)S(1)}, f32[2,64,128]{2,1,0:T(8,128)S(1)}, u32[]{:S(2)}, u32[]{:S(2)}) collective-permute-start(f32[2,64,128]{2,1,0:T(8,128)S(1)} %fusion.138), channel_id=1, source_target_pairs={{192,0},{193,1},{194,2},{195,3},{196,4},{197,5},{198,6},{199,7},{2... | collective-permute-start | bytes 196616 | tf_op jit(solution)/shard_map/ppermute | solution.py:85
  139.6 11.1 %copy-start.3 = (f32[256,256]{1,0:T(8,128)S(1)}, f32[256,256]{1,0:T(8,128)}, u32[]{:S(2)}) copy-start(f32[256,256]{1,0:T(8,128)} %copy-done.2) | copy-start | bytes 786436
  139.7 11.1 %collective-permute-start.12 = (f32[2,64,128]{2,1,0:T(8,128)S(1)}, f32[2,64,128]{2,1,0:T(8,128)S(1)}, u32[]{:S(2)}, u32[]{:S(2)}) collective-permute-start(f32[2,64,128]{2,1,0:T(8,128)S(1)} %fusion.143), channel_id=1, source_target_pairs={{254,0},{255,1},{192,2},{193,3},{194,4},{195,5},{196,6},{197,7},{1... | collective-permute-start | bytes 196616 | tf_op jit(solution)/shard_map/ppermute | solution.py:85
  139.8 11.1 %collective-permute-start.13 = (f32[2,64,128]{2,1,0:T(8,128)S(1)}, f32[2,64,128]{2,1,0:T(8,128)S(1)}, u32[]{:S(2)}, u32[]{:S(2)}) collective-permute-start(f32[2,64,128]{2,1,0:T(8,128)S(1)} %fusion.143), channel_id=1, source_target_pairs={{192,0},{193,1},{194,2},{195,3},{196,4},{197,5},{198,6},{199,7},{2... | collective-permute-start | bytes 196616 | tf_op jit(solution)/shard_map/ppermute | solution.py:85
  141.4 10.1 %collective-permute-start.14 = (f32[2,64,128]{2,1,0:T(8,128)S(1)}, f32[2,64,128]{2,1,0:T(8,128)}, u32[]{:S(2)}, u32[]{:S(2)}) collective-permute-start(f32[2,64,128]{2,1,0:T(8,128)S(1)} %fusion.143), channel_id=1, source_target_pairs={{194,0},{195,1},{196,2},{197,3},{198,4},{199,5},{200,6},{201,7},{2... | collective-permute-start | bytes 196616 | tf_op jit(solution)/shard_map/ppermute | solution.py:85
  150.8 6.4 %collective-permute-start.11 = (f32[2,128,256]{1,2,0:T(8,128)S(1)}, f32[2,128,256]{1,2,0:T(8,128)S(1)}, u32[]{:S(2)}, u32[]{:S(2)}) collective-permute-start(f32[2,128,256]{1,2,0:T(8,128)S(1)} %copy.120), channel_id=1, source_target_pairs={{192,0},{193,1},{194,2},{195,3},{196,4},{197,5},{198,6},{199,7},{2... | collective-permute-start | bytes 786440 | tf_op jit(solution)/shard_map/ppermute | solution.py:85
  152.6 0.9 copy-start.7
  152.8 0.7 copy-start.10
  152.8 0.7 copy-start.11
  152.8 0.7 copy-start.13
  152.8 0.7 copy-start.17
  153.0 1.1 copy-start.9
  153.0 1.1 copy-start.14
  153.0 1.1 copy-start.15
  153.0 1.1 copy-start.16
